TPU v7x, 256 devices: a whole 4x4x8 slice. The times are simulated.
256 devices in a mesh: seq: 64 (over y_lo, x, z), chan: 4 (over y_hi, core).
Axes of the slice: x: 4, y: 4 (y_hi: 2, y_lo: 2; y = y_hi * 2 + y_lo), z: 8, core: 2. Of those that a mesh axis runs over, the one named last changes fastest.
Arguments:
- qkv: bfloat16 [3, 4096, 8192], P(None, 'chan', 'seq'), may hold values from -6 to 6
- taps: float32 [3, 3, 4096], P(None, None, 'chan'), may hold values from -3 to 3
- lifetimes: float32 [16, 4096], P(None, 'chan'), may hold values from 12 to 32768, as said below
- residues: float32 [16, 4096], P(None, 'chan'), may hold values from -1 to 1
- out_weight: bfloat16 [4096, 4096], P('chan'), may hold values from -0.09375 to 0.09375
Outputs:
- output: bfloat16 [4096, 8192], P('chan', 'seq')
Inputs may be any that keep to these rules, and one draw needn't show every extreme that they name: `lifetimes`: of every channel.
All inputs are finite; a program needn't handle non-finite values.
Results may differ from a plain program's by a relative error of at most 0.012.
Values may be sent and summed in bfloat16 or wider, within the bound.
No kernel may reach another device: no remote copies, remote signals or barrier semaphores. Data moves between devices by JAX's collectives and lax.ppermute only.
A program may use at most 128 MiB of HBM per device.

v0:
```python
import math

import jax
import jax.numpy as jnp
from jax import lax
from jax.sharding import PartitionSpec as P


def from_behind(x, axis, by):
    devices = lax.axis_size(axis)
    pairs = [(i, i + by) for i in range(devices) if 0 <= i + by < devices]
    return lax.ppermute(x, axis, pairs)


def angles(products, modulus):
    return 2.0 * math.pi / modulus * (products % modulus).astype(jnp.float32)


def filter_spectrum(life_slice, resid_slice, length, fft_rows, fft_cols):
    fft_size = 2 * length
    freq_index = (
        jnp.arange(fft_rows, dtype=jnp.int32)[:, None]
        + fft_rows * jnp.arange(fft_cols, dtype=jnp.int32)[None, :]
    )
    half_sine = jnp.sin(math.pi / fft_size * freq_index.astype(jnp.float32))
    full_sine = jnp.sin(angles(freq_index, fft_size))
    parity = 1.0 - 2.0 * (jnp.arange(fft_rows, dtype=jnp.int32)[:, None] % 2).astype(jnp.float32)

    def add_mode(mode_index, partial_value):
        spec_re, spec_im = partial_value
        life_mode = lax.dynamic_index_in_dim(life_slice, mode_index, 0, keepdims=False)[
            :, None, None
        ]
        resid_mode = lax.dynamic_index_in_dim(resid_slice, mode_index, 0, keepdims=False)[
            :, None, None
        ]
        inverse = 1.0 / life_mode
        decay = jnp.exp(-inverse)
        remain = -jnp.expm1(-inverse)
        tail_part = jnp.exp(-length * inverse)
        den_re = remain + 2.0 * decay * half_sine * half_sine
        den_im = decay * full_sine
        weight = resid_mode * (1.0 - tail_part * parity) / (den_re * den_re + den_im * den_im)
        return (spec_re + weight * den_re, spec_im - weight * den_im)

    zeros_init = jnp.zeros((life_slice.shape[1], fft_rows, fft_cols), jnp.float32)
    return lax.fori_loop(0, life_slice.shape[0], add_mode, (zeros_init, zeros_init))


def long_conv(pencils, life_slice, resid_slice):
    chan_here, length = pencils.shape
    fft_cols = 128
    fft_size = 2 * length
    fft_rows = fft_size // fft_cols
    used_rows = fft_rows // 2
    precise = lax.Precision.HIGH
    signal = pencils.astype(jnp.float32).reshape(chan_here, used_rows, fft_cols)
    outer_angle = angles(
        jnp.arange(fft_rows, dtype=jnp.int32)[:, None]
        * jnp.arange(used_rows, dtype=jnp.int32)[None, :],
        fft_rows,
    )
    cos_outer, sin_outer = (jnp.cos(outer_angle), jnp.sin(outer_angle))
    twist_angle = angles(
        jnp.arange(fft_rows, dtype=jnp.int32)[:, None]
        * jnp.arange(fft_cols, dtype=jnp.int32)[None, :],
        fft_size,
    )
    cos_twist, sin_twist = (jnp.cos(twist_angle), jnp.sin(twist_angle))
    inner_angle = angles(
        jnp.arange(fft_cols, dtype=jnp.int32)[:, None]
        * jnp.arange(fft_cols, dtype=jnp.int32)[None, :],
        fft_cols,
    )
    cos_inner, sin_inner = (jnp.cos(inner_angle), jnp.sin(inner_angle))
    first_re = jnp.einsum("kn,cnm->ckm", cos_outer, signal, precision=precise)
    first_im = -jnp.einsum("kn,cnm->ckm", sin_outer, signal, precision=precise)
    turned_re = first_re * cos_twist + first_im * sin_twist
    turned_im = first_im * cos_twist - first_re * sin_twist
    freq_re = jnp.dot(turned_re, cos_inner, precision=precise) + jnp.dot(
        turned_im, sin_inner, precision=precise
    )
    freq_im = jnp.dot(turned_im, cos_inner, precision=precise) - jnp.dot(
        turned_re, sin_inner, precision=precise
    )
    spec_re, spec_im = filter_spectrum(life_slice, resid_slice, length, fft_rows, fft_cols)
    prod_re = freq_re * spec_re - freq_im * spec_im
    prod_im = freq_re * spec_im + freq_im * spec_re
    back_re = jnp.dot(prod_re, cos_inner, precision=precise) - jnp.dot(
        prod_im, sin_inner, precision=precise
    )
    back_im = jnp.dot(prod_im, cos_inner, precision=precise) + jnp.dot(
        prod_re, sin_inner, precision=precise
    )
    undo_re = back_re * cos_twist - back_im * sin_twist
    undo_im = back_im * cos_twist + back_re * sin_twist
    result = (
        jnp.einsum("kn,ckm->cnm", cos_outer, undo_re, precision=precise)
        - jnp.einsum("kn,ckm->cnm", sin_outer, undo_im, precision=precise)
    ) / fft_size
    return result.reshape(chan_here, length)


def local(qkv, taps, lifetimes, residues, out_weight):
    chan_local = qkv.shape[1]
    tok_count = qkv.shape[2]
    edge_block = qkv[:, :, tok_count - 2 :]
    earlier = from_behind(edge_block, "seq", 1)
    extended = jnp.concatenate([earlier, qkv], axis=2).astype(jnp.float32)
    filtered = (
        taps[:, 0, :, None] * extended[:, :, 2:]
        + taps[:, 1, :, None] * extended[:, :, 1:-1]
        + taps[:, 2, :, None] * extended[:, :, :-2]
    )
    product = (filtered[1] * filtered[2]).astype(jnp.bfloat16)
    groups = lax.axis_size("seq")
    per_group = chan_local // groups
    pencils = lax.all_to_all(product, "seq", split_axis=0, concat_axis=1, tiled=True)
    first_chan = lax.axis_index("seq") * per_group
    life_slice = lax.dynamic_slice_in_dim(lifetimes, first_chan, per_group, 1)
    resid_slice = lax.dynamic_slice_in_dim(residues, first_chan, per_group, 1)
    convolved = long_conv(pencils, life_slice, resid_slice).astype(jnp.bfloat16)
    returned = lax.all_to_all(convolved, "seq", split_axis=1, concat_axis=0, tiled=True)
    gated_rows = (filtered[0] * returned.astype(jnp.float32)).astype(jnp.bfloat16)
    return lax.psum_scatter(
        lax.dot_general(
            out_weight, gated_rows, (((0,), (0,)), ((), ())), preferred_element_type=jnp.float32
        ).astype(jnp.bfloat16),
        "chan",
        scatter_dimension=0,
        tiled=True,
    )


def solution(mesh):
    placed = (
        P(None, "chan", "seq"),
        P(None, None, "chan"),
        P(None, "chan"),
        P(None, "chan"),
        P("chan", None),
    )
    return jax.shard_map(
        local, mesh=mesh, in_specs=placed, out_specs=P("chan", "seq"), check_vma=False
    )
```

profile of v0, /device:TPU:1, one launch (start us, length us, event | category | flops | bytes accessed | tf_op | source)
XLA Modules:
  0.0 140.5 jit_solution(13175586827502405312)
XLA Ops:
  6.5 1.5 %slice.31 = bf16[3,1024,2]{2,1,0:T(8,128)(2,1)S(1)} slice(bf16[3,1024,128]{2,1,0:T(8,128)(2,1)} %param.7), slice={[0:3], [0:1024], [126:128]} | slice | bytes 24576 | tf_op jit(solution)/shard_map/slice | solution.py:107
  8.3 4.4 %collective-permute-start = (bf16[3,1024,2]{1,2,0:T(2,128)(2,1)S(1)}, bf16[3,1024,2]{1,2,0:T(2,128)(2,1)S(1)}, u32[]{:S(2)}, u32[]{:S(2)}) collective-permute-start(bf16[3,1024,2]{1,2,0:T(2,128)(2,1)S(1)} %copy.64), channel_id=1, source_target_pairs={{0,4},{4,8},{8,12},{12,16},{16,20},{20,24},{24,28},{28,32},{32,36}... | collective-permute-start | bytes 36872 | tf_op jit(solution)/shard_map/ppermute | solution.py:12
  12.8 0.8 constant_dynamic-slice_fusion
  13.6 1.2 copy.35
  14.8 1.7 %maximum_convert_fusion = f32[3,1024,130]{2,1,0:T(8,128)S(1)} fusion(bf16[3,1024,128]{2,1,0:T(8,128)(2,1)S(1)} %copy-done.1, bf16[3,1024,2]{2,1,0:T(8,128)(2,1)} %copy.35), kind=kLoop, calls=%fused_computation.41 | loop fusion | flops 1597440 | bytes 2396160 | tf_op jit(solution)/shard_map/convert_element_type | solution.py:109
  16.6 2.4 %fusion.21 = f32[3,1024,128]{2,1,0:T(8,128)S(1)} fusion(f32[3,1024,130]{2,1,0:T(8,128)S(1)} %maximum_convert_fusion, f32[3,1024]{1,0:T(4,128)S(1)} %get-tuple-element.263, f32[3,1024]{1,0:T(4,128)S(1)} %get-tuple-element.264, f32[3,1024]{1,0:T(4,128)S(1)} %bitcast.91), kind=kLoop, calls=%fused_computation.37 | loop fusion | flops 1966080 | bytes 6328320 | tf_op jit(solution)/shard_map/add | solution.py:111
  18.9 1.2 copy-done
  20.1 0.8 fusion.34
  20.8 13.9 %all-to-all-start = ((bf16[64,16,128]{2,1,0:T(8,128)(2,1)}), bf16[64,16,128]{2,1,0:T(8,128)(2,1)S(1)}, u32[]{:S(2)}, u32[]{:S(2)}) async-start(bf16[64,16,128]{2,1,0:T(8,128)(2,1)} %bitcast.1), calls=%async_computation | async-start | bytes 524288 | tf_op jit(solution)/shard_map/all_to_all | solution.py:118
  34.8 24.5 %while.19 = (s32[]{:T(128)}, f32[16,128,128]{2,1,0:T(8,128)S(1)}, f32[16,128,128]{2,1,0:T(8,128)S(1)}, f32[16,16]{1,0:T(8,128)S(1)}, f32[16,16]{1,0:T(8,128)S(1)}, /*index=5*/s32[128]{0:T(128)S(1)}, s32[]{:T(128)}, s32[]{:T(128)}) while((s32[]{:T(128)}, f32[16,128,128]{2,1,0:T(8,128)S(1)}, ...), condition=%wide.region_1.2_spmd.clone.clone.clone.clone, body=%wide.region_0.1_spmd.clone.clone.clone.clone.sunk | while | flops 3939555 | bytes 4475439 | solution.py:47
  35.0 0.5 fusion.154
  35.4 0.9 fusion.156
  36.5 0.5 fusion.154
  36.9 0.9 fusion.156
  38.0 0.5 fusion.154
  38.5 0.9 fusion.156
  39.5 0.5 fusion.154
  40.0 0.9 fusion.156
  41.0 0.5 fusion.154
  41.5 0.9 fusion.156
  43.0 0.9 fusion.156
  44.5 0.9 fusion.156
  46.1 0.9 fusion.156
  47.6 0.9 fusion.156
  49.1 0.9 fusion.156
  50.6 0.9 fusion.156
  52.2 0.9 fusion.156
  53.7 0.9 fusion.156
  55.2 0.9 fusion.156
  56.7 0.9 fusion.156
  58.2 0.9 fusion.156
  60.0 0.6 fusion.23
  60.6 0.6 convolution_bitcast_fusion
  61.2 1.2 fusion.42
  62.5 1.2 fusion.41
  63.7 1.2 convolution_add_fusion.1
  64.9 1.4 multiply_subtract_fusion
  66.3 0.8 fusion.57
  67.2 0.8 fusion.55
  68.0 0.9 convolution_subtract_fusion
  68.9 0.9 convolution_add_fusion
  69.8 0.8 fusion.30
  70.6 0.8 fusion.26
  71.6 21.5 %all_to_all.23 = bf16[16,64,128]{2,0,1:T(8,128)(2,1)S(1)} all-to-all(bf16[16,64,128]{2,0,1:T(8,128)(2,1)S(1)} %copy.49), channel_id=1, replica_groups=mesh['seq'=64,'chan'=4] {'seq'}, dimensions={1} | all-to-all | bytes 524288 | tf_op jit(solution)/shard_map/all_to_all | solution.py:123
  93.2 1.1 fusion.36
  94.3 2.3 %fusion.20 = bf16[4096,128]{0,1:T(8,128)(2,1)} fusion(bf16[1024,128]{1,0:T(8,128)(2,1)S(1)} %fusion.36, bf16[1024,4096]{1,0:T(8,128)(2,1)S(1)} %bitcast.90), kind=kOutput, calls=%fused_computation.35 | convolution fusion | flops 1074266112 | bytes 9699328 | tf_op jit(solution)/shard_map/dot_general | solution.py:126
  96.6 35.2 %reduce-scatter.2.cloned.1.call-done = bf16[1024,128]{0,1:T(8,128)(2,1)} async-done(((bf16[4096,128]{0,1:T(8,128)(2,1)}), bf16[1024,128]{0,1:T(8,128)(2,1)}) %reduce-scatter.2.cloned.1.call-update) | async-done | bytes 262160 | tf_op jit(solution)/shard_map/reduce_scatter | solution.py:125
  131.9 1.8 %copy.50 = bf16[1024,128]{1,0:T(8,128)(2,1)} copy(bf16[1024,128]{0,1:T(8,128)(2,1)} %reduce-scatter.2.cloned.1.call-done) | data formatting | bytes 524288 | tf_op jit(solution)/shard_map/reduce_scatter | solution.py:125
  (133 shorter events, 8.5 us)
Async XLA Ops:
  6.5 8.3 %copy-start.1 = (bf16[3,1024,128]{2,1,0:T(8,128)(2,1)S(1)}, bf16[3,1024,128]{2,1,0:T(8,128)(2,1)}, u32[]{:S(2)}) copy-start(bf16[3,1024,128]{2,1,0:T(8,128)(2,1)} %param.7) | copy-start | bytes 2359300
  6.5 6.2 %copy-start.2 = (f32[3,3,1024]{2,1,0:T(4,128)S(1)}, f32[3,3,1024]{2,1,0:T(4,128)}, u32[]{:S(2)}) copy-start(f32[3,3,1024]{2,1,0:T(4,128)} %param.8) | copy-start | bytes 110596
  8.3 5.2 %collective-permute-start = (bf16[3,1024,2]{1,2,0:T(2,128)(2,1)S(1)}, bf16[3,1024,2]{1,2,0:T(2,128)(2,1)S(1)}, u32[]{:S(2)}, u32[]{:S(2)}) collective-permute-start(bf16[3,1024,2]{1,2,0:T(2,128)(2,1)S(1)} %copy.64), channel_id=1, source_target_pairs={{0,4},{4,8},{8,12},{12,16},{16,20},{20,24},{24,28},{28,32},{32,36}... | collective-permute-start | bytes 36872 | tf_op jit(solution)/shard_map/ppermute | solution.py:12
  18.9 1.2 copy-start
  20.8 39.2 %all-to-all-start = ((bf16[64,16,128]{2,1,0:T(8,128)(2,1)}), bf16[64,16,128]{2,1,0:T(8,128)(2,1)S(1)}, u32[]{:S(2)}, u32[]{:S(2)}) async-start(bf16[64,16,128]{2,1,0:T(8,128)(2,1)} %bitcast.1), calls=%async_computation | async-start | bytes 524288 | tf_op jit(solution)/shard_map/all_to_all | solution.py:118
  34.7 97.1 %reduce-scatter.2.cloned.1.call-start = ((), (), s32[]{:S(2)}) async-start(), calls=%async_computation.3 | async-start | bytes 1310720 | tf_op jit(solution)/shard_map/reduce_scatter | solution.py:125
  67.2 27.1 %slice-start = ((s8[8388608]{0:T(1024)(128)(4,1)}), s8[4194304]{0:T(1024)(128)(4,1)S(1)}, s32[]{:S(2)}) async-start(s8[8388608]{0:T(1024)(128)(4,1)} %bitcast.89), calls=%async_computation.4 | async-start | bytes 8388608
  68.9 25.4 %slice-start.1 = ((s8[8388608]{0:T(1024)(128)(4,1)}), s8[4194304]{0:T(1024)(128)(4,1)S(1)}, s32[]{:S(2)}) async-start(s8[8388608]{0:T(1024)(128)(4,1)} %bitcast.89), calls=%async_computation.5 | async-start | bytes 8388608
Sparse Core Ops, SparseCore 0:
  96.7 35.0 reduce-scatter.1
where the time goes:
time: 141 us; the launch traced here: 140 us
  waiting for transfers between devices  35.3 us (25%)
  other arithmetic  29.6 us (21%)
  blocking collectives  21.5 us (15%)
  starting transfers between devices  18.3 us (13%)
  between operations  13.7 us (10%)
  matrix products  13.6 us (10%)
  local copies, waits for them, and re-layouts  7.39 us (5%)
    reduce_scatter x1, waiting for transfers between devices, local(): lax.psum_scatter(lax.dot_general(out_weight, gated_rows, (((0,), (0,)), (...  35.2 us
    all_to_all x1, blocking collectives, local(): lax.all_to_all(convolved, 'seq', split_axis=1, concat_axis=0, tiled=True)  21.5 us
    all_to_all x1, starting transfers between devices, local(): lax.all_to_all(product, 'seq', split_axis=0, concat_axis=1, tiled=True)  13.9 us
    sub x16, other arithmetic, add_mode(): return (spec_re + weight * den_re, spec_im - weight * den_im)  13.8 us
    sin x16, other arithmetic, filter_spectrum(): full_sine = jnp.sin(angles(freq_index, fft_size))  7.49 us
    ppermute x1, starting transfers between devices, from_behind(): return lax.ppermute(x, axis, pairs)  4.36 us
  transfers between devices with their start and end apart: 3, of which 1 were waited for; matrix products, arithmetic and copies ran while one was open for 18% of the time, Pallas kernels for 0%

commit v1 on v0

v1 whole, which is shorter than its diff:
```python
import jax
import jax.numpy as jnp
from jax import lax
from jax.sharding import PartitionSpec as P


def from_behind(x, axis, by):
    devices = lax.axis_size(axis)
    pairs = [(i, i + by) for i in range(devices) if 0 <= i + by < devices]
    return lax.ppermute(x, axis, pairs)


def chunk_conv(product, lifetimes, residues):
    chan_here, tok = product.shape
    inv = 1.0 / lifetimes
    mid = tok // 2
    offs = (jnp.arange(tok, dtype=jnp.int32) - mid).astype(jnp.float32)
    grow = jnp.exp(offs[None, None, :] * inv[:, :, None])
    weighted = grow * product[None]
    upper = (
        jnp.arange(tok, dtype=jnp.int32)[:, None] <= jnp.arange(tok, dtype=jnp.int32)[None, :]
    ).astype(jnp.float32)
    sums = jnp.dot(weighted, upper, precision=lax.Precision.HIGH)
    decay = jnp.exp(-offs[None, None, :] * inv[:, :, None])
    local_part = jnp.sum(residues[:, :, None] * decay * sums, axis=0)
    state = jnp.exp(-float(tok - 1 - mid) * inv) * sums[:, :, tok - 1]

    seq_n = lax.axis_size("seq")
    inclusive = state
    exclusive = jnp.zeros_like(state)
    dist = 1
    while dist < seq_n:
        got = from_behind(inclusive, "seq", dist)
        exclusive = exclusive + jnp.exp(-float(tok * (dist - 1)) * inv) * got
        if 2 * dist < seq_n:
            inclusive = inclusive + jnp.exp(-float(tok * dist) * inv) * got
        dist *= 2

    steps = (jnp.arange(tok, dtype=jnp.int32) + 1).astype(jnp.float32)
    carried = jnp.sum(
        (residues * exclusive)[:, :, None] * jnp.exp(-steps[None, None, :] * inv[:, :, None]),
        axis=0,
    )
    return local_part + carried


def local(qkv, taps, lifetimes, residues, out_weight):
    tok_count = qkv.shape[2]
    edge_block = qkv[:, :, tok_count - 2 :]
    earlier = from_behind(edge_block, "seq", 1)
    extended = jnp.concatenate([earlier, qkv], axis=2).astype(jnp.float32)
    filtered = (
        taps[:, 0, :, None] * extended[:, :, 2:]
        + taps[:, 1, :, None] * extended[:, :, 1:-1]
        + taps[:, 2, :, None] * extended[:, :, :-2]
    )
    product = (filtered[1] * filtered[2]).astype(jnp.bfloat16).astype(jnp.float32)
    convolved = chunk_conv(product, lifetimes, residues).astype(jnp.bfloat16)
    gated_rows = (filtered[0] * convolved.astype(jnp.float32)).astype(jnp.bfloat16)
    return lax.psum_scatter(
        lax.dot_general(
            out_weight, gated_rows, (((0,), (0,)), ((), ())), preferred_element_type=jnp.float32
        ).astype(jnp.bfloat16),
        "chan",
        scatter_dimension=0,
        tiled=True,
    )


def solution(mesh):
    placed = (
        P(None, "chan", "seq"),
        P(None, None, "chan"),
        P(None, "chan"),
        P(None, "chan"),
        P("chan", None),
    )
    return jax.shard_map(
        local, mesh=mesh, in_specs=placed, out_specs=P("chan", "seq"), check_vma=False
    )
```

time: 141 us -> 131 us (0.929)
  starting transfers between devices: 18.3 us -> 51 us
  other arithmetic: 29.6 us -> 5.25 us
  blocking collectives: 21.5 us -> 0 us
  waiting for transfers between devices: 35.3 us -> 46.8 us
  matrix products: 13.6 us -> 7.3 us
    ppermute x1 -> x7, starting transfers between devices: 4.36 us -> 51 us  [from_behind(): return lax.ppermute(x, axis, pairs)]
    all_to_all x1 -> x0, blocking collectives: 21.5 us -> none  [local(): lax.all_to_all(convolved, 'seq', split_axis=1, concat_axis=0, tiled=True)]
    all_to_all x1 -> x0, starting transfers between devices: 13.9 us -> none  [local(): lax.all_to_all(product, 'seq', split_axis=0, concat_axis=1, tiled=True)]
    sub x16 -> x0, other arithmetic: 13.8 us -> none  [add_mode(): return (spec_re + weight * den_re, spec_im - weight * den_im)]
    ppermute x1 -> x7, waiting for transfers between devices: 0.01 us -> 8.44 us  [from_behind(): return lax.ppermute(x, axis, pairs)]
    sin x17 -> x0, other arithmetic: 7.76 us -> none  [the longest x16 7.49 us: filter_spectrum(): full_sine = jnp.sin(angles(freq_index, fft_size))]
    dot_general x12 -> x1, matrix products: 11.3 us -> 5 us  [chunk_conv(): sums = jnp.dot(weighted, upper, precision=lax.Precision.HIGH)]
    reduce_sum x0 -> x1, other arithmetic: none -> 3.35 us  [chunk_conv(): jnp.sum((residues * exclusive)[:, :, None] * jnp.exp(-steps[None, None, :...]
  transfers between devices with their start and end apart: 3 -> 8, of which waited for: 1 -> 7; matrix products, arithmetic and copies ran while one was open for 18% -> 2% of each run, Pallas kernels for 0% -> 0%
where the time goes in v1:
time: 131 us; the launch traced here: 130 us
  starting transfers between devices  51 us (39%)
  waiting for transfers between devices  46.8 us (36%)
  between operations  13.6 us (10%)
  matrix products  7.3 us (6%)
  local copies, waits for them, and re-layouts  6.05 us (5%)
  other arithmetic  5.25 us (4%)
    ppermute x7, starting transfers between devices, from_behind(): return lax.ppermute(x, axis, pairs)  51 us
    reduce_scatter x1, waiting for transfers between devices, local(): lax.psum_scatter(lax.dot_general(out_weight, gated_rows, (((0,), (0,)), (...  38.4 us
    ppermute x7, waiting for transfers between devices, from_behind(): return lax.ppermute(x, axis, pairs)  8.44 us
    dot_general x1, matrix products, chunk_conv(): sums = jnp.dot(weighted, upper, precision=lax.Precision.HIGH)  5 us
    reduce_sum x1, other arithmetic, chunk_conv(): jnp.sum((residues * exclusive)[:, :, None] * jnp.exp(-steps[None, None, :...  3.35 us
  transfers between devices with their start and end apart: 8, of which 7 were waited for; matrix products, arithmetic and copies ran while one was open for 2% of the time, Pallas kernels for 0%

profile of v1, /device:TPU:1, one launch (start us, length us, event | category | flops | bytes accessed | tf_op | source)
XLA Modules:
  0.0 130.1 jit_solution(12438599793332560898)
XLA Ops:
  6.5 0.0 reduce-scatter.2.cloned.1.call-start
  6.5 1.4 %slice.34 = bf16[3,1024,2]{2,1,0:T(8,128)(2,1)S(1)} slice(bf16[3,1024,128]{2,1,0:T(8,128)(2,1)} %param.5), slice={[0:3], [0:1024], [126:128]} | slice | bytes 24576 | tf_op jit(solution)/shard_map/slice | solution.py:49
  8.0 0.4 copy.22
  8.3 4.4 %collective-permute-start = (bf16[3,1024,2]{1,0,2:T(4,128)(2,1)S(1)}, bf16[3,1024,2]{1,0,2:T(4,128)(2,1)S(1)}, u32[]{:S(2)}, u32[]{:S(2)}) collective-permute-start(bf16[3,1024,2]{1,0,2:T(4,128)(2,1)S(1)} %copy.22), channel_id=1, source_target_pairs={{0,4},{4,8},{8,12},{12,16},{16,20},{20,24},{24,28},{28,32},{32,36}... | collective-permute-start | bytes 36872 | tf_op jit(solution)/shard_map/ppermute | solution.py:10
  12.7 0.9 fusion.19
  13.6 0.9 broadcast_divide_fusion
  14.5 1.4 %copy.14 = bf16[3,1024,128]{1,2,0:T(8,128)(2,1)S(1)} copy(bf16[3,1024,128]{2,1,0:T(8,128)(2,1)} %param.5) | data formatting | bytes 1572864 | tf_op args[0]
  16.0 0.0 collective-permute-done
  16.0 0.2 maximum_convert_fusion
  16.2 0.0 copy-start
  16.2 0.0 copy-start.1
  16.3 0.5 fusion.8
  16.7 0.1 fusion.15
  16.8 0.0 slice-start
  16.8 5.0 %fusion = f32[16,1024,128]{1,2,0:T(8,128)S(1)} fusion(f32[1024,128]{0,1:T(8,128)S(1)} %fusion.15, f32[128]{0:T(128)S(1)} %add_convert_fusion.1, f32[16,1024]{1,0:T(8,128)S(1)} %broadcast_divide_fusion), kind=kOutput, calls=%fused_computation.2 | convolution fusion | flops 1614823424 | bytes 8978944 | tf_op jit(solution)/shard_map/dot_general | solution.py:23
  21.8 0.1 slice.50
  21.9 0.0 copy-done
  21.9 3.5 %collective-permute-start.1 = (f32[16,1024]{1,0:T(8,128)S(1)}, f32[16,1024]{1,0:T(8,128)S(1)}, u32[]{:S(2)}, u32[]{:S(2)}) collective-permute-start(f32[16,1024]{1,0:T(8,128)S(1)} %bitcast_multiply_fusion), channel_id=1, source_target_pairs={{0,4},{4,8},{8,12},{12,16},{16,20},{20,24},{24,28},{28,32},{32,36}... | collective-permute-start | bytes 196616 | tf_op jit(solution)/shard_map/ppermute | solution.py:10
  25.5 1.3 %collective-permute-done.1 = f32[16,1024]{1,0:T(8,128)S(1)} collective-permute-done((f32[16,1024]{1,0:T(8,128)S(1)}, f32[16,1024]{1,0:T(8,128)S(1)}, u32[]{:S(2)}, u32[]{:S(2)}) %collective-permute-start.1) | collective-permute-done | bytes 65568 | tf_op jit(solution)/shard_map/ppermute | solution.py:10
  26.9 6.1 %collective-permute-start.2 = (f32[16,1024]{1,0:T(8,128)S(1)}, f32[16,1024]{1,0:T(8,128)S(1)}, u32[]{:S(2)}, u32[]{:S(2)}) collective-permute-start(f32[16,1024]{1,0:T(8,128)S(1)} %multiply_add_fusion.4), channel_id=1, source_target_pairs={{0,8},{4,12},{8,16},{12,20},{16,24},{20,28},{24,32},{28,36},{32,40... | collective-permute-start | bytes 196616 | tf_op jit(solution)/shard_map/ppermute | solution.py:10
  33.0 1.3 %collective-permute-done.2 = f32[16,1024]{1,0:T(8,128)S(1)} collective-permute-done((f32[16,1024]{1,0:T(8,128)S(1)}, f32[16,1024]{1,0:T(8,128)S(1)}, u32[]{:S(2)}, u32[]{:S(2)}) %collective-permute-start.2) | collective-permute-done | bytes 65568 | tf_op jit(solution)/shard_map/ppermute | solution.py:10
  34.3 9.0 %collective-permute-start.3 = (f32[16,1024]{1,0:T(8,128)S(1)}, f32[16,1024]{1,0:T(8,128)S(1)}, u32[]{:S(2)}, u32[]{:S(2)}) collective-permute-start(f32[16,1024]{1,0:T(8,128)S(1)} %multiply_add_fusion.3), channel_id=1, source_target_pairs={{0,16},{4,20},{8,24},{12,28},{16,32},{20,36},{24,40},{28,44},{32,4... | collective-permute-start | bytes 196616 | tf_op jit(solution)/shard_map/ppermute | solution.py:10
  43.3 1.9 %collective-permute-done.3 = f32[16,1024]{1,0:T(8,128)S(1)} collective-permute-done((f32[16,1024]{1,0:T(8,128)S(1)}, f32[16,1024]{1,0:T(8,128)S(1)}, u32[]{:S(2)}, u32[]{:S(2)}) %collective-permute-start.3) | collective-permute-done | bytes 65568 | tf_op jit(solution)/shard_map/ppermute | solution.py:10
  45.2 7.4 %collective-permute-start.4 = (f32[16,1024]{1,0:T(8,128)S(1)}, f32[16,1024]{1,0:T(8,128)S(1)}, u32[]{:S(2)}, u32[]{:S(2)}) collective-permute-start(f32[16,1024]{1,0:T(8,128)S(1)} %multiply_add_fusion.2), channel_id=1, source_target_pairs={{0,32},{4,36},{8,40},{12,44},{16,48},{20,52},{24,56},{28,60},{32,6... | collective-permute-start | bytes 196616 | tf_op jit(solution)/shard_map/ppermute | solution.py:10
  52.6 1.3 %collective-permute-done.4 = f32[16,1024]{1,0:T(8,128)S(1)} collective-permute-done((f32[16,1024]{1,0:T(8,128)S(1)}, f32[16,1024]{1,0:T(8,128)S(1)}, u32[]{:S(2)}, u32[]{:S(2)}) %collective-permute-start.4) | collective-permute-done | bytes 65568 | tf_op jit(solution)/shard_map/ppermute | solution.py:10
  54.0 0.0 slice-start.1
  54.0 5.5 %collective-permute-start.5 = (f32[16,1024]{1,0:T(8,128)S(1)}, f32[16,1024]{1,0:T(8,128)S(1)}, u32[]{:S(2)}, u32[]{:S(2)}) collective-permute-start(f32[16,1024]{1,0:T(8,128)S(1)} %multiply_add_fusion.1), channel_id=1, source_target_pairs={{0,64},{4,68},{8,72},{12,76},{16,80},{20,84},{24,88},{28,92},{32,9... | collective-permute-start | bytes 196616 | tf_op jit(solution)/shard_map/ppermute | solution.py:10
  59.5 1.3 %collective-permute-done.5 = f32[16,1024]{1,0:T(8,128)S(1)} collective-permute-done((f32[16,1024]{1,0:T(8,128)S(1)}, f32[16,1024]{1,0:T(8,128)S(1)}, u32[]{:S(2)}, u32[]{:S(2)}) %collective-permute-start.5) | collective-permute-done | bytes 65568 | tf_op jit(solution)/shard_map/ppermute | solution.py:10
  60.8 15.1 %collective-permute-start.6 = (f32[16,1024]{1,0:T(8,128)S(1)}, f32[16,1024]{1,0:T(8,128)S(1)}, u32[]{:S(2)}, u32[]{:S(2)}) collective-permute-start(f32[16,1024]{1,0:T(8,128)S(1)} %multiply_add_fusion), channel_id=1, source_target_pairs={{0,128},{4,132},{8,136},{12,140},{16,144},{20,148},{24,152},{28,15... | collective-permute-start | bytes 196616 | tf_op jit(solution)/shard_map/ppermute | solution.py:10
  76.0 1.3 collective-permute-done.6
  77.3 0.0 copy-done.1
  77.3 0.1 add_multiply_fusion
  77.4 3.4 %multiply_reduce_fusion = (f32[1024,128]{0,1:T(8,128)S(1)}, f32[1024,128]{0,1:T(8,128)S(1)}) fusion(f32[128]{0:T(128)S(1)} %get-tuple-element.12, f32[16,1024]{1,0:T(8,128)S(1)} %add_multiply_fusion, f32[16,1024]{1,0:T(8,128)S(1)} %broadcast_divide_fusion, f32[16,1024,128]{1,2,0:T(8,128)S(1)} %fusion, f32[128]{0:T(128)S(1)} %get-tuple-element.13, ...), kind=kLoop, calls=%fused_computation | loop fusion | flops 14417920 | bytes 9634816 | tf_op jit(solution)/shard_map/reduce_sum | solution.py:40
  80.7 0.0 slice-done
  80.7 0.0 slice-done.1
  80.8 2.3 %fusion.4 = bf16[4096,128]{0,1:T(8,128)(2,1)} fusion(bf16[1024,4096]{1,0:T(8,128)(2,1)S(1)} %bitcast.30, f32[3,1024,128]{1,2,0:T(8,128)S(1)} %fusion.8, f32[1024,128]{0,1:T(8,128)S(1)} %get-tuple-element.6, f32[1024,128]{0,1:T(8,128)S(1)} %get-tuple-element.5), kind=kOutput, calls=%fused_computation.7 | convolution fusion | flops 1074921472 | bytes 11010048 | tf_op jit(solution)/shard_map/dot_general | solution.py:61
  83.1 0.0 reduce-scatter.2.cloned.1.call-update
  83.1 38.4 %reduce-scatter.2.cloned.1.call-done = bf16[1024,128]{0,1:T(8,128)(2,1)} async-done(((bf16[4096,128]{0,1:T(8,128)(2,1)}), bf16[1024,128]{0,1:T(8,128)(2,1)}) %reduce-scatter.2.cloned.1.call-update) | async-done | bytes 262160 | tf_op jit(solution)/shard_map/reduce_scatter | solution.py:60
  121.5 1.8 %copy.16 = bf16[1024,128]{1,0:T(8,128)(2,1)} copy(bf16[1024,128]{0,1:T(8,128)(2,1)} %reduce-scatter.2.cloned.1.call-done) | data formatting | bytes 524288 | tf_op jit(solution)/shard_map/reduce_scatter | solution.py:60
  (12 shorter events, 0.2 us)
Async XLA Ops:
  6.5 114.9 %reduce-scatter.2.cloned.1.call-start = ((), (), s32[]{:S(2)}) async-start(), calls=%async_computation.1 | async-start | bytes 1310720 | tf_op jit(solution)/shard_map/reduce_scatter | solution.py:60
  8.3 7.6 %collective-permute-start = (bf16[3,1024,2]{1,0,2:T(4,128)(2,1)S(1)}, bf16[3,1024,2]{1,0,2:T(4,128)(2,1)S(1)}, u32[]{:S(2)}, u32[]{:S(2)}) collective-permute-start(bf16[3,1024,2]{1,0,2:T(4,128)(2,1)S(1)} %copy.22), channel_id=1, source_target_pairs={{0,4},{4,8},{8,12},{12,16},{16,20},{20,24},{24,28},{28,32},{32,36}... | collective-permute-start | bytes 36872 | tf_op jit(solution)/shard_map/ppermute | solution.py:10
  16.2 5.7 %copy-start = (f32[16,1024]{1,0:T(8,128)S(1)}, f32[16,1024]{1,0:T(8,128)}, u32[]{:S(2)}) copy-start(f32[16,1024]{1,0:T(8,128)} %param.7) | copy-start | bytes 196612
  16.2 61.0 %copy-start.1 = (f32[16,1024]{1,0:T(8,128)S(1)}, f32[16,1024]{1,0:T(8,128)}, u32[]{:S(2)}) copy-start(f32[16,1024]{1,0:T(8,128)} %param.8) | copy-start | bytes 196612
  16.8 63.9 %slice-start = ((s8[8388608]{0:T(1024)(128)(4,1)}), s8[4194304]{0:T(1024)(128)(4,1)S(1)}, s32[]{:S(2)}) async-start(s8[8388608]{0:T(1024)(128)(4,1)} %bitcast.29), calls=%async_computation.2 | async-start | bytes 8388608
  21.9 4.9 %collective-permute-start.1 = (f32[16,1024]{1,0:T(8,128)S(1)}, f32[16,1024]{1,0:T(8,128)S(1)}, u32[]{:S(2)}, u32[]{:S(2)}) collective-permute-start(f32[16,1024]{1,0:T(8,128)S(1)} %bitcast_multiply_fusion), channel_id=1, source_target_pairs={{0,4},{4,8},{8,12},{12,16},{16,20},{20,24},{24,28},{28,32},{32,36}... | collective-permute-start | bytes 196616 | tf_op jit(solution)/shard_map/ppermute | solution.py:10
  26.9 7.4 %collective-permute-start.2 = (f32[16,1024]{1,0:T(8,128)S(1)}, f32[16,1024]{1,0:T(8,128)S(1)}, u32[]{:S(2)}, u32[]{:S(2)}) collective-permute-start(f32[16,1024]{1,0:T(8,128)S(1)} %multiply_add_fusion.4), channel_id=1, source_target_pairs={{0,8},{4,12},{8,16},{12,20},{16,24},{20,28},{24,32},{28,36},{32,40... | collective-permute-start | bytes 196616 | tf_op jit(solution)/shard_map/ppermute | solution.py:10
  34.3 10.9 %collective-permute-start.3 = (f32[16,1024]{1,0:T(8,128)S(1)}, f32[16,1024]{1,0:T(8,128)S(1)}, u32[]{:S(2)}, u32[]{:S(2)}) collective-permute-start(f32[16,1024]{1,0:T(8,128)S(1)} %multiply_add_fusion.3), channel_id=1, source_target_pairs={{0,16},{4,20},{8,24},{12,28},{16,32},{20,36},{24,40},{28,44},{32,4... | collective-permute-start | bytes 196616 | tf_op jit(solution)/shard_map/ppermute | solution.py:10
  45.2 8.7 %collective-permute-start.4 = (f32[16,1024]{1,0:T(8,128)S(1)}, f32[16,1024]{1,0:T(8,128)S(1)}, u32[]{:S(2)}, u32[]{:S(2)}) collective-permute-start(f32[16,1024]{1,0:T(8,128)S(1)} %multiply_add_fusion.2), channel_id=1, source_target_pairs={{0,32},{4,36},{8,40},{12,44},{16,48},{20,52},{24,56},{28,60},{32,6... | collective-permute-start | bytes 196616 | tf_op jit(solution)/shard_map/ppermute | solution.py:10
  54.0 26.8 %slice-start.1 = ((s8[8388608]{0:T(1024)(128)(4,1)}), s8[4194304]{0:T(1024)(128)(4,1)S(1)}, s32[]{:S(2)}) async-start(s8[8388608]{0:T(1024)(128)(4,1)} %bitcast.29), calls=%async_computation.3 | async-start | bytes 8388608
  54.0 6.8 %collective-permute-start.5 = (f32[16,1024]{1,0:T(8,128)S(1)}, f32[16,1024]{1,0:T(8,128)S(1)}, u32[]{:S(2)}, u32[]{:S(2)}) collective-permute-start(f32[16,1024]{1,0:T(8,128)S(1)} %multiply_add_fusion.1), channel_id=1, source_target_pairs={{0,64},{4,68},{8,72},{12,76},{16,80},{20,84},{24,88},{28,92},{32,9... | collective-permute-start | bytes 196616 | tf_op jit(solution)/shard_map/ppermute | solution.py:10
  60.8 16.5 %collective-permute-start.6 = (f32[16,1024]{1,0:T(8,128)S(1)}, f32[16,1024]{1,0:T(8,128)S(1)}, u32[]{:S(2)}, u32[]{:S(2)}) collective-permute-start(f32[16,1024]{1,0:T(8,128)S(1)} %multiply_add_fusion), channel_id=1, source_target_pairs={{0,128},{4,132},{8,136},{12,140},{16,144},{20,148},{24,152},{28,15... | collective-permute-start | bytes 196616 | tf_op jit(solution)/shard_map/ppermute | solution.py:10
Sparse Core Ops, SparseCore 0:
  83.2 38.2 reduce-scatter.1

commit v2 on v1

v2 whole, which is shorter than its diff:
```python
import jax
import jax.numpy as jnp
from jax import lax
from jax.sharding import PartitionSpec as P


def from_behind(x, axis, by):
    devices = lax.axis_size(axis)
    pairs = [(i, i + by) for i in range(devices) if 0 <= i + by < devices]
    return lax.ppermute(x, axis, pairs)


def modal_conv(pencils, life_slice, resid_slice, block=128):
    chan_here, length = pencils.shape
    blocks = length // block
    inv = 1.0 / life_slice
    mid = block // 2
    offs = (jnp.arange(block, dtype=jnp.int32) - mid).astype(jnp.float32)
    grow = jnp.exp(offs[None, None, :] * inv[:, :, None])
    shrink = jnp.exp(-offs[None, None, :] * inv[:, :, None])
    signal = pencils.astype(jnp.float32).reshape(chan_here, blocks, block)
    weighted = grow[:, :, None, :] * signal[None]
    upper = (
        jnp.arange(block, dtype=jnp.int32)[:, None] <= jnp.arange(block, dtype=jnp.int32)[None, :]
    ).astype(jnp.float32)
    sums = jnp.dot(weighted, upper, precision=lax.Precision.HIGH)
    leaving = jnp.exp(-float(block - 1 - mid) * inv)[:, :, None] * sums[..., block - 1]
    n_idx = jnp.arange(blocks, dtype=jnp.int32)
    gap = (n_idx[:, None] - 1 - n_idx[None, :]).astype(jnp.float32)
    exponent = jnp.where(
        (n_idx[:, None] > n_idx[None, :])[None, None],
        -float(block) * gap[None, None] * inv[:, :, None, None],
        -jnp.inf,
    )
    entering = jnp.sum(jnp.exp(exponent) * leaving[:, :, None, :], axis=-1)
    carry_in = jnp.exp(-float(mid + 1) * inv)[:, :, None] * entering
    total = sums + carry_in[..., None]
    result = jnp.sum((resid_slice[:, :, None] * shrink)[:, :, None, :] * total, axis=0)
    return result.reshape(chan_here, length)


def reduce_scatter_chan(partial):
    index = lax.axis_index("chan")
    chip, core = index // 2, index % 2
    quarters = partial.reshape(2, 2, partial.shape[0] // 4, partial.shape[1])
    send = lax.dynamic_index_in_dim(quarters, 1 - core, 1, keepdims=False)
    keep = lax.dynamic_index_in_dim(quarters, core, 1, keepdims=False)
    got = lax.ppermute(send, "chan", [(j, j ^ 1) for j in range(4)])
    halves = keep.astype(jnp.float32) + got.astype(jnp.float32)
    send2 = lax.dynamic_index_in_dim(halves, 1 - chip, 0, keepdims=False).astype(jnp.bfloat16)
    keep2 = lax.dynamic_index_in_dim(halves, chip, 0, keepdims=False)
    got2 = lax.ppermute(send2, "chan", [(j, j ^ 2) for j in range(4)])
    return (keep2 + got2.astype(jnp.float32)).astype(jnp.bfloat16)


def local(qkv, taps, lifetimes, residues, out_weight):
    chan_local = qkv.shape[1]
    tok_count = qkv.shape[2]
    edge_block = qkv[:, :, tok_count - 2 :]
    earlier = from_behind(edge_block, "seq", 1)
    extended = jnp.concatenate([earlier, qkv], axis=2).astype(jnp.float32)
    filtered = (
        taps[:, 0, :, None] * extended[:, :, 2:]
        + taps[:, 1, :, None] * extended[:, :, 1:-1]
        + taps[:, 2, :, None] * extended[:, :, :-2]
    )
    product = (filtered[1] * filtered[2]).astype(jnp.bfloat16)
    groups = lax.axis_size("seq")
    per_group = chan_local // groups
    pencils = lax.all_to_all(product, "seq", split_axis=0, concat_axis=1, tiled=True)
    first_chan = lax.axis_index("seq") * per_group
    life_slice = lax.dynamic_slice_in_dim(lifetimes, first_chan, per_group, 1)
    resid_slice = lax.dynamic_slice_in_dim(residues, first_chan, per_group, 1)
    convolved = modal_conv(pencils, life_slice, resid_slice).astype(jnp.bfloat16)
    returned = lax.all_to_all(convolved, "seq", split_axis=1, concat_axis=0, tiled=True)
    gated_rows = (filtered[0] * returned.astype(jnp.float32)).astype(jnp.bfloat16)
    partial = lax.dot_general(
        out_weight, gated_rows, (((0,), (0,)), ((), ())), preferred_element_type=jnp.float32
    ).astype(jnp.bfloat16)
    return reduce_scatter_chan(partial)


def solution(mesh):
    placed = (
        P(None, "chan", "seq"),
        P(None, None, "chan"),
        P(None, "chan"),
        P(None, "chan"),
        P("chan", None),
    )
    return jax.shard_map(
        local, mesh=mesh, in_specs=placed, out_specs=P("chan", "seq"), check_vma=False
    )
```

time: 131 us -> 91.8 us (0.70)
  starting transfers between devices: 51 us -> 29.9 us
  waiting for transfers between devices: 46.8 us -> 28.4 us
  between operations: 13.6 us -> 0.25 us
  local copies, waits for them, and re-layouts: 6.05 us -> 13.4 us
  other arithmetic: 5.25 us -> 12.4 us
    ppermute x7 -> x1, starting transfers between devices: 51 us -> 4.36 us  [from_behind(): return lax.ppermute(x, axis, pairs)]
    reduce_scatter x1 -> x0, waiting for transfers between devices: 38.4 us -> none  [local(): lax.psum_scatter(lax.dot_general(out_weight, gated_rows, (((0,), (0,)), (...]
    all_to_all x0 -> x2, waiting for transfers between devices: none -> 21.4 us  [the longest x1 10.8 us: local(): lax.all_to_all(convolved, 'seq', split_axis=1, concat_axis=0, tiled=True)]
    all_to_all x0 -> x2, starting transfers between devices: none -> 18.2 us  [the longest x1 13.1 us: local(): lax.all_to_all(product, 'seq', split_axis=0, concat_axis=1, tiled=True)]
    ppermute x7 -> x1, waiting for transfers between devices: 8.44 us -> 0.01 us  [from_behind(): return lax.ppermute(x, axis, pairs)]
    ppermute x0 -> x2, starting transfers between devices: none -> 7.34 us  [the longest x1 4.63 us: reduce_scatter_chan(): got = lax.ppermute(send, 'chan', [(j, j ^ 1) for j in range(4)])]
    ppermute x0 -> x2, waiting for transfers between devices: none -> 7.05 us  [the longest x1 6.37 us: reduce_scatter_chan(): got2 = lax.ppermute(send2, 'chan', [(j, j ^ 2) for j in range(4)])]
    slice x1, local copies, waits for them, and re-layouts: 0.06 us -> 4.4 us  [modal_conv(): sums[..., block - 1]]
  transfers between devices with their start and end apart: 8 -> 5, of which waited for: 7 -> 4; matrix products, arithmetic and copies ran while one was open for 2% -> 3% of each run, Pallas kernels for 0% -> 0%
where the time goes in v2:
time: 91.8 us; the launch traced here: 91.4 us
  starting transfers between devices  29.9 us (33%)
  waiting for transfers between devices  28.4 us (31%)
  local copies, waits for them, and re-layouts  13.4 us (15%)
  other arithmetic  12.4 us (14%)
  matrix products  7.02 us (8%)
    all_to_all x1, starting transfers between devices, local(): lax.all_to_all(product, 'seq', split_axis=0, concat_axis=1, tiled=True)  13.1 us
    all_to_all x1, waiting for transfers between devices, local(): lax.all_to_all(convolved, 'seq', split_axis=1, concat_axis=0, tiled=True)  10.8 us
    all_to_all x1, waiting for transfers between devices, local(): lax.all_to_all(product, 'seq', split_axis=0, concat_axis=1, tiled=True)  10.6 us
    ppermute x1, waiting for transfers between devices, reduce_scatter_chan(): got2 = lax.ppermute(send2, 'chan', [(j, j ^ 2) for j in range(4)])  6.37 us
    all_to_all x1, starting transfers between devices, local(): lax.all_to_all(convolved, 'seq', split_axis=1, concat_axis=0, tiled=True)  5.07 us
    dot_general x1, matrix products, local(): lax.dot_general(out_weight, gated_rows, (((0,), (0,)), ((), ())), preferr...  4.68 us
    ppermute x1, starting transfers between devices, reduce_scatter_chan(): got = lax.ppermute(send, 'chan', [(j, j ^ 1) for j in range(4)])  4.63 us
    slice x1, local copies, waits for them, and re-layouts, modal_conv(): sums[..., block - 1]  4.4 us
  transfers between devices with their start and end apart: 5, of which 4 were waited for; matrix products, arithmetic and copies ran while one was open for 3% of the time, Pallas kernels for 0%

profile of v2, /device:TPU:1, one launch (start us, length us, event | category | flops | bytes accessed | tf_op | source)
XLA Modules:
  0.0 91.4 jit_solution(7444314693919929881)
XLA Ops:
  0.0 1.4 %slice.34 = bf16[3,1024,2]{2,1,0:T(8,128)(2,1)S(1)} slice(bf16[3,1024,128]{2,1,0:T(8,128)(2,1)} %param.5), slice={[0:3], [0:1024], [126:128]} | slice | bytes 24576 | tf_op jit(solution)/shard_map/slice | solution.py:59
  1.4 0.4 copy.39
  1.8 4.4 %collective-permute-start = (bf16[3,1024,2]{1,0,2:T(4,128)(2,1)S(1)}, bf16[3,1024,2]{1,0,2:T(4,128)(2,1)S(1)}, u32[]{:S(2)}, u32[]{:S(2)}) collective-permute-start(bf16[3,1024,2]{1,0,2:T(4,128)(2,1)S(1)} %copy.39), channel_id=1, source_target_pairs={{0,4},{4,8},{8,12},{12,16},{16,20},{20,24},{24,28},{28,32},{32,36}... | collective-permute-start | bytes 36872 | tf_op jit(solution)/shard_map/ppermute | solution.py:10
  6.2 0.9 %fusion.15 = (f32[3,1,1024]{2,1,0:T(1,128)S(1)}, f32[3,1,1024]{2,1,0:T(1,128)S(1)}, f32[3,1,1024]{2,1,0:T(1,128)S(1)}) fusion(f32[3,3,1024]{2,1,0:T(4,128)} %param.6), kind=kLoop, calls=%fused_computation.46 | loop fusion | bytes 73728 | tf_op jit(solution)/shard_map/slice | solution.py:63
  7.1 0.8 multiply_exponential_fusion.2
  8.0 0.0 collective-permute-done
  8.0 0.4 copy.30
  8.4 1.7 %maximum_convert_fusion = f32[3,1024,130]{2,1,0:T(8,128)S(1)} fusion(bf16[3,1024,128]{2,1,0:T(8,128)(2,1)} %param.5, bf16[3,1024,2]{2,1,0:T(8,128)(2,1)S(1)} %copy.30), kind=kLoop, calls=%fused_computation.14 | loop fusion | flops 1597440 | bytes 2396160 | tf_op jit(solution)/shard_map/convert_element_type | solution.py:61
  10.2 2.4 %fusion.5 = f32[3,1024,128]{2,1,0:T(8,128)S(1)} fusion(f32[3,1024,130]{2,1,0:T(8,128)S(1)} %maximum_convert_fusion, f32[3,1024]{1,0:T(4,128)S(1)} %get-tuple-element.14, f32[3,1024]{1,0:T(4,128)S(1)} %get-tuple-element.15, f32[3,1024]{1,0:T(4,128)S(1)} %bitcast.42), kind=kLoop, calls=%fused_computation.10 | loop fusion | flops 1966080 | bytes 6328320 | tf_op jit(solution)/shard_map/add | solution.py:63
  12.5 0.8 fusion.7
  13.3 13.1 %all-to-all-start = ((bf16[64,16,128]{2,1,0:T(8,128)(2,1)}), bf16[64,16,128]{2,1,0:T(8,128)(2,1)S(1)}, u32[]{:S(2)}, u32[]{:S(2)}) async-start(bf16[64,16,128]{2,1,0:T(8,128)(2,1)} %bitcast.1), calls=%async_computation | async-start | bytes 524288 | tf_op jit(solution)/shard_map/all_to_all | solution.py:70
  26.4 0.1 convert_multiply_fusion
  26.5 0.1 exponential_multiply_fusion
  26.7 10.6 %all-to-all-done = bf16[64,16,128]{2,1,0:T(8,128)(2,1)S(1)} async-done(((bf16[64,16,128]{2,1,0:T(8,128)(2,1)}), bf16[64,16,128]{2,1,0:T(8,128)(2,1)S(1)}, u32[]{:S(2)}, u32[]{:S(2)}) %all-to-all-start) | async-done | bytes 262176 | tf_op jit(solution)/shard_map/all_to_all | solution.py:70
  37.3 0.2 copy.31
  37.5 2.3 %fusion = f32[16,16,64,128]{3,2,1,0:T(8,128)S(1)} fusion(f32[16,64,128]{2,1,0:T(8,128)S(1)} %copy.31, f32[16,16,128]{2,1,0:T(8,128)S(1)} %get-tuple-element.13), kind=kOutput, calls=%fused_computation.3 | convolution fusion | flops 1612726272 | bytes 9043968 | tf_op jit(solution)/shard_map/dot_general | solution.py:26
  39.8 4.4 %slice_reduce_fusion = f32[16,16,64]{2,1,0:T(8,128)S(1)} fusion(f32[16,16,64,128]{3,2,1,0:T(8,128)S(1)} %fusion), kind=kLoop, calls=%fused_computation | loop fusion | bytes 131072 | tf_op jit(solution)/shard_map/slice | solution.py:27
  44.2 0.1 broadcast_multiply_fusion
  44.3 2.6 %multiply_reduce_fusion.1 = f32[16,16,64]{2,1,0:T(8,128)S(1)} fusion(f32[16,16,64]{2,1,0:T(8,128)S(1)} %broadcast_multiply_fusion, f32[16,16]{1,0:T(8,128)S(1)} %get-tuple-element.6, f32[64,64]{1,0:T(8,128)S(1)} %convert_multiply_fusion, pred[64,64]{1,0:T(8,128)(4,1)S(1)} %iota_compare_fusion.1), kind=kLoop, calls=%fused_computation.2 | loop fusion | flops 4177920 | bytes 152576 | tf_op jit(solution)/shard_map/reduce_sum | solution.py:35
  47.0 0.1 broadcast_multiply_fusion.1
  47.1 2.8 %multiply_reduce_fusion = bf16[16,64,128]{2,1,0:T(8,128)(2,1)S(1)} fusion(f32[16,16,64,128]{3,2,1,0:T(8,128)S(1)} %fusion, f32[16,16,64]{2,1,0:T(8,128)S(1)} %broadcast_multiply_fusion.1, f32[16,16,128]{2,1,0:T(8,128)S(1)} %get-tuple-element.12), kind=kLoop, calls=%fused_computation.1 | loop fusion | flops 6160384 | bytes 8847360 | tf_op jit(solution)/shard_map/reduce_sum | solution.py:38
  49.8 0.9 copy.32
  50.7 5.1 %all-to-all-start.1 = ((bf16[16,64,128]{2,0,1:T(8,128)(2,1)}), bf16[16,64,128]{2,0,1:T(8,128)(2,1)S(1)}, u32[]{:S(2)}, u32[]{:S(2)}) async-start(bf16[16,64,128]{2,0,1:T(8,128)(2,1)} %copy.32), calls=%async_computation.1 | async-start | bytes 524288 | tf_op jit(solution)/shard_map/all_to_all | solution.py:75
  55.8 10.8 %all-to-all-done.1 = bf16[16,64,128]{2,0,1:T(8,128)(2,1)S(1)} async-done(((bf16[16,64,128]{2,0,1:T(8,128)(2,1)}), bf16[16,64,128]{2,0,1:T(8,128)(2,1)S(1)}, u32[]{:S(2)}, u32[]{:S(2)}) %all-to-all-start.1) | async-done | bytes 262176 | tf_op jit(solution)/shard_map/all_to_all | solution.py:75
  66.6 0.1 fusion.9
  66.7 4.7 %fusion.2 = bf16[4096,128]{0,1:T(8,128)(2,1)S(1)} fusion(bf16[1024,128]{1,0:T(8,128)(2,1)S(1)} %fusion.9, bf16[1024,4096]{1,0:T(8,128)(2,1)} %param.9), kind=kOutput, calls=%fused_computation.6 | convolution fusion | flops 1074266112 | bytes 9699328 | tf_op jit(solution)/shard_map/dot_general | solution.py:77
  71.3 0.8 reshape.91
  72.1 2.2 %constant_dynamic-slice_fusion.1 = (bf16[2,1,1024,128]{2,1,0,3:T(2,128)(2,1)S(1)}, bf16[2,1,1024,128]{2,1,0,3:T(2,128)(2,1)S(1)}) fusion(bf16[2,2,1024,128]{2,1,0,3:T(2,128)(2,1)S(1)} %reshape.91, s32[]{:T(128)S(6)} %select_n.36, s32[]{:T(128)S(6)} %select_n.37), kind=kLoop, calls=%fused_computation.41 | loop fusion | bytes 2097160 | tf_op jit(solution)/shard_map/jit(dynamic_index_in_dim)/dynamic_slice | solution.py:47
  74.3 0.9 copy.34
  75.2 4.6 %collective-permute-start.1 = (bf16[2,1024,128]{2,1,0:T(8,128)(2,1)S(1)}, bf16[2,1024,128]{2,1,0:T(8,128)(2,1)S(1)}, u32[]{:S(2)}, u32[]{:S(2)}) collective-permute-start(bf16[2,1024,128]{2,1,0:T(8,128)(2,1)S(1)} %bitcast.41), channel_id=1, source_target_pairs={{0,1},{1,0},{2,3},{3,2},{4,5},{5,4},{6,7},{7,6},{8,9},{9,8},{10,11... | collective-permute-start | bytes 1572872 | tf_op jit(solution)/shard_map/ppermute | solution.py:48
  79.8 0.9 copy.40
  80.7 0.7 collective-permute-done.1
  81.4 0.1 convert_add_fusion
  81.5 2.7 %collective-permute-start.2 = (bf16[1024,128]{1,0:T(8,128)(2,1)S(1)}, bf16[1024,128]{1,0:T(8,128)(2,1)S(1)}, u32[]{:S(2)}, u32[]{:S(2)}) collective-permute-start(bf16[1024,128]{1,0:T(8,128)(2,1)S(1)} %fusion.11), channel_id=1, source_target_pairs={{0,2},{1,3},{2,0},{3,1},{4,6},{5,7},{6,4},{7,5},{8,10},{9,11},{10,... | collective-permute-start | bytes 786440 | tf_op jit(solution)/shard_map/ppermute | solution.py:52
  84.2 6.4 %collective-permute-done.2 = bf16[1024,128]{1,0:T(8,128)(2,1)S(1)} collective-permute-done((bf16[1024,128]{1,0:T(8,128)(2,1)S(1)}, bf16[1024,128]{1,0:T(8,128)(2,1)S(1)}, u32[]{:S(2)}, u32[]{:S(2)}) %collective-permute-start.2) | collective-permute-done | bytes 262176 | tf_op jit(solution)/shard_map/ppermute | solution.py:52
  90.6 0.8 fusion.10
  (9 shorter events, 0.1 us)
Async XLA Ops:
  1.8 6.2 %collective-permute-start = (bf16[3,1024,2]{1,0,2:T(4,128)(2,1)S(1)}, bf16[3,1024,2]{1,0,2:T(4,128)(2,1)S(1)}, u32[]{:S(2)}, u32[]{:S(2)}) collective-permute-start(bf16[3,1024,2]{1,0,2:T(4,128)(2,1)S(1)} %copy.39), channel_id=1, source_target_pairs={{0,4},{4,8},{8,12},{12,16},{16,20},{20,24},{24,28},{28,32},{32,36}... | collective-permute-start | bytes 36872 | tf_op jit(solution)/shard_map/ppermute | solution.py:10
  13.3 24.0 %all-to-all-start = ((bf16[64,16,128]{2,1,0:T(8,128)(2,1)}), bf16[64,16,128]{2,1,0:T(8,128)(2,1)S(1)}, u32[]{:S(2)}, u32[]{:S(2)}) async-start(bf16[64,16,128]{2,1,0:T(8,128)(2,1)} %bitcast.1), calls=%async_computation | async-start | bytes 524288 | tf_op jit(solution)/shard_map/all_to_all | solution.py:70
  50.7 15.9 %all-to-all-start.1 = ((bf16[16,64,128]{2,0,1:T(8,128)(2,1)}), bf16[16,64,128]{2,0,1:T(8,128)(2,1)S(1)}, u32[]{:S(2)}, u32[]{:S(2)}) async-start(bf16[16,64,128]{2,0,1:T(8,128)(2,1)} %copy.32), calls=%async_computation.1 | async-start | bytes 524288 | tf_op jit(solution)/shard_map/all_to_all | solution.py:75
  75.2 6.2 %collective-permute-start.1 = (bf16[2,1024,128]{2,1,0:T(8,128)(2,1)S(1)}, bf16[2,1024,128]{2,1,0:T(8,128)(2,1)S(1)}, u32[]{:S(2)}, u32[]{:S(2)}) collective-permute-start(bf16[2,1024,128]{2,1,0:T(8,128)(2,1)S(1)} %bitcast.41), channel_id=1, source_target_pairs={{0,1},{1,0},{2,3},{3,2},{4,5},{5,4},{6,7},{7,6},{8,9},{9,8},{10,11... | collective-permute-start | bytes 1572872 | tf_op jit(solution)/shard_map/ppermute | solution.py:48
  81.5 9.1 %collective-permute-start.2 = (bf16[1024,128]{1,0:T(8,128)(2,1)S(1)}, bf16[1024,128]{1,0:T(8,128)(2,1)S(1)}, u32[]{:S(2)}, u32[]{:S(2)}) collective-permute-start(bf16[1024,128]{1,0:T(8,128)(2,1)S(1)} %fusion.11), channel_id=1, source_target_pairs={{0,2},{1,3},{2,0},{3,1},{4,6},{5,7},{6,4},{7,5},{8,10},{9,11},{10,... | collective-permute-start | bytes 786440 | tf_op jit(solution)/shard_map/ppermute | solution.py:52

commit v3 on v2

--- a/solution.py
+++ b/solution.py
@@ -13,30 +13,28 @@
 def modal_conv(pencils, life_slice, resid_slice, block=128):
     chan_here, length = pencils.shape
     blocks = length // block
-    inv = 1.0 / life_slice
-    mid = block // 2
-    offs = (jnp.arange(block, dtype=jnp.int32) - mid).astype(jnp.float32)
-    grow = jnp.exp(offs[None, None, :] * inv[:, :, None])
-    shrink = jnp.exp(-offs[None, None, :] * inv[:, :, None])
+    steps = jnp.arange(block, dtype=jnp.int32).astype(jnp.float32)
+    life = life_slice[:, :, None]
+    resid = resid_slice[:, :, None]
+    taps = jnp.sum(resid * jnp.exp(-steps[None, None, :] / life), axis=0)
+    lag = jnp.arange(block, dtype=jnp.int32)[None, :] - jnp.arange(block, dtype=jnp.int32)[:, None]
+    toeplitz = jnp.where(lag[None] >= 0, jnp.take(taps, jnp.maximum(lag, 0), axis=1), 0.0)
     signal = pencils.astype(jnp.float32).reshape(chan_here, blocks, block)
-    weighted = grow[:, :, None, :] * signal[None]
-    upper = (
-        jnp.arange(block, dtype=jnp.int32)[:, None] <= jnp.arange(block, dtype=jnp.int32)[None, :]
-    ).astype(jnp.float32)
-    sums = jnp.dot(weighted, upper, precision=lax.Precision.HIGH)
-    leaving = jnp.exp(-float(block - 1 - mid) * inv)[:, :, None] * sums[..., block - 1]
+    precise = lax.Precision.HIGH
+    inside = jnp.einsum("cnj,cjt->cnt", signal, toeplitz, precision=precise)
+    to_end = jnp.exp(-(float(block - 1) - steps)[None, None, :] / life)
+    leaving = jnp.einsum("cnj,rcj->rcn", signal, to_end, precision=precise)
     n_idx = jnp.arange(blocks, dtype=jnp.int32)
     gap = (n_idx[:, None] - 1 - n_idx[None, :]).astype(jnp.float32)
     exponent = jnp.where(
         (n_idx[:, None] > n_idx[None, :])[None, None],
-        -float(block) * gap[None, None] * inv[:, :, None, None],
+        -float(block) * gap[None, None] / life[..., None],
         -jnp.inf,
     )
     entering = jnp.sum(jnp.exp(exponent) * leaving[:, :, None, :], axis=-1)
-    carry_in = jnp.exp(-float(mid + 1) * inv)[:, :, None] * entering
-    total = sums + carry_in[..., None]
-    result = jnp.sum((resid_slice[:, :, None] * shrink)[:, :, None, :] * total, axis=0)
-    return result.reshape(chan_here, length)
+    from_start = resid * jnp.exp(-(steps + 1.0)[None, None, :] / life)
+    carried = jnp.einsum("rcn,rct->cnt", entering, from_start, precision=precise)
+    return (inside + carried).reshape(chan_here, length)
 
 
 def reduce_scatter_chan(partial):

time: 91.8 us -> 142 us (1.55)
  local copies, waits for them, and re-layouts: 13.4 us -> 69.5 us
  other arithmetic: 12.4 us -> 7.56 us
    gather x0 -> x2, local copies, waits for them, and re-layouts: none -> 59.7 us  [modal_conv(): jnp.take(taps, jnp.maximum(lag, 0), axis=1)]
    slice x1 -> x0, local copies, waits for them, and re-layouts: 4.4 us -> none  [modal_conv(): sums[..., block - 1]]
    reduce_sum x1, other arithmetic: 2.77 us -> 0.14 us  [modal_conv(): taps = jnp.sum(resid * jnp.exp(-steps[None, None, :] / life), axis=0)]
  transfers between devices with their start and end apart: 5 -> 5, of which waited for: 4 -> 4; matrix products, arithmetic and copies ran while one was open for 3% -> 45% of each run, Pallas kernels for 0% -> 0%
where the time goes in v3:
time: 142 us; the launch traced here: 141 us
  local copies, waits for them, and re-layouts  69.5 us (49%)
  waiting for transfers between devices  29.1 us (20%)
  starting transfers between devices  28.5 us (20%)
  other arithmetic  7.56 us (5%)
  matrix products  6.31 us (4%)
    gather x2, local copies, waits for them, and re-layouts, modal_conv(): jnp.take(taps, jnp.maximum(lag, 0), axis=1)  59.7 us
    all_to_all x1, starting transfers between devices, local(): lax.all_to_all(product, 'seq', split_axis=0, concat_axis=1, tiled=True)  11.8 us
    all_to_all x1, waiting for transfers between devices, local(): lax.all_to_all(product, 'seq', split_axis=0, concat_axis=1, tiled=True)  11.3 us
    all_to_all x1, waiting for transfers between devices, local(): lax.all_to_all(convolved, 'seq', split_axis=1, concat_axis=0, tiled=True)  10.8 us
    ppermute x1, waiting for transfers between devices, reduce_scatter_chan(): got2 = lax.ppermute(send2, 'chan', [(j, j ^ 2) for j in range(4)])  6.38 us
    all_to_all x1, starting transfers between devices, local(): lax.all_to_all(convolved, 'seq', split_axis=1, concat_axis=0, tiled=True)  5.94 us
    dot_general x1, matrix products, local(): lax.dot_general(out_weight, gated_rows, (((0,), (0,)), ((), ())), preferr...  4.68 us
    ppermute x1, starting transfers between devices, from_behind(): return lax.ppermute(x, axis, pairs)  4.36 us
  transfers between devices with their start and end apart: 5, of which 4 were waited for; matrix products, arithmetic and copies ran while one was open for 45% of the time, Pallas kernels for 0%

profile of v3, /device:TPU:1, one launch (start us, length us, event | category | flops | bytes accessed | tf_op | source)
XLA Modules:
  0.0 141.2 jit_solution(8397588836542954821)
XLA Ops:
  0.0 1.4 slice.31
  1.4 0.3 copy.44
  1.7 4.4 %collective-permute-start = (bf16[3,1024,2]{1,2,0:T(2,128)(2,1)S(1)}, bf16[3,1024,2]{1,2,0:T(2,128)(2,1)S(1)}, u32[]{:S(2)}, u32[]{:S(2)}) collective-permute-start(bf16[3,1024,2]{1,2,0:T(2,128)(2,1)S(1)} %copy.44), channel_id=1, source_target_pairs={{0,4},{4,8},{8,12},{12,16},{16,20},{20,24},{24,28},{28,32},{32,36}... | collective-permute-start | bytes 36872 | tf_op jit(solution)/shard_map/ppermute | solution.py:10
  6.1 0.9 fusion.37
  7.1 0.8 constant_dynamic-slice_fusion.2
  7.9 0.1 copy.33
  8.0 0.1 copy.32
  8.1 0.1 fusion.27
  8.2 0.1 copy.34
  8.3 54.4 %gather_fusion = f32[16384,16]{1,0:T(8,128)} fusion(f32[16,128]{0,1:T(8,128)S(1)} %copy.34, s32[16384]{0:T(1024)S(1)} %bitcast_clamp_fusion), kind=kCustom, calls=%fused_computation | custom fusion | bytes 2162688 | tf_op jit(solution)/shard_map/jit(_take)/gather | solution.py:21
  62.7 0.0 copy-start
  62.7 5.3 %copy.35 = f32[128,128,16]{1,0,2:T(8,128)S(1)} copy(f32[128,128,16]{2,1,0:T(8,128)} %bitcast.47) | data formatting | bytes 2097152 | tf_op jit(solution)/shard_map/jit(_take)/gather | solution.py:21
  68.0 0.0 collective-permute-done
  68.1 0.4 copy.30
  68.5 0.0 copy-done
  68.5 0.6 maximum_convert_fusion
  69.1 2.4 %fusion.4 = f32[3,1024,128]{2,1,0:T(8,128)S(1)} fusion(f32[3,1024,130]{2,1,0:T(8,128)S(1)} %maximum_convert_fusion, f32[3,1024]{1,0:T(4,128)S(1)} %get-tuple-element.10, f32[3,1024]{1,0:T(4,128)S(1)} %get-tuple-element.11, f32[3,1024]{1,0:T(4,128)S(1)} %bitcast.49), kind=kLoop, calls=%fused_computation.8 | loop fusion | flops 1966080 | bytes 6328320 | tf_op jit(solution)/shard_map/add | solution.py:61
  71.4 0.8 fusion.10
  72.2 11.8 %all-to-all-start = ((bf16[64,16,128]{2,1,0:T(8,128)(2,1)}), bf16[64,16,128]{2,1,0:T(8,128)(2,1)S(1)}, u32[]{:S(2)}, u32[]{:S(2)}) async-start(bf16[64,16,128]{2,1,0:T(8,128)(2,1)} %bitcast.1), calls=%async_computation | async-start | bytes 524288 | tf_op jit(solution)/shard_map/all_to_all | solution.py:68
  84.0 0.1 convert_multiply_fusion
  84.1 11.3 %all-to-all-done = bf16[64,16,128]{2,1,0:T(8,128)(2,1)S(1)} async-done(((bf16[64,16,128]{2,1,0:T(8,128)(2,1)}), bf16[64,16,128]{2,1,0:T(8,128)(2,1)S(1)}, u32[]{:S(2)}, u32[]{:S(2)}) %all-to-all-start) | async-done | bytes 262176 | tf_op jit(solution)/shard_map/all_to_all | solution.py:68
  95.4 0.4 convolution_bitcast_fusion
  95.9 2.6 %fusion.2 = f32[16,16,64]{2,1,0:T(8,128)S(1)} fusion(f32[16,16,64]{2,1,0:T(8,128)S(1)} %copy.36, f32[16,16]{1,0:T(8,128)S(1)} %get-tuple-element.12, f32[64,64]{1,0:T(8,128)S(1)} %convert_multiply_fusion, pred[64,64]{1,0:T(8,128)(4,1)S(1)} %iota_compare_fusion), kind=kLoop, calls=%fused_computation.4 | loop fusion | flops 4177920 | bytes 152576 | tf_op jit(solution)/shard_map/reduce_sum | solution.py:34
  98.5 0.7 fusion.24
  99.2 0.5 fusion.6
  99.7 0.9 copy.38
  100.6 5.9 %all-to-all-start.1 = ((bf16[16,64,128]{2,0,1:T(8,128)(2,1)}), bf16[16,64,128]{2,0,1:T(8,128)(2,1)S(1)}, u32[]{:S(2)}, u32[]{:S(2)}) async-start(bf16[16,64,128]{2,0,1:T(8,128)(2,1)} %copy.38), calls=%async_computation.1 | async-start | bytes 524288 | tf_op jit(solution)/shard_map/all_to_all | solution.py:73
  106.6 10.8 %all-to-all-done.1 = bf16[16,64,128]{2,0,1:T(8,128)(2,1)S(1)} async-done(((bf16[16,64,128]{2,0,1:T(8,128)(2,1)}), bf16[16,64,128]{2,0,1:T(8,128)(2,1)S(1)}, u32[]{:S(2)}, u32[]{:S(2)}) %all-to-all-start.1) | async-done | bytes 262176 | tf_op jit(solution)/shard_map/all_to_all | solution.py:73
  117.4 0.1 fusion.12
  117.4 4.7 %fusion.3 = bf16[4096,128]{0,1:T(8,128)(2,1)S(1)} fusion(bf16[1024,128]{1,0:T(8,128)(2,1)S(1)} %fusion.12, bf16[1024,4096]{1,0:T(8,128)(2,1)} %param.9), kind=kOutput, calls=%fused_computation.6 | convolution fusion | flops 1074266112 | bytes 9699328 | tf_op jit(solution)/shard_map/dot_general | solution.py:75
  122.1 0.8 reshape.130
  122.9 2.2 %constant_dynamic-slice_fusion.1 = (bf16[2,1,1024,128]{2,1,0,3:T(2,128)(2,1)S(1)}, bf16[2,1,1024,128]{2,1,0,3:T(2,128)(2,1)S(1)}) fusion(bf16[2,2,1024,128]{2,1,0,3:T(2,128)(2,1)S(1)} %reshape.130, s32[]{:T(128)S(6)} %select_n.49, s32[]{:T(128)S(6)} %select_n.50), kind=kLoop, calls=%fused_computation.60 | loop fusion | bytes 2097160 | tf_op jit(solution)/shard_map/jit(dynamic_index_in_dim)/dynamic_slice | solution.py:45
  125.1 0.9 copy.40
  126.0 3.7 %collective-permute-start.1 = (bf16[2,1024,128]{2,1,0:T(8,128)(2,1)S(1)}, bf16[2,1024,128]{2,1,0:T(8,128)(2,1)S(1)}, u32[]{:S(2)}, u32[]{:S(2)}) collective-permute-start(bf16[2,1024,128]{2,1,0:T(8,128)(2,1)S(1)} %bitcast.48), channel_id=1, source_target_pairs={{0,1},{1,0},{2,3},{3,2},{4,5},{5,4},{6,7},{7,6},{8,9},{9,8},{10,11... | collective-permute-start | bytes 1572872 | tf_op jit(solution)/shard_map/ppermute | solution.py:46
  129.7 0.9 copy.45
  130.5 0.7 collective-permute-done.1
  131.2 0.1 convert_add_fusion
  131.4 2.7 %collective-permute-start.2 = (bf16[1024,128]{1,0:T(8,128)(2,1)S(1)}, bf16[1024,128]{1,0:T(8,128)(2,1)S(1)}, u32[]{:S(2)}, u32[]{:S(2)}) collective-permute-start(bf16[1024,128]{1,0:T(8,128)(2,1)S(1)} %fusion.18), channel_id=1, source_target_pairs={{0,2},{1,3},{2,0},{3,1},{4,6},{5,7},{6,4},{7,5},{8,10},{9,11},{10,... | collective-permute-start | bytes 786440 | tf_op jit(solution)/shard_map/ppermute | solution.py:50
  134.1 6.4 %collective-permute-done.2 = bf16[1024,128]{1,0:T(8,128)(2,1)S(1)} collective-permute-done((bf16[1024,128]{1,0:T(8,128)(2,1)S(1)}, bf16[1024,128]{1,0:T(8,128)(2,1)S(1)}, u32[]{:S(2)}, u32[]{:S(2)}) %collective-permute-start.2) | collective-permute-done | bytes 262176 | tf_op jit(solution)/shard_map/ppermute | solution.py:50
  140.4 0.8 fusion.13
  (11 shorter events, 0.2 us)
Async XLA Ops:
  1.7 66.3 %collective-permute-start = (bf16[3,1024,2]{1,2,0:T(2,128)(2,1)S(1)}, bf16[3,1024,2]{1,2,0:T(2,128)(2,1)S(1)}, u32[]{:S(2)}, u32[]{:S(2)}) collective-permute-start(bf16[3,1024,2]{1,2,0:T(2,128)(2,1)S(1)} %copy.44), channel_id=1, source_target_pairs={{0,4},{4,8},{8,12},{12,16},{16,20},{20,24},{24,28},{28,32},{32,36}... | collective-permute-start | bytes 36872 | tf_op jit(solution)/shard_map/ppermute | solution.py:10
  62.7 5.7 %copy-start = (bf16[3,1024,128]{2,1,0:T(8,128)(2,1)S(1)}, bf16[3,1024,128]{2,1,0:T(8,128)(2,1)}, u32[]{:S(2)}) copy-start(bf16[3,1024,128]{2,1,0:T(8,128)(2,1)} %param.5) | copy-start | bytes 2359300
  72.2 23.2 %all-to-all-start = ((bf16[64,16,128]{2,1,0:T(8,128)(2,1)}), bf16[64,16,128]{2,1,0:T(8,128)(2,1)S(1)}, u32[]{:S(2)}, u32[]{:S(2)}) async-start(bf16[64,16,128]{2,1,0:T(8,128)(2,1)} %bitcast.1), calls=%async_computation | async-start | bytes 524288 | tf_op jit(solution)/shard_map/all_to_all | solution.py:68
  100.6 16.8 %all-to-all-start.1 = ((bf16[16,64,128]{2,0,1:T(8,128)(2,1)}), bf16[16,64,128]{2,0,1:T(8,128)(2,1)S(1)}, u32[]{:S(2)}, u32[]{:S(2)}) async-start(bf16[16,64,128]{2,0,1:T(8,128)(2,1)} %copy.38), calls=%async_computation.1 | async-start | bytes 524288 | tf_op jit(solution)/shard_map/all_to_all | solution.py:73
  126.0 5.2 %collective-permute-start.1 = (bf16[2,1024,128]{2,1,0:T(8,128)(2,1)S(1)}, bf16[2,1024,128]{2,1,0:T(8,128)(2,1)S(1)}, u32[]{:S(2)}, u32[]{:S(2)}) collective-permute-start(bf16[2,1024,128]{2,1,0:T(8,128)(2,1)S(1)} %bitcast.48), channel_id=1, source_target_pairs={{0,1},{1,0},{2,3},{3,2},{4,5},{5,4},{6,7},{7,6},{8,9},{9,8},{10,11... | collective-permute-start | bytes 1572872 | tf_op jit(solution)/shard_map/ppermute | solution.py:46
  131.4 9.1 %collective-permute-start.2 = (bf16[1024,128]{1,0:T(8,128)(2,1)S(1)}, bf16[1024,128]{1,0:T(8,128)(2,1)S(1)}, u32[]{:S(2)}, u32[]{:S(2)}) collective-permute-start(bf16[1024,128]{1,0:T(8,128)(2,1)S(1)} %fusion.18), channel_id=1, source_target_pairs={{0,2},{1,3},{2,0},{3,1},{4,6},{5,7},{6,4},{7,5},{8,10},{9,11},{10,... | collective-permute-start | bytes 786440 | tf_op jit(solution)/shard_map/ppermute | solution.py:50

commit v4 on v3

--- a/solution.py
+++ b/solution.py
@@ -17,8 +17,9 @@
     life = life_slice[:, :, None]
     resid = resid_slice[:, :, None]
     taps = jnp.sum(resid * jnp.exp(-steps[None, None, :] / life), axis=0)
-    lag = jnp.arange(block, dtype=jnp.int32)[None, :] - jnp.arange(block, dtype=jnp.int32)[:, None]
-    toeplitz = jnp.where(lag[None] >= 0, jnp.take(taps, jnp.maximum(lag, 0), axis=1), 0.0)
+    padded = jnp.concatenate([taps, jnp.zeros_like(taps)], axis=1)
+    repeated = jnp.tile(padded, (1, block))[:, : block * (2 * block - 1)]
+    toeplitz = repeated.reshape(chan_here, block, 2 * block - 1)[:, :, :block]
     signal = pencils.astype(jnp.float32).reshape(chan_here, blocks, block)
     precise = lax.Precision.HIGH
     inside = jnp.einsum("cnj,cjt->cnt", signal, toeplitz, precision=precise)

time: 142 us -> 86.9 us (0.61)
  local copies, waits for them, and re-layouts: 69.5 us -> 14.9 us
    gather x2 -> x0, local copies, waits for them, and re-layouts: 59.7 us -> none  [modal_conv(): jnp.take(taps, jnp.maximum(lag, 0), axis=1)]
    reshape x0 -> x1, local copies, waits for them, and re-layouts: none -> 4.59 us  [modal_conv(): toeplitz = repeated.reshape(chan_here, block, 2 * block - 1)[:, :, :block]]
  transfers between devices with their start and end apart: 5 -> 5, of which waited for: 4 -> 4; matrix products, arithmetic and copies ran while one was open for 45% -> 9% of each run, Pallas kernels for 0% -> 0%
where the time goes in v4:
time: 86.9 us; the launch traced here: 86.5 us
  waiting for transfers between devices  29.1 us (33%)
  starting transfers between devices  28.5 us (33%)
  local copies, waits for them, and re-layouts  14.9 us (17%)
  other arithmetic  7.52 us (9%)
  matrix products  6.24 us (7%)
    all_to_all x1, starting transfers between devices, local(): lax.all_to_all(product, 'seq', split_axis=0, concat_axis=1, tiled=True)  11.8 us
    all_to_all x1, waiting for transfers between devices, local(): lax.all_to_all(product, 'seq', split_axis=0, concat_axis=1, tiled=True)  11.3 us
    all_to_all x1, waiting for transfers between devices, local(): lax.all_to_all(convolved, 'seq', split_axis=1, concat_axis=0, tiled=True)  10.8 us
    ppermute x1, waiting for transfers between devices, reduce_scatter_chan(): got2 = lax.ppermute(send2, 'chan', [(j, j ^ 2) for j in range(4)])  6.38 us
    all_to_all x1, starting transfers between devices, local(): lax.all_to_all(convolved, 'seq', split_axis=1, concat_axis=0, tiled=True)  5.94 us
    dot_general x1, matrix products, local(): lax.dot_general(out_weight, gated_rows, (((0,), (0,)), ((), ())), preferr...  4.68 us
    reshape x1, local copies, waits for them, and re-layouts, modal_conv(): toeplitz = repeated.reshape(chan_here, block, 2 * block - 1)[:, :, :block]  4.59 us
    ppermute x1, starting transfers between devices, from_behind(): return lax.ppermute(x, axis, pairs)  4.36 us
  transfers between devices with their start and end apart: 5, of which 4 were waited for; matrix products, arithmetic and copies ran while one was open for 9% of the time, Pallas kernels for 0%

profile of v4, /device:TPU:1, one launch (start us, length us, event | category | flops | bytes accessed | tf_op | source)
XLA Modules:
  0.0 86.5 jit_solution(728776242512803945)
XLA Ops:
  0.0 0.0 copy-start.2
  0.0 1.4 %slice.37 = bf16[3,1024,2]{2,1,0:T(8,128)(2,1)S(1)} slice(bf16[3,1024,128]{2,1,0:T(8,128)(2,1)} %param.5), slice={[0:3], [0:1024], [126:128]} | slice | bytes 24576 | tf_op jit(solution)/shard_map/slice | solution.py:58
  1.4 0.3 copy.38
  1.7 4.4 %collective-permute-start = (bf16[3,1024,2]{1,2,0:T(2,128)(2,1)S(1)}, bf16[3,1024,2]{1,2,0:T(2,128)(2,1)S(1)}, u32[]{:S(2)}, u32[]{:S(2)}) collective-permute-start(bf16[3,1024,2]{1,2,0:T(2,128)(2,1)S(1)} %copy.38), channel_id=1, source_target_pairs={{0,4},{4,8},{8,12},{12,16},{16,20},{20,24},{24,28},{28,32},{32,36}... | collective-permute-start | bytes 36872 | tf_op jit(solution)/shard_map/ppermute | solution.py:10
  6.1 0.0 copy-done.2
  6.2 0.8 constant_dynamic-slice_fusion.2
  6.9 0.1 copy.29
  7.0 0.1 copy.28
  7.1 0.1 fusion.21
  7.3 0.2 tile.4
  7.5 1.2 %copy.40 = f32[2,8,128,256]{3,1,2,0:T(8,128)S(1)} copy(f32[2,8,128,256]{3,2,1,0:T(8,128)S(1)} %bitcast.43) | data formatting | bytes 4194304
  8.7 0.1 slice.54
  8.8 0.0 copy-start.1
  8.8 4.6 %reshape.90 = f32[16,128,255]{2,1,0:T(8,128)} reshape(f32[16,32640]{1,0:T(8,128)S(1)} %slice.54) | data formatting | bytes 4177920 | tf_op jit(solution)/shard_map/reshape | solution.py:22
  13.4 0.0 collective-permute-done
  13.4 0.4 copy.26
  13.9 0.0 copy-done.1
  13.9 0.6 maximum_convert_fusion
  14.5 2.4 %fusion.4 = f32[3,1024,128]{2,1,0:T(8,128)S(1)} fusion(f32[3,1024,130]{2,1,0:T(8,128)S(1)} %maximum_convert_fusion, f32[3,1024]{1,0:T(4,128)S(1)} %get-tuple-element.10, f32[3,1024]{1,0:T(4,128)S(1)} %get-tuple-element.11, f32[3,1024]{1,0:T(4,128)S(1)} %bitcast.46), kind=kLoop, calls=%fused_computation.7 | loop fusion | flops 1966080 | bytes 6328320 | tf_op jit(solution)/shard_map/add | solution.py:62
  16.8 0.8 fusion.8
  17.6 11.8 %all-to-all-start = ((bf16[64,16,128]{2,1,0:T(8,128)(2,1)}), bf16[64,16,128]{2,1,0:T(8,128)(2,1)S(1)}, u32[]{:S(2)}, u32[]{:S(2)}) async-start(bf16[64,16,128]{2,1,0:T(8,128)(2,1)} %bitcast.1), calls=%async_computation | async-start | bytes 524288 | tf_op jit(solution)/shard_map/all_to_all | solution.py:69
  29.4 0.1 convert_multiply_fusion
  29.5 11.3 %all-to-all-done = bf16[64,16,128]{2,1,0:T(8,128)(2,1)S(1)} async-done(((bf16[64,16,128]{2,1,0:T(8,128)(2,1)}), bf16[64,16,128]{2,1,0:T(8,128)(2,1)S(1)}, u32[]{:S(2)}, u32[]{:S(2)}) %all-to-all-start) | async-done | bytes 262176 | tf_op jit(solution)/shard_map/all_to_all | solution.py:69
  40.8 0.0 copy-start
  40.8 0.4 convolution_bitcast_fusion
  41.3 2.6 %fusion.2 = f32[16,16,64]{2,1,0:T(8,128)S(1)} fusion(f32[16,16,64]{2,1,0:T(8,128)S(1)} %copy.30, f32[16,16]{1,0:T(8,128)S(1)} %get-tuple-element.12, f32[64,64]{1,0:T(8,128)S(1)} %convert_multiply_fusion, pred[64,64]{1,0:T(8,128)(4,1)S(1)} %iota_compare_fusion), kind=kLoop, calls=%fused_computation.3 | loop fusion | flops 4177920 | bytes 152576 | tf_op jit(solution)/shard_map/reduce_sum | solution.py:35
  43.9 0.7 fusion.18
  44.6 0.0 copy-done
  44.6 0.4 fusion.6
  45.1 0.9 %copy.32 = bf16[16,64,128]{2,0,1:T(8,128)(2,1)} copy(bf16[16,64,128]{2,1,0:T(8,128)(2,1)S(1)} %fusion.6) | data formatting | bytes 524288 | tf_op jit(solution)/shard_map/convert_element_type | solution.py:73
  45.9 5.9 %all-to-all-start.1 = ((bf16[16,64,128]{2,0,1:T(8,128)(2,1)}), bf16[16,64,128]{2,0,1:T(8,128)(2,1)S(1)}, u32[]{:S(2)}, u32[]{:S(2)}) async-start(bf16[16,64,128]{2,0,1:T(8,128)(2,1)} %copy.32), calls=%async_computation.1 | async-start | bytes 524288 | tf_op jit(solution)/shard_map/all_to_all | solution.py:74
  51.9 10.8 %all-to-all-done.1 = bf16[16,64,128]{2,0,1:T(8,128)(2,1)S(1)} async-done(((bf16[16,64,128]{2,0,1:T(8,128)(2,1)}), bf16[16,64,128]{2,0,1:T(8,128)(2,1)S(1)}, u32[]{:S(2)}, u32[]{:S(2)}) %all-to-all-start.1) | async-done | bytes 262176 | tf_op jit(solution)/shard_map/all_to_all | solution.py:74
  62.7 0.1 fusion.10
  62.8 4.7 %fusion.3 = bf16[4096,128]{0,1:T(8,128)(2,1)S(1)} fusion(bf16[1024,128]{1,0:T(8,128)(2,1)S(1)} %fusion.10, bf16[1024,4096]{1,0:T(8,128)(2,1)} %param.9), kind=kOutput, calls=%fused_computation.5 | convolution fusion | flops 1074266112 | bytes 9699328 | tf_op jit(solution)/shard_map/dot_general | solution.py:76
  67.4 0.8 reshape.91
  68.3 2.2 %constant_dynamic-slice_fusion.1 = (bf16[2,1,1024,128]{2,1,0,3:T(2,128)(2,1)S(1)}, bf16[2,1,1024,128]{2,1,0,3:T(2,128)(2,1)S(1)}) fusion(bf16[2,2,1024,128]{2,1,0,3:T(2,128)(2,1)S(1)} %reshape.91, s32[]{:T(128)S(6)} %select_n.36, s32[]{:T(128)S(6)} %select_n.37), kind=kLoop, calls=%fused_computation.49 | loop fusion | bytes 2097160 | tf_op jit(solution)/shard_map/jit(dynamic_index_in_dim)/dynamic_slice | solution.py:46
  70.4 0.9 %copy.34 = bf16[2,1,1024,128]{3,2,0,1:T(8,128)(2,1)S(1)} copy(bf16[2,1,1024,128]{2,1,0,3:T(2,128)(2,1)S(1)} %get-tuple-element.6) | data formatting | bytes 1048576 | tf_op jit(solution)/shard_map/jit(dynamic_index_in_dim)/dynamic_slice | solution.py:45
  71.3 3.7 %collective-permute-start.1 = (bf16[2,1024,128]{2,1,0:T(8,128)(2,1)S(1)}, bf16[2,1024,128]{2,1,0:T(8,128)(2,1)S(1)}, u32[]{:S(2)}, u32[]{:S(2)}) collective-permute-start(bf16[2,1024,128]{2,1,0:T(8,128)(2,1)S(1)} %bitcast.45), channel_id=1, source_target_pairs={{0,1},{1,0},{2,3},{3,2},{4,5},{5,4},{6,7},{7,6},{8,9},{9,8},{10,11... | collective-permute-start | bytes 1572872 | tf_op jit(solution)/shard_map/ppermute | solution.py:47
  75.0 0.9 copy.39
  75.9 0.7 collective-permute-done.1
  76.6 0.1 convert_add_fusion
  76.7 2.7 %collective-permute-start.2 = (bf16[1024,128]{1,0:T(8,128)(2,1)S(1)}, bf16[1024,128]{1,0:T(8,128)(2,1)S(1)}, u32[]{:S(2)}, u32[]{:S(2)}) collective-permute-start(bf16[1024,128]{1,0:T(8,128)(2,1)S(1)} %fusion.12), channel_id=1, source_target_pairs={{0,2},{1,3},{2,0},{3,1},{4,6},{5,7},{6,4},{7,5},{8,10},{9,11},{10,... | collective-permute-start | bytes 786440 | tf_op jit(solution)/shard_map/ppermute | solution.py:51
  79.4 6.4 %collective-permute-done.2 = bf16[1024,128]{1,0:T(8,128)(2,1)S(1)} collective-permute-done((bf16[1024,128]{1,0:T(8,128)(2,1)S(1)}, bf16[1024,128]{1,0:T(8,128)(2,1)S(1)}, u32[]{:S(2)}, u32[]{:S(2)}) %collective-permute-start.2) | collective-permute-done | bytes 262176 | tf_op jit(solution)/shard_map/ppermute | solution.py:51
  85.8 0.8 fusion.11
  (11 shorter events, 0.2 us)
Async XLA Ops:
  0.0 6.1 %copy-start.2 = (f32[3,3,1024]{2,1,0:T(4,128)S(1)}, f32[3,3,1024]{2,1,0:T(4,128)}, u32[]{:S(2)}) copy-start(f32[3,3,1024]{2,1,0:T(4,128)} %param.6) | copy-start | bytes 110596
  1.7 11.7 %collective-permute-start = (bf16[3,1024,2]{1,2,0:T(2,128)(2,1)S(1)}, bf16[3,1024,2]{1,2,0:T(2,128)(2,1)S(1)}, u32[]{:S(2)}, u32[]{:S(2)}) collective-permute-start(bf16[3,1024,2]{1,2,0:T(2,128)(2,1)S(1)} %copy.38), channel_id=1, source_target_pairs={{0,4},{4,8},{8,12},{12,16},{16,20},{20,24},{24,28},{28,32},{32,36}... | collective-permute-start | bytes 36872 | tf_op jit(solution)/shard_map/ppermute | solution.py:10
  8.8 5.0 %copy-start.1 = (bf16[3,1024,128]{2,1,0:T(8,128)(2,1)S(1)}, bf16[3,1024,128]{2,1,0:T(8,128)(2,1)}, u32[]{:S(2)}) copy-start(bf16[3,1024,128]{2,1,0:T(8,128)(2,1)} %param.5) | copy-start | bytes 2359300
  17.6 23.2 %all-to-all-start = ((bf16[64,16,128]{2,1,0:T(8,128)(2,1)}), bf16[64,16,128]{2,1,0:T(8,128)(2,1)S(1)}, u32[]{:S(2)}, u32[]{:S(2)}) async-start(bf16[64,16,128]{2,1,0:T(8,128)(2,1)} %bitcast.1), calls=%async_computation | async-start | bytes 524288 | tf_op jit(solution)/shard_map/all_to_all | solution.py:69
  40.8 3.9 %copy-start = (f32[16,128,255]{2,1,0:T(8,128)S(1)}, f32[16,128,255]{2,1,0:T(8,128)}, u32[]{:S(2)}) copy-start(f32[16,128,255]{2,1,0:T(8,128)} %reshape.90) | copy-start | bytes 6266884
  45.9 16.8 %all-to-all-start.1 = ((bf16[16,64,128]{2,0,1:T(8,128)(2,1)}), bf16[16,64,128]{2,0,1:T(8,128)(2,1)S(1)}, u32[]{:S(2)}, u32[]{:S(2)}) async-start(bf16[16,64,128]{2,0,1:T(8,128)(2,1)} %copy.32), calls=%async_computation.1 | async-start | bytes 524288 | tf_op jit(solution)/shard_map/all_to_all | solution.py:74
  71.3 5.2 %collective-permute-start.1 = (bf16[2,1024,128]{2,1,0:T(8,128)(2,1)S(1)}, bf16[2,1024,128]{2,1,0:T(8,128)(2,1)S(1)}, u32[]{:S(2)}, u32[]{:S(2)}) collective-permute-start(bf16[2,1024,128]{2,1,0:T(8,128)(2,1)S(1)} %bitcast.45), channel_id=1, source_target_pairs={{0,1},{1,0},{2,3},{3,2},{4,5},{5,4},{6,7},{7,6},{8,9},{9,8},{10,11... | collective-permute-start | bytes 1572872 | tf_op jit(solution)/shard_map/ppermute | solution.py:47
  76.7 9.1 %collective-permute-start.2 = (bf16[1024,128]{1,0:T(8,128)(2,1)S(1)}, bf16[1024,128]{1,0:T(8,128)(2,1)S(1)}, u32[]{:S(2)}, u32[]{:S(2)}) collective-permute-start(bf16[1024,128]{1,0:T(8,128)(2,1)S(1)} %fusion.12), channel_id=1, source_target_pairs={{0,2},{1,3},{2,0},{3,1},{4,6},{5,7},{6,4},{7,5},{8,10},{9,11},{10,... | collective-permute-start | bytes 786440 | tf_op jit(solution)/shard_map/ppermute | solution.py:51

commit v5 on v3

--- a/solution.py
+++ b/solution.py
@@ -16,9 +16,12 @@
     steps = jnp.arange(block, dtype=jnp.int32).astype(jnp.float32)
     life = life_slice[:, :, None]
     resid = resid_slice[:, :, None]
-    taps = jnp.sum(resid * jnp.exp(-steps[None, None, :] / life), axis=0)
+    offs = steps - float(block // 2)
+    rising = resid * jnp.exp(offs[None, None, :] / life)
+    falling = jnp.exp(-offs[None, None, :] / life)
+    full = jnp.einsum("rcj,rct->cjt", rising, falling, precision=lax.Precision.HIGHEST)
     lag = jnp.arange(block, dtype=jnp.int32)[None, :] - jnp.arange(block, dtype=jnp.int32)[:, None]
-    toeplitz = jnp.where(lag[None] >= 0, jnp.take(taps, jnp.maximum(lag, 0), axis=1), 0.0)
+    toeplitz = jnp.where(lag[None] >= 0, full, 0.0)
     signal = pencils.astype(jnp.float32).reshape(chan_here, blocks, block)
     precise = lax.Precision.HIGH
     inside = jnp.einsum("cnj,cjt->cnt", signal, toeplitz, precision=precise)
@@ -40,15 +43,15 @@
 def reduce_scatter_chan(partial):
     index = lax.axis_index("chan")
     chip, core = index // 2, index % 2
-    quarters = partial.reshape(2, 2, partial.shape[0] // 4, partial.shape[1])
-    send = lax.dynamic_index_in_dim(quarters, 1 - core, 1, keepdims=False)
-    keep = lax.dynamic_index_in_dim(quarters, core, 1, keepdims=False)
+    quarters = partial.reshape(partial.shape[0], 2, 2, partial.shape[1] // 4)
+    send = lax.dynamic_index_in_dim(quarters, 1 - core, 2, keepdims=False)
+    keep = lax.dynamic_index_in_dim(quarters, core, 2, keepdims=False)
     got = lax.ppermute(send, "chan", [(j, j ^ 1) for j in range(4)])
     halves = keep.astype(jnp.float32) + got.astype(jnp.float32)
-    send2 = lax.dynamic_index_in_dim(halves, 1 - chip, 0, keepdims=False).astype(jnp.bfloat16)
-    keep2 = lax.dynamic_index_in_dim(halves, chip, 0, keepdims=False)
+    send2 = lax.dynamic_index_in_dim(halves, 1 - chip, 1, keepdims=False).astype(jnp.bfloat16)
+    keep2 = lax.dynamic_index_in_dim(halves, chip, 1, keepdims=False)
     got2 = lax.ppermute(send2, "chan", [(j, j ^ 2) for j in range(4)])
-    return (keep2 + got2.astype(jnp.float32)).astype(jnp.bfloat16)
+    return (keep2 + got2.astype(jnp.float32)).astype(jnp.bfloat16).T
 
 
 def local(qkv, taps, lifetimes, residues, out_weight):
@@ -73,7 +76,7 @@
     returned = lax.all_to_all(convolved, "seq", split_axis=1, concat_axis=0, tiled=True)
     gated_rows = (filtered[0] * returned.astype(jnp.float32)).astype(jnp.bfloat16)
     partial = lax.dot_general(
-        out_weight, gated_rows, (((0,), (0,)), ((), ())), preferred_element_type=jnp.float32
+        gated_rows, out_weight, (((0,), (0,)), ((), ())), preferred_element_type=jnp.float32
     ).astype(jnp.bfloat16)
     return reduce_scatter_chan(partial)
 

time: 142 us -> 82.2 us (0.58)
  local copies, waits for them, and re-layouts: 69.5 us -> 9.76 us
  waiting for transfers between devices: 29.1 us -> 26.7 us
  matrix products: 6.31 us -> 8.18 us
    gather x2 -> x0, local copies, waits for them, and re-layouts: 59.7 us -> none  [modal_conv(): jnp.take(taps, jnp.maximum(lag, 0), axis=1)]
    all_to_all x1, waiting for transfers between devices: 11.3 us -> 8.82 us  [local(): lax.all_to_all(product, 'seq', split_axis=0, concat_axis=1, tiled=True)]
    dot_general x1 -> x2, matrix products: 4.68 us -> 6.61 us  [the longest x1 4.68 us: local(): lax.dot_general(gated_rows, out_weight, (((0,), (0,)), ((), ())), preferr...]
  transfers between devices with their start and end apart: 5 -> 5, of which waited for: 4 -> 4; matrix products, arithmetic and copies ran while one was open for 45% -> 6% of each run, Pallas kernels for 0% -> 0%
where the time goes in v5:
time: 82.2 us; the launch traced here: 81.9 us
  starting transfers between devices  29.6 us (36%)
  waiting for transfers between devices  26.7 us (32%)
  local copies, waits for them, and re-layouts  9.76 us (12%)
  matrix products  8.18 us (10%)
  other arithmetic  7.38 us (9%)
    all_to_all x1, starting transfers between devices, local(): lax.all_to_all(product, 'seq', split_axis=0, concat_axis=1, tiled=True)  12.9 us
    all_to_all x1, waiting for transfers between devices, local(): lax.all_to_all(convolved, 'seq', split_axis=1, concat_axis=0, tiled=True)  10.8 us
    all_to_all x1, waiting for transfers between devices, local(): lax.all_to_all(product, 'seq', split_axis=0, concat_axis=1, tiled=True)  8.82 us
    ppermute x1, waiting for transfers between devices, reduce_scatter_chan(): got2 = lax.ppermute(send2, 'chan', [(j, j ^ 2) for j in range(4)])  6.38 us
    all_to_all x1, starting transfers between devices, local(): lax.all_to_all(convolved, 'seq', split_axis=1, concat_axis=0, tiled=True)  5.03 us
    dot_general x1, matrix products, local(): lax.dot_general(gated_rows, out_weight, (((0,), (0,)), ((), ())), preferr...  4.68 us
    ppermute x1, starting transfers between devices, reduce_scatter_chan(): got = lax.ppermute(send, 'chan', [(j, j ^ 1) for j in range(4)])  4.63 us
    ppermute x1, starting transfers between devices, from_behind(): return lax.ppermute(x, axis, pairs)  4.36 us
  transfers between devices with their start and end apart: 5, of which 4 were waited for; matrix products, arithmetic and copies ran while one was open for 6% of the time, Pallas kernels for 0%

profile of v5, /device:TPU:1, one launch (start us, length us, event | category | flops | bytes accessed | tf_op | source)
XLA Modules:
  0.0 81.9 jit_solution(16104759910760346392)
XLA Ops:
  0.0 0.0 copy-start
  0.0 1.5 %slice.31 = bf16[3,1024,2]{2,1,0:T(8,128)(2,1)S(1)} slice(bf16[3,1024,128]{2,1,0:T(8,128)(2,1)} %param.5), slice={[0:3], [0:1024], [126:128]} | slice | bytes 24576 | tf_op jit(solution)/shard_map/slice | solution.py:60
  1.5 0.3 copy.38
  1.8 4.4 %collective-permute-start = (bf16[3,1024,2]{1,2,0:T(2,128)(2,1)S(1)}, bf16[3,1024,2]{1,2,0:T(2,128)(2,1)S(1)}, u32[]{:S(2)}, u32[]{:S(2)}) collective-permute-start(bf16[3,1024,2]{1,2,0:T(2,128)(2,1)S(1)} %copy.38), channel_id=1, source_target_pairs={{0,4},{4,8},{8,12},{12,16},{16,20},{20,24},{24,28},{28,32},{32,36}... | collective-permute-start | bytes 36872 | tf_op jit(solution)/shard_map/ppermute | solution.py:10
  6.2 0.9 %fusion.32 = (f32[3,1,1024]{2,1,0:T(1,128)S(1)}, f32[3,1,1024]{2,1,0:T(1,128)S(1)}, f32[3,1,1024]{2,1,0:T(1,128)S(1)}) fusion(f32[3,3,1024]{2,1,0:T(4,128)} %param.6), kind=kLoop, calls=%fused_computation.62 | loop fusion | bytes 73728 | tf_op jit(solution)/shard_map/slice | solution.py:64
  7.2 0.8 constant_dynamic-slice_fusion.2
  8.0 0.0 collective-permute-done
  8.0 0.4 copy.26
  8.4 0.0 copy-done
  8.4 0.6 maximum_convert_fusion
  9.1 2.4 %fusion.3 = f32[3,1024,128]{2,1,0:T(8,128)S(1)} fusion(f32[3,1024,130]{2,1,0:T(8,128)S(1)} %maximum_convert_fusion, f32[3,1024]{1,0:T(4,128)S(1)} %get-tuple-element.10, f32[3,1024]{1,0:T(4,128)S(1)} %get-tuple-element.11, f32[3,1024]{1,0:T(4,128)S(1)} %bitcast.43), kind=kLoop, calls=%fused_computation.6 | loop fusion | flops 1966080 | bytes 6328320 | tf_op jit(solution)/shard_map/add | solution.py:64
  11.4 0.8 fusion.6
  12.2 12.9 %all-to-all-start = ((bf16[64,16,128]{2,1,0:T(8,128)(2,1)}), bf16[64,16,128]{2,1,0:T(8,128)(2,1)S(1)}, u32[]{:S(2)}, u32[]{:S(2)}) async-start(bf16[64,16,128]{2,1,0:T(8,128)(2,1)} %bitcast.1), calls=%async_computation | async-start | bytes 524288 | tf_op jit(solution)/shard_map/all_to_all | solution.py:71
  25.1 0.1 copy.29
  25.2 0.1 copy.28
  25.2 0.1 convert_multiply_fusion
  25.3 1.9 %convolution_select_fusion = f32[16,128,128]{2,1,0:T(8,128)S(1)} fusion(pred[128,128]{1,0:T(8,128)(4,1)S(1)} %subtract_compare_fusion, f32[128]{0:T(128)S(1)} %get-tuple-element.15, f32[16,16]{0,1:T(8,128)S(1)} %copy.29, f32[128]{0:T(128)S(1)} %get-tuple-element.14, f32[16,16]{0,1:T(8,128)S(1)} %copy.28), kind=kOutput, calls=%fused_computation.11 | convolution fusion | flops 50692096 | bytes 1068032 | tf_op jit(solution)/shard_map/rcj,rct->cjt/dot_general | solution.py:22
  27.2 8.8 %all-to-all-done = bf16[64,16,128]{2,1,0:T(8,128)(2,1)S(1)} async-done(((bf16[64,16,128]{2,1,0:T(8,128)(2,1)}), bf16[64,16,128]{2,1,0:T(8,128)(2,1)S(1)}, u32[]{:S(2)}, u32[]{:S(2)}) %all-to-all-start) | async-done | bytes 262176 | tf_op jit(solution)/shard_map/all_to_all | solution.py:71
  36.1 0.4 convolution_bitcast_fusion
  36.6 2.6 %fusion.2 = f32[16,16,64]{2,1,0:T(8,128)S(1)} fusion(f32[16,16,64]{2,1,0:T(8,128)S(1)} %copy.30, f32[16,16]{1,0:T(8,128)S(1)} %get-tuple-element.12, f32[64,64]{1,0:T(8,128)S(1)} %convert_multiply_fusion, pred[64,64]{1,0:T(8,128)(4,1)S(1)} %iota_compare_fusion), kind=kLoop, calls=%fused_computation.3 | loop fusion | flops 4177920 | bytes 152576 | tf_op jit(solution)/shard_map/reduce_sum | solution.py:37
  39.2 0.7 fusion.17
  39.9 0.4 fusion.5
  40.3 0.9 %copy.32 = bf16[16,64,128]{2,0,1:T(8,128)(2,1)} copy(bf16[16,64,128]{2,1,0:T(8,128)(2,1)S(1)} %fusion.5) | data formatting | bytes 524288 | tf_op jit(solution)/shard_map/convert_element_type | solution.py:75
  41.2 5.0 %all-to-all-start.1 = ((bf16[16,64,128]{2,0,1:T(8,128)(2,1)}), bf16[16,64,128]{2,0,1:T(8,128)(2,1)S(1)}, u32[]{:S(2)}, u32[]{:S(2)}) async-start(bf16[16,64,128]{2,0,1:T(8,128)(2,1)} %copy.32), calls=%async_computation.1 | async-start | bytes 524288 | tf_op jit(solution)/shard_map/all_to_all | solution.py:76
  46.3 10.8 %all-to-all-done.1 = bf16[16,64,128]{2,0,1:T(8,128)(2,1)S(1)} async-done(((bf16[16,64,128]{2,0,1:T(8,128)(2,1)}), bf16[16,64,128]{2,0,1:T(8,128)(2,1)S(1)}, u32[]{:S(2)}, u32[]{:S(2)}) %all-to-all-start.1) | async-done | bytes 262176 | tf_op jit(solution)/shard_map/all_to_all | solution.py:76
  57.1 0.1 fusion.8
  57.2 4.7 %convolution_convert_fusion = bf16[128,4096]{1,0:T(8,128)(2,1)S(1)} fusion(bf16[1024,128]{1,0:T(8,128)(2,1)S(1)} %fusion.8, bf16[1024,4096]{1,0:T(8,128)(2,1)} %param.9), kind=kOutput, calls=%fused_computation.4 | convolution fusion | flops 1074266112 | bytes 9699328 | tf_op jit(solution)/shard_map/dot_general | solution.py:78
  61.8 0.8 reshape.100
  62.6 2.2 %constant_dynamic-slice_fusion.1 = (bf16[128,2,1,1024]{3,2,1,0:T(2,128)(2,1)S(1)}, bf16[128,2,1,1024]{3,2,1,0:T(2,128)(2,1)S(1)}) fusion(bf16[128,2,2,1024]{3,2,1,0:T(2,128)(2,1)S(1)} %reshape.100, s32[]{:T(128)S(6)} %select_n.41, s32[]{:T(128)S(6)} %select_n.42), kind=kLoop, calls=%fused_computation.54 | loop fusion | bytes 2097160 | tf_op jit(solution)/shard_map/jit(dynamic_index_in_dim)/dynamic_slice | solution.py:48
  64.8 0.9 %copy.34 = bf16[128,2,1,1024]{0,3,1,2:T(8,128)(2,1)S(1)} copy(bf16[128,2,1,1024]{3,2,1,0:T(2,128)(2,1)S(1)} %get-tuple-element.6) | data formatting | bytes 1048576 | tf_op jit(solution)/shard_map/jit(dynamic_index_in_dim)/dynamic_slice | solution.py:47
  65.7 4.6 %collective-permute-start.1 = (bf16[128,2,1024]{0,2,1:T(8,128)(2,1)S(1)}, bf16[128,2,1024]{0,2,1:T(8,128)(2,1)S(1)}, u32[]{:S(2)}, u32[]{:S(2)}) collective-permute-start(bf16[128,2,1024]{0,2,1:T(8,128)(2,1)S(1)} %bitcast.42), channel_id=1, source_target_pairs={{0,1},{1,0},{2,3},{3,2},{4,5},{5,4},{6,7},{7,6},{8,9},{9,8},{10,11... | collective-permute-start | bytes 1572872 | tf_op jit(solution)/shard_map/ppermute | solution.py:49
  70.3 0.9 %copy.39 = bf16[128,2,1,1024]{0,3,1,2:T(8,128)(2,1)S(1)} copy(bf16[128,2,1,1024]{3,2,1,0:T(2,128)(2,1)S(1)} %get-tuple-element.5) | data formatting | bytes 1048576
  71.2 0.7 collective-permute-done.1
  71.9 0.1 convert_add_fusion
  72.0 2.7 %collective-permute-start.2 = (bf16[128,1024]{0,1:T(8,128)(2,1)S(1)}, bf16[128,1024]{0,1:T(8,128)(2,1)S(1)}, u32[]{:S(2)}, u32[]{:S(2)}) collective-permute-start(bf16[128,1024]{0,1:T(8,128)(2,1)S(1)} %fusion.10), channel_id=1, source_target_pairs={{0,2},{1,3},{2,0},{3,1},{4,6},{5,7},{6,4},{7,5},{8,10},{9,11},{10,... | collective-permute-start | bytes 786440 | tf_op jit(solution)/shard_map/ppermute | solution.py:53
  74.7 6.4 %collective-permute-done.2 = bf16[128,1024]{0,1:T(8,128)(2,1)S(1)} collective-permute-done((bf16[128,1024]{0,1:T(8,128)(2,1)S(1)}, bf16[128,1024]{0,1:T(8,128)(2,1)S(1)}, u32[]{:S(2)}, u32[]{:S(2)}) %collective-permute-start.2) | collective-permute-done | bytes 262176 | tf_op jit(solution)/shard_map/ppermute | solution.py:53
  81.1 0.8 fusion.11
  (10 shorter events, 0.1 us)
Async XLA Ops:
  0.0 8.4 %copy-start = (bf16[3,1024,128]{2,1,0:T(8,128)(2,1)S(1)}, bf16[3,1024,128]{2,1,0:T(8,128)(2,1)}, u32[]{:S(2)}) copy-start(bf16[3,1024,128]{2,1,0:T(8,128)(2,1)} %param.5) | copy-start | bytes 2359300
  1.8 6.2 %collective-permute-start = (bf16[3,1024,2]{1,2,0:T(2,128)(2,1)S(1)}, bf16[3,1024,2]{1,2,0:T(2,128)(2,1)S(1)}, u32[]{:S(2)}, u32[]{:S(2)}) collective-permute-start(bf16[3,1024,2]{1,2,0:T(2,128)(2,1)S(1)} %copy.38), channel_id=1, source_target_pairs={{0,4},{4,8},{8,12},{12,16},{16,20},{20,24},{24,28},{28,32},{32,36}... | collective-permute-start | bytes 36872 | tf_op jit(solution)/shard_map/ppermute | solution.py:10
  12.2 23.9 %all-to-all-start = ((bf16[64,16,128]{2,1,0:T(8,128)(2,1)}), bf16[64,16,128]{2,1,0:T(8,128)(2,1)S(1)}, u32[]{:S(2)}, u32[]{:S(2)}) async-start(bf16[64,16,128]{2,1,0:T(8,128)(2,1)} %bitcast.1), calls=%async_computation | async-start | bytes 524288 | tf_op jit(solution)/shard_map/all_to_all | solution.py:71
  41.2 15.9 %all-to-all-start.1 = ((bf16[16,64,128]{2,0,1:T(8,128)(2,1)}), bf16[16,64,128]{2,0,1:T(8,128)(2,1)S(1)}, u32[]{:S(2)}, u32[]{:S(2)}) async-start(bf16[16,64,128]{2,0,1:T(8,128)(2,1)} %copy.32), calls=%async_computation.1 | async-start | bytes 524288 | tf_op jit(solution)/shard_map/all_to_all | solution.py:76
  65.7 6.2 %collective-permute-start.1 = (bf16[128,2,1024]{0,2,1:T(8,128)(2,1)S(1)}, bf16[128,2,1024]{0,2,1:T(8,128)(2,1)S(1)}, u32[]{:S(2)}, u32[]{:S(2)}) collective-permute-start(bf16[128,2,1024]{0,2,1:T(8,128)(2,1)S(1)} %bitcast.42), channel_id=1, source_target_pairs={{0,1},{1,0},{2,3},{3,2},{4,5},{5,4},{6,7},{7,6},{8,9},{9,8},{10,11... | collective-permute-start | bytes 1572872 | tf_op jit(solution)/shard_map/ppermute | solution.py:49
  72.0 9.1 %collective-permute-start.2 = (bf16[128,1024]{0,1:T(8,128)(2,1)S(1)}, bf16[128,1024]{0,1:T(8,128)(2,1)S(1)}, u32[]{:S(2)}, u32[]{:S(2)}) collective-permute-start(bf16[128,1024]{0,1:T(8,128)(2,1)S(1)} %fusion.10), channel_id=1, source_target_pairs={{0,2},{1,3},{2,0},{3,1},{4,6},{5,7},{6,4},{7,5},{8,10},{9,11},{10,... | collective-permute-start | bytes 786440 | tf_op jit(solution)/shard_map/ppermute | solution.py:53

commit v6 on v5

--- a/solution.py
+++ b/solution.py
@@ -43,13 +43,16 @@
 def reduce_scatter_chan(partial):
     index = lax.axis_index("chan")
     chip, core = index // 2, index % 2
-    quarters = partial.reshape(partial.shape[0], 2, 2, partial.shape[1] // 4)
-    send = lax.dynamic_index_in_dim(quarters, 1 - core, 2, keepdims=False)
-    keep = lax.dynamic_index_in_dim(quarters, core, 2, keepdims=False)
+    width = partial.shape[1] // 4
+    quarter = [partial[:, q * width : (q + 1) * width] for q in range(4)]
+    mine = core == 0
+    send = jnp.stack([jnp.where(mine, quarter[2 * h + 1], quarter[2 * h]) for h in range(2)])
+    keep = jnp.stack([jnp.where(mine, quarter[2 * h], quarter[2 * h + 1]) for h in range(2)])
     got = lax.ppermute(send, "chan", [(j, j ^ 1) for j in range(4)])
     halves = keep.astype(jnp.float32) + got.astype(jnp.float32)
-    send2 = lax.dynamic_index_in_dim(halves, 1 - chip, 1, keepdims=False).astype(jnp.bfloat16)
-    keep2 = lax.dynamic_index_in_dim(halves, chip, 1, keepdims=False)
+    first = chip == 0
+    send2 = jnp.where(first, halves[1], halves[0]).astype(jnp.bfloat16)
+    keep2 = jnp.where(first, halves[0], halves[1])
     got2 = lax.ppermute(send2, "chan", [(j, j ^ 2) for j in range(4)])
     return (keep2 + got2.astype(jnp.float32)).astype(jnp.bfloat16).T
 

time: 82.2 us -> 78.8 us (0.959)
  local copies, waits for them, and re-layouts: 9.76 us -> 5.87 us
  waiting for transfers between devices: 26.7 us -> 27.7 us
    dynamic_slice x2 -> x0, local copies, waits for them, and re-layouts: 3.04 us -> none  [the longest x1 2.17 us: reduce_scatter_chan(): keep = lax.dynamic_index_in_dim(quarters, core, 2, keepdims=False)]
    ppermute x1, waiting for transfers between devices: 0.67 us -> 1.54 us  [reduce_scatter_chan(): got = lax.ppermute(send, 'chan', [(j, j ^ 1) for j in range(4)])]
    unnamed x6 -> x5, local copies, waits for them, and re-layouts: 1.18 us -> 0.32 us
    transpose x0 -> x1, local copies, waits for them, and re-layouts: none -> 0.84 us  [reduce_scatter_chan(): return (keep2 + got2.astype(jnp.float32)).astype(jnp.bfloat16).T]
  transfers between devices with their start and end apart: 5 -> 5, of which waited for: 4 -> 4; matrix products, arithmetic and copies ran while one was open for 6% -> 5% of each run, Pallas kernels for 0% -> 0%
where the time goes in v6:
time: 78.8 us; the launch traced here: 78.4 us
  starting transfers between devices  29.4 us (37%)
  waiting for transfers between devices  27.7 us (35%)
  matrix products  8.18 us (10%)
  other arithmetic  6.96 us (9%)
  local copies, waits for them, and re-layouts  5.87 us (7%)
    all_to_all x1, starting transfers between devices, local(): lax.all_to_all(product, 'seq', split_axis=0, concat_axis=1, tiled=True)  12.9 us
    all_to_all x1, waiting for transfers between devices, local(): lax.all_to_all(convolved, 'seq', split_axis=1, concat_axis=0, tiled=True)  11 us
    all_to_all x1, waiting for transfers between devices, local(): lax.all_to_all(product, 'seq', split_axis=0, concat_axis=1, tiled=True)  8.82 us
    ppermute x1, waiting for transfers between devices, reduce_scatter_chan(): got2 = lax.ppermute(send2, 'chan', [(j, j ^ 2) for j in range(4)])  6.37 us
    all_to_all x1, starting transfers between devices, local(): lax.all_to_all(convolved, 'seq', split_axis=1, concat_axis=0, tiled=True)  4.85 us
    dot_general x1, matrix products, local(): lax.dot_general(gated_rows, out_weight, (((0,), (0,)), ((), ())), preferr...  4.67 us
    ppermute x1, starting transfers between devices, reduce_scatter_chan(): got = lax.ppermute(send, 'chan', [(j, j ^ 1) for j in range(4)])  4.63 us
    ppermute x1, starting transfers between devices, from_behind(): return lax.ppermute(x, axis, pairs)  4.36 us
  transfers between devices with their start and end apart: 5, of which 4 were waited for; matrix products, arithmetic and copies ran while one was open for 5% of the time, Pallas kernels for 0%

profile of v6, /device:TPU:1, one launch (start us, length us, event | category | flops | bytes accessed | tf_op | source)
XLA Modules:
  0.0 78.4 jit_solution(623749131742524891)
XLA Ops:
  0.0 0.0 copy-start
  0.0 1.5 %slice.51 = bf16[3,1024,2]{2,1,0:T(8,128)(2,1)S(1)} slice(bf16[3,1024,128]{2,1,0:T(8,128)(2,1)} %param.5), slice={[0:3], [0:1024], [126:128]} | slice | bytes 24576 | tf_op jit(solution)/shard_map/slice | solution.py:63
  1.5 0.3 copy.34
  1.8 4.4 %collective-permute-start = (bf16[3,1024,2]{1,2,0:T(2,128)(2,1)S(1)}, bf16[3,1024,2]{1,2,0:T(2,128)(2,1)S(1)}, u32[]{:S(2)}, u32[]{:S(2)}) collective-permute-start(bf16[3,1024,2]{1,2,0:T(2,128)(2,1)S(1)} %copy.34), channel_id=1, source_target_pairs={{0,4},{4,8},{8,12},{12,16},{16,20},{20,24},{24,28},{28,32},{32,36}... | collective-permute-start | bytes 36872 | tf_op jit(solution)/shard_map/ppermute | solution.py:10
  6.2 0.9 %fusion.32 = (f32[3,1,1024]{2,1,0:T(1,128)S(1)}, f32[3,1,1024]{2,1,0:T(1,128)S(1)}, f32[3,1,1024]{2,1,0:T(1,128)S(1)}) fusion(f32[3,3,1024]{2,1,0:T(4,128)} %param.6), kind=kLoop, calls=%fused_computation.65 | loop fusion | bytes 73728 | tf_op jit(solution)/shard_map/slice | solution.py:67
  7.2 0.8 %constant_dynamic-slice_fusion = (f32[16,16]{1,0:T(8,128)S(1)}, f32[16,16]{1,0:T(8,128)S(1)}) fusion(f32[16,1024]{1,0:T(8,128)} %param.7, s32[]{:T(128)S(6)} %select_n.63, f32[16,1024]{1,0:T(8,128)} %param.8), kind=kLoop, calls=%fused_computation.62 | loop fusion | bytes 4100 | tf_op jit(solution)/shard_map/dynamic_slice | solution.py:76
  8.0 0.0 collective-permute-done
  8.0 0.4 copy.23
  8.4 0.0 copy-done
  8.4 0.6 maximum_convert_fusion
  9.1 2.4 %fusion.3 = f32[3,1024,128]{2,1,0:T(8,128)S(1)} fusion(f32[3,1024,130]{2,1,0:T(8,128)S(1)} %maximum_convert_fusion, f32[3,1024]{1,0:T(4,128)S(1)} %get-tuple-element.12, f32[3,1024]{1,0:T(4,128)S(1)} %get-tuple-element.13, f32[3,1024]{1,0:T(4,128)S(1)} %bitcast.46), kind=kLoop, calls=%fused_computation.6 | loop fusion | flops 1966080 | bytes 6328320 | tf_op jit(solution)/shard_map/add | solution.py:67
  11.4 0.8 fusion.6
  12.2 12.9 %all-to-all-start = ((bf16[64,16,128]{2,1,0:T(8,128)(2,1)}), bf16[64,16,128]{2,1,0:T(8,128)(2,1)S(1)}, u32[]{:S(2)}, u32[]{:S(2)}) async-start(bf16[64,16,128]{2,1,0:T(8,128)(2,1)} %bitcast.1), calls=%async_computation | async-start | bytes 524288 | tf_op jit(solution)/shard_map/all_to_all | solution.py:74
  25.1 0.1 copy.26
  25.2 0.1 copy.25
  25.2 0.1 convert_multiply_fusion
  25.3 1.9 %convolution_select_fusion = f32[16,128,128]{2,1,0:T(8,128)S(1)} fusion(pred[128,128]{1,0:T(8,128)(4,1)S(1)} %subtract_compare_fusion, f32[128]{0:T(128)S(1)} %get-tuple-element.17, f32[16,16]{0,1:T(8,128)S(1)} %copy.26, f32[128]{0:T(128)S(1)} %get-tuple-element.16, f32[16,16]{0,1:T(8,128)S(1)} %copy.25), kind=kOutput, calls=%fused_computation.11 | convolution fusion | flops 50692096 | bytes 1068032 | tf_op jit(solution)/shard_map/rcj,rct->cjt/dot_general | solution.py:22
  27.2 8.8 %all-to-all-done = bf16[64,16,128]{2,1,0:T(8,128)(2,1)S(1)} async-done(((bf16[64,16,128]{2,1,0:T(8,128)(2,1)}), bf16[64,16,128]{2,1,0:T(8,128)(2,1)S(1)}, u32[]{:S(2)}, u32[]{:S(2)}) %all-to-all-start) | async-done | bytes 262176 | tf_op jit(solution)/shard_map/all_to_all | solution.py:74
  36.1 0.4 convolution_bitcast_fusion
  36.6 2.6 %fusion.2 = f32[16,16,64]{2,1,0:T(8,128)S(1)} fusion(f32[16,16,64]{2,1,0:T(8,128)S(1)} %copy.27, f32[16,16]{1,0:T(8,128)S(1)} %get-tuple-element.14, f32[64,64]{1,0:T(8,128)S(1)} %convert_multiply_fusion, pred[64,64]{1,0:T(8,128)(4,1)S(1)} %iota_compare_fusion), kind=kLoop, calls=%fused_computation.3 | loop fusion | flops 4177920 | bytes 152576 | tf_op jit(solution)/shard_map/reduce_sum | solution.py:37
  39.2 0.7 fusion.17
  39.9 0.4 fusion.5
  40.3 0.9 %copy.29 = bf16[16,64,128]{2,0,1:T(8,128)(2,1)} copy(bf16[16,64,128]{2,1,0:T(8,128)(2,1)S(1)} %fusion.5) | data formatting | bytes 524288 | tf_op jit(solution)/shard_map/convert_element_type | solution.py:78
  41.2 4.9 %all-to-all-start.1 = ((bf16[16,64,128]{2,0,1:T(8,128)(2,1)}), bf16[16,64,128]{2,0,1:T(8,128)(2,1)S(1)}, u32[]{:S(2)}, u32[]{:S(2)}) async-start(bf16[16,64,128]{2,0,1:T(8,128)(2,1)} %copy.29), calls=%async_computation.1 | async-start | bytes 524288 | tf_op jit(solution)/shard_map/all_to_all | solution.py:79
  46.1 11.0 %all-to-all-done.1 = bf16[16,64,128]{2,0,1:T(8,128)(2,1)S(1)} async-done(((bf16[16,64,128]{2,0,1:T(8,128)(2,1)}), bf16[16,64,128]{2,0,1:T(8,128)(2,1)S(1)}, u32[]{:S(2)}, u32[]{:S(2)}) %all-to-all-start.1) | async-done | bytes 262176 | tf_op jit(solution)/shard_map/all_to_all | solution.py:79
  57.1 0.1 fusion.8
  57.2 4.7 %convolution_convert_fusion = bf16[128,4096]{1,0:T(8,128)(2,1)S(1)} fusion(bf16[1024,128]{1,0:T(8,128)(2,1)S(1)} %fusion.8, bf16[1024,4096]{1,0:T(8,128)(2,1)} %param.9), kind=kOutput, calls=%fused_computation.4 | convolution fusion | flops 1074266112 | bytes 9699328 | tf_op jit(solution)/shard_map/dot_general | solution.py:81
  61.8 0.1 select_bitcast_fusion.3
  61.9 0.1 pad_maximum_fusion
  62.0 4.6 %collective-permute-start.1 = (bf16[2,128,1024]{2,1,0:T(8,128)(2,1)S(1)}, bf16[2,128,1024]{2,1,0:T(8,128)(2,1)S(1)}, u32[]{:S(2)}, u32[]{:S(2)}) collective-permute-start(bf16[2,128,1024]{2,1,0:T(8,128)(2,1)S(1)} %pad_maximum_fusion), channel_id=1, source_target_pairs={{0,1},{1,0},{2,3},{3,2},{4,5},{5,4},{6,7},{7,6},{8,9},{9,8},{10,11... | collective-permute-start | bytes 1572872 | tf_op jit(solution)/shard_map/ppermute | solution.py:51
  66.6 1.5 %collective-permute-done.1 = bf16[2,128,1024]{2,1,0:T(8,128)(2,1)S(1)} collective-permute-done((bf16[2,128,1024]{2,1,0:T(8,128)(2,1)S(1)}, bf16[2,128,1024]{2,1,0:T(8,128)(2,1)S(1)}, u32[]{:S(2)}, u32[]{:S(2)}) %collective-permute-start.1) | collective-permute-done | bytes 524320 | tf_op jit(solution)/shard_map/ppermute | solution.py:51
  68.1 0.2 convert_add_fusion
  68.3 0.1 fusion.10
  68.4 2.7 %collective-permute-start.2 = (bf16[128,1024]{1,0:T(8,128)(2,1)S(1)}, bf16[128,1024]{1,0:T(8,128)(2,1)S(1)}, u32[]{:S(2)}, u32[]{:S(2)}) collective-permute-start(bf16[128,1024]{1,0:T(8,128)(2,1)S(1)} %fusion.10), channel_id=1, source_target_pairs={{0,2},{1,3},{2,0},{3,1},{4,6},{5,7},{6,4},{7,5},{8,10},{9,11},{10,... | collective-permute-start | bytes 786440 | tf_op jit(solution)/shard_map/ppermute | solution.py:56
  71.1 6.4 %collective-permute-done.2 = bf16[128,1024]{1,0:T(8,128)(2,1)S(1)} collective-permute-done((bf16[128,1024]{1,0:T(8,128)(2,1)S(1)}, bf16[128,1024]{1,0:T(8,128)(2,1)S(1)}, u32[]{:S(2)}, u32[]{:S(2)}) %collective-permute-start.2) | collective-permute-done | bytes 262176 | tf_op jit(solution)/shard_map/ppermute | solution.py:56
  77.5 0.1 fusion.11
  77.6 0.8 %copy.30 = bf16[1024,128]{1,0:T(8,128)(2,1)} copy(bf16[1024,128]{0,1:T(8,128)(2,1)S(1)} %fusion.11) | data formatting | bytes 524288 | tf_op jit(solution)/shard_map/transpose | solution.py:57
  (9 shorter events, 0.1 us)
Async XLA Ops:
  0.0 8.4 %copy-start = (bf16[3,1024,128]{2,1,0:T(8,128)(2,1)S(1)}, bf16[3,1024,128]{2,1,0:T(8,128)(2,1)}, u32[]{:S(2)}) copy-start(bf16[3,1024,128]{2,1,0:T(8,128)(2,1)} %param.5) | copy-start | bytes 2359300
  1.8 6.2 %collective-permute-start = (bf16[3,1024,2]{1,2,0:T(2,128)(2,1)S(1)}, bf16[3,1024,2]{1,2,0:T(2,128)(2,1)S(1)}, u32[]{:S(2)}, u32[]{:S(2)}) collective-permute-start(bf16[3,1024,2]{1,2,0:T(2,128)(2,1)S(1)} %copy.34), channel_id=1, source_target_pairs={{0,4},{4,8},{8,12},{12,16},{16,20},{20,24},{24,28},{28,32},{32,36}... | collective-permute-start | bytes 36872 | tf_op jit(solution)/shard_map/ppermute | solution.py:10
  12.2 23.9 %all-to-all-start = ((bf16[64,16,128]{2,1,0:T(8,128)(2,1)}), bf16[64,16,128]{2,1,0:T(8,128)(2,1)S(1)}, u32[]{:S(2)}, u32[]{:S(2)}) async-start(bf16[64,16,128]{2,1,0:T(8,128)(2,1)} %bitcast.1), calls=%async_computation | async-start | bytes 524288 | tf_op jit(solution)/shard_map/all_to_all | solution.py:74
  41.2 15.9 %all-to-all-start.1 = ((bf16[16,64,128]{2,0,1:T(8,128)(2,1)}), bf16[16,64,128]{2,0,1:T(8,128)(2,1)S(1)}, u32[]{:S(2)}, u32[]{:S(2)}) async-start(bf16[16,64,128]{2,0,1:T(8,128)(2,1)} %copy.29), calls=%async_computation.1 | async-start | bytes 524288 | tf_op jit(solution)/shard_map/all_to_all | solution.py:79
  62.0 6.2 %collective-permute-start.1 = (bf16[2,128,1024]{2,1,0:T(8,128)(2,1)S(1)}, bf16[2,128,1024]{2,1,0:T(8,128)(2,1)S(1)}, u32[]{:S(2)}, u32[]{:S(2)}) collective-permute-start(bf16[2,128,1024]{2,1,0:T(8,128)(2,1)S(1)} %pad_maximum_fusion), channel_id=1, source_target_pairs={{0,1},{1,0},{2,3},{3,2},{4,5},{5,4},{6,7},{7,6},{8,9},{9,8},{10,11... | collective-permute-start | bytes 1572872 | tf_op jit(solution)/shard_map/ppermute | solution.py:51
  68.4 9.1 %collective-permute-start.2 = (bf16[128,1024]{1,0:T(8,128)(2,1)S(1)}, bf16[128,1024]{1,0:T(8,128)(2,1)S(1)}, u32[]{:S(2)}, u32[]{:S(2)}) collective-permute-start(bf16[128,1024]{1,0:T(8,128)(2,1)S(1)} %fusion.10), channel_id=1, source_target_pairs={{0,2},{1,3},{2,0},{3,1},{4,6},{5,7},{6,4},{7,5},{8,10},{9,11},{10,... | collective-permute-start | bytes 786440 | tf_op jit(solution)/shard_map/ppermute | solution.py:56

commit v7 on v6

--- a/solution.py
+++ b/solution.py
@@ -10,9 +10,8 @@
     return lax.ppermute(x, axis, pairs)
 
 
-def modal_conv(pencils, life_slice, resid_slice, block=128):
-    chan_here, length = pencils.shape
-    blocks = length // block
+def modal_conv(pencils, life_slice, resid_slice):
+    block = pencils.shape[2]
     steps = jnp.arange(block, dtype=jnp.int32).astype(jnp.float32)
     life = life_slice[:, :, None]
     resid = resid_slice[:, :, None]
@@ -22,22 +21,23 @@
     full = jnp.einsum("rcj,rct->cjt", rising, falling, precision=lax.Precision.HIGHEST)
     lag = jnp.arange(block, dtype=jnp.int32)[None, :] - jnp.arange(block, dtype=jnp.int32)[:, None]
     toeplitz = jnp.where(lag[None] >= 0, full, 0.0)
-    signal = pencils.astype(jnp.float32).reshape(chan_here, blocks, block)
+    signal = pencils.astype(jnp.float32)
     precise = lax.Precision.HIGH
-    inside = jnp.einsum("cnj,cjt->cnt", signal, toeplitz, precision=precise)
+    inside = jnp.einsum("ncj,cjt->nct", signal, toeplitz, precision=precise)
     to_end = jnp.exp(-(float(block - 1) - steps)[None, None, :] / life)
-    leaving = jnp.einsum("cnj,rcj->rcn", signal, to_end, precision=precise)
+    leaving = jnp.einsum("ncj,rcj->rcn", signal, to_end, precision=precise)
+    blocks = signal.shape[0]
     n_idx = jnp.arange(blocks, dtype=jnp.int32)
-    gap = (n_idx[:, None] - 1 - n_idx[None, :]).astype(jnp.float32)
+    gap = (n_idx[None, :] - 1 - n_idx[:, None]).astype(jnp.float32)
     exponent = jnp.where(
-        (n_idx[:, None] > n_idx[None, :])[None, None],
+        (n_idx[None, :] > n_idx[:, None])[None, None],
         -float(block) * gap[None, None] / life[..., None],
         -jnp.inf,
     )
-    entering = jnp.sum(jnp.exp(exponent) * leaving[:, :, None, :], axis=-1)
+    entering = jnp.sum(jnp.exp(exponent) * leaving[:, :, :, None], axis=2)
     from_start = resid * jnp.exp(-(steps + 1.0)[None, None, :] / life)
-    carried = jnp.einsum("rcn,rct->cnt", entering, from_start, precision=precise)
-    return (inside + carried).reshape(chan_here, length)
+    carried = jnp.einsum("rcn,rct->nct", entering, from_start, precision=precise)
+    return inside + carried
 
 
 def reduce_scatter_chan(partial):
@@ -71,12 +71,16 @@
     product = (filtered[1] * filtered[2]).astype(jnp.bfloat16)
     groups = lax.axis_size("seq")
     per_group = chan_local // groups
-    pencils = lax.all_to_all(product, "seq", split_axis=0, concat_axis=1, tiled=True)
+    pencils = lax.all_to_all(
+        product.reshape(groups, per_group, tok_count), "seq", split_axis=0, concat_axis=0, tiled=True
+    )
     first_chan = lax.axis_index("seq") * per_group
     life_slice = lax.dynamic_slice_in_dim(lifetimes, first_chan, per_group, 1)
     resid_slice = lax.dynamic_slice_in_dim(residues, first_chan, per_group, 1)
     convolved = modal_conv(pencils, life_slice, resid_slice).astype(jnp.bfloat16)
-    returned = lax.all_to_all(convolved, "seq", split_axis=1, concat_axis=0, tiled=True)
+    returned = lax.all_to_all(convolved, "seq", split_axis=0, concat_axis=0, tiled=True).reshape(
+        chan_local, tok_count
+    )
     gated_rows = (filtered[0] * returned.astype(jnp.float32)).astype(jnp.bfloat16)
     partial = lax.dot_general(
         gated_rows, out_weight, (((0,), (0,)), ((), ())), preferred_element_type=jnp.float32

time: 78.8 us -> 79.3 us (level)
  starting transfers between devices: 29.4 us -> 30.4 us
  local copies, waits for them, and re-layouts: 5.87 us -> 4.96 us
    slice x1, local copies, waits for them, and re-layouts: 0.95 us -> 0.03 us  [local(): taps[:, 0, :, None] * extended[:, :, 2:]]
    all_to_all x2, starting transfers between devices: 17.8 us -> 18.7 us  [the longest x1 13.8 us: local(): lax.all_to_all(product.reshape(groups, per_group, tok_count), 'seq', spli...]
  transfers between devices with their start and end apart: 5 -> 5, of which waited for: 4 -> 4; matrix products, arithmetic and copies ran while one was open for 5% -> 4% of each run, Pallas kernels for 0% -> 0%
where the time goes in v7:
time: 79.3 us; the launch traced here: 79 us
  starting transfers between devices  30.4 us (38%)
  waiting for transfers between devices  27.8 us (35%)
  matrix products  8.17 us (10%)
  other arithmetic  7.46 us (9%)
  local copies, waits for them, and re-layouts  4.96 us (6%)
    all_to_all x1, starting transfers between devices, local(): lax.all_to_all(product.reshape(groups, per_group, tok_count), 'seq', spli...  13.8 us
    all_to_all x1, waiting for transfers between devices, local(): lax.all_to_all(convolved, 'seq', split_axis=0, concat_axis=0, tiled=True)  11 us
    all_to_all x1, waiting for transfers between devices, local(): lax.all_to_all(product.reshape(groups, per_group, tok_count), 'seq', spli...  8.88 us
    ppermute x1, waiting for transfers between devices, reduce_scatter_chan(): got2 = lax.ppermute(send2, 'chan', [(j, j ^ 2) for j in range(4)])  6.37 us
    all_to_all x1, starting transfers between devices, local(): lax.all_to_all(convolved, 'seq', split_axis=0, concat_axis=0, tiled=True)  4.85 us
    dot_general x1, matrix products, local(): lax.dot_general(gated_rows, out_weight, (((0,), (0,)), ((), ())), preferr...  4.67 us
    ppermute x1, starting transfers between devices, reduce_scatter_chan(): got = lax.ppermute(send, 'chan', [(j, j ^ 1) for j in range(4)])  4.62 us
    ppermute x1, starting transfers between devices, from_behind(): return lax.ppermute(x, axis, pairs)  4.36 us
  transfers between devices with their start and end apart: 5, of which 4 were waited for; matrix products, arithmetic and copies ran while one was open for 4% of the time, Pallas kernels for 0%

profile of v7, /device:TPU:1, one launch (start us, length us, event | category | flops | bytes accessed | tf_op | source)
XLA Modules:
  0.0 79.0 jit_solution(3812081680293169743)
XLA Ops:
  0.0 0.0 copy-start
  0.0 0.0 copy-start.1
  0.0 1.5 %slice.51 = bf16[3,1024,2]{2,1,0:T(8,128)(2,1)S(1)} slice(bf16[3,1024,128]{2,1,0:T(8,128)(2,1)} %param.5), slice={[0:3], [0:1024], [126:128]} | slice | bytes 24576 | tf_op jit(solution)/shard_map/slice | solution.py:63
  1.5 0.3 copy.36
  1.8 4.4 %collective-permute-start = (bf16[3,1024,2]{1,2,0:T(2,128)(2,1)S(1)}, bf16[3,1024,2]{1,2,0:T(2,128)(2,1)S(1)}, u32[]{:S(2)}, u32[]{:S(2)}) collective-permute-start(bf16[3,1024,2]{1,2,0:T(2,128)(2,1)S(1)} %copy.36), channel_id=1, source_target_pairs={{0,4},{4,8},{8,12},{12,16},{16,20},{20,24},{24,28},{28,32},{32,36}... | collective-permute-start | bytes 36872 | tf_op jit(solution)/shard_map/ppermute | solution.py:10
  6.2 0.0 copy-done.1
  6.3 0.8 %constant_dynamic-slice_fusion = (f32[16,16]{1,0:T(8,128)S(1)}, f32[16,16]{1,0:T(8,128)S(1)}) fusion(f32[16,1024]{1,0:T(8,128)} %param.7, s32[]{:T(128)S(6)} %select_n.63, f32[16,1024]{1,0:T(8,128)} %param.8), kind=kLoop, calls=%fused_computation.61 | loop fusion | bytes 4100 | tf_op jit(solution)/shard_map/dynamic_slice | solution.py:78
  7.1 0.0 collective-permute-done
  7.1 0.4 copy.24
  7.5 0.0 copy-done
  7.5 0.6 maximum_convert_fusion
  8.2 2.4 %fusion.3 = f32[3,1024,128]{2,1,0:T(8,128)S(1)} fusion(f32[3,1024,130]{2,1,0:T(8,128)S(1)} %maximum_convert_fusion, f32[3,1024]{1,0:T(4,128)S(1)} %get-tuple-element.12, f32[3,1024]{1,0:T(4,128)S(1)} %get-tuple-element.13, f32[3,1024]{1,0:T(4,128)S(1)} %bitcast.42), kind=kLoop, calls=%fused_computation.6 | loop fusion | flops 1966080 | bytes 6328320 | tf_op jit(solution)/shard_map/add | solution.py:67
  10.5 0.8 fusion.7
  11.3 13.8 %all-to-all-start = ((bf16[64,16,128]{2,1,0:T(8,128)(2,1)}), bf16[64,16,128]{2,1,0:T(8,128)(2,1)S(1)}, u32[]{:S(2)}, u32[]{:S(2)}) async-start(bf16[64,16,128]{2,1,0:T(8,128)(2,1)} %bitcast.1), calls=%async_computation | async-start | bytes 524288 | tf_op jit(solution)/shard_map/all_to_all | solution.py:74
  25.1 0.1 copy.26
  25.2 0.1 copy.25
  25.3 1.9 %convolution_select_fusion = f32[16,128,128]{2,1,0:T(8,128)S(1)} fusion(pred[128,128]{1,0:T(8,128)(4,1)S(1)} %subtract_compare_fusion, f32[128]{0:T(128)S(1)} %get-tuple-element.17, f32[16,16]{0,1:T(8,128)S(1)} %copy.26, f32[128]{0:T(128)S(1)} %get-tuple-element.16, f32[16,16]{0,1:T(8,128)S(1)} %copy.25), kind=kOutput, calls=%fused_computation.11 | convolution fusion | flops 50692096 | bytes 1068032 | tf_op jit(solution)/shard_map/rcj,rct->cjt/dot_general | solution.py:21
  27.2 8.9 %all-to-all-done = bf16[64,16,128]{2,1,0:T(8,128)(2,1)S(1)} async-done(((bf16[64,16,128]{2,1,0:T(8,128)(2,1)}), bf16[64,16,128]{2,1,0:T(8,128)(2,1)S(1)}, u32[]{:S(2)}, u32[]{:S(2)}) %all-to-all-start) | async-done | bytes 262176 | tf_op jit(solution)/shard_map/all_to_all | solution.py:74
  36.1 0.4 convolution_bitcast_fusion
  36.6 3.3 %fusion.2 = f32[16,16,64]{2,1,0:T(8,128)S(1)} fusion(f32[16,16,64]{2,1,0:T(8,128)S(1)} %copy.29, f32[16,16]{1,0:T(8,128)S(1)} %get-tuple-element.14, f32[64,64]{1,0:T(8,128)S(1)} %convert_multiply_fusion, pred[64,64]{1,0:T(8,128)(4,1)S(1)} %iota_compare_fusion), kind=kLoop, calls=%fused_computation.3 | loop fusion | flops 4177920 | bytes 152576 | tf_op jit(solution)/shard_map/reduce_sum | solution.py:37
  39.8 0.7 fusion.17
  40.6 0.4 fusion.6
  41.0 0.9 %copy.31 = bf16[64,16,128]{2,1,0:T(8,128)(2,1)} copy(bf16[64,16,128]{2,0,1:T(8,128)(2,1)S(1)} %fusion.6) | data formatting | bytes 524288 | tf_op jit(solution)/shard_map/convert_element_type | solution.py:80
  41.9 4.8 %all-to-all-start.1 = ((bf16[64,16,128]{2,1,0:T(8,128)(2,1)}), bf16[64,16,128]{2,1,0:T(8,128)(2,1)S(1)}, u32[]{:S(2)}, u32[]{:S(2)}) async-start(bf16[64,16,128]{2,1,0:T(8,128)(2,1)} %copy.31), calls=%async_computation.1 | async-start | bytes 524288 | tf_op jit(solution)/shard_map/all_to_all | solution.py:81
  46.7 11.0 %all-to-all-done.1 = bf16[64,16,128]{2,1,0:T(8,128)(2,1)S(1)} async-done(((bf16[64,16,128]{2,1,0:T(8,128)(2,1)}), bf16[64,16,128]{2,1,0:T(8,128)(2,1)S(1)}, u32[]{:S(2)}, u32[]{:S(2)}) %all-to-all-start.1) | async-done | bytes 262176 | tf_op jit(solution)/shard_map/all_to_all | solution.py:81
  57.7 4.7 %convolution_convert_fusion = bf16[128,4096]{1,0:T(8,128)(2,1)S(1)} fusion(bf16[1024,4096]{1,0:T(8,128)(2,1)} %param.9, f32[3,1024,128]{2,1,0:T(8,128)S(1)} %fusion.3, bf16[1024,128]{1,0:T(8,128)(2,1)S(1)} %bitcast.41), kind=kOutput, calls=%fused_computation.4 | convolution fusion | flops 1074659328 | bytes 10223616 | tf_op jit(solution)/shard_map/dot_general | solution.py:85
  62.4 0.1 select_bitcast_fusion.3
  62.5 0.1 pad_maximum_fusion
  62.5 4.6 %collective-permute-start.1 = (bf16[2,128,1024]{2,1,0:T(8,128)(2,1)S(1)}, bf16[2,128,1024]{2,1,0:T(8,128)(2,1)S(1)}, u32[]{:S(2)}, u32[]{:S(2)}) collective-permute-start(bf16[2,128,1024]{2,1,0:T(8,128)(2,1)S(1)} %pad_maximum_fusion), channel_id=1, source_target_pairs={{0,1},{1,0},{2,3},{3,2},{4,5},{5,4},{6,7},{7,6},{8,9},{9,8},{10,11... | collective-permute-start | bytes 1572872 | tf_op jit(solution)/shard_map/ppermute | solution.py:51
  67.2 1.5 %collective-permute-done.1 = bf16[2,128,1024]{2,1,0:T(8,128)(2,1)S(1)} collective-permute-done((bf16[2,128,1024]{2,1,0:T(8,128)(2,1)S(1)}, bf16[2,128,1024]{2,1,0:T(8,128)(2,1)S(1)}, u32[]{:S(2)}, u32[]{:S(2)}) %collective-permute-start.1) | collective-permute-done | bytes 524320 | tf_op jit(solution)/shard_map/ppermute | solution.py:51
  68.7 0.2 convert_add_fusion
  68.9 0.1 fusion.11
  68.9 2.7 %collective-permute-start.2 = (bf16[128,1024]{1,0:T(8,128)(2,1)S(1)}, bf16[128,1024]{1,0:T(8,128)(2,1)S(1)}, u32[]{:S(2)}, u32[]{:S(2)}) collective-permute-start(bf16[128,1024]{1,0:T(8,128)(2,1)S(1)} %fusion.11), channel_id=1, source_target_pairs={{0,2},{1,3},{2,0},{3,1},{4,6},{5,7},{6,4},{7,5},{8,10},{9,11},{10,... | collective-permute-start | bytes 786440 | tf_op jit(solution)/shard_map/ppermute | solution.py:56
  71.7 6.4 %collective-permute-done.2 = bf16[128,1024]{1,0:T(8,128)(2,1)S(1)} collective-permute-done((bf16[128,1024]{1,0:T(8,128)(2,1)S(1)}, bf16[128,1024]{1,0:T(8,128)(2,1)S(1)}, u32[]{:S(2)}, u32[]{:S(2)}) %collective-permute-start.2) | collective-permute-done | bytes 262176 | tf_op jit(solution)/shard_map/ppermute | solution.py:56
  78.0 0.1 fusion.12
  78.1 0.8 %copy.32 = bf16[1024,128]{1,0:T(8,128)(2,1)} copy(bf16[1024,128]{0,1:T(8,128)(2,1)S(1)} %fusion.12) | data formatting | bytes 524288 | tf_op jit(solution)/shard_map/transpose | solution.py:57
  (11 shorter events, 0.1 us)
Async XLA Ops:
  0.0 7.5 %copy-start = (bf16[3,1024,128]{2,1,0:T(8,128)(2,1)S(1)}, bf16[3,1024,128]{2,1,0:T(8,128)(2,1)}, u32[]{:S(2)}) copy-start(bf16[3,1024,128]{2,1,0:T(8,128)(2,1)} %param.5) | copy-start | bytes 2359300
  0.0 6.2 %copy-start.1 = (f32[3,3,1024]{2,1,0:T(4,128)S(1)}, f32[3,3,1024]{2,1,0:T(4,128)}, u32[]{:S(2)}) copy-start(f32[3,3,1024]{2,1,0:T(4,128)} %param.6) | copy-start | bytes 110596
  1.8 5.3 %collective-permute-start = (bf16[3,1024,2]{1,2,0:T(2,128)(2,1)S(1)}, bf16[3,1024,2]{1,2,0:T(2,128)(2,1)S(1)}, u32[]{:S(2)}, u32[]{:S(2)}) collective-permute-start(bf16[3,1024,2]{1,2,0:T(2,128)(2,1)S(1)} %copy.36), channel_id=1, source_target_pairs={{0,4},{4,8},{8,12},{12,16},{16,20},{20,24},{24,28},{28,32},{32,36}... | collective-permute-start | bytes 36872 | tf_op jit(solution)/shard_map/ppermute | solution.py:10
  11.3 24.8 %all-to-all-start = ((bf16[64,16,128]{2,1,0:T(8,128)(2,1)}), bf16[64,16,128]{2,1,0:T(8,128)(2,1)S(1)}, u32[]{:S(2)}, u32[]{:S(2)}) async-start(bf16[64,16,128]{2,1,0:T(8,128)(2,1)} %bitcast.1), calls=%async_computation | async-start | bytes 524288 | tf_op jit(solution)/shard_map/all_to_all | solution.py:74
  41.9 15.9 %all-to-all-start.1 = ((bf16[64,16,128]{2,1,0:T(8,128)(2,1)}), bf16[64,16,128]{2,1,0:T(8,128)(2,1)S(1)}, u32[]{:S(2)}, u32[]{:S(2)}) async-start(bf16[64,16,128]{2,1,0:T(8,128)(2,1)} %copy.31), calls=%async_computation.1 | async-start | bytes 524288 | tf_op jit(solution)/shard_map/all_to_all | solution.py:81
  62.5 6.2 %collective-permute-start.1 = (bf16[2,128,1024]{2,1,0:T(8,128)(2,1)S(1)}, bf16[2,128,1024]{2,1,0:T(8,128)(2,1)S(1)}, u32[]{:S(2)}, u32[]{:S(2)}) collective-permute-start(bf16[2,128,1024]{2,1,0:T(8,128)(2,1)S(1)} %pad_maximum_fusion), channel_id=1, source_target_pairs={{0,1},{1,0},{2,3},{3,2},{4,5},{5,4},{6,7},{7,6},{8,9},{9,8},{10,11... | collective-permute-start | bytes 1572872 | tf_op jit(solution)/shard_map/ppermute | solution.py:51
  68.9 9.1 %collective-permute-start.2 = (bf16[128,1024]{1,0:T(8,128)(2,1)S(1)}, bf16[128,1024]{1,0:T(8,128)(2,1)S(1)}, u32[]{:S(2)}, u32[]{:S(2)}) collective-permute-start(bf16[128,1024]{1,0:T(8,128)(2,1)S(1)} %fusion.11), channel_id=1, source_target_pairs={{0,2},{1,3},{2,0},{3,1},{4,6},{5,7},{6,4},{7,5},{8,10},{9,11},{10,... | collective-permute-start | bytes 786440 | tf_op jit(solution)/shard_map/ppermute | solution.py:56

commit v8 on v7

--- a/solution.py
+++ b/solution.py
@@ -62,13 +62,18 @@
     tok_count = qkv.shape[2]
     edge_block = qkv[:, :, tok_count - 2 :]
     earlier = from_behind(edge_block, "seq", 1)
-    extended = jnp.concatenate([earlier, qkv], axis=2).astype(jnp.float32)
-    filtered = (
-        taps[:, 0, :, None] * extended[:, :, 2:]
-        + taps[:, 1, :, None] * extended[:, :, 1:-1]
-        + taps[:, 2, :, None] * extended[:, :, :-2]
-    )
-    product = (filtered[1] * filtered[2]).astype(jnp.bfloat16)
+
+    def short_filter(stream):
+        signal = qkv[stream].astype(jnp.float32)
+        back1 = jnp.concatenate([earlier[stream, :, 1:], qkv[stream, :, :-1]], axis=1)
+        back2 = jnp.concatenate([earlier[stream], qkv[stream, :, :-2]], axis=1)
+        return (
+            taps[stream, 0][:, None] * signal
+            + taps[stream, 1][:, None] * back1.astype(jnp.float32)
+            + taps[stream, 2][:, None] * back2.astype(jnp.float32)
+        )
+
+    product = (short_filter(1) * short_filter(2)).astype(jnp.bfloat16)
     groups = lax.axis_size("seq")
     per_group = chan_local // groups
     pencils = lax.all_to_all(
@@ -81,7 +86,7 @@
     returned = lax.all_to_all(convolved, "seq", split_axis=0, concat_axis=0, tiled=True).reshape(
         chan_local, tok_count
     )
-    gated_rows = (filtered[0] * returned.astype(jnp.float32)).astype(jnp.bfloat16)
+    gated_rows = (short_filter(0) * returned.astype(jnp.float32)).astype(jnp.bfloat16)
     partial = lax.dot_general(
         gated_rows, out_weight, (((0,), (0,)), ((), ())), preferred_element_type=jnp.float32
     ).astype(jnp.bfloat16)

time: 79.3 us -> 92.6 us (1.17)
  local copies, waits for them, and re-layouts: 4.96 us -> 16.8 us
  other arithmetic: 7.46 us -> 11.6 us
  waiting for transfers between devices: 27.8 us -> 25 us
  starting transfers between devices: 30.4 us -> 28.4 us
  matrix products: 8.17 us -> 9.83 us
    slice x1 -> x4, local copies, waits for them, and re-layouts: 0.03 us -> 3.99 us  [the longest x1 1.84 us: short_filter(): signal = qkv[stream].astype(jnp.float32)]
    squeeze x0 -> x3, local copies, waits for them, and re-layouts: none -> 2.61 us  [the longest x1 1.23 us: short_filter(): qkv[stream, :, :-1]]
    all_to_all x1, waiting for transfers between devices: 8.88 us -> 6.51 us  [local(): lax.all_to_all(product.reshape(groups, per_group, tok_count), 'seq', spli...]
    add x1 -> x0, other arithmetic: 2.35 us -> none  [local(): taps[:, 0, :, None] * extended[:, :, 2:]]
    concatenate x0 -> x4, local copies, waits for them, and re-layouts: none -> 1.94 us  [the longest x2 1.53 us: short_filter(): jnp.concatenate([earlier[stream, :, 1:], qkv[stream, :, :-1]], axis=1)]
    all_to_all x1, starting transfers between devices: 13.8 us -> 11.9 us  [local(): lax.all_to_all(product.reshape(groups, per_group, tok_count), 'seq', spli...]
    mul x0 -> x6, local copies, waits for them, and re-layouts: none -> 1.65 us  [the longest x2 0.76 us: short_filter(): taps[stream, 1][:, None] * back1.astype(jnp.float32)]
    convert_element_type x2 -> x1, other arithmetic: 1.35 us -> 2.91 us  [local(): product = (short_filter(1) * short_filter(2)).astype(jnp.bfloat16)]
  transfers between devices with their start and end apart: 5 -> 5, of which waited for: 4 -> 4; matrix products, arithmetic and copies ran while one was open for 4% -> 18% of each run, Pallas kernels for 0% -> 0%
where the time goes in v8:
time: 92.6 us; the launch traced here: 91.8 us
  starting transfers between devices  28.4 us (31%)
  waiting for transfers between devices  25 us (27%)
  local copies, waits for them, and re-layouts  16.8 us (18%)
  other arithmetic  11.6 us (13%)
  matrix products  9.83 us (11%)
    all_to_all x1, starting transfers between devices, local(): lax.all_to_all(product.reshape(groups, per_group, tok_count), 'seq', spli...  11.9 us
    all_to_all x1, waiting for transfers between devices, local(): lax.all_to_all(convolved, 'seq', split_axis=0, concat_axis=0, tiled=True)  10.6 us
    all_to_all x1, waiting for transfers between devices, local(): lax.all_to_all(product.reshape(groups, per_group, tok_count), 'seq', spli...  6.51 us
    ppermute x1, waiting for transfers between devices, reduce_scatter_chan(): got2 = lax.ppermute(send2, 'chan', [(j, j ^ 2) for j in range(4)])  6.38 us
    all_to_all x1, starting transfers between devices, local(): lax.all_to_all(convolved, 'seq', split_axis=0, concat_axis=0, tiled=True)  5.76 us
    dot_general x1, matrix products, local(): lax.dot_general(gated_rows, out_weight, (((0,), (0,)), ((), ())), preferr...  4.92 us
    reduce_sum x1, other arithmetic, modal_conv(): entering = jnp.sum(jnp.exp(exponent) * leaving[:, :, :, None], axis=2)  4.52 us
    ppermute x1, starting transfers between devices, from_behind(): return lax.ppermute(x, axis, pairs)  4.36 us
  transfers between devices with their start and end apart: 5, of which 4 were waited for; matrix products, arithmetic and copies ran while one was open for 18% of the time, Pallas kernels for 0%

profile of v8, /device:TPU:1, one launch (start us, length us, event | category | flops | bytes accessed | tf_op | source)
XLA Modules:
  0.0 91.8 jit_solution(14660107731217703855)
XLA Ops:
  0.0 1.4 %slice.98 = bf16[3,1024,2]{2,1,0:T(8,128)(2,1)S(1)} slice(bf16[3,1024,128]{2,1,0:T(8,128)(2,1)} %param.5), slice={[0:3], [0:1024], [126:128]} | slice | bytes 24576 | tf_op jit(solution)/shard_map/slice | solution.py:63
  1.4 0.3 copy.81
  1.7 4.4 %collective-permute-start = (bf16[3,1024,2]{1,2,0:T(2,128)(2,1)S(1)}, bf16[3,1024,2]{1,2,0:T(2,128)(2,1)S(1)}, u32[]{:S(2)}, u32[]{:S(2)}) collective-permute-start(bf16[3,1024,2]{1,2,0:T(2,128)(2,1)S(1)} %copy.81), channel_id=1, source_target_pairs={{0,4},{4,8},{8,12},{12,16},{16,20},{20,24},{24,28},{28,32},{32,36}... | collective-permute-start | bytes 36872 | tf_op jit(solution)/shard_map/ppermute | solution.py:10
  6.1 1.2 %slice_bitcast_fusion = (bf16[1024,126]{1,0:T(8,128)(2,1)S(1)}, bf16[1,1024,126]{2,1,0:T(8,128)(2,1)S(1)}, bf16[1,1024,126]{2,1,0:T(8,128)(2,1)S(1)}) fusion(bf16[3,1024,128]{2,1,0:T(8,128)(2,1)} %param.5), kind=kLoop, calls=%fused_computation.41 | loop fusion | bytes 1548288 | tf_op jit(solution)/shard_map/squeeze | solution.py:69
  7.3 1.2 %slice_bitcast_fusion.1 = (bf16[1024,127]{1,0:T(8,128)(2,1)S(1)}, bf16[1,1024,127]{2,1,0:T(8,128)(2,1)S(1)}, bf16[1,1024,127]{2,1,0:T(8,128)(2,1)S(1)}) fusion(bf16[3,1024,128]{2,1,0:T(8,128)(2,1)} %param.5), kind=kLoop, calls=%fused_computation.43 | loop fusion | bytes 1560576 | tf_op jit(solution)/shard_map/squeeze | solution.py:68
  8.5 1.8 %fusion.48 = (bf16[1,1024,128]{2,1,0:T(8,128)(2,1)}, bf16[1,1024,128]{2,1,0:T(8,128)(2,1)}) fusion(bf16[3,1024,128]{2,1,0:T(8,128)(2,1)} %param.5), kind=kLoop, calls=%fused_computation.86 | loop fusion | bytes 1048576 | tf_op jit(solution)/shard_map/slice | solution.py:67
  10.3 0.6 subtract_negate_fusion
  10.9 0.6 iota_compare_fusion
  11.5 0.6 convert_add_fusion.1
  12.1 0.6 subtract_compare_fusion
  12.7 0.9 %fusion.49 = (f32[1,1,1024]{2,1,0:T(1,128)S(1)}, f32[1,1,1024]{2,1,0:T(1,128)S(1)}, f32[1024]{0:T(1024)S(1)}, f32[1024]{0:T(1024)S(1)}, f32[1024]{0:T(1024)S(1)}...) fusion(f32[3,3,1024]{2,1,0:T(4,128)} %param.6), kind=kLoop, calls=%fused_computation.87 | loop fusion | bytes 73728 | tf_op jit(solution)/shard_map/slice | solution.py:71
  13.7 1.4 %constant_dynamic-slice_fusion = (f32[16,16]{1,0:T(8,128)}, f32[16,16]{1,0:T(8,128)}) fusion(f32[16,1024]{1,0:T(8,128)} %param.7, s32[]{:T(128)S(6)} %select_n.63, f32[16,1024]{1,0:T(8,128)} %param.8), kind=kLoop, calls=%fused_computation.82 | loop fusion | bytes 4100 | tf_op jit(solution)/shard_map/dynamic_slice | solution.py:83
  15.1 0.6 iota_add_fusion
  15.8 0.1 mul.157
  15.9 0.1 mul.160
  16.0 0.7 mul.163
  16.7 0.7 mul.166
  17.3 0.6 fusion.50
  17.9 0.2 copy.79
  18.1 0.2 copy.80
  18.4 0.6 slice_reduce_fusion
  18.9 0.4 concatenate.52
  19.4 1.1 %concatenate.53 = bf16[64,16,1]{2,1,0:T(8,128)(2,1)S(1)} reshape(bf16[1024]{0:T(1024)(128)(2,1)} %get-tuple-element.11) | data formatting | bytes 4096 | tf_op jit(solution)/shard_map/concatenate | solution.py:68
  20.5 2.9 %fusion.9 = bf16[64,16,128]{2,1,0:T(8,128)(2,1)} fusion(bf16[64,16,128]{2,1,0:T(8,128)(2,1)} %bitcast.61, bf16[64,16,128]{2,1,0:T(8,128)(2,1)} %bitcast.60, bf16[64,16,127]{2,1,0:T(8,128)(2,1)S(1)} %bitcast.58, bf16[64,16,1]{2,1,0:T(8,128)(2,1)S(1)} %concatenate.52, bf16[64,16,126]{2,1,0:T(8,128)(2,1)S(1)} %bitcast.56, bf16[64,16,2]{2,1,0:T(8,128)(2,1)S(1)} %bitcast.54, ...), kind=kLoop, calls=%fused_computation.18 | loop fusion | flops 3932160 | bytes 1859584 | tf_op jit(solution)/shard_map/convert_element_type | solution.py:76
  23.4 11.9 %all-to-all-start = ((bf16[64,16,128]{2,1,0:T(8,128)(2,1)}), bf16[64,16,128]{2,1,0:T(8,128)(2,1)S(1)}, u32[]{:S(2)}, u32[]{:S(2)}) async-start(bf16[64,16,128]{2,1,0:T(8,128)(2,1)} %fusion.9), calls=%async_computation | async-start | bytes 524288 | tf_op jit(solution)/shard_map/all_to_all | solution.py:79
  35.3 0.8 copy.68
  36.1 0.8 copy.67
  36.9 0.7 convert_multiply_fusion.4
  37.5 2.7 %convolution_select_fusion = f32[16,128,128]{2,1,0:T(8,128)S(1)} fusion(pred[128,128]{1,0:T(8,128)(4,1)} %subtract_compare_fusion, f32[128]{0:T(128)} %get-tuple-element.41, f32[16,16]{0,1:T(8,128)S(1)} %copy.68, f32[128]{0:T(128)} %get-tuple-element.40, f32[16,16]{0,1:T(8,128)S(1)} %copy.67), kind=kOutput, calls=%fused_computation.5 | convolution fusion | flops 50692096 | bytes 1068032 | tf_op jit(solution)/shard_map/rcj,rct->cjt/dot_general | solution.py:21
  40.2 6.5 %all-to-all-done = bf16[64,16,128]{2,1,0:T(8,128)(2,1)S(1)} async-done(((bf16[64,16,128]{2,1,0:T(8,128)(2,1)}), bf16[64,16,128]{2,1,0:T(8,128)(2,1)S(1)}, u32[]{:S(2)}, u32[]{:S(2)}) %all-to-all-start) | async-done | bytes 262176 | tf_op jit(solution)/shard_map/all_to_all | solution.py:79
  46.7 1.1 %convolution_bitcast_fusion = f32[16,16,64]{2,0,1:T(8,128)S(1)} fusion(bf16[64,16,128]{2,1,0:T(8,128)(2,1)S(1)} %all-to-all-done, f32[128]{0:T(128)} %subtract_negate_fusion, f32[16,16]{0,1:T(8,128)S(1)} %copy.68), kind=kOutput, calls=%fused_computation.9 | convolution fusion | flops 12615680 | bytes 329216 | tf_op jit(solution)/shard_map/ncj,rcj->rcn/dot_general | solution.py:28
  47.9 4.5 %fusion.2 = f32[16,16,64]{2,1,0:T(8,128)S(1)} fusion(f32[16,16,64]{2,1,0:T(8,128)S(1)} %copy.75, f32[16,16]{1,0:T(8,128)} %get-tuple-element.38, f32[64,64]{1,0:T(8,128)S(1)} %convert_multiply_fusion.4, pred[64,64]{1,0:T(8,128)(4,1)} %iota_compare_fusion), kind=kLoop, calls=%fused_computation.3 | loop fusion | flops 4177920 | bytes 152576 | tf_op jit(solution)/shard_map/reduce_sum | solution.py:37
  52.4 0.7 fusion.32
  53.1 0.4 fusion.4
  53.6 0.9 copy.77
  54.4 5.8 %all-to-all-start.1 = ((bf16[64,16,128]{2,1,0:T(8,128)(2,1)}), bf16[64,16,128]{2,1,0:T(8,128)(2,1)S(1)}, u32[]{:S(2)}, u32[]{:S(2)}) async-start(bf16[64,16,128]{2,1,0:T(8,128)(2,1)} %copy.77), calls=%async_computation.1 | async-start | bytes 524288 | tf_op jit(solution)/shard_map/all_to_all | solution.py:86
  60.2 0.2 copy.82
  60.5 0.2 copy.65
  60.7 10.6 %all-to-all-done.1 = bf16[64,16,128]{2,1,0:T(8,128)(2,1)S(1)} async-done(((bf16[64,16,128]{2,1,0:T(8,128)(2,1)}), bf16[64,16,128]{2,1,0:T(8,128)(2,1)S(1)}, u32[]{:S(2)}, u32[]{:S(2)}) %all-to-all-start.1) | async-done | bytes 262176 | tf_op jit(solution)/shard_map/all_to_all | solution.py:86
  71.2 4.9 %convolution_convert_fusion = bf16[128,4096]{1,0:T(8,128)(2,1)S(1)} fusion(bf16[1024,4096]{1,0:T(8,128)(2,1)} %param.9, bf16[1024,128]{1,0:T(8,128)(2,1)S(1)} %bitcast.52, bf16[1024,127]{1,0:T(8,128)(2,1)S(1)} %get-tuple-element.20, bf16[1024,1]{1,0:T(8,128)(2,1)S(1)} %copy.65, bf16[1024,126]{1,0:T(8,128)(2,1)S(1)} %get-tuple-element.17, ...), kind=kOutput, calls=%fused_computation.4 | convolution fusion | flops 1076494336 | bytes 11022336 | tf_op jit(solution)/shard_map/dot_general | solution.py:90
  76.2 0.1 select_bitcast_fusion.3
  76.3 3.7 %collective-permute-start.1 = (bf16[2,128,1024]{2,1,0:T(8,128)(2,1)S(1)}, bf16[2,128,1024]{2,1,0:T(8,128)(2,1)S(1)}, u32[]{:S(2)}, u32[]{:S(2)}) collective-permute-start(bf16[2,128,1024]{2,1,0:T(8,128)(2,1)S(1)} %pad_maximum_fusion), channel_id=1, source_target_pairs={{0,1},{1,0},{2,3},{3,2},{4,5},{5,4},{6,7},{7,6},{8,9},{9,8},{10,11... | collective-permute-start | bytes 1572872 | tf_op jit(solution)/shard_map/ppermute | solution.py:51
  80.0 1.5 %collective-permute-done.1 = bf16[2,128,1024]{2,1,0:T(8,128)(2,1)S(1)} collective-permute-done((bf16[2,128,1024]{2,1,0:T(8,128)(2,1)S(1)}, bf16[2,128,1024]{2,1,0:T(8,128)(2,1)S(1)}, u32[]{:S(2)}, u32[]{:S(2)}) %collective-permute-start.1) | collective-permute-done | bytes 524320 | tf_op jit(solution)/shard_map/ppermute | solution.py:51
  81.5 0.2 convert_add_fusion
  81.8 2.7 %collective-permute-start.2 = (bf16[128,1024]{1,0:T(8,128)(2,1)S(1)}, bf16[128,1024]{1,0:T(8,128)(2,1)S(1)}, u32[]{:S(2)}, u32[]{:S(2)}) collective-permute-start(bf16[128,1024]{1,0:T(8,128)(2,1)S(1)} %fusion.15), channel_id=1, source_target_pairs={{0,2},{1,3},{2,0},{3,1},{4,6},{5,7},{6,4},{7,5},{8,10},{9,11},{10,... | collective-permute-start | bytes 786440 | tf_op jit(solution)/shard_map/ppermute | solution.py:56
  84.5 6.4 %collective-permute-done.2 = bf16[128,1024]{1,0:T(8,128)(2,1)S(1)} collective-permute-done((bf16[128,1024]{1,0:T(8,128)(2,1)S(1)}, bf16[128,1024]{1,0:T(8,128)(2,1)S(1)}, u32[]{:S(2)}, u32[]{:S(2)}) %collective-permute-start.2) | collective-permute-done | bytes 262176 | tf_op jit(solution)/shard_map/ppermute | solution.py:56
  90.9 0.1 fusion.16
  91.0 0.8 copy.78
  (11 shorter events, 0.3 us)
Async XLA Ops:
  1.7 15.6 %collective-permute-start = (bf16[3,1024,2]{1,2,0:T(2,128)(2,1)S(1)}, bf16[3,1024,2]{1,2,0:T(2,128)(2,1)S(1)}, u32[]{:S(2)}, u32[]{:S(2)}) collective-permute-start(bf16[3,1024,2]{1,2,0:T(2,128)(2,1)S(1)} %copy.81), channel_id=1, source_target_pairs={{0,4},{4,8},{8,12},{12,16},{16,20},{20,24},{24,28},{28,32},{32,36}... | collective-permute-start | bytes 36872 | tf_op jit(solution)/shard_map/ppermute | solution.py:10
  7.2 64.0 %copy-start = (bf16[3,1024,128]{2,1,0:T(8,128)(2,1)S(1)}, bf16[3,1024,128]{2,1,0:T(8,128)(2,1)}, u32[]{:S(2)}) copy-start(bf16[3,1024,128]{2,1,0:T(8,128)(2,1)} %param.5) | copy-start | bytes 2359300
  23.4 36.8 %copy-start.1 = (bf16[1,1024,2]{1,2,0:T(2,128)(2,1)S(1)}, bf16[1,1024,2]{1,2,0:T(2,128)(2,1)}, u32[]{:S(2)}) copy-start(bf16[1,1024,2]{1,2,0:T(2,128)(2,1)} %get-tuple-element.34) | copy-start | bytes 12292
  23.4 23.3 %all-to-all-start = ((bf16[64,16,128]{2,1,0:T(8,128)(2,1)}), bf16[64,16,128]{2,1,0:T(8,128)(2,1)S(1)}, u32[]{:S(2)}, u32[]{:S(2)}) async-start(bf16[64,16,128]{2,1,0:T(8,128)(2,1)} %fusion.9), calls=%async_computation | async-start | bytes 524288 | tf_op jit(solution)/shard_map/all_to_all | solution.py:79
  54.4 16.8 %all-to-all-start.1 = ((bf16[64,16,128]{2,1,0:T(8,128)(2,1)}), bf16[64,16,128]{2,1,0:T(8,128)(2,1)S(1)}, u32[]{:S(2)}, u32[]{:S(2)}) async-start(bf16[64,16,128]{2,1,0:T(8,128)(2,1)} %copy.77), calls=%async_computation.1 | async-start | bytes 524288 | tf_op jit(solution)/shard_map/all_to_all | solution.py:86
  76.3 5.2 %collective-permute-start.1 = (bf16[2,128,1024]{2,1,0:T(8,128)(2,1)S(1)}, bf16[2,128,1024]{2,1,0:T(8,128)(2,1)S(1)}, u32[]{:S(2)}, u32[]{:S(2)}) collective-permute-start(bf16[2,128,1024]{2,1,0:T(8,128)(2,1)S(1)} %pad_maximum_fusion), channel_id=1, source_target_pairs={{0,1},{1,0},{2,3},{3,2},{4,5},{5,4},{6,7},{7,6},{8,9},{9,8},{10,11... | collective-permute-start | bytes 1572872 | tf_op jit(solution)/shard_map/ppermute | solution.py:51
  81.8 9.1 %collective-permute-start.2 = (bf16[128,1024]{1,0:T(8,128)(2,1)S(1)}, bf16[128,1024]{1,0:T(8,128)(2,1)S(1)}, u32[]{:S(2)}, u32[]{:S(2)}) collective-permute-start(bf16[128,1024]{1,0:T(8,128)(2,1)S(1)} %fusion.15), channel_id=1, source_target_pairs={{0,2},{1,3},{2,0},{3,1},{4,6},{5,7},{6,4},{7,5},{8,10},{9,11},{10,... | collective-permute-start | bytes 786440 | tf_op jit(solution)/shard_map/ppermute | solution.py:56

commit v9 on v6

--- a/solution.py
+++ b/solution.py
@@ -8,6 +8,33 @@
     devices = lax.axis_size(axis)
     pairs = [(i, i + by) for i in range(devices) if 0 <= i + by < devices]
     return lax.ppermute(x, axis, pairs)
+
+
+def exclusive_decay(states, life, stride):
+    count = states.shape[-1]
+    idx = jnp.arange(count, dtype=jnp.int32)
+    gap = (idx[:, None] - 1 - idx[None, :]).astype(jnp.float32)
+    extra = states.ndim - 3
+    scale = life.reshape(life.shape[:2] + (1,) * (extra + 2))
+    exponent = jnp.where(idx[:, None] > idx[None, :], -stride * gap / scale, -jnp.inf)
+    return jnp.sum(jnp.exp(exponent) * states[..., None, :], axis=-1)
+
+
+def state_scan(leaving, life, block):
+    modes, chan, blocks = leaving.shape
+    inner = 8 if blocks % 8 == 0 else 1
+    outer = blocks // inner
+    grouped = leaving.reshape(modes, chan, outer, inner)
+    within = exclusive_decay(grouped, life, block)
+    to_group_end = jnp.exp(
+        -block * (float(inner - 1) - jnp.arange(inner, dtype=jnp.int32).astype(jnp.float32))
+        / life
+    )
+    totals = jnp.sum(to_group_end[:, :, None, :] * grouped, axis=-1)
+    before = exclusive_decay(totals, life, block * inner)
+    into = jnp.exp(-block * jnp.arange(inner, dtype=jnp.int32).astype(jnp.float32) / life)
+    result = within + into[:, :, None, :] * before[..., None]
+    return result.reshape(modes, chan, blocks)
 
 
 def modal_conv(pencils, life_slice, resid_slice, block=128):
@@ -27,14 +54,7 @@
     inside = jnp.einsum("cnj,cjt->cnt", signal, toeplitz, precision=precise)
     to_end = jnp.exp(-(float(block - 1) - steps)[None, None, :] / life)
     leaving = jnp.einsum("cnj,rcj->rcn", signal, to_end, precision=precise)
-    n_idx = jnp.arange(blocks, dtype=jnp.int32)
-    gap = (n_idx[:, None] - 1 - n_idx[None, :]).astype(jnp.float32)
-    exponent = jnp.where(
-        (n_idx[:, None] > n_idx[None, :])[None, None],
-        -float(block) * gap[None, None] / life[..., None],
-        -jnp.inf,
-    )
-    entering = jnp.sum(jnp.exp(exponent) * leaving[:, :, None, :], axis=-1)
+    entering = state_scan(leaving, life, float(block))
     from_start = resid * jnp.exp(-(steps + 1.0)[None, None, :] / life)
     carried = jnp.einsum("rcn,rct->cnt", entering, from_start, precision=precise)
     return (inside + carried).reshape(chan_here, length)

time: 78.8 us -> 80.1 us (1.016)
  matrix products: 8.18 us -> 10.1 us
  waiting for transfers between devices: 27.7 us -> 26.2 us
    all_to_all x1, waiting for transfers between devices: 8.82 us -> 7.25 us  [local(): lax.all_to_all(product, 'seq', split_axis=0, concat_axis=1, tiled=True)]
    reduce_sum x1 -> x2, other arithmetic: 2.64 us -> 1.61 us  [the longest x1 1.44 us: exclusive_decay(): return jnp.sum(jnp.exp(exponent) * states[..., None, :], axis=-1)]
    dot_general x1, matrix products: 1.94 us -> 2.91 us  [modal_conv(): jnp.einsum('rcj,rct->cjt', rising, falling, precision=lax.Precision.HIGHEST)]
    slice x1, local copies, waits for them, and re-layouts: 0.95 us -> 0.03 us  [local(): taps[:, 0, :, None] * extended[:, :, 2:]]
    mul x1 -> x3, other arithmetic: 0.07 us -> 0.99 us  [the longest x1 0.67 us: exclusive_decay(): -stride * gap / scale]
    dot_general x1, matrix products: 0.7 us -> 1.61 us  [modal_conv(): jnp.einsum('rcn,rct->cnt', entering, from_start, precision=precise)]
    add x0 -> x1, local copies, waits for them, and re-layouts: none -> 0.85 us  [state_scan(): result = within + into[:, :, None, :] * before[..., None]]
  transfers between devices with their start and end apart: 5 -> 5, of which waited for: 4 -> 4; matrix products, arithmetic and copies ran while one was open for 5% -> 7% of each run, Pallas kernels for 0% -> 0%
where the time goes in v9:
time: 80.1 us; the launch traced here: 79.7 us
  starting transfers between devices  29.5 us (37%)
  waiting for transfers between devices  26.2 us (33%)
  matrix products  10.1 us (13%)
  other arithmetic  7.62 us (10%)
  local copies, waits for them, and re-layouts  6.07 us (8%)
    all_to_all x1, starting transfers between devices, local(): lax.all_to_all(product, 'seq', split_axis=0, concat_axis=1, tiled=True)  13 us
    all_to_all x1, waiting for transfers between devices, local(): lax.all_to_all(convolved, 'seq', split_axis=1, concat_axis=0, tiled=True)  11 us
    all_to_all x1, waiting for transfers between devices, local(): lax.all_to_all(product, 'seq', split_axis=0, concat_axis=1, tiled=True)  7.25 us
    ppermute x1, waiting for transfers between devices, reduce_scatter_chan(): got2 = lax.ppermute(send2, 'chan', [(j, j ^ 2) for j in range(4)])  6.37 us
    all_to_all x1, starting transfers between devices, local(): lax.all_to_all(convolved, 'seq', split_axis=1, concat_axis=0, tiled=True)  4.85 us
    dot_general x1, matrix products, local(): lax.dot_general(gated_rows, out_weight, (((0,), (0,)), ((), ())), preferr...  4.67 us
    ppermute x1, starting transfers between devices, reduce_scatter_chan(): got = lax.ppermute(send, 'chan', [(j, j ^ 1) for j in range(4)])  4.63 us
    ppermute x1, starting transfers between devices, from_behind(): return lax.ppermute(x, axis, pairs)  4.36 us
  transfers between devices with their start and end apart: 5, of which 4 were waited for; matrix products, arithmetic and copies ran while one was open for 7% of the time, Pallas kernels for 0%

profile of v9, /device:TPU:1, one launch (start us, length us, event | category | flops | bytes accessed | tf_op | source)
XLA Modules:
  0.0 79.7 jit_solution(8497616663300258571)
XLA Ops:
  0.0 0.0 copy-start
  0.0 1.5 %slice.51 = bf16[3,1024,2]{2,1,0:T(8,128)(2,1)S(1)} slice(bf16[3,1024,128]{2,1,0:T(8,128)(2,1)} %param.5), slice={[0:3], [0:1024], [126:128]} | slice | bytes 24576 | tf_op jit(solution)/shard_map/slice | solution.py:83
  1.5 0.3 copy.42
  1.8 4.4 %collective-permute-start = (bf16[3,1024,2]{1,2,0:T(2,128)(2,1)S(1)}, bf16[3,1024,2]{1,2,0:T(2,128)(2,1)S(1)}, u32[]{:S(2)}, u32[]{:S(2)}) collective-permute-start(bf16[3,1024,2]{1,2,0:T(2,128)(2,1)S(1)} %copy.42), channel_id=1, source_target_pairs={{0,4},{4,8},{8,12},{12,16},{16,20},{20,24},{24,28},{28,32},{32,36}... | collective-permute-start | bytes 36872 | tf_op jit(solution)/shard_map/ppermute | solution.py:10
  6.2 0.0 copy-start.6
  6.3 0.0 copy-done.4
  6.3 0.7 convert_multiply_fusion
  7.0 0.0 copy-done
  7.0 0.1 constant_dynamic-slice_fusion
  7.1 0.8 constant_dynamic-slice_fusion.1
  7.8 0.1 divide_exponential_fusion.7
  8.0 0.0 collective-permute-done
  8.0 0.4 copy.31
  8.4 0.0 copy-done.1
  8.4 0.6 maximum_convert_fusion
  9.0 2.4 %fusion.1 = f32[3,1024,128]{2,1,0:T(8,128)S(1)} fusion(f32[3,1024,130]{2,1,0:T(8,128)S(1)} %maximum_convert_fusion, f32[3,1024]{1,0:T(4,128)S(1)} %get-tuple-element.16, f32[3,1024]{1,0:T(4,128)S(1)} %get-tuple-element.17, f32[3,1024]{1,0:T(4,128)S(1)} %bitcast.52), kind=kLoop, calls=%fused_computation.4 | loop fusion | flops 1966080 | bytes 6328320 | tf_op jit(solution)/shard_map/add | solution.py:87
  11.4 0.8 fusion.10
  12.1 13.0 %all-to-all-start = ((bf16[64,16,128]{2,1,0:T(8,128)(2,1)}), bf16[64,16,128]{2,1,0:T(8,128)(2,1)S(1)}, u32[]{:S(2)}, u32[]{:S(2)}) async-start(bf16[64,16,128]{2,1,0:T(8,128)(2,1)} %bitcast.1), calls=%async_computation | async-start | bytes 524288 | tf_op jit(solution)/shard_map/all_to_all | solution.py:94
  25.1 0.5 add_negate_fusion
  25.6 0.1 copy.34
  25.7 0.1 copy.33
  25.8 0.0 copy-done.6
  25.8 0.2 fusion.9
  25.9 2.9 %convolution_select_fusion = f32[16,128,128]{2,1,0:T(8,128)} fusion(pred[128,128]{1,0:T(8,128)(4,1)S(1)} %subtract_compare_fusion, f32[128]{0:T(128)S(1)} %get-tuple-element.21, f32[16,16]{0,1:T(8,128)S(1)} %copy.34, f32[128]{0:T(128)S(1)} %get-tuple-element.20, f32[16,16]{0,1:T(8,128)S(1)} %copy.33), kind=kOutput, calls=%fused_computation.9 | convolution fusion | flops 50692096 | bytes 1068032 | tf_op jit(solution)/shard_map/rcj,rct->cjt/dot_general | solution.py:49
  28.9 7.2 %all-to-all-done = bf16[64,16,128]{2,1,0:T(8,128)(2,1)S(1)} async-done(((bf16[64,16,128]{2,1,0:T(8,128)(2,1)}), bf16[64,16,128]{2,1,0:T(8,128)(2,1)S(1)}, u32[]{:S(2)}, u32[]{:S(2)}) %all-to-all-start) | async-done | bytes 262176 | tf_op jit(solution)/shard_map/all_to_all | solution.py:94
  36.1 0.4 convolution_bitcast_fusion
  36.5 0.2 copy.35
  36.8 0.2 multiply_reduce_fusion.1
  37.0 1.4 %multiply_reduce_fusion = f32[16,16,8,8]{1,3,2,0:T(8,128)S(1)} fusion(f32[16,16,8,8]{1,3,2,0:T(8,128)S(1)} %bitcast.51, f32[16,16,8,8]{1,3,2,0:T(8,128)S(1)} %fusion.9), kind=kLoop, calls=%fused_computation.2 | loop fusion | flops 245760 | bytes 196608 | tf_op jit(solution)/shard_map/reduce_sum | solution.py:20
  38.4 0.3 fusion.5
  38.8 0.8 %copy.36 = f32[16,16,64]{2,0,1:T(8,128)} copy(f32[16,16,64]{1,2,0:T(8,128)S(1)} %fusion.5) | data formatting | bytes 131072 | tf_op jit(solution)/shard_map/add | solution.py:36
  39.6 1.6 %fusion.28 = f32[16,64,128]{2,1,0:T(8,128)S(1)} fusion(f32[16,16,64]{2,0,1:T(8,128)} %copy.36, f32[128]{0:T(128)} %add_negate_fusion, f32[16,16]{0,1:T(8,128)S(1)} %copy.34, f32[16,16]{0,1:T(8,128)} %copy-done.3), kind=kOutput, calls=%fused_computation.50 | convolution fusion | flops 12648448 | bytes 592384 | tf_op jit(solution)/shard_map/rcn,rct->cnt/dot_general | solution.py:59
  41.2 0.4 fusion.6
  41.7 0.9 %copy.37 = bf16[16,64,128]{2,0,1:T(8,128)(2,1)} copy(bf16[16,64,128]{2,1,0:T(8,128)(2,1)S(1)} %fusion.6) | data formatting | bytes 524288 | tf_op jit(solution)/shard_map/convert_element_type | solution.py:98
  42.5 4.8 %all-to-all-start.1 = ((bf16[16,64,128]{2,0,1:T(8,128)(2,1)}), bf16[16,64,128]{2,0,1:T(8,128)(2,1)S(1)}, u32[]{:S(2)}, u32[]{:S(2)}) async-start(bf16[16,64,128]{2,0,1:T(8,128)(2,1)} %copy.37), calls=%async_computation.1 | async-start | bytes 524288 | tf_op jit(solution)/shard_map/all_to_all | solution.py:99
  47.4 11.0 %all-to-all-done.1 = bf16[16,64,128]{2,0,1:T(8,128)(2,1)S(1)} async-done(((bf16[16,64,128]{2,0,1:T(8,128)(2,1)}), bf16[16,64,128]{2,0,1:T(8,128)(2,1)S(1)}, u32[]{:S(2)}, u32[]{:S(2)}) %all-to-all-start.1) | async-done | bytes 262176 | tf_op jit(solution)/shard_map/all_to_all | solution.py:99
  58.4 0.1 fusion.12
  58.5 4.7 %convolution_convert_fusion = bf16[128,4096]{1,0:T(8,128)(2,1)S(1)} fusion(bf16[1024,128]{1,0:T(8,128)(2,1)S(1)} %fusion.12, bf16[1024,4096]{1,0:T(8,128)(2,1)} %param.9), kind=kOutput, calls=%fused_computation.1 | convolution fusion | flops 1074266112 | bytes 9699328 | tf_op jit(solution)/shard_map/dot_general | solution.py:101
  63.2 0.1 select_bitcast_fusion.3
  63.2 0.1 pad_maximum_fusion
  63.3 4.6 %collective-permute-start.1 = (bf16[2,128,1024]{2,1,0:T(8,128)(2,1)S(1)}, bf16[2,128,1024]{2,1,0:T(8,128)(2,1)S(1)}, u32[]{:S(2)}, u32[]{:S(2)}) collective-permute-start(bf16[2,128,1024]{2,1,0:T(8,128)(2,1)S(1)} %pad_maximum_fusion), channel_id=1, source_target_pairs={{0,1},{1,0},{2,3},{3,2},{4,5},{5,4},{6,7},{7,6},{8,9},{9,8},{10,11... | collective-permute-start | bytes 1572872 | tf_op jit(solution)/shard_map/ppermute | solution.py:71
  67.9 1.5 %collective-permute-done.1 = bf16[2,128,1024]{2,1,0:T(8,128)(2,1)S(1)} collective-permute-done((bf16[2,128,1024]{2,1,0:T(8,128)(2,1)S(1)}, bf16[2,128,1024]{2,1,0:T(8,128)(2,1)S(1)}, u32[]{:S(2)}, u32[]{:S(2)}) %collective-permute-start.1) | collective-permute-done | bytes 524320 | tf_op jit(solution)/shard_map/ppermute | solution.py:71
  69.5 0.2 convert_add_fusion
  69.6 0.1 fusion.16
  69.7 2.7 %collective-permute-start.2 = (bf16[128,1024]{1,0:T(8,128)(2,1)S(1)}, bf16[128,1024]{1,0:T(8,128)(2,1)S(1)}, u32[]{:S(2)}, u32[]{:S(2)}) collective-permute-start(bf16[128,1024]{1,0:T(8,128)(2,1)S(1)} %fusion.16), channel_id=1, source_target_pairs={{0,2},{1,3},{2,0},{3,1},{4,6},{5,7},{6,4},{7,5},{8,10},{9,11},{10,... | collective-permute-start | bytes 786440 | tf_op jit(solution)/shard_map/ppermute | solution.py:76
  72.4 6.4 %collective-permute-done.2 = bf16[128,1024]{1,0:T(8,128)(2,1)S(1)} collective-permute-done((bf16[128,1024]{1,0:T(8,128)(2,1)S(1)}, bf16[128,1024]{1,0:T(8,128)(2,1)S(1)}, u32[]{:S(2)}, u32[]{:S(2)}) %collective-permute-start.2) | collective-permute-done | bytes 262176 | tf_op jit(solution)/shard_map/ppermute | solution.py:76
  78.8 0.1 fusion.17
  78.9 0.8 %copy.38 = bf16[1024,128]{1,0:T(8,128)(2,1)} copy(bf16[1024,128]{0,1:T(8,128)(2,1)S(1)} %fusion.17) | data formatting | bytes 524288 | tf_op jit(solution)/shard_map/transpose | solution.py:77
  (19 shorter events, 0.1 us)
Async XLA Ops:
  0.0 7.0 %copy-start = (f32[16,1024]{1,0:T(8,128)S(1)}, f32[16,1024]{1,0:T(8,128)}, u32[]{:S(2)}) copy-start(f32[16,1024]{1,0:T(8,128)} %param.7) | copy-start | bytes 196612
  0.0 8.4 %copy-start.1 = (bf16[3,1024,128]{2,1,0:T(8,128)(2,1)S(1)}, bf16[3,1024,128]{2,1,0:T(8,128)(2,1)}, u32[]{:S(2)}) copy-start(bf16[3,1024,128]{2,1,0:T(8,128)(2,1)} %param.5) | copy-start | bytes 2359300
  0.0 6.3 %copy-start.4 = (f32[3,3,1024]{2,1,0:T(4,128)S(1)}, f32[3,3,1024]{2,1,0:T(4,128)}, u32[]{:S(2)}) copy-start(f32[3,3,1024]{2,1,0:T(4,128)} %param.6) | copy-start | bytes 110596
  1.8 6.2 %collective-permute-start = (bf16[3,1024,2]{1,2,0:T(2,128)(2,1)S(1)}, bf16[3,1024,2]{1,2,0:T(2,128)(2,1)S(1)}, u32[]{:S(2)}, u32[]{:S(2)}) collective-permute-start(bf16[3,1024,2]{1,2,0:T(2,128)(2,1)S(1)} %copy.42), channel_id=1, source_target_pairs={{0,4},{4,8},{8,12},{12,16},{16,20},{20,24},{24,28},{28,32},{32,36}... | collective-permute-start | bytes 36872 | tf_op jit(solution)/shard_map/ppermute | solution.py:10
  6.2 19.6 %copy-start.6 = (pred[8,8]{1,0:T(8,128)(4,1)}, pred[8,8]{1,0:T(8,128)(4,1)S(1)}, u32[]{:S(2)}) copy-start(pred[8,8]{1,0:T(8,128)(4,1)S(1)} %iota_compare_fusion) | copy-start | bytes 196
  12.1 24.0 %all-to-all-start = ((bf16[64,16,128]{2,1,0:T(8,128)(2,1)}), bf16[64,16,128]{2,1,0:T(8,128)(2,1)S(1)}, u32[]{:S(2)}, u32[]{:S(2)}) async-start(bf16[64,16,128]{2,1,0:T(8,128)(2,1)} %bitcast.1), calls=%async_computation | async-start | bytes 524288 | tf_op jit(solution)/shard_map/all_to_all | solution.py:94
  25.8 3.1 %copy-start.3 = (f32[16,16]{0,1:T(8,128)}, f32[16,16]{0,1:T(8,128)S(1)}, u32[]{:S(2)}) copy-start(f32[16,16]{0,1:T(8,128)S(1)} %copy.33) | copy-start | bytes 3076
  36.8 1.6 %copy-start.5 = (f32[8,8]{1,0:T(8,128)S(1)}, f32[8,8]{1,0:T(8,128)}, u32[]{:S(2)}) copy-start(f32[8,8]{1,0:T(8,128)} %get-tuple-element.14) | copy-start | bytes 772
  36.8 1.6 %copy-start.7 = (pred[8,8]{1,0:T(8,128)(4,1)S(1)}, pred[8,8]{1,0:T(8,128)(4,1)}, u32[]{:S(2)}) copy-start(pred[8,8]{1,0:T(8,128)(4,1)} %copy-done.6) | copy-start | bytes 196
  38.4 2.8 %copy-start.2 = (f32[16,128,128]{2,1,0:T(8,128)S(1)}, f32[16,128,128]{2,1,0:T(8,128)}, u32[]{:S(2)}) copy-start(f32[16,128,128]{2,1,0:T(8,128)} %convolution_select_fusion) | copy-start | bytes 3145732
  42.5 15.9 %all-to-all-start.1 = ((bf16[16,64,128]{2,0,1:T(8,128)(2,1)}), bf16[16,64,128]{2,0,1:T(8,128)(2,1)S(1)}, u32[]{:S(2)}, u32[]{:S(2)}) async-start(bf16[16,64,128]{2,0,1:T(8,128)(2,1)} %copy.37), calls=%async_computation.1 | async-start | bytes 524288 | tf_op jit(solution)/shard_map/all_to_all | solution.py:99
  63.3 6.2 %collective-permute-start.1 = (bf16[2,128,1024]{2,1,0:T(8,128)(2,1)S(1)}, bf16[2,128,1024]{2,1,0:T(8,128)(2,1)S(1)}, u32[]{:S(2)}, u32[]{:S(2)}) collective-permute-start(bf16[2,128,1024]{2,1,0:T(8,128)(2,1)S(1)} %pad_maximum_fusion), channel_id=1, source_target_pairs={{0,1},{1,0},{2,3},{3,2},{4,5},{5,4},{6,7},{7,6},{8,9},{9,8},{10,11... | collective-permute-start | bytes 1572872 | tf_op jit(solution)/shard_map/ppermute | solution.py:71
  69.7 9.1 %collective-permute-start.2 = (bf16[128,1024]{1,0:T(8,128)(2,1)S(1)}, bf16[128,1024]{1,0:T(8,128)(2,1)S(1)}, u32[]{:S(2)}, u32[]{:S(2)}) collective-permute-start(bf16[128,1024]{1,0:T(8,128)(2,1)S(1)} %fusion.16), channel_id=1, source_target_pairs={{0,2},{1,3},{2,0},{3,1},{4,6},{5,7},{6,4},{7,5},{8,10},{9,11},{10,... | collective-permute-start | bytes 786440 | tf_op jit(solution)/shard_map/ppermute | solution.py:76

commit v10 on v6

--- a/solution.py
+++ b/solution.py
@@ -60,8 +60,14 @@
 def local(qkv, taps, lifetimes, residues, out_weight):
     chan_local = qkv.shape[1]
     tok_count = qkv.shape[2]
-    edge_block = qkv[:, :, tok_count - 2 :]
-    earlier = from_behind(edge_block, "seq", 1)
+    pick = (
+        jnp.arange(tok_count, dtype=jnp.int32)[:, None]
+        == tok_count - 2 + jnp.arange(2, dtype=jnp.int32)[None, :]
+    ).astype(qkv.dtype)
+    edge_block = jnp.einsum(
+        "sct,tk->skc", qkv, pick, preferred_element_type=jnp.float32
+    ).astype(qkv.dtype)
+    earlier = jnp.swapaxes(from_behind(edge_block, "seq", 1), 1, 2)
     extended = jnp.concatenate([earlier, qkv], axis=2).astype(jnp.float32)
     filtered = (
         taps[:, 0, :, None] * extended[:, :, 2:]

time: 78.8 us -> 79.7 us (1.011)
  local copies, waits for them, and re-layouts: 5.87 us -> 4.09 us
  matrix products: 8.18 us -> 9.65 us
  other arithmetic: 6.96 us -> 8.09 us
    slice x1 -> x0, local copies, waits for them, and re-layouts: 1.48 us -> none  [local(): edge_block = qkv[:, :, tok_count - 2:]]
    dot_general x0 -> x1, matrix products: none -> 1.47 us  [local(): jnp.einsum('sct,tk->skc', qkv, pick, preferred_element_type=jnp.float32)]
    convert_element_type x1, other arithmetic: 0.6 us -> 1.73 us  [local(): extended = jnp.concatenate([earlier, qkv], axis=2).astype(jnp.float32)]
where the time goes in v10:
time: 79.7 us; the launch traced here: 79.2 us
  starting transfers between devices  29.5 us (37%)
  waiting for transfers between devices  27.7 us (35%)
  matrix products  9.65 us (12%)
  other arithmetic  8.09 us (10%)
  local copies, waits for them, and re-layouts  4.09 us (5%)
    all_to_all x1, starting transfers between devices, local(): lax.all_to_all(product, 'seq', split_axis=0, concat_axis=1, tiled=True)  12.9 us
    all_to_all x1, waiting for transfers between devices, local(): lax.all_to_all(convolved, 'seq', split_axis=1, concat_axis=0, tiled=True)  11 us
    all_to_all x1, waiting for transfers between devices, local(): lax.all_to_all(product, 'seq', split_axis=0, concat_axis=1, tiled=True)  8.82 us
    ppermute x1, waiting for transfers between devices, reduce_scatter_chan(): got2 = lax.ppermute(send2, 'chan', [(j, j ^ 2) for j in range(4)])  6.37 us
    all_to_all x1, starting transfers between devices, local(): lax.all_to_all(convolved, 'seq', split_axis=1, concat_axis=0, tiled=True)  4.85 us
    dot_general x1, matrix products, local(): lax.dot_general(gated_rows, out_weight, (((0,), (0,)), ((), ())), preferr...  4.67 us
    ppermute x1, starting transfers between devices, reduce_scatter_chan(): got = lax.ppermute(send, 'chan', [(j, j ^ 1) for j in range(4)])  4.63 us
    ppermute x1, starting transfers between devices, from_behind(): return lax.ppermute(x, axis, pairs)  4.37 us
  transfers between devices with their start and end apart: 5, of which 4 were waited for; matrix products, arithmetic and copies ran while one was open for 5% of the time, Pallas kernels for 0%

profile of v10, /device:TPU:1, one launch (start us, length us, event | category | flops | bytes accessed | tf_op | source)
XLA Modules:
  0.0 79.2 jit_solution(14042325894225201602)
XLA Ops:
  0.0 1.5 %fusion.6 = bf16[3,2,1024]{2,1,0:T(2,128)(2,1)S(1)} fusion(bf16[3,1024,128]{2,1,0:T(8,128)(2,1)} %param.5, s32[2]{0:T(128)S(1)} %iota_add_fusion.1), kind=kOutput, calls=%fused_computation.16 | convolution fusion | flops 1579264 | bytes 798728 | tf_op jit(solution)/shard_map/sct,tk->skc/dot_general | solution.py:67
  1.5 4.4 %collective-permute-start = (bf16[3,2,1024]{2,1,0:T(2,128)(2,1)S(1)}, bf16[3,2,1024]{2,1,0:T(2,128)(2,1)S(1)}, u32[]{:S(2)}, u32[]{:S(2)}) collective-permute-start(bf16[3,2,1024]{2,1,0:T(2,128)(2,1)S(1)} %fusion.6), channel_id=1, source_target_pairs={{0,4},{4,8},{8,12},{12,16},{16,20},{20,24},{24,28},{28,32},{32,36}... | collective-permute-start | bytes 36872 | tf_op jit(solution)/shard_map/ppermute | solution.py:10
  5.9 0.9 %fusion.37 = (f32[3,1,1024]{2,1,0:T(1,128)S(1)}, f32[3,1,1024]{2,1,0:T(1,128)S(1)}, f32[3,1,1024]{2,1,0:T(1,128)S(1)}) fusion(f32[3,3,1024]{2,1,0:T(4,128)} %param.6), kind=kLoop, calls=%fused_computation.72 | loop fusion | bytes 73728 | tf_op jit(solution)/shard_map/slice | solution.py:73
  6.9 0.8 %constant_dynamic-slice_fusion = (f32[16,16]{1,0:T(8,128)S(1)}, f32[16,16]{1,0:T(8,128)S(1)}) fusion(f32[16,1024]{1,0:T(8,128)} %param.7, s32[]{:T(128)S(6)} %select_n.63, f32[16,1024]{1,0:T(8,128)} %param.8), kind=kLoop, calls=%fused_computation.69 | loop fusion | bytes 4100 | tf_op jit(solution)/shard_map/dynamic_slice | solution.py:82
  7.7 0.0 collective-permute-done
  7.7 0.4 copy.23
  8.1 1.7 %maximum_convert_fusion = f32[3,1024,130]{2,1,0:T(8,128)S(1)} fusion(bf16[3,1024,128]{2,1,0:T(8,128)(2,1)} %param.5, bf16[3,1024,2]{2,1,0:T(8,128)(2,1)S(1)} %copy.23), kind=kLoop, calls=%fused_computation.10 | loop fusion | flops 1597440 | bytes 2396160 | tf_op jit(solution)/shard_map/convert_element_type | solution.py:71
  9.9 2.4 %fusion.3 = f32[3,1024,128]{2,1,0:T(8,128)S(1)} fusion(f32[3,1024,130]{2,1,0:T(8,128)S(1)} %maximum_convert_fusion, f32[3,1024]{1,0:T(4,128)S(1)} %get-tuple-element.12, f32[3,1024]{1,0:T(4,128)S(1)} %get-tuple-element.13, f32[3,1024]{1,0:T(4,128)S(1)} %bitcast.53), kind=kLoop, calls=%fused_computation.6 | loop fusion | flops 1966080 | bytes 6328320 | tf_op jit(solution)/shard_map/add | solution.py:73
  12.2 0.8 fusion.7
  13.0 12.9 %all-to-all-start = ((bf16[64,16,128]{2,1,0:T(8,128)(2,1)}), bf16[64,16,128]{2,1,0:T(8,128)(2,1)S(1)}, u32[]{:S(2)}, u32[]{:S(2)}) async-start(bf16[64,16,128]{2,1,0:T(8,128)(2,1)} %bitcast.4), calls=%async_computation | async-start | bytes 524288 | tf_op jit(solution)/shard_map/all_to_all | solution.py:80
  25.9 0.1 copy.26
  26.0 0.1 copy.25
  26.0 0.1 convert_multiply_fusion
  26.1 1.9 %convolution_select_fusion = f32[16,128,128]{2,1,0:T(8,128)S(1)} fusion(pred[128,128]{1,0:T(8,128)(4,1)S(1)} %subtract_compare_fusion, f32[128]{0:T(128)S(1)} %get-tuple-element.17, f32[16,16]{0,1:T(8,128)S(1)} %copy.26, f32[128]{0:T(128)S(1)} %get-tuple-element.16, f32[16,16]{0,1:T(8,128)S(1)} %copy.25), kind=kOutput, calls=%fused_computation.11 | convolution fusion | flops 50692096 | bytes 1068032 | tf_op jit(solution)/shard_map/rcj,rct->cjt/dot_general | solution.py:22
  28.1 8.8 %all-to-all-done = bf16[64,16,128]{2,1,0:T(8,128)(2,1)S(1)} async-done(((bf16[64,16,128]{2,1,0:T(8,128)(2,1)}), bf16[64,16,128]{2,1,0:T(8,128)(2,1)S(1)}, u32[]{:S(2)}, u32[]{:S(2)}) %all-to-all-start) | async-done | bytes 262176 | tf_op jit(solution)/shard_map/all_to_all | solution.py:80
  36.9 0.4 convolution_bitcast_fusion
  37.4 2.6 %fusion.2 = f32[16,16,64]{2,1,0:T(8,128)S(1)} fusion(f32[16,16,64]{2,1,0:T(8,128)S(1)} %copy.27, f32[16,16]{1,0:T(8,128)S(1)} %get-tuple-element.14, f32[64,64]{1,0:T(8,128)S(1)} %convert_multiply_fusion, pred[64,64]{1,0:T(8,128)(4,1)S(1)} %iota_compare_fusion), kind=kLoop, calls=%fused_computation.3 | loop fusion | flops 4177920 | bytes 152576 | tf_op jit(solution)/shard_map/reduce_sum | solution.py:37
  40.0 0.7 fusion.18
  40.7 0.4 fusion.5
  41.2 0.9 %copy.29 = bf16[16,64,128]{2,0,1:T(8,128)(2,1)} copy(bf16[16,64,128]{2,1,0:T(8,128)(2,1)S(1)} %fusion.5) | data formatting | bytes 524288 | tf_op jit(solution)/shard_map/convert_element_type | solution.py:84
  42.0 4.8 %all-to-all-start.1 = ((bf16[16,64,128]{2,0,1:T(8,128)(2,1)}), bf16[16,64,128]{2,0,1:T(8,128)(2,1)S(1)}, u32[]{:S(2)}, u32[]{:S(2)}) async-start(bf16[16,64,128]{2,0,1:T(8,128)(2,1)} %copy.29), calls=%async_computation.1 | async-start | bytes 524288 | tf_op jit(solution)/shard_map/all_to_all | solution.py:85
  46.9 11.0 %all-to-all-done.1 = bf16[16,64,128]{2,0,1:T(8,128)(2,1)S(1)} async-done(((bf16[16,64,128]{2,0,1:T(8,128)(2,1)}), bf16[16,64,128]{2,0,1:T(8,128)(2,1)S(1)}, u32[]{:S(2)}, u32[]{:S(2)}) %all-to-all-start.1) | async-done | bytes 262176 | tf_op jit(solution)/shard_map/all_to_all | solution.py:85
  57.9 0.1 fusion.9
  58.0 4.7 %convolution_convert_fusion = bf16[128,4096]{1,0:T(8,128)(2,1)S(1)} fusion(bf16[1024,128]{1,0:T(8,128)(2,1)S(1)} %fusion.9, bf16[1024,4096]{1,0:T(8,128)(2,1)} %param.9), kind=kOutput, calls=%fused_computation.4 | convolution fusion | flops 1074266112 | bytes 9699328 | tf_op jit(solution)/shard_map/dot_general | solution.py:87
  62.7 0.1 select_bitcast_fusion.3
  62.7 0.1 pad_maximum_fusion
  62.8 4.6 %collective-permute-start.1 = (bf16[2,128,1024]{2,1,0:T(8,128)(2,1)S(1)}, bf16[2,128,1024]{2,1,0:T(8,128)(2,1)S(1)}, u32[]{:S(2)}, u32[]{:S(2)}) collective-permute-start(bf16[2,128,1024]{2,1,0:T(8,128)(2,1)S(1)} %pad_maximum_fusion), channel_id=1, source_target_pairs={{0,1},{1,0},{2,3},{3,2},{4,5},{5,4},{6,7},{7,6},{8,9},{9,8},{10,11... | collective-permute-start | bytes 1572872 | tf_op jit(solution)/shard_map/ppermute | solution.py:51
  67.4 1.5 %collective-permute-done.1 = bf16[2,128,1024]{2,1,0:T(8,128)(2,1)S(1)} collective-permute-done((bf16[2,128,1024]{2,1,0:T(8,128)(2,1)S(1)}, bf16[2,128,1024]{2,1,0:T(8,128)(2,1)S(1)}, u32[]{:S(2)}, u32[]{:S(2)}) %collective-permute-start.1) | collective-permute-done | bytes 524320 | tf_op jit(solution)/shard_map/ppermute | solution.py:51
  69.0 0.2 convert_add_fusion
  69.1 0.1 fusion.11
  69.2 2.7 %collective-permute-start.2 = (bf16[128,1024]{1,0:T(8,128)(2,1)S(1)}, bf16[128,1024]{1,0:T(8,128)(2,1)S(1)}, u32[]{:S(2)}, u32[]{:S(2)}) collective-permute-start(bf16[128,1024]{1,0:T(8,128)(2,1)S(1)} %fusion.11), channel_id=1, source_target_pairs={{0,2},{1,3},{2,0},{3,1},{4,6},{5,7},{6,4},{7,5},{8,10},{9,11},{10,... | collective-permute-start | bytes 786440 | tf_op jit(solution)/shard_map/ppermute | solution.py:56
  71.9 6.4 %collective-permute-done.2 = bf16[128,1024]{1,0:T(8,128)(2,1)S(1)} collective-permute-done((bf16[128,1024]{1,0:T(8,128)(2,1)S(1)}, bf16[128,1024]{1,0:T(8,128)(2,1)S(1)}, u32[]{:S(2)}, u32[]{:S(2)}) %collective-permute-start.2) | collective-permute-done | bytes 262176 | tf_op jit(solution)/shard_map/ppermute | solution.py:56
  78.3 0.1 fusion.12
  78.4 0.8 %copy.30 = bf16[1024,128]{1,0:T(8,128)(2,1)} copy(bf16[1024,128]{0,1:T(8,128)(2,1)S(1)} %fusion.12) | data formatting | bytes 524288 | tf_op jit(solution)/shard_map/transpose | solution.py:57
  (10 shorter events, 0.1 us)
Async XLA Ops:
  1.5 6.2 %collective-permute-start = (bf16[3,2,1024]{2,1,0:T(2,128)(2,1)S(1)}, bf16[3,2,1024]{2,1,0:T(2,128)(2,1)S(1)}, u32[]{:S(2)}, u32[]{:S(2)}) collective-permute-start(bf16[3,2,1024]{2,1,0:T(2,128)(2,1)S(1)} %fusion.6), channel_id=1, source_target_pairs={{0,4},{4,8},{8,12},{12,16},{16,20},{20,24},{24,28},{28,32},{32,36}... | collective-permute-start | bytes 36872 | tf_op jit(solution)/shard_map/ppermute | solution.py:10
  13.0 23.9 %all-to-all-start = ((bf16[64,16,128]{2,1,0:T(8,128)(2,1)}), bf16[64,16,128]{2,1,0:T(8,128)(2,1)S(1)}, u32[]{:S(2)}, u32[]{:S(2)}) async-start(bf16[64,16,128]{2,1,0:T(8,128)(2,1)} %bitcast.4), calls=%async_computation | async-start | bytes 524288 | tf_op jit(solution)/shard_map/all_to_all | solution.py:80
  42.0 15.9 %all-to-all-start.1 = ((bf16[16,64,128]{2,0,1:T(8,128)(2,1)}), bf16[16,64,128]{2,0,1:T(8,128)(2,1)S(1)}, u32[]{:S(2)}, u32[]{:S(2)}) async-start(bf16[16,64,128]{2,0,1:T(8,128)(2,1)} %copy.29), calls=%async_computation.1 | async-start | bytes 524288 | tf_op jit(solution)/shard_map/all_to_all | solution.py:85
  62.8 6.2 %collective-permute-start.1 = (bf16[2,128,1024]{2,1,0:T(8,128)(2,1)S(1)}, bf16[2,128,1024]{2,1,0:T(8,128)(2,1)S(1)}, u32[]{:S(2)}, u32[]{:S(2)}) collective-permute-start(bf16[2,128,1024]{2,1,0:T(8,128)(2,1)S(1)} %pad_maximum_fusion), channel_id=1, source_target_pairs={{0,1},{1,0},{2,3},{3,2},{4,5},{5,4},{6,7},{7,6},{8,9},{9,8},{10,11... | collective-permute-start | bytes 1572872 | tf_op jit(solution)/shard_map/ppermute | solution.py:51
  69.2 9.1 %collective-permute-start.2 = (bf16[128,1024]{1,0:T(8,128)(2,1)S(1)}, bf16[128,1024]{1,0:T(8,128)(2,1)S(1)}, u32[]{:S(2)}, u32[]{:S(2)}) collective-permute-start(bf16[128,1024]{1,0:T(8,128)(2,1)S(1)} %fusion.11), channel_id=1, source_target_pairs={{0,2},{1,3},{2,0},{3,1},{4,6},{5,7},{6,4},{7,5},{8,10},{9,11},{10,... | collective-permute-start | bytes 786440 | tf_op jit(solution)/shard_map/ppermute | solution.py:56

commit v11 on v6

--- a/solution.py
+++ b/solution.py
@@ -62,13 +62,27 @@
     tok_count = qkv.shape[2]
     edge_block = qkv[:, :, tok_count - 2 :]
     earlier = from_behind(edge_block, "seq", 1)
-    extended = jnp.concatenate([earlier, qkv], axis=2).astype(jnp.float32)
-    filtered = (
-        taps[:, 0, :, None] * extended[:, :, 2:]
-        + taps[:, 1, :, None] * extended[:, :, 1:-1]
-        + taps[:, 2, :, None] * extended[:, :, :-2]
+
+    signal = qkv.astype(jnp.float32)
+    pad1 = jnp.zeros(signal.shape[:2] + (1,), jnp.float32)
+    pad2 = jnp.zeros(signal.shape[:2] + (2,), jnp.float32)
+    no_halo = (
+        taps[:, 0, :, None] * signal
+        + taps[:, 1, :, None] * jnp.concatenate([pad1, signal[:, :, :-1]], axis=2)
+        + taps[:, 2, :, None] * jnp.concatenate([pad2, signal[:, :, :-2]], axis=2)
     )
-    product = (filtered[1] * filtered[2]).astype(jnp.bfloat16)
+    head_in = jnp.concatenate([earlier, qkv[:, :, :2]], axis=2).astype(jnp.float32)
+    head = (
+        taps[:, 0, :, None] * head_in[:, :, 2:]
+        + taps[:, 1, :, None] * head_in[:, :, 1:3]
+        + taps[:, 2, :, None] * head_in[:, :, :2]
+    )
+    product = lax.dynamic_update_slice(
+        (no_halo[1] * no_halo[2]).astype(jnp.bfloat16),
+        (head[1] * head[2]).astype(jnp.bfloat16),
+        (0, 0),
+    )
+    filtered_q = lax.dynamic_update_slice(no_halo[0], head[0], (0, 0))
     groups = lax.axis_size("seq")
     per_group = chan_local // groups
     pencils = lax.all_to_all(product, "seq", split_axis=0, concat_axis=1, tiled=True)
@@ -77,7 +91,7 @@
     resid_slice = lax.dynamic_slice_in_dim(residues, first_chan, per_group, 1)
     convolved = modal_conv(pencils, life_slice, resid_slice).astype(jnp.bfloat16)
     returned = lax.all_to_all(convolved, "seq", split_axis=1, concat_axis=0, tiled=True)
-    gated_rows = (filtered[0] * returned.astype(jnp.float32)).astype(jnp.bfloat16)
+    gated_rows = (filtered_q * returned.astype(jnp.float32)).astype(jnp.bfloat16)
     partial = lax.dot_general(
         gated_rows, out_weight, (((0,), (0,)), ((), ())), preferred_element_type=jnp.float32
     ).astype(jnp.bfloat16)

time: 78.8 us -> 82 us (1.041)
  local copies, waits for them, and re-layouts: 5.87 us -> 12 us
  waiting for transfers between devices: 27.7 us -> 25.7 us
  starting transfers between devices: 29.4 us -> 28.5 us
    dynamic_update_slice x0 -> x2, local copies, waits for them, and re-layouts: none -> 5.09 us  [the longest x1 2.8 us: local(): lax.dynamic_update_slice((no_halo[1] * no_halo[2]).astype(jnp.bfloat16),...]
    all_to_all x1, waiting for transfers between devices: 11 us -> 8.5 us  [local(): lax.all_to_all(convolved, 'seq', split_axis=1, concat_axis=0, tiled=True)]
    all_to_all x1, starting transfers between devices: 12.9 us -> 11.8 us  [local(): lax.all_to_all(product, 'seq', split_axis=0, concat_axis=1, tiled=True)]
    all_to_all x1, starting transfers between devices: 4.85 us -> 5.94 us  [local(): lax.all_to_all(convolved, 'seq', split_axis=1, concat_axis=0, tiled=True)]
    unnamed x5 -> x10, local copies, waits for them, and re-layouts: 0.32 us -> 1.24 us
    ppermute x1, starting transfers between devices: 4.63 us -> 3.71 us  [reduce_scatter_chan(): got = lax.ppermute(send, 'chan', [(j, j ^ 1) for j in range(4)])]
    add x1 -> x2, other arithmetic: 2.35 us -> 2.5 us  [the longest x1 2.34 us: local(): taps[:, 0, :, None] * signal]
  transfers between devices with their start and end apart: 5 -> 5, of which waited for: 4 -> 4; matrix products, arithmetic and copies ran while one was open for 5% -> 11% of each run, Pallas kernels for 0% -> 0%
where the time goes in v11:
time: 82 us; the launch traced here: 81.5 us
  starting transfers between devices  28.5 us (35%)
  waiting for transfers between devices  25.7 us (31%)
  local copies, waits for them, and re-layouts  12 us (15%)
  matrix products  8.18 us (10%)
  other arithmetic  6.88 us (8%)
    all_to_all x1, starting transfers between devices, local(): lax.all_to_all(product, 'seq', split_axis=0, concat_axis=1, tiled=True)  11.8 us
    all_to_all x1, waiting for transfers between devices, local(): lax.all_to_all(product, 'seq', split_axis=0, concat_axis=1, tiled=True)  9.24 us
    all_to_all x1, waiting for transfers between devices, local(): lax.all_to_all(convolved, 'seq', split_axis=1, concat_axis=0, tiled=True)  8.5 us
    ppermute x1, waiting for transfers between devices, reduce_scatter_chan(): got2 = lax.ppermute(send2, 'chan', [(j, j ^ 2) for j in range(4)])  6.38 us
    all_to_all x1, starting transfers between devices, local(): lax.all_to_all(convolved, 'seq', split_axis=1, concat_axis=0, tiled=True)  5.94 us
    dot_general x1, matrix products, local(): lax.dot_general(gated_rows, out_weight, (((0,), (0,)), ((), ())), preferr...  4.67 us
    ppermute x1, starting transfers between devices, from_behind(): return lax.ppermute(x, axis, pairs)  4.36 us
    ppermute x1, starting transfers between devices, reduce_scatter_chan(): got = lax.ppermute(send, 'chan', [(j, j ^ 1) for j in range(4)])  3.71 us
  transfers between devices with their start and end apart: 5, of which 4 were waited for; matrix products, arithmetic and copies ran while one was open for 11% of the time, Pallas kernels for 0%

profile of v11, /device:TPU:1, one launch (start us, length us, event | category | flops | bytes accessed | tf_op | source)
XLA Modules:
  0.0 81.5 jit_solution(4712545192222851355)
XLA Ops:
  0.0 0.0 copy-start
  0.0 1.8 %fusion.33 = (bf16[3,1024,2]{2,1,0:T(8,128)(2,1)S(1)}, bf16[3,1024,2]{2,1,0:T(8,128)(2,1)S(1)}) fusion(bf16[3,1024,128]{2,1,0:T(8,128)(2,1)} %param.5), kind=kLoop, calls=%fused_computation.70 | loop fusion | bytes 49152 | tf_op jit(solution)/shard_map/slice | solution.py:63
  1.8 0.3 copy.44
  2.1 4.4 %collective-permute-start = (bf16[3,1024,2]{1,2,0:T(2,128)(2,1)S(1)}, bf16[3,1024,2]{1,2,0:T(2,128)(2,1)S(1)}, u32[]{:S(2)}, u32[]{:S(2)}) collective-permute-start(bf16[3,1024,2]{1,2,0:T(2,128)(2,1)S(1)} %copy.44), channel_id=1, source_target_pairs={{0,4},{4,8},{8,12},{12,16},{16,20},{20,24},{24,28},{28,32},{32,36}... | collective-permute-start | bytes 36872 | tf_op jit(solution)/shard_map/ppermute | solution.py:10
  6.4 0.0 copy-done
  6.4 0.1 slice.94
  6.6 0.0 copy-start.2
  6.6 0.1 slice.93
  6.7 0.6 copy-done.2
  7.4 2.3 %multiply_add_fusion = f32[3,1024,128]{2,1,0:T(8,128)S(1)} fusion(f32[3,1024,126]{2,1,0:T(8,128)S(1)} %slice.94, f32[3,1024,127]{2,1,0:T(8,128)S(1)} %slice.93, f32[3,1024]{1,0:T(4,128)S(1)} %get-tuple-element.20, f32[3,1024]{1,0:T(4,128)S(1)} %get-tuple-element.21, f32[3,1024]{1,0:T(4,128)S(1)} %bitcast.53, bf16[3,1024,128]{2,1,0:T(8,128)(2,1)S(1)} %copy-done), kind=kLoop, calls=%fused_computation.5 | loop fusion | flops 2359296 | bytes 5505024 | tf_op jit(solution)/shard_map/add | solution.py:70
  9.8 1.0 %fusion.10 = (bf16[1024,128]{1,0:T(8,128)(2,1)}, f32[1024,128]{1,0:T(8,128)}) fusion(f32[3,1024,128]{2,1,0:T(8,128)S(1)} %multiply_add_fusion), kind=kLoop, calls=%fused_computation.25 | loop fusion | flops 262144 | bytes 2359296 | tf_op jit(solution)/shard_map/convert_element_type | solution.py:81
  10.7 0.8 constant_dynamic-slice_fusion
  11.5 0.3 copy.45
  11.8 0.0 collective-permute-done
  11.9 0.5 copy.32
  12.4 0.5 copy.33
  12.9 0.2 add.62
  13.1 0.1 fusion.11
  13.2 2.8 %dynamic_update_slice.7 = bf16[1024,128]{1,0:T(8,128)(2,1)} dynamic-update-slice(bf16[1024,128]{1,0:T(8,128)(2,1)} %get-tuple-element.7, bf16[1024,2]{1,0:T(8,128)(2,1)S(1)} %get-tuple-element.5, s32[]{:T(128)} %constant.43.clone.1, s32[]{:T(128)} %constant.43.clone.1) | dynamic-update-slice | bytes 8196 | tf_op jit(solution)/shard_map/dynamic_update_slice | solution.py:80
  16.0 11.8 %all-to-all-start = ((bf16[64,16,128]{2,1,0:T(8,128)(2,1)}), bf16[64,16,128]{2,1,0:T(8,128)(2,1)S(1)}, u32[]{:S(2)}, u32[]{:S(2)}) async-start(bf16[64,16,128]{2,1,0:T(8,128)(2,1)} %bitcast.4), calls=%async_computation | async-start | bytes 524288 | tf_op jit(solution)/shard_map/all_to_all | solution.py:88
  27.8 0.1 copy.36
  27.9 0.1 copy.35
  27.9 0.1 convert_multiply_fusion
  28.0 1.9 %convolution_select_fusion = f32[16,128,128]{2,1,0:T(8,128)S(1)} fusion(pred[128,128]{1,0:T(8,128)(4,1)S(1)} %subtract_compare_fusion, f32[128]{0:T(128)S(1)} %get-tuple-element.25, f32[16,16]{0,1:T(8,128)S(1)} %copy.36, f32[128]{0:T(128)S(1)} %get-tuple-element.24, f32[16,16]{0,1:T(8,128)S(1)} %copy.35), kind=kOutput, calls=%fused_computation.6 | convolution fusion | flops 50692096 | bytes 1068032 | tf_op jit(solution)/shard_map/rcj,rct->cjt/dot_general | solution.py:22
  30.0 9.2 %all-to-all-done = bf16[64,16,128]{2,1,0:T(8,128)(2,1)S(1)} async-done(((bf16[64,16,128]{2,1,0:T(8,128)(2,1)}), bf16[64,16,128]{2,1,0:T(8,128)(2,1)S(1)}, u32[]{:S(2)}, u32[]{:S(2)}) %all-to-all-start) | async-done | bytes 262176 | tf_op jit(solution)/shard_map/all_to_all | solution.py:88
  39.2 0.4 convolution_bitcast_fusion
  39.7 2.6 %fusion.2 = f32[16,16,64]{2,1,0:T(8,128)S(1)} fusion(f32[16,16,64]{2,1,0:T(8,128)S(1)} %copy.37, f32[16,16]{1,0:T(8,128)S(1)} %get-tuple-element.22, f32[64,64]{1,0:T(8,128)S(1)} %convert_multiply_fusion, pred[64,64]{1,0:T(8,128)(4,1)S(1)} %iota_compare_fusion), kind=kLoop, calls=%fused_computation.3 | loop fusion | flops 4177920 | bytes 152576 | tf_op jit(solution)/shard_map/reduce_sum | solution.py:37
  42.3 0.7 fusion.17
  43.1 0.0 copy-start.1
  43.1 0.4 fusion.3
  43.5 0.9 %copy.39 = bf16[16,64,128]{2,0,1:T(8,128)(2,1)} copy(bf16[16,64,128]{2,1,0:T(8,128)(2,1)S(1)} %fusion.3) | data formatting | bytes 524288 | tf_op jit(solution)/shard_map/convert_element_type | solution.py:92
  44.4 5.9 %all-to-all-start.1 = ((bf16[16,64,128]{2,0,1:T(8,128)(2,1)}), bf16[16,64,128]{2,0,1:T(8,128)(2,1)S(1)}, u32[]{:S(2)}, u32[]{:S(2)}) async-start(bf16[16,64,128]{2,0,1:T(8,128)(2,1)} %copy.39), calls=%async_computation.1 | async-start | bytes 524288 | tf_op jit(solution)/shard_map/all_to_all | solution.py:93
  50.3 0.0 copy-done.1
  50.3 2.3 %dynamic_update_slice.6 = f32[1024,128]{1,0:T(8,128)S(1)} dynamic-update-slice(f32[1024,128]{1,0:T(8,128)S(1)} %copy-done.1, f32[1024,2]{1,0:T(8,128)S(1)} %get-tuple-element.6, s32[]{:T(128)} %constant.43.clone.1, s32[]{:T(128)} %constant.43.clone.1) | dynamic-update-slice | bytes 16388 | tf_op jit(solution)/shard_map/dynamic_update_slice | solution.py:85
  52.6 8.5 %all-to-all-done.1 = bf16[16,64,128]{2,0,1:T(8,128)(2,1)S(1)} async-done(((bf16[16,64,128]{2,0,1:T(8,128)(2,1)}), bf16[16,64,128]{2,0,1:T(8,128)(2,1)S(1)}, u32[]{:S(2)}, u32[]{:S(2)}) %all-to-all-start.1) | async-done | bytes 262176 | tf_op jit(solution)/shard_map/all_to_all | solution.py:93
  61.1 0.1 fusion.6
  61.2 4.7 %convolution_convert_fusion = bf16[128,4096]{1,0:T(8,128)(2,1)S(1)} fusion(bf16[1024,128]{1,0:T(8,128)(2,1)S(1)} %fusion.6, bf16[1024,4096]{1,0:T(8,128)(2,1)} %param.9), kind=kOutput, calls=%fused_computation.4 | convolution fusion | flops 1074266112 | bytes 9699328 | tf_op jit(solution)/shard_map/dot_general | solution.py:95
  65.9 0.1 select_bitcast_fusion.3
  66.0 0.1 pad_maximum_fusion
  66.0 3.7 %collective-permute-start.1 = (bf16[2,128,1024]{2,1,0:T(8,128)(2,1)S(1)}, bf16[2,128,1024]{2,1,0:T(8,128)(2,1)S(1)}, u32[]{:S(2)}, u32[]{:S(2)}) collective-permute-start(bf16[2,128,1024]{2,1,0:T(8,128)(2,1)S(1)} %pad_maximum_fusion), channel_id=1, source_target_pairs={{0,1},{1,0},{2,3},{3,2},{4,5},{5,4},{6,7},{7,6},{8,9},{9,8},{10,11... | collective-permute-start | bytes 1572872 | tf_op jit(solution)/shard_map/ppermute | solution.py:51
  69.7 1.5 %collective-permute-done.1 = bf16[2,128,1024]{2,1,0:T(8,128)(2,1)S(1)} collective-permute-done((bf16[2,128,1024]{2,1,0:T(8,128)(2,1)S(1)}, bf16[2,128,1024]{2,1,0:T(8,128)(2,1)S(1)}, u32[]{:S(2)}, u32[]{:S(2)}) %collective-permute-start.1) | collective-permute-done | bytes 524320 | tf_op jit(solution)/shard_map/ppermute | solution.py:51
  71.3 0.2 convert_add_fusion
  71.4 0.1 fusion.8
  71.5 2.7 %collective-permute-start.2 = (bf16[128,1024]{1,0:T(8,128)(2,1)S(1)}, bf16[128,1024]{1,0:T(8,128)(2,1)S(1)}, u32[]{:S(2)}, u32[]{:S(2)}) collective-permute-start(bf16[128,1024]{1,0:T(8,128)(2,1)S(1)} %fusion.8), channel_id=1, source_target_pairs={{0,2},{1,3},{2,0},{3,1},{4,6},{5,7},{6,4},{7,5},{8,10},{9,11},{10,... | collective-permute-start | bytes 786440 | tf_op jit(solution)/shard_map/ppermute | solution.py:56
  74.2 6.4 %collective-permute-done.2 = bf16[128,1024]{1,0:T(8,128)(2,1)S(1)} collective-permute-done((bf16[128,1024]{1,0:T(8,128)(2,1)S(1)}, bf16[128,1024]{1,0:T(8,128)(2,1)S(1)}, u32[]{:S(2)}, u32[]{:S(2)}) %collective-permute-start.2) | collective-permute-done | bytes 262176 | tf_op jit(solution)/shard_map/ppermute | solution.py:56
  80.6 0.1 fusion.9
  80.7 0.8 %copy.40 = bf16[1024,128]{1,0:T(8,128)(2,1)} copy(bf16[1024,128]{0,1:T(8,128)(2,1)S(1)} %fusion.9) | data formatting | bytes 524288 | tf_op jit(solution)/shard_map/transpose | solution.py:57
  (12 shorter events, 0.2 us)
Async XLA Ops:
  0.0 6.4 %copy-start = (bf16[3,1024,128]{2,1,0:T(8,128)(2,1)S(1)}, bf16[3,1024,128]{2,1,0:T(8,128)(2,1)}, u32[]{:S(2)}) copy-start(bf16[3,1024,128]{2,1,0:T(8,128)(2,1)} %param.5) | copy-start | bytes 2359300
  2.1 9.8 %collective-permute-start = (bf16[3,1024,2]{1,2,0:T(2,128)(2,1)S(1)}, bf16[3,1024,2]{1,2,0:T(2,128)(2,1)S(1)}, u32[]{:S(2)}, u32[]{:S(2)}) collective-permute-start(bf16[3,1024,2]{1,2,0:T(2,128)(2,1)S(1)} %copy.44), channel_id=1, source_target_pairs={{0,4},{4,8},{8,12},{12,16},{16,20},{20,24},{24,28},{28,32},{32,36}... | collective-permute-start | bytes 36872 | tf_op jit(solution)/shard_map/ppermute | solution.py:10
  6.6 0.8 copy-start.2
  16.0 23.2 %all-to-all-start = ((bf16[64,16,128]{2,1,0:T(8,128)(2,1)}), bf16[64,16,128]{2,1,0:T(8,128)(2,1)S(1)}, u32[]{:S(2)}, u32[]{:S(2)}) async-start(bf16[64,16,128]{2,1,0:T(8,128)(2,1)} %bitcast.4), calls=%async_computation | async-start | bytes 524288 | tf_op jit(solution)/shard_map/all_to_all | solution.py:88
  43.1 7.3 %copy-start.1 = (f32[1024,128]{1,0:T(8,128)S(1)}, f32[1024,128]{1,0:T(8,128)}, u32[]{:S(2)}) copy-start(f32[1024,128]{1,0:T(8,128)} %get-tuple-element.8) | copy-start | bytes 1572868
  44.4 16.8 %all-to-all-start.1 = ((bf16[16,64,128]{2,0,1:T(8,128)(2,1)}), bf16[16,64,128]{2,0,1:T(8,128)(2,1)S(1)}, u32[]{:S(2)}, u32[]{:S(2)}) async-start(bf16[16,64,128]{2,0,1:T(8,128)(2,1)} %copy.39), calls=%async_computation.1 | async-start | bytes 524288 | tf_op jit(solution)/shard_map/all_to_all | solution.py:93
  66.0 5.3 %collective-permute-start.1 = (bf16[2,128,1024]{2,1,0:T(8,128)(2,1)S(1)}, bf16[2,128,1024]{2,1,0:T(8,128)(2,1)S(1)}, u32[]{:S(2)}, u32[]{:S(2)}) collective-permute-start(bf16[2,128,1024]{2,1,0:T(8,128)(2,1)S(1)} %pad_maximum_fusion), channel_id=1, source_target_pairs={{0,1},{1,0},{2,3},{3,2},{4,5},{5,4},{6,7},{7,6},{8,9},{9,8},{10,11... | collective-permute-start | bytes 1572872 | tf_op jit(solution)/shard_map/ppermute | solution.py:51
  71.5 9.1 %collective-permute-start.2 = (bf16[128,1024]{1,0:T(8,128)(2,1)S(1)}, bf16[128,1024]{1,0:T(8,128)(2,1)S(1)}, u32[]{:S(2)}, u32[]{:S(2)}) collective-permute-start(bf16[128,1024]{1,0:T(8,128)(2,1)S(1)} %fusion.8), channel_id=1, source_target_pairs={{0,2},{1,3},{2,0},{3,1},{4,6},{5,7},{6,4},{7,5},{8,10},{9,11},{10,... | collective-permute-start | bytes 786440 | tf_op jit(solution)/shard_map/ppermute | solution.py:56

commit v12 on v7

--- a/solution.py
+++ b/solution.py
@@ -28,13 +28,13 @@
     leaving = jnp.einsum("ncj,rcj->rcn", signal, to_end, precision=precise)
     blocks = signal.shape[0]
     n_idx = jnp.arange(blocks, dtype=jnp.int32)
-    gap = (n_idx[None, :] - 1 - n_idx[:, None]).astype(jnp.float32)
+    gap = (n_idx[:, None] - 1 - n_idx[None, :]).astype(jnp.float32)
     exponent = jnp.where(
-        (n_idx[None, :] > n_idx[:, None])[None, None],
+        (n_idx[:, None] > n_idx[None, :])[None, None],
         -float(block) * gap[None, None] / life[..., None],
         -jnp.inf,
     )
-    entering = jnp.sum(jnp.exp(exponent) * leaving[:, :, :, None], axis=2)
+    entering = jnp.sum(jnp.exp(exponent) * leaving[:, :, None, :], axis=-1)
     from_start = resid * jnp.exp(-(steps + 1.0)[None, None, :] / life)
     carried = jnp.einsum("rcn,rct->nct", entering, from_start, precision=precise)
     return inside + carried
@@ -57,31 +57,75 @@
     return (keep2 + got2.astype(jnp.float32)).astype(jnp.bfloat16).T
 
 
+def pack_rows(values, width):
+    groups, count = values.shape
+    rows = -(-count // width)
+    padded = jnp.pad(values, ((0, 0), (0, rows * width - count)))
+    return padded.reshape(groups, rows, width)
+
+
 def local(qkv, taps, lifetimes, residues, out_weight):
     chan_local = qkv.shape[1]
     tok_count = qkv.shape[2]
-    edge_block = qkv[:, :, tok_count - 2 :]
-    earlier = from_behind(edge_block, "seq", 1)
-    extended = jnp.concatenate([earlier, qkv], axis=2).astype(jnp.float32)
-    filtered = (
-        taps[:, 0, :, None] * extended[:, :, 2:]
-        + taps[:, 1, :, None] * extended[:, :, 1:-1]
-        + taps[:, 2, :, None] * extended[:, :, :-2]
-    )
-    product = (filtered[1] * filtered[2]).astype(jnp.bfloat16)
     groups = lax.axis_size("seq")
     per_group = chan_local // groups
-    pencils = lax.all_to_all(
-        product.reshape(groups, per_group, tok_count), "seq", split_axis=0, concat_axis=0, tiled=True
+
+    signal = qkv[1:].astype(jnp.float32)
+    pad1 = jnp.zeros(signal.shape[:2] + (1,), jnp.float32)
+    pad2 = jnp.zeros(signal.shape[:2] + (2,), jnp.float32)
+    no_halo = (
+        taps[1:, 0, :, None] * signal
+        + taps[1:, 1, :, None] * jnp.concatenate([pad1, signal[:, :, :-1]], axis=2)
+        + taps[1:, 2, :, None] * jnp.concatenate([pad2, signal[:, :, :-2]], axis=2)
     )
+    product = (no_halo[0] * no_halo[1]).astype(jnp.bfloat16)
+    ends = jnp.concatenate([qkv[1:, :, :2], qkv[1:, :, tok_count - 2 :]], axis=2)
+    edges = jnp.concatenate(
+        [jnp.swapaxes(ends, 0, 1).reshape(chan_local, 8), qkv[0, :, tok_count - 2 :]], axis=1
+    )
+    edge_count = edges.shape[1]
+    payload = jnp.concatenate(
+        [
+            product.reshape(groups, per_group, tok_count),
+            pack_rows(edges.reshape(groups, per_group * edge_count), tok_count),
+        ],
+        axis=1,
+    )
+    arrived = lax.all_to_all(payload, "seq", split_axis=0, concat_axis=0, tiled=True)
     first_chan = lax.axis_index("seq") * per_group
     life_slice = lax.dynamic_slice_in_dim(lifetimes, first_chan, per_group, 1)
     resid_slice = lax.dynamic_slice_in_dim(residues, first_chan, per_group, 1)
+    tap_slice = lax.dynamic_slice_in_dim(taps, first_chan, per_group, 2)
+
+    got_edges = (
+        arrived[:, per_group:, :]
+        .reshape(groups, -1)[:, : per_group * edge_count]
+        .reshape(groups, per_group, edge_count)
+        .astype(jnp.float32)
+    )
+    before = jnp.concatenate([jnp.zeros_like(got_edges[:1]), got_edges[:-1]], axis=0)
+
+    def head(stream, at):
+        t0, t1, t2 = (tap_slice[stream, i][None, :] for i in range(3))
+        x0, x1 = got_edges[..., at], got_edges[..., at + 1]
+        m2, m1 = before[..., at + 2], before[..., at + 3]
+        return jnp.stack([t0 * x0 + t1 * m1 + t2 * m2, t0 * x1 + t1 * x0 + t2 * m1], axis=-1)
+
+    fixed = (head(1, 0) * head(2, 4)).astype(jnp.bfloat16)
+    pencils = jnp.concatenate([fixed, arrived[:, :per_group, 2:]], axis=2)
     convolved = modal_conv(pencils, life_slice, resid_slice).astype(jnp.bfloat16)
-    returned = lax.all_to_all(convolved, "seq", split_axis=0, concat_axis=0, tiled=True).reshape(
-        chan_local, tok_count
+    q_before = before[..., 8:10].astype(jnp.bfloat16).reshape(groups, per_group * 2)
+    back = jnp.concatenate([convolved, pack_rows(q_before, tok_count)], axis=1)
+    returned = lax.all_to_all(back, "seq", split_axis=0, concat_axis=0, tiled=True)
+    conv_rows = returned[:, :per_group, :].reshape(chan_local, tok_count)
+    q_halo = returned[:, per_group, : per_group * 2].reshape(chan_local, 2)
+    extended = jnp.concatenate([q_halo, qkv[0]], axis=1).astype(jnp.float32)
+    filtered_q = (
+        taps[0, 0, :, None] * extended[:, 2:]
+        + taps[0, 1, :, None] * extended[:, 1:-1]
+        + taps[0, 2, :, None] * extended[:, :-2]
     )
-    gated_rows = (filtered[0] * returned.astype(jnp.float32)).astype(jnp.bfloat16)
+    gated_rows = (filtered_q * conv_rows.astype(jnp.float32)).astype(jnp.bfloat16)
     partial = lax.dot_general(
         gated_rows, out_weight, (((0,), (0,)), ((), ())), preferred_element_type=jnp.float32
     ).astype(jnp.bfloat16)

time: 79.3 us -> 84.4 us (1.064)
  local copies, waits for them, and re-layouts: 4.96 us -> 11.4 us
  starting transfers between devices: 30.4 us -> 25.5 us
  waiting for transfers between devices: 27.8 us -> 29.9 us
    ppermute x1 -> x0, starting transfers between devices: 4.36 us -> none  [from_behind(): return lax.ppermute(x, axis, pairs)]
    slice x2 -> x13, local copies, waits for them, and re-layouts: 1.52 us -> 4.73 us  [the longest x1 1.45 us: local(): ends = jnp.concatenate([qkv[1:, :, :2], qkv[1:, :, tok_count - 2:]], axis=2)]
    all_to_all x2, waiting for transfers between devices: 19.9 us -> 21.9 us  [the longest x1 11.6 us: local(): lax.all_to_all(back, 'seq', split_axis=0, concat_axis=0, tiled=True)]
    concatenate x0 -> x2, local copies, waits for them, and re-layouts: none -> 1.14 us  [the longest x1 0.94 us: local(): back = jnp.concatenate([convolved, pack_rows(q_before, tok_count)], axis=1)]
    ppermute x1, starting transfers between devices: 4.62 us -> 3.55 us  [reduce_scatter_chan(): got = lax.ppermute(send, 'chan', [(j, j ^ 1) for j in range(4)])]
    squeeze x0 -> x1, local copies, waits for them, and re-layouts: none -> 0.97 us  [local(): extended = jnp.concatenate([q_halo, qkv[0]], axis=1).astype(jnp.float32)]
    mul x0 -> x1, local copies, waits for them, and re-layouts: none -> 0.91 us  [head(): t0 * x0 + t1 * m1 + t2 * m2]
    add x1 -> x2, other arithmetic: 2.35 us -> 2.58 us  [the longest x1 2.48 us: local(): taps[1:, 0, :, None] * signal]
  transfers between devices with their start and end apart: 5 -> 4, of which waited for: 4 -> 4; matrix products, arithmetic and copies ran while one was open for 4% -> 7% of each run, Pallas kernels for 0% -> 0%
where the time goes in v12:
time: 84.4 us; the launch traced here: 83.8 us
  waiting for transfers between devices  29.9 us (35%)
  starting transfers between devices  25.5 us (30%)
  local copies, waits for them, and re-layouts  11.4 us (14%)
  matrix products  8.51 us (10%)
  other arithmetic  8.08 us (10%)
    all_to_all x1, starting transfers between devices, local(): lax.all_to_all(payload, 'seq', split_axis=0, concat_axis=0, tiled=True)  13.5 us
    all_to_all x1, waiting for transfers between devices, local(): lax.all_to_all(back, 'seq', split_axis=0, concat_axis=0, tiled=True)  11.6 us
    all_to_all x1, waiting for transfers between devices, local(): lax.all_to_all(payload, 'seq', split_axis=0, concat_axis=0, tiled=True)  10.4 us
    ppermute x1, waiting for transfers between devices, reduce_scatter_chan(): got2 = lax.ppermute(send2, 'chan', [(j, j ^ 2) for j in range(4)])  6.38 us
    all_to_all x1, starting transfers between devices, local(): lax.all_to_all(back, 'seq', split_axis=0, concat_axis=0, tiled=True)  5.76 us
    dot_general x1, matrix products, local(): lax.dot_general(gated_rows, out_weight, (((0,), (0,)), ((), ())), preferr...  4.92 us
    ppermute x1, starting transfers between devices, reduce_scatter_chan(): got = lax.ppermute(send, 'chan', [(j, j ^ 1) for j in range(4)])  3.55 us
    ppermute x1, starting transfers between devices, reduce_scatter_chan(): got2 = lax.ppermute(send2, 'chan', [(j, j ^ 2) for j in range(4)])  2.71 us
  transfers between devices with their start and end apart: 4, of which 4 were waited for; matrix products, arithmetic and copies ran while one was open for 7% of the time, Pallas kernels for 0%

profile of v12, /device:TPU:1, one launch (start us, length us, event | category | flops | bytes accessed | tf_op | source)
XLA Modules:
  0.0 83.8 jit_solution(5725367992580984316)
XLA Ops:
  0.0 1.1 %slice_convert_fusion = f32[2,1024,128]{2,1,0:T(8,128)S(1)} fusion(bf16[3,1024,128]{2,1,0:T(8,128)(2,1)} %param.5), kind=kLoop, calls=%fused_computation.26 | loop fusion | flops 262144 | bytes 1572864 | tf_op jit(solution)/shard_map/convert_element_type | solution.py:73
  1.1 1.4 %fusion.42 = (bf16[2,1024,2]{2,1,0:T(8,128)(2,1)S(1)}, bf16[2,1024,2]{2,1,0:T(8,128)(2,1)S(1)}) fusion(bf16[3,1024,128]{2,1,0:T(8,128)(2,1)} %param.5), kind=kLoop, calls=%fused_computation.99 | loop fusion | bytes 32768 | tf_op jit(solution)/shard_map/slice | solution.py:82
  2.6 1.1 %slice.153 = bf16[1,1024,2]{2,1,0:T(8,128)(2,1)S(1)} slice(bf16[3,1024,128]{2,1,0:T(8,128)(2,1)} %param.5), slice={[0:1], [0:1024], [126:128]} | slice | bytes 8192 | tf_op jit(solution)/shard_map/slice | solution.py:84
  3.7 0.9 %fusion.45 = (f32[2,1,1024]{2,1,0:T(1,128)S(1)}, f32[2,1,1024]{2,1,0:T(1,128)S(1)}, f32[2,1,1024]{2,1,0:T(1,128)S(1)}) fusion(f32[3,3,1024]{2,1,0:T(4,128)} %param.6), kind=kLoop, calls=%fused_computation.102 | loop fusion | bytes 49152 | tf_op jit(solution)/shard_map/slice | solution.py:77
  4.6 2.5 %multiply_add_fusion = f32[2,1024,128]{2,1,0:T(8,128)S(1)} fusion(f32[2,1024,126]{2,1,0:T(8,128)S(1)} %bitcast.74, f32[2,1024,127]{2,1,0:T(8,128)S(1)} %bitcast.75, f32[2,1024]{1,0:T(2,128)S(1)} %get-tuple-element.33, f32[2,1024]{1,0:T(2,128)S(1)} %get-tuple-element.34, f32[2,1024]{1,0:T(2,128)S(1)} %bitcast.81, bf16[3,1024,128]{2,1,0:T(8,128)(2,1)} %param.5), kind=kLoop, calls=%fused_computation.11 | loop fusion | flops 1572864 | bytes 3670016 | tf_op jit(solution)/shard_map/add | solution.py:77
  7.2 0.2 copy.91
  7.4 0.2 copy.92
  7.7 0.1 copy.93
  7.8 0.2 copy.72
  8.0 0.3 reshape.207
  8.3 0.8 pad_maximum_fusion.1
  9.1 13.5 %all-to-all-start = ((bf16[64,18,128]{2,1,0:T(8,128)(2,1)}), bf16[64,18,128]{2,1,0:T(8,128)(2,1)S(1)}, u32[]{:S(2)}, u32[]{:S(2)}) async-start(bf16[64,18,128]{2,1,0:T(8,128)(2,1)} %pad_maximum_fusion.1), calls=%async_computation | async-start | bytes 786432 | tf_op jit(solution)/shard_map/all_to_all | solution.py:94
  22.7 0.1 constant_dynamic-slice_fusion.2
  22.8 0.1 copy.68
  22.9 0.8 constant_dynamic-slice_fusion.3
  23.6 0.1 copy.67
  23.7 0.9 %fusion.38 = (f32[16]{0:T(128)S(1)}, f32[16]{0:T(128)S(1)}, f32[16]{0:T(128)S(1)}, f32[16]{0:T(128)S(1)}, f32[16]{0:T(128)S(1)}, /*index=5*/f32[16]{0:T(128)S(1)}) fusion(f32[3,3,1024]{2,1,0:T(4,128)} %param.6, s32[]{:T(128)S(6)} %add.122, s32[]{:T(128)S(6)} %select_n.64, s32[]{:T(128)S(6)} %add.118), kind=kLoop, calls=%fused_computation.87 | loop fusion | bytes 780 | tf_op jit(solution)/shard_map/mul | solution.py:112
  24.6 0.1 convert_multiply_fusion
  24.7 1.9 %convolution_select_fusion = f32[16,128,128]{2,1,0:T(8,128)S(1)} fusion(pred[128,128]{1,0:T(8,128)(4,1)S(1)} %subtract_compare_fusion, f32[128]{0:T(128)S(1)} %get-tuple-element.36, f32[16,16]{0,1:T(8,128)S(1)} %copy.68, f32[128]{0:T(128)S(1)} %get-tuple-element.35, f32[16,16]{0,1:T(8,128)S(1)} %copy.67), kind=kOutput, calls=%fused_computation.5 | convolution fusion | flops 50692096 | bytes 1068032 | tf_op jit(solution)/shard_map/rcj,rct->cjt/dot_general | solution.py:21
  26.6 10.4 %all-to-all-done = bf16[64,18,128]{2,1,0:T(8,128)(2,1)S(1)} async-done(((bf16[64,18,128]{2,1,0:T(8,128)(2,1)}), bf16[64,18,128]{2,1,0:T(8,128)(2,1)S(1)}, u32[]{:S(2)}, u32[]{:S(2)}) %all-to-all-start) | async-done | bytes 294944 | tf_op jit(solution)/shard_map/all_to_all | solution.py:94
  37.1 0.1 copy.73
  37.2 0.1 copy.75
  37.4 0.1 pad_convert_fusion
  37.5 0.1 fusion.36
  37.6 0.2 copy.81
  37.8 0.1 slice.198
  38.0 0.5 convolution_bitcast_fusion
  38.6 0.1 copy.85
  38.7 2.6 %fusion.2 = f32[16,16,64]{2,1,0:T(8,128)S(1)} fusion(f32[16,16,64]{2,1,0:T(8,128)S(1)} %copy.82, f32[16,16]{1,0:T(8,128)S(1)} %constant_dynamic-slice_fusion.2, f32[64,64]{1,0:T(8,128)S(1)} %convert_multiply_fusion, pred[64,64]{1,0:T(8,128)(4,1)S(1)} %iota_compare_fusion), kind=kLoop, calls=%fused_computation.3 | loop fusion | flops 4177920 | bytes 152576 | tf_op jit(solution)/shard_map/reduce_sum | solution.py:37
  41.3 0.7 fusion.18
  42.0 0.5 fusion.4
  42.6 0.9 %copy.86 = bf16[64,17,128]{2,1,0:T(8,128)(2,1)} copy(bf16[64,17,128]{2,0,1:T(8,128)(2,1)S(1)} %pad_maximum_fusion.2) | data formatting | bytes 557056 | tf_op jit(solution)/shard_map/concatenate | solution.py:118
  43.5 5.8 %all-to-all-start.1 = ((bf16[64,17,128]{2,1,0:T(8,128)(2,1)}), bf16[64,17,128]{2,1,0:T(8,128)(2,1)S(1)}, u32[]{:S(2)}, u32[]{:S(2)}) async-start(bf16[64,17,128]{2,1,0:T(8,128)(2,1)} %copy.86), calls=%async_computation.1 | async-start | bytes 786432 | tf_op jit(solution)/shard_map/all_to_all | solution.py:119
  49.3 0.8 %fusion.44 = (f32[1,1,1024]{2,1,0:T(1,128)S(1)}, f32[1,1,1024]{2,1,0:T(1,128)S(1)}, f32[1,1,1024]{2,1,0:T(1,128)S(1)}) fusion(f32[3,3,1024]{2,1,0:T(4,128)} %param.6), kind=kLoop, calls=%fused_computation.101 | loop fusion | bytes 24576 | tf_op jit(solution)/shard_map/slice | solution.py:124
  50.1 1.0 %slice_bitcast_fusion = bf16[1024,128]{1,0:T(8,128)(2,1)S(1)} fusion(bf16[3,1024,128]{2,1,0:T(8,128)(2,1)} %param.5), kind=kLoop, calls=%fused_computation.38 | loop fusion | bytes 524288 | tf_op jit(solution)/shard_map/squeeze | solution.py:122
  51.1 11.6 %all-to-all-done.1 = bf16[64,17,128]{2,1,0:T(8,128)(2,1)S(1)} async-done(((bf16[64,17,128]{2,1,0:T(8,128)(2,1)}), bf16[64,17,128]{2,1,0:T(8,128)(2,1)S(1)}, u32[]{:S(2)}, u32[]{:S(2)}) %all-to-all-start.1) | async-done | bytes 278560 | tf_op jit(solution)/shard_map/all_to_all | solution.py:119
  62.7 0.1 slice_reduce_fusion
  62.8 0.3 reshape_squeeze.3
  63.1 0.2 maximum_convert_fusion
  63.4 4.9 %convolution_convert_fusion = bf16[128,4096]{1,0:T(8,128)(2,1)S(1)} fusion(bf16[1024,4096]{1,0:T(8,128)(2,1)} %param.9, f32[1024,130]{1,0:T(8,128)S(1)} %maximum_convert_fusion, bf16[1024,128]{1,0:T(8,128)(2,1)S(1)} %bitcast.77, f32[1024]{0:T(1024)S(1)} %bitcast.88, f32[1024]{0:T(1024)S(1)} %bitcast.89, f32[1024]{0:T(1024)S(1)} %bitcast.87), kind=kOutput, calls=%fused_computation.4 | convolution fusion | flops 1075314688 | bytes 11284480 | tf_op jit(solution)/shard_map/dot_general | solution.py:129
  68.3 0.1 select_bitcast_fusion.3
  68.4 3.5 %collective-permute-start = (bf16[2,128,1024]{2,1,0:T(8,128)(2,1)S(1)}, bf16[2,128,1024]{2,1,0:T(8,128)(2,1)S(1)}, u32[]{:S(2)}, u32[]{:S(2)}) collective-permute-start(bf16[2,128,1024]{2,1,0:T(8,128)(2,1)S(1)} %pad_maximum_fusion), channel_id=1, source_target_pairs={{0,1},{1,0},{2,3},{3,2},{4,5},{5,4},{6,7},{7,6},{8,9},{9,8},{10,11... | collective-permute-start | bytes 1572872 | tf_op jit(solution)/shard_map/ppermute | solution.py:51
  72.0 1.5 %collective-permute-done = bf16[2,128,1024]{2,1,0:T(8,128)(2,1)S(1)} collective-permute-done((bf16[2,128,1024]{2,1,0:T(8,128)(2,1)S(1)}, bf16[2,128,1024]{2,1,0:T(8,128)(2,1)S(1)}, u32[]{:S(2)}, u32[]{:S(2)}) %collective-permute-start) | collective-permute-done | bytes 524320 | tf_op jit(solution)/shard_map/ppermute | solution.py:51
  73.5 0.2 convert_add_fusion
  73.8 2.7 %collective-permute-start.1 = (bf16[128,1024]{1,0:T(8,128)(2,1)S(1)}, bf16[128,1024]{1,0:T(8,128)(2,1)S(1)}, u32[]{:S(2)}, u32[]{:S(2)}) collective-permute-start(bf16[128,1024]{1,0:T(8,128)(2,1)S(1)} %fusion.11), channel_id=1, source_target_pairs={{0,2},{1,3},{2,0},{3,1},{4,6},{5,7},{6,4},{7,5},{8,10},{9,11},{10,... | collective-permute-start | bytes 786440 | tf_op jit(solution)/shard_map/ppermute | solution.py:56
  76.5 6.4 %collective-permute-done.1 = bf16[128,1024]{1,0:T(8,128)(2,1)S(1)} collective-permute-done((bf16[128,1024]{1,0:T(8,128)(2,1)S(1)}, bf16[128,1024]{1,0:T(8,128)(2,1)S(1)}, u32[]{:S(2)}, u32[]{:S(2)}) %collective-permute-start.1) | collective-permute-done | bytes 262176 | tf_op jit(solution)/shard_map/ppermute | solution.py:56
  82.8 0.1 fusion.12
  82.9 0.8 %copy.87 = bf16[1024,128]{1,0:T(8,128)(2,1)} copy(bf16[1024,128]{0,1:T(8,128)(2,1)S(1)} %fusion.12) | data formatting | bytes 524288 | tf_op jit(solution)/shard_map/transpose | solution.py:57
  (32 shorter events, 0.6 us)
Async XLA Ops:
  0.0 22.7 %copy-start = (f32[16,1024]{1,0:T(8,128)S(1)}, f32[16,1024]{1,0:T(8,128)}, u32[]{:S(2)}) copy-start(f32[16,1024]{1,0:T(8,128)} %param.7) | copy-start | bytes 196612
  9.1 27.9 %all-to-all-start = ((bf16[64,18,128]{2,1,0:T(8,128)(2,1)}), bf16[64,18,128]{2,1,0:T(8,128)(2,1)S(1)}, u32[]{:S(2)}, u32[]{:S(2)}) async-start(bf16[64,18,128]{2,1,0:T(8,128)(2,1)} %pad_maximum_fusion.1), calls=%async_computation | async-start | bytes 786432 | tf_op jit(solution)/shard_map/all_to_all | solution.py:94
  43.5 19.2 %all-to-all-start.1 = ((bf16[64,17,128]{2,1,0:T(8,128)(2,1)}), bf16[64,17,128]{2,1,0:T(8,128)(2,1)S(1)}, u32[]{:S(2)}, u32[]{:S(2)}) async-start(bf16[64,17,128]{2,1,0:T(8,128)(2,1)} %copy.86), calls=%async_computation.1 | async-start | bytes 786432 | tf_op jit(solution)/shard_map/all_to_all | solution.py:119
  68.4 5.1 %collective-permute-start = (bf16[2,128,1024]{2,1,0:T(8,128)(2,1)S(1)}, bf16[2,128,1024]{2,1,0:T(8,128)(2,1)S(1)}, u32[]{:S(2)}, u32[]{:S(2)}) collective-permute-start(bf16[2,128,1024]{2,1,0:T(8,128)(2,1)S(1)} %pad_maximum_fusion), channel_id=1, source_target_pairs={{0,1},{1,0},{2,3},{3,2},{4,5},{5,4},{6,7},{7,6},{8,9},{9,8},{10,11... | collective-permute-start | bytes 1572872 | tf_op jit(solution)/shard_map/ppermute | solution.py:51
  73.8 9.1 %collective-permute-start.1 = (bf16[128,1024]{1,0:T(8,128)(2,1)S(1)}, bf16[128,1024]{1,0:T(8,128)(2,1)S(1)}, u32[]{:S(2)}, u32[]{:S(2)}) collective-permute-start(bf16[128,1024]{1,0:T(8,128)(2,1)S(1)} %fusion.11), channel_id=1, source_target_pairs={{0,2},{1,3},{2,0},{3,1},{4,6},{5,7},{6,4},{7,5},{8,10},{9,11},{10,... | collective-permute-start | bytes 786440 | tf_op jit(solution)/shard_map/ppermute | solution.py:56

commit v13 on v6

--- a/solution.py
+++ b/solution.py
@@ -1,6 +1,7 @@
 import jax
 import jax.numpy as jnp
 from jax import lax
+from jax.experimental import pallas as pl
 from jax.sharding import PartitionSpec as P
 
 
@@ -57,6 +58,28 @@
     return (keep2 + got2.astype(jnp.float32)).astype(jnp.bfloat16).T
 
 
+def project_kernel(gated_ref, weight_ref, out_ref):
+    out_ref[...] = lax.dot_general(
+        gated_ref[...], weight_ref[...], (((0,), (0,)), ((), ())),
+        preferred_element_type=jnp.float32,
+    ).astype(out_ref.dtype)
+
+
+def project(gated_rows, out_weight, cols=512):
+    chans, toks = gated_rows.shape
+    outs = out_weight.shape[1]
+    return pl.pallas_call(
+        project_kernel,
+        grid=(outs // cols,),
+        in_specs=[
+            pl.BlockSpec((chans, toks), lambda j: (0, 0)),
+            pl.BlockSpec((chans, cols), lambda j: (0, j)),
+        ],
+        out_specs=pl.BlockSpec((toks, cols), lambda j: (0, j)),
+        out_shape=jax.ShapeDtypeStruct((toks, outs), jnp.bfloat16),
+    )(gated_rows, out_weight)
+
+
 def local(qkv, taps, lifetimes, residues, out_weight):
     chan_local = qkv.shape[1]
     tok_count = qkv.shape[2]
@@ -78,9 +101,7 @@
     convolved = modal_conv(pencils, life_slice, resid_slice).astype(jnp.bfloat16)
     returned = lax.all_to_all(convolved, "seq", split_axis=1, concat_axis=0, tiled=True)
     gated_rows = (filtered[0] * returned.astype(jnp.float32)).astype(jnp.bfloat16)
-    partial = lax.dot_general(
-        gated_rows, out_weight, (((0,), (0,)), ((), ())), preferred_element_type=jnp.float32
-    ).astype(jnp.bfloat16)
+    partial = project(gated_rows, out_weight)
     return reduce_scatter_chan(partial)
 
 

time: 78.8 us -> 84.1 us (1.067)
  Pallas kernels: 0 us -> 8 us
  matrix products: 8.18 us -> 3.51 us
  other arithmetic: 6.96 us -> 8.85 us
  local copies, waits for them, and re-layouts: 5.87 us -> 4.96 us
  starting transfers between devices: 29.4 us -> 30.3 us
    pallas_call x0 -> x1, Pallas kernels: none -> 8 us  [project(): pl.pallas_call(project_kernel, grid=(outs // cols,), in_specs=[pl.BlockSp...]
    dot_general x1 -> x0, matrix products: 4.67 us -> none  [local(): lax.dot_general(gated_rows, out_weight, (((0,), (0,)), ((), ())), preferr...]
    another operation x1, other arithmetic: 0.07 us -> 1.26 us  [reduce_scatter_chan(): jnp.stack([jnp.where(mine, quarter[2 * h], quarter[2 * h + 1]) for h in r...]
    slice x1, local copies, waits for them, and re-layouts: 0.95 us -> 0.03 us  [local(): taps[:, 0, :, None] * extended[:, :, 2:]]
    all_to_all x1, starting transfers between devices: 12.9 us -> 13.8 us  [local(): lax.all_to_all(product, 'seq', split_axis=0, concat_axis=1, tiled=True)]
  transfers between devices with their start and end apart: 5 -> 5, of which waited for: 4 -> 4; matrix products, arithmetic and copies ran while one was open for 5% -> 4% of each run, Pallas kernels for 0% -> 0%
where the time goes in v13:
time: 84.1 us; the launch traced here: 83.6 us
  starting transfers between devices  30.3 us (36%)
  waiting for transfers between devices  27.7 us (33%)
  other arithmetic  8.85 us (11%)
  Pallas kernels  8 us (10%)
  local copies, waits for them, and re-layouts  4.96 us (6%)
  matrix products  3.51 us (4%)
    all_to_all x1, starting transfers between devices, local(): lax.all_to_all(product, 'seq', split_axis=0, concat_axis=1, tiled=True)  13.8 us
    all_to_all x1, waiting for transfers between devices, local(): lax.all_to_all(convolved, 'seq', split_axis=1, concat_axis=0, tiled=True)  11 us
    all_to_all x1, waiting for transfers between devices, local(): lax.all_to_all(product, 'seq', split_axis=0, concat_axis=1, tiled=True)  8.82 us
    pallas_call x1, Pallas kernels, project(): pl.pallas_call(project_kernel, grid=(outs // cols,), in_specs=[pl.BlockSp...  8 us
    ppermute x1, waiting for transfers between devices, reduce_scatter_chan(): got2 = lax.ppermute(send2, 'chan', [(j, j ^ 2) for j in range(4)])  6.38 us
    all_to_all x1, starting transfers between devices, local(): lax.all_to_all(convolved, 'seq', split_axis=1, concat_axis=0, tiled=True)  4.85 us
    ppermute x1, starting transfers between devices, reduce_scatter_chan(): got = lax.ppermute(send, 'chan', [(j, j ^ 1) for j in range(4)])  4.63 us
    ppermute x1, starting transfers between devices, from_behind(): return lax.ppermute(x, axis, pairs)  4.36 us
  transfers between devices with their start and end apart: 5, of which 4 were waited for; matrix products, arithmetic and copies ran while one was open for 4% of the time, Pallas kernels for 0%

profile of v13, /device:TPU:1, one launch (start us, length us, event | category | flops | bytes accessed | tf_op | source)
XLA Modules:
  0.0 83.6 jit_solution(16895887299887279560)
XLA Ops:
  0.0 0.0 copy-start
  0.0 0.0 copy-start.1
  0.0 1.5 %slice.51 = bf16[3,1024,2]{2,1,0:T(8,128)(2,1)S(1)} slice(bf16[3,1024,128]{2,1,0:T(8,128)(2,1)} %param.5), slice={[0:3], [0:1024], [126:128]} | slice | bytes 24576 | tf_op jit(solution)/shard_map/slice | solution.py:86
  1.5 0.3 copy.36
  1.8 4.4 %collective-permute-start = (bf16[3,1024,2]{1,2,0:T(2,128)(2,1)S(1)}, bf16[3,1024,2]{1,2,0:T(2,128)(2,1)S(1)}, u32[]{:S(2)}, u32[]{:S(2)}) collective-permute-start(bf16[3,1024,2]{1,2,0:T(2,128)(2,1)S(1)} %copy.36), channel_id=1, source_target_pairs={{0,4},{4,8},{8,12},{12,16},{16,20},{20,24},{24,28},{28,32},{32,36}... | collective-permute-start | bytes 36872 | tf_op jit(solution)/shard_map/ppermute | solution.py:11
  6.2 0.0 copy-done.1
  6.3 0.8 constant_dynamic-slice_fusion
  7.1 0.0 collective-permute-done
  7.1 0.4 copy.25
  7.5 0.0 copy-done
  7.5 0.6 maximum_convert_fusion
  8.2 2.4 %fusion.3 = f32[3,1024,128]{2,1,0:T(8,128)S(1)} fusion(f32[3,1024,130]{2,1,0:T(8,128)S(1)} %maximum_convert_fusion, f32[3,1024]{1,0:T(4,128)S(1)} %get-tuple-element.12, f32[3,1024]{1,0:T(4,128)S(1)} %get-tuple-element.13, f32[3,1024]{1,0:T(4,128)S(1)} %bitcast.44), kind=kLoop, calls=%fused_computation.5 | loop fusion | flops 1966080 | bytes 6328320 | tf_op jit(solution)/shard_map/add | solution.py:90
  10.5 0.8 fusion.6
  11.3 13.8 %all-to-all-start = ((bf16[64,16,128]{2,1,0:T(8,128)(2,1)}), bf16[64,16,128]{2,1,0:T(8,128)(2,1)S(1)}, u32[]{:S(2)}, u32[]{:S(2)}) async-start(bf16[64,16,128]{2,1,0:T(8,128)(2,1)} %bitcast.1), calls=%async_computation | async-start | bytes 524288 | tf_op jit(solution)/shard_map/all_to_all | solution.py:97
  25.1 0.1 copy.28
  25.2 0.1 copy.27
  25.2 0.1 convert_multiply_fusion
  25.3 1.9 %convolution_select_fusion = f32[16,128,128]{2,1,0:T(8,128)S(1)} fusion(pred[128,128]{1,0:T(8,128)(4,1)S(1)} %subtract_compare_fusion, f32[128]{0:T(128)S(1)} %get-tuple-element.17, f32[16,16]{0,1:T(8,128)S(1)} %copy.28, f32[128]{0:T(128)S(1)} %get-tuple-element.16, f32[16,16]{0,1:T(8,128)S(1)} %copy.27), kind=kOutput, calls=%fused_computation.10 | convolution fusion | flops 50692096 | bytes 1068032 | tf_op jit(solution)/shard_map/rcj,rct->cjt/dot_general | solution.py:23
  27.3 8.8 %all-to-all-done = bf16[64,16,128]{2,1,0:T(8,128)(2,1)S(1)} async-done(((bf16[64,16,128]{2,1,0:T(8,128)(2,1)}), bf16[64,16,128]{2,1,0:T(8,128)(2,1)S(1)}, u32[]{:S(2)}, u32[]{:S(2)}) %all-to-all-start) | async-done | bytes 262176 | tf_op jit(solution)/shard_map/all_to_all | solution.py:97
  36.1 0.4 convolution_bitcast_fusion
  36.6 2.6 %fusion.2 = f32[16,16,64]{2,1,0:T(8,128)S(1)} fusion(f32[16,16,64]{2,1,0:T(8,128)S(1)} %copy.29, f32[16,16]{1,0:T(8,128)S(1)} %get-tuple-element.14, f32[64,64]{1,0:T(8,128)S(1)} %convert_multiply_fusion, pred[64,64]{1,0:T(8,128)(4,1)S(1)} %iota_compare_fusion), kind=kLoop, calls=%fused_computation.3 | loop fusion | flops 4177920 | bytes 152576 | tf_op jit(solution)/shard_map/reduce_sum | solution.py:38
  39.2 0.7 fusion.17
  39.9 0.4 fusion.5
  40.4 0.9 %copy.31 = bf16[16,64,128]{2,0,1:T(8,128)(2,1)} copy(bf16[16,64,128]{2,1,0:T(8,128)(2,1)S(1)} %fusion.5) | data formatting | bytes 524288 | tf_op jit(solution)/shard_map/convert_element_type | solution.py:101
  41.2 4.8 %all-to-all-start.1 = ((bf16[16,64,128]{2,0,1:T(8,128)(2,1)}), bf16[16,64,128]{2,0,1:T(8,128)(2,1)S(1)}, u32[]{:S(2)}, u32[]{:S(2)}) async-start(bf16[16,64,128]{2,0,1:T(8,128)(2,1)} %copy.31), calls=%async_computation.1 | async-start | bytes 524288 | tf_op jit(solution)/shard_map/all_to_all | solution.py:102
  46.1 11.0 %all-to-all-done.1 = bf16[16,64,128]{2,0,1:T(8,128)(2,1)S(1)} async-done(((bf16[16,64,128]{2,0,1:T(8,128)(2,1)}), bf16[16,64,128]{2,0,1:T(8,128)(2,1)S(1)}, u32[]{:S(2)}, u32[]{:S(2)}) %all-to-all-start.1) | async-done | bytes 262176 | tf_op jit(solution)/shard_map/all_to_all | solution.py:102
  57.1 0.8 fusion.8.gated_ref
  57.9 8.0 %shard_map.55 = bf16[128,4096]{1,0:T(8,128)(2,1)} custom-call(bf16[1024,128]{1,0:T(8,128)(2,1)} %fusion.8.gated_ref, bf16[1024,4096]{1,0:T(8,128)(2,1)} %weight_ref.1), custom_call_target="tpu_custom_call" | custom-call | tf_op jit(solution)/shard_map/pallas_call | solution.py:71
  65.9 1.3 %select_bitcast_fusion.3 = (bf16[1,128,1024]{2,1,0:T(8,128)(2,1)S(1)}, bf16[1,128,1024]{2,1,0:T(8,128)(2,1)S(1)}, bf16[1,128,1024]{2,1,0:T(8,128)(2,1)S(1)}, bf16[1,128,1024]{2,1,0:T(8,128)(2,1)S(1)}) fusion(pred[]{:T(512)S(6)} %eq.9, bf16[128,4096]{1,0:T(8,128)(2,1)} %shard_map.55), kind=kLoop, calls=%fused_computation.31 | loop fusion | flops 524288 | bytes 2097153 | tf_op jit(solution)/shard_map/stack | solution.py:51
  67.1 0.1 pad_maximum_fusion
  67.2 4.6 %collective-permute-start.1 = (bf16[2,128,1024]{2,1,0:T(8,128)(2,1)S(1)}, bf16[2,128,1024]{2,1,0:T(8,128)(2,1)S(1)}, u32[]{:S(2)}, u32[]{:S(2)}) collective-permute-start(bf16[2,128,1024]{2,1,0:T(8,128)(2,1)S(1)} %pad_maximum_fusion), channel_id=1, source_target_pairs={{0,1},{1,0},{2,3},{3,2},{4,5},{5,4},{6,7},{7,6},{8,9},{9,8},{10,11... | collective-permute-start | bytes 1572872 | tf_op jit(solution)/shard_map/ppermute | solution.py:52
  71.8 1.5 %collective-permute-done.1 = bf16[2,128,1024]{2,1,0:T(8,128)(2,1)S(1)} collective-permute-done((bf16[2,128,1024]{2,1,0:T(8,128)(2,1)S(1)}, bf16[2,128,1024]{2,1,0:T(8,128)(2,1)S(1)}, u32[]{:S(2)}, u32[]{:S(2)}) %collective-permute-start.1) | collective-permute-done | bytes 524320 | tf_op jit(solution)/shard_map/ppermute | solution.py:52
  73.3 0.2 convert_add_fusion
  73.5 0.1 fusion.10
  73.6 2.7 %collective-permute-start.2 = (bf16[128,1024]{1,0:T(8,128)(2,1)S(1)}, bf16[128,1024]{1,0:T(8,128)(2,1)S(1)}, u32[]{:S(2)}, u32[]{:S(2)}) collective-permute-start(bf16[128,1024]{1,0:T(8,128)(2,1)S(1)} %fusion.10), channel_id=1, source_target_pairs={{0,2},{1,3},{2,0},{3,1},{4,6},{5,7},{6,4},{7,5},{8,10},{9,11},{10,... | collective-permute-start | bytes 786440 | tf_op jit(solution)/shard_map/ppermute | solution.py:57
  76.3 6.4 %collective-permute-done.2 = bf16[128,1024]{1,0:T(8,128)(2,1)S(1)} collective-permute-done((bf16[128,1024]{1,0:T(8,128)(2,1)S(1)}, bf16[128,1024]{1,0:T(8,128)(2,1)S(1)}, u32[]{:S(2)}, u32[]{:S(2)}) %collective-permute-start.2) | collective-permute-done | bytes 262176 | tf_op jit(solution)/shard_map/ppermute | solution.py:57
  82.7 0.1 fusion.11
  82.8 0.8 %copy.32 = bf16[1024,128]{1,0:T(8,128)(2,1)} copy(bf16[1024,128]{0,1:T(8,128)(2,1)S(1)} %fusion.11) | data formatting | bytes 524288 | tf_op jit(solution)/shard_map/transpose | solution.py:58
  (10 shorter events, 0.1 us)
Async XLA Ops:
  0.0 7.5 %copy-start = (bf16[3,1024,128]{2,1,0:T(8,128)(2,1)S(1)}, bf16[3,1024,128]{2,1,0:T(8,128)(2,1)}, u32[]{:S(2)}) copy-start(bf16[3,1024,128]{2,1,0:T(8,128)(2,1)} %param.5) | copy-start | bytes 2359300
  0.0 6.2 %copy-start.1 = (f32[3,3,1024]{2,1,0:T(4,128)S(1)}, f32[3,3,1024]{2,1,0:T(4,128)}, u32[]{:S(2)}) copy-start(f32[3,3,1024]{2,1,0:T(4,128)} %param.6) | copy-start | bytes 110596
  1.8 5.3 %collective-permute-start = (bf16[3,1024,2]{1,2,0:T(2,128)(2,1)S(1)}, bf16[3,1024,2]{1,2,0:T(2,128)(2,1)S(1)}, u32[]{:S(2)}, u32[]{:S(2)}) collective-permute-start(bf16[3,1024,2]{1,2,0:T(2,128)(2,1)S(1)} %copy.36), channel_id=1, source_target_pairs={{0,4},{4,8},{8,12},{12,16},{16,20},{20,24},{24,28},{28,32},{32,36}... | collective-permute-start | bytes 36872 | tf_op jit(solution)/shard_map/ppermute | solution.py:11
  11.3 24.8 %all-to-all-start = ((bf16[64,16,128]{2,1,0:T(8,128)(2,1)}), bf16[64,16,128]{2,1,0:T(8,128)(2,1)S(1)}, u32[]{:S(2)}, u32[]{:S(2)}) async-start(bf16[64,16,128]{2,1,0:T(8,128)(2,1)} %bitcast.1), calls=%async_computation | async-start | bytes 524288 | tf_op jit(solution)/shard_map/all_to_all | solution.py:97
  41.2 15.9 %all-to-all-start.1 = ((bf16[16,64,128]{2,0,1:T(8,128)(2,1)}), bf16[16,64,128]{2,0,1:T(8,128)(2,1)S(1)}, u32[]{:S(2)}, u32[]{:S(2)}) async-start(bf16[16,64,128]{2,0,1:T(8,128)(2,1)} %copy.31), calls=%async_computation.1 | async-start | bytes 524288 | tf_op jit(solution)/shard_map/all_to_all | solution.py:102
  67.2 6.2 %collective-permute-start.1 = (bf16[2,128,1024]{2,1,0:T(8,128)(2,1)S(1)}, bf16[2,128,1024]{2,1,0:T(8,128)(2,1)S(1)}, u32[]{:S(2)}, u32[]{:S(2)}) collective-permute-start(bf16[2,128,1024]{2,1,0:T(8,128)(2,1)S(1)} %pad_maximum_fusion), channel_id=1, source_target_pairs={{0,1},{1,0},{2,3},{3,2},{4,5},{5,4},{6,7},{7,6},{8,9},{9,8},{10,11... | collective-permute-start | bytes 1572872 | tf_op jit(solution)/shard_map/ppermute | solution.py:52
  73.6 9.1 %collective-permute-start.2 = (bf16[128,1024]{1,0:T(8,128)(2,1)S(1)}, bf16[128,1024]{1,0:T(8,128)(2,1)S(1)}, u32[]{:S(2)}, u32[]{:S(2)}) collective-permute-start(bf16[128,1024]{1,0:T(8,128)(2,1)S(1)} %fusion.10), channel_id=1, source_target_pairs={{0,2},{1,3},{2,0},{3,1},{4,6},{5,7},{6,4},{7,5},{8,10},{9,11},{10,... | collective-permute-start | bytes 786440 | tf_op jit(solution)/shard_map/ppermute | solution.py:57

commit v14 on v6

--- a/solution.py
+++ b/solution.py
@@ -1,6 +1,8 @@
 import jax
 import jax.numpy as jnp
 from jax import lax
+from jax.experimental import pallas as pl
+from jax.experimental.pallas import tpu as pltpu
 from jax.sharding import PartitionSpec as P
 
 
@@ -40,14 +42,39 @@
     return (inside + carried).reshape(chan_here, length)
 
 
-def reduce_scatter_chan(partial):
+def project_kernel(core_ref, gated_ref, weight_ref, out_ref):
+    out_ref[...] = jnp.dot(
+        gated_ref[...], weight_ref[...], preferred_element_type=jnp.float32
+    ).astype(out_ref.dtype)
+
+
+def quarter_slot(quarter, core):
+    differ = quarter % 2 - core
+    return quarter // 2 + 2 * (1 - differ * differ)
+
+
+def project_and_reduce(gated_rows, out_weight):
+    chans, toks = gated_rows.shape
+    outs = out_weight.shape[1]
+    width = outs // 4
     index = lax.axis_index("chan")
     chip, core = index // 2, index % 2
-    width = partial.shape[1] // 4
-    quarter = [partial[:, q * width : (q + 1) * width] for q in range(4)]
-    mine = core == 0
-    send = jnp.stack([jnp.where(mine, quarter[2 * h + 1], quarter[2 * h]) for h in range(2)])
-    keep = jnp.stack([jnp.where(mine, quarter[2 * h], quarter[2 * h + 1]) for h in range(2)])
+    partial = pl.pallas_call(
+        project_kernel,
+        grid_spec=pltpu.PrefetchScalarGridSpec(
+            num_scalar_prefetch=1,
+            grid=(4,),
+            in_specs=[
+                pl.BlockSpec((toks, chans), lambda j, c: (0, 0)),
+                pl.BlockSpec((chans, width), lambda j, c: (0, j)),
+            ],
+            out_specs=pl.BlockSpec((toks, width), lambda j, c: (0, quarter_slot(j, c[0]))),
+        ),
+        out_shape=jax.ShapeDtypeStruct((toks, outs), jnp.bfloat16),
+    )(jnp.reshape(core, (1,)).astype(jnp.int32), gated_rows.T, out_weight)
+    slot = [partial[:, q * width : (q + 1) * width] for q in range(4)]
+    send = jnp.stack(slot[:2])
+    keep = jnp.stack(slot[2:])
     got = lax.ppermute(send, "chan", [(j, j ^ 1) for j in range(4)])
     halves = keep.astype(jnp.float32) + got.astype(jnp.float32)
     first = chip == 0
@@ -78,10 +105,7 @@
     convolved = modal_conv(pencils, life_slice, resid_slice).astype(jnp.bfloat16)
     returned = lax.all_to_all(convolved, "seq", split_axis=1, concat_axis=0, tiled=True)
     gated_rows = (filtered[0] * returned.astype(jnp.float32)).astype(jnp.bfloat16)
-    partial = lax.dot_general(
-        gated_rows, out_weight, (((0,), (0,)), ((), ())), preferred_element_type=jnp.float32
-    ).astype(jnp.bfloat16)
-    return reduce_scatter_chan(partial)
+    return project_and_reduce(gated_rows, out_weight)
 
 
 def solution(mesh):

time: 78.8 us -> 79.2 us (level)
  Pallas kernels: 0 us -> 5.77 us
  matrix products: 8.18 us -> 3.51 us
  other arithmetic: 6.96 us -> 4.69 us
  local copies, waits for them, and re-layouts: 5.87 us -> 7.4 us
    pallas_call x0 -> x1, Pallas kernels: none -> 5.77 us  [project_and_reduce(): pl.pallas_call(project_kernel, grid_spec=pltpu.PrefetchScalarGridSpec(num...]
    dot_general x1 -> x0, matrix products: 4.67 us -> none  [local(): lax.dot_general(gated_rows, out_weight, (((0,), (0,)), ((), ())), preferr...]
    add x1, other arithmetic: 2.35 us -> 0.47 us  [local(): taps[:, 0, :, None] * extended[:, :, 2:]]
    slice x1, local copies, waits for them, and re-layouts: 1.48 us -> 0.02 us  [local(): edge_block = qkv[:, :, tok_count - 2:]]
    another operation x0 -> x1, local copies, waits for them, and re-layouts: none -> 1.28 us  [project_and_reduce(): keep = jnp.stack(slot[2:])]
    unnamed x5 -> x3, local copies, waits for them, and re-layouts: 0.32 us -> 1.42 us
    convert_element_type x0 -> x2, local copies, waits for them, and re-layouts: none -> 1.04 us  [the longest x1 0.84 us: local(): product = (filtered[1] * filtered[2]).astype(jnp.bfloat16)]
where the time goes in v14:
time: 79.2 us; the launch traced here: 78.8 us
  starting transfers between devices  29.5 us (37%)
  waiting for transfers between devices  27.7 us (35%)
  local copies, waits for them, and re-layouts  7.4 us (9%)
  Pallas kernels  5.77 us (7%)
  other arithmetic  4.69 us (6%)
  matrix products  3.51 us (4%)
    all_to_all x1, starting transfers between devices, local(): lax.all_to_all(product, 'seq', split_axis=0, concat_axis=1, tiled=True)  12.9 us
    all_to_all x1, waiting for transfers between devices, local(): lax.all_to_all(convolved, 'seq', split_axis=1, concat_axis=0, tiled=True)  11 us
    all_to_all x1, waiting for transfers between devices, local(): lax.all_to_all(product, 'seq', split_axis=0, concat_axis=1, tiled=True)  8.82 us
    ppermute x1, waiting for transfers between devices, project_and_reduce(): got2 = lax.ppermute(send2, 'chan', [(j, j ^ 2) for j in range(4)])  6.37 us
    pallas_call x1, Pallas kernels, project_and_reduce(): pl.pallas_call(project_kernel, grid_spec=pltpu.PrefetchScalarGridSpec(num...  5.77 us
    all_to_all x1, starting transfers between devices, local(): lax.all_to_all(convolved, 'seq', split_axis=1, concat_axis=0, tiled=True)  4.85 us
    ppermute x1, starting transfers between devices, project_and_reduce(): got = lax.ppermute(send, 'chan', [(j, j ^ 1) for j in range(4)])  4.63 us
    ppermute x1, starting transfers between devices, from_behind(): return lax.ppermute(x, axis, pairs)  4.36 us
  transfers between devices with their start and end apart: 5, of which 4 were waited for; matrix products, arithmetic and copies ran while one was open for 5% of the time, Pallas kernels for 0%

profile of v14, /device:TPU:1, one launch (start us, length us, event | category | flops | bytes accessed | tf_op | source)
XLA Modules:
  0.0 78.8 jit_solution(7524046226351846534)
XLA Ops:
  0.0 1.4 %copy.32 = bf16[3,1024,128]{1,2,0:T(8,128)(2,1)S(1)} copy(bf16[3,1024,128]{2,1,0:T(8,128)(2,1)} %param.5) | data formatting | bytes 1572864 | tf_op args[0]
  1.4 4.4 %collective-permute-start = (bf16[3,1024,2]{1,2,0:T(2,128)(2,1)S(1)}, bf16[3,1024,2]{1,2,0:T(2,128)(2,1)S(1)}, u32[]{:S(2)}, u32[]{:S(2)}) collective-permute-start(bf16[3,1024,2]{1,2,0:T(2,128)(2,1)S(1)} %slice.66), channel_id=1, source_target_pairs={{0,4},{4,8},{8,12},{12,16},{16,20},{20,24},{24,28},{28,32},{32,36}... | collective-permute-start | bytes 36872 | tf_op jit(solution)/shard_map/ppermute | solution.py:12
  5.9 0.9 %fusion.33 = (f32[3,1,1024]{2,1,0:T(1,128)S(1)}, f32[3,1,1024]{2,1,0:T(1,128)S(1)}, f32[3,1,1024]{2,1,0:T(1,128)S(1)}) fusion(f32[3,3,1024]{2,1,0:T(4,128)} %param.6), kind=kLoop, calls=%fused_computation.65 | loop fusion | bytes 73728 | tf_op jit(solution)/shard_map/slice | solution.py:94
  6.8 0.8 %constant_dynamic-slice_fusion = (f32[16,16]{1,0:T(8,128)S(1)}, f32[16,16]{1,0:T(8,128)S(1)}) fusion(f32[16,1024]{1,0:T(8,128)} %param.7, s32[]{:T(128)S(6)} %select_n.42, f32[16,1024]{1,0:T(8,128)} %param.8), kind=kLoop, calls=%fused_computation.62 | loop fusion | bytes 4100 | tf_op jit(solution)/shard_map/dynamic_slice | solution.py:103
  7.7 0.0 collective-permute-done
  7.7 0.2 maximum_convert_fusion
  7.9 0.5 fusion.3
  8.4 0.1 fusion.6
  8.4 0.8 %copy.34 = bf16[1,1024,128]{2,1,0:T(8,128)(2,1)} copy(bf16[1,1024,128]{1,2,0:T(8,128)(2,1)S(1)} %fusion.6) | data formatting | bytes 524288 | tf_op jit(solution)/shard_map/convert_element_type | solution.py:98
  9.3 12.9 %all-to-all-start = ((bf16[64,16,128]{2,1,0:T(8,128)(2,1)}), bf16[64,16,128]{2,1,0:T(8,128)(2,1)S(1)}, u32[]{:S(2)}, u32[]{:S(2)}) async-start(bf16[64,16,128]{2,1,0:T(8,128)(2,1)} %bitcast.2), calls=%async_computation | async-start | bytes 524288 | tf_op jit(solution)/shard_map/all_to_all | solution.py:101
  22.2 0.1 copy.37
  22.3 0.1 copy.36
  22.3 0.1 convert_multiply_fusion
  22.4 1.9 %convolution_select_fusion = f32[16,128,128]{2,1,0:T(8,128)S(1)} fusion(pred[128,128]{1,0:T(8,128)(4,1)S(1)} %subtract_compare_fusion, f32[128]{0:T(128)S(1)} %get-tuple-element.17, f32[16,16]{0,1:T(8,128)S(1)} %copy.37, f32[128]{0:T(128)S(1)} %get-tuple-element.16, f32[16,16]{0,1:T(8,128)S(1)} %copy.36), kind=kOutput, calls=%fused_computation.9 | convolution fusion | flops 50692096 | bytes 1068032 | tf_op jit(solution)/shard_map/rcj,rct->cjt/dot_general | solution.py:24
  24.4 8.8 %all-to-all-done = bf16[64,16,128]{2,1,0:T(8,128)(2,1)S(1)} async-done(((bf16[64,16,128]{2,1,0:T(8,128)(2,1)}), bf16[64,16,128]{2,1,0:T(8,128)(2,1)S(1)}, u32[]{:S(2)}, u32[]{:S(2)}) %all-to-all-start) | async-done | bytes 262176 | tf_op jit(solution)/shard_map/all_to_all | solution.py:101
  33.2 0.4 convolution_bitcast_fusion
  33.7 2.6 %fusion.2 = f32[16,16,64]{2,1,0:T(8,128)S(1)} fusion(f32[16,16,64]{2,1,0:T(8,128)S(1)} %copy.38, f32[16,16]{1,0:T(8,128)S(1)} %get-tuple-element.14, f32[64,64]{1,0:T(8,128)S(1)} %convert_multiply_fusion, pred[64,64]{1,0:T(8,128)(4,1)S(1)} %iota_compare_fusion), kind=kLoop, calls=%fused_computation.3 | loop fusion | flops 4177920 | bytes 152576 | tf_op jit(solution)/shard_map/reduce_sum | solution.py:39
  36.3 0.7 fusion.18
  37.0 0.4 fusion.5
  37.5 0.9 %copy.40 = bf16[16,64,128]{2,0,1:T(8,128)(2,1)} copy(bf16[16,64,128]{2,1,0:T(8,128)(2,1)S(1)} %fusion.5) | data formatting | bytes 524288 | tf_op jit(solution)/shard_map/convert_element_type | solution.py:105
  38.3 4.9 %all-to-all-start.1 = ((bf16[16,64,128]{2,0,1:T(8,128)(2,1)}), bf16[16,64,128]{2,0,1:T(8,128)(2,1)S(1)}, u32[]{:S(2)}, u32[]{:S(2)}) async-start(bf16[16,64,128]{2,0,1:T(8,128)(2,1)} %copy.40), calls=%async_computation.1 | async-start | bytes 524288 | tf_op jit(solution)/shard_map/all_to_all | solution.py:106
  43.2 11.0 %all-to-all-done.1 = bf16[16,64,128]{2,0,1:T(8,128)(2,1)S(1)} async-done(((bf16[16,64,128]{2,0,1:T(8,128)(2,1)}), bf16[16,64,128]{2,0,1:T(8,128)(2,1)S(1)}, u32[]{:S(2)}, u32[]{:S(2)}) %all-to-all-start.1) | async-done | bytes 262176 | tf_op jit(solution)/shard_map/all_to_all | solution.py:106
  54.3 0.2 copy.41
  54.5 0.8 fusion.12.gated_ref
  55.2 5.8 %shard_map.55 = bf16[128,4096]{1,0:T(8,128)(2,1)} custom-call(s32[1]{0:T(128)} %bitcast.core_ref, bf16[128,1024]{1,0:T(8,128)(2,1)} %fusion.12.gated_ref, bf16[1024,4096]{1,0:T(8,128)(2,1)} %weight_ref.1), custom_call_target="tpu_custom_call" | custom-call | tf_op jit(solution)/shard_map/pallas_call | solution.py:62
  61.0 1.3 %slice_bitcast_fusion.4 = (bf16[1,128,1024]{2,1,0:T(8,128)(2,1)S(1)}, bf16[1,128,1024]{2,1,0:T(8,128)(2,1)S(1)}, bf16[1,128,1024]{2,1,0:T(8,128)(2,1)S(1)}, bf16[1,128,1024]{2,1,0:T(8,128)(2,1)S(1)}) fusion(bf16[128,4096]{1,0:T(8,128)(2,1)} %shard_map.55), kind=kLoop, calls=%fused_computation.30 | loop fusion | bytes 2097152 | tf_op jit(solution)/shard_map/stack | solution.py:77
  62.3 0.1 pad_maximum_fusion
  62.3 4.6 %collective-permute-start.1 = (bf16[2,128,1024]{2,1,0:T(8,128)(2,1)S(1)}, bf16[2,128,1024]{2,1,0:T(8,128)(2,1)S(1)}, u32[]{:S(2)}, u32[]{:S(2)}) collective-permute-start(bf16[2,128,1024]{2,1,0:T(8,128)(2,1)S(1)} %pad_maximum_fusion), channel_id=1, source_target_pairs={{0,1},{1,0},{2,3},{3,2},{4,5},{5,4},{6,7},{7,6},{8,9},{9,8},{10,11... | collective-permute-start | bytes 1572872 | tf_op jit(solution)/shard_map/ppermute | solution.py:78
  67.0 1.5 %collective-permute-done.1 = bf16[2,128,1024]{2,1,0:T(8,128)(2,1)S(1)} collective-permute-done((bf16[2,128,1024]{2,1,0:T(8,128)(2,1)S(1)}, bf16[2,128,1024]{2,1,0:T(8,128)(2,1)S(1)}, u32[]{:S(2)}, u32[]{:S(2)}) %collective-permute-start.1) | collective-permute-done | bytes 524320 | tf_op jit(solution)/shard_map/ppermute | solution.py:78
  68.5 0.2 convert_add_fusion
  68.7 0.1 fusion.10
  68.8 2.7 %collective-permute-start.2 = (bf16[128,1024]{1,0:T(8,128)(2,1)S(1)}, bf16[128,1024]{1,0:T(8,128)(2,1)S(1)}, u32[]{:S(2)}, u32[]{:S(2)}) collective-permute-start(bf16[128,1024]{1,0:T(8,128)(2,1)S(1)} %fusion.10), channel_id=1, source_target_pairs={{0,2},{1,3},{2,0},{3,1},{4,6},{5,7},{6,4},{7,5},{8,10},{9,11},{10,... | collective-permute-start | bytes 786440 | tf_op jit(solution)/shard_map/ppermute | solution.py:83
  71.5 6.4 %collective-permute-done.2 = bf16[128,1024]{1,0:T(8,128)(2,1)S(1)} collective-permute-done((bf16[128,1024]{1,0:T(8,128)(2,1)S(1)}, bf16[128,1024]{1,0:T(8,128)(2,1)S(1)}, u32[]{:S(2)}, u32[]{:S(2)}) %collective-permute-start.2) | collective-permute-done | bytes 262176 | tf_op jit(solution)/shard_map/ppermute | solution.py:83
  77.8 0.1 fusion.11
  77.9 0.8 %copy.42 = bf16[1024,128]{1,0:T(8,128)(2,1)} copy(bf16[1024,128]{0,1:T(8,128)(2,1)S(1)} %fusion.11) | data formatting | bytes 524288 | tf_op jit(solution)/shard_map/transpose | solution.py:84
  (11 shorter events, 0.2 us)
Async XLA Ops:
  1.4 6.2 %collective-permute-start = (bf16[3,1024,2]{1,2,0:T(2,128)(2,1)S(1)}, bf16[3,1024,2]{1,2,0:T(2,128)(2,1)S(1)}, u32[]{:S(2)}, u32[]{:S(2)}) collective-permute-start(bf16[3,1024,2]{1,2,0:T(2,128)(2,1)S(1)} %slice.66), channel_id=1, source_target_pairs={{0,4},{4,8},{8,12},{12,16},{16,20},{20,24},{24,28},{28,32},{32,36}... | collective-permute-start | bytes 36872 | tf_op jit(solution)/shard_map/ppermute | solution.py:12
  9.3 23.9 %all-to-all-start = ((bf16[64,16,128]{2,1,0:T(8,128)(2,1)}), bf16[64,16,128]{2,1,0:T(8,128)(2,1)S(1)}, u32[]{:S(2)}, u32[]{:S(2)}) async-start(bf16[64,16,128]{2,1,0:T(8,128)(2,1)} %bitcast.2), calls=%async_computation | async-start | bytes 524288 | tf_op jit(solution)/shard_map/all_to_all | solution.py:101
  38.3 15.9 %all-to-all-start.1 = ((bf16[16,64,128]{2,0,1:T(8,128)(2,1)}), bf16[16,64,128]{2,0,1:T(8,128)(2,1)S(1)}, u32[]{:S(2)}, u32[]{:S(2)}) async-start(bf16[16,64,128]{2,0,1:T(8,128)(2,1)} %copy.40), calls=%async_computation.1 | async-start | bytes 524288 | tf_op jit(solution)/shard_map/all_to_all | solution.py:106
  62.3 6.2 %collective-permute-start.1 = (bf16[2,128,1024]{2,1,0:T(8,128)(2,1)S(1)}, bf16[2,128,1024]{2,1,0:T(8,128)(2,1)S(1)}, u32[]{:S(2)}, u32[]{:S(2)}) collective-permute-start(bf16[2,128,1024]{2,1,0:T(8,128)(2,1)S(1)} %pad_maximum_fusion), channel_id=1, source_target_pairs={{0,1},{1,0},{2,3},{3,2},{4,5},{5,4},{6,7},{7,6},{8,9},{9,8},{10,11... | collective-permute-start | bytes 1572872 | tf_op jit(solution)/shard_map/ppermute | solution.py:78
  68.8 9.1 %collective-permute-start.2 = (bf16[128,1024]{1,0:T(8,128)(2,1)S(1)}, bf16[128,1024]{1,0:T(8,128)(2,1)S(1)}, u32[]{:S(2)}, u32[]{:S(2)}) collective-permute-start(bf16[128,1024]{1,0:T(8,128)(2,1)S(1)} %fusion.10), channel_id=1, source_target_pairs={{0,2},{1,3},{2,0},{3,1},{4,6},{5,7},{6,4},{7,5},{8,10},{9,11},{10,... | collective-permute-start | bytes 786440 | tf_op jit(solution)/shard_map/ppermute | solution.py:83

commit v15 on v11

--- a/solution.py
+++ b/solution.py
@@ -71,18 +71,17 @@
         + taps[:, 1, :, None] * jnp.concatenate([pad1, signal[:, :, :-1]], axis=2)
         + taps[:, 2, :, None] * jnp.concatenate([pad2, signal[:, :, :-2]], axis=2)
     )
+    body, filtered_q = lax.optimization_barrier(
+        ((no_halo[1] * no_halo[2]).astype(jnp.bfloat16), no_halo[0])
+    )
     head_in = jnp.concatenate([earlier, qkv[:, :, :2]], axis=2).astype(jnp.float32)
     head = (
         taps[:, 0, :, None] * head_in[:, :, 2:]
         + taps[:, 1, :, None] * head_in[:, :, 1:3]
         + taps[:, 2, :, None] * head_in[:, :, :2]
     )
-    product = lax.dynamic_update_slice(
-        (no_halo[1] * no_halo[2]).astype(jnp.bfloat16),
-        (head[1] * head[2]).astype(jnp.bfloat16),
-        (0, 0),
-    )
-    filtered_q = lax.dynamic_update_slice(no_halo[0], head[0], (0, 0))
+    product = lax.dynamic_update_slice(body, (head[1] * head[2]).astype(jnp.bfloat16), (0, 0))
+    filtered_q = lax.dynamic_update_slice(filtered_q, head[0], (0, 0))
     groups = lax.axis_size("seq")
     per_group = chan_local // groups
     pencils = lax.all_to_all(product, "seq", split_axis=0, concat_axis=1, tiled=True)

time: 82 us -> 82 us (level)
    squeeze x0 -> x1, other arithmetic: none -> 0.96 us  [local(): no_halo[0]]
    convert_element_type x1 -> x0, other arithmetic: 0.96 us -> none  [local(): (no_halo[1] * no_halo[2]).astype(jnp.bfloat16)]
where the time goes in v15:
time: 82 us; the launch traced here: 81.5 us
  starting transfers between devices  28.5 us (35%)
  waiting for transfers between devices  25.7 us (31%)
  local copies, waits for them, and re-layouts  12 us (15%)
  matrix products  8.18 us (10%)
  other arithmetic  6.88 us (8%)
    all_to_all x1, starting transfers between devices, local(): lax.all_to_all(product, 'seq', split_axis=0, concat_axis=1, tiled=True)  11.8 us
    all_to_all x1, waiting for transfers between devices, local(): lax.all_to_all(product, 'seq', split_axis=0, concat_axis=1, tiled=True)  9.24 us
    all_to_all x1, waiting for transfers between devices, local(): lax.all_to_all(convolved, 'seq', split_axis=1, concat_axis=0, tiled=True)  8.5 us
    ppermute x1, waiting for transfers between devices, reduce_scatter_chan(): got2 = lax.ppermute(send2, 'chan', [(j, j ^ 2) for j in range(4)])  6.38 us
    all_to_all x1, starting transfers between devices, local(): lax.all_to_all(convolved, 'seq', split_axis=1, concat_axis=0, tiled=True)  5.94 us
    dot_general x1, matrix products, local(): lax.dot_general(gated_rows, out_weight, (((0,), (0,)), ((), ())), preferr...  4.67 us
    ppermute x1, starting transfers between devices, from_behind(): return lax.ppermute(x, axis, pairs)  4.36 us
    ppermute x1, starting transfers between devices, reduce_scatter_chan(): got = lax.ppermute(send, 'chan', [(j, j ^ 1) for j in range(4)])  3.71 us
  transfers between devices with their start and end apart: 5, of which 4 were waited for; matrix products, arithmetic and copies ran while one was open for 11% of the time, Pallas kernels for 0%

profile of v15, /device:TPU:1, one launch (start us, length us, event | category | flops | bytes accessed | tf_op | source)
XLA Modules:
  0.0 81.5 jit_solution(5343475884631946764)
XLA Ops:
  0.0 0.0 copy-start
  0.0 1.8 %fusion.33 = (bf16[3,1024,2]{2,1,0:T(8,128)(2,1)S(1)}, bf16[3,1024,2]{2,1,0:T(8,128)(2,1)S(1)}) fusion(bf16[3,1024,128]{2,1,0:T(8,128)(2,1)} %param.5), kind=kLoop, calls=%fused_computation.70 | loop fusion | bytes 49152 | tf_op jit(solution)/shard_map/slice | solution.py:63
  1.8 0.3 copy.44
  2.1 4.4 %collective-permute-start = (bf16[3,1024,2]{1,2,0:T(2,128)(2,1)S(1)}, bf16[3,1024,2]{1,2,0:T(2,128)(2,1)S(1)}, u32[]{:S(2)}, u32[]{:S(2)}) collective-permute-start(bf16[3,1024,2]{1,2,0:T(2,128)(2,1)S(1)} %copy.44), channel_id=1, source_target_pairs={{0,4},{4,8},{8,12},{12,16},{16,20},{20,24},{24,28},{28,32},{32,36}... | collective-permute-start | bytes 36872 | tf_op jit(solution)/shard_map/ppermute | solution.py:10
  6.4 0.0 copy-done
  6.4 0.1 slice.94
  6.6 0.0 copy-start.2
  6.6 0.1 slice.93
  6.7 0.6 copy-done.2
  7.4 2.3 %multiply_add_fusion = f32[3,1024,128]{2,1,0:T(8,128)S(1)} fusion(f32[3,1024,126]{2,1,0:T(8,128)S(1)} %slice.94, f32[3,1024,127]{2,1,0:T(8,128)S(1)} %slice.93, f32[3,1024]{1,0:T(4,128)S(1)} %get-tuple-element.24, f32[3,1024]{1,0:T(4,128)S(1)} %get-tuple-element.25, f32[3,1024]{1,0:T(4,128)S(1)} %bitcast.53, bf16[3,1024,128]{2,1,0:T(8,128)(2,1)S(1)} %copy-done), kind=kLoop, calls=%fused_computation.5 | loop fusion | flops 2359296 | bytes 5505024 | tf_op jit(solution)/shard_map/add | solution.py:70
  9.8 1.0 %slice_bitcast_fusion.1 = (f32[1024,128]{1,0:T(8,128)}, bf16[1024,128]{1,0:T(8,128)(2,1)}) fusion(f32[3,1024,128]{2,1,0:T(8,128)S(1)} %multiply_add_fusion), kind=kLoop, calls=%fused_computation.14 | loop fusion | flops 262144 | bytes 2359296 | tf_op jit(solution)/shard_map/squeeze | solution.py:75
  10.7 0.8 constant_dynamic-slice_fusion
  11.5 0.3 copy.45
  11.8 0.0 collective-permute-done
  11.9 0.5 copy.32
  12.4 0.5 copy.33
  12.9 0.2 add.62
  13.1 0.1 fusion.11
  13.2 2.8 %dynamic_update_slice.7 = bf16[1024,128]{1,0:T(8,128)(2,1)} dynamic-update-slice(bf16[1024,128]{1,0:T(8,128)(2,1)} %get-tuple-element.8, bf16[1024,2]{1,0:T(8,128)(2,1)S(1)} %get-tuple-element.9, s32[]{:T(128)} %constant.43.clone.1, s32[]{:T(128)} %constant.43.clone.1) | dynamic-update-slice | bytes 8196 | tf_op jit(solution)/shard_map/dynamic_update_slice | solution.py:83
  16.0 11.8 %all-to-all-start = ((bf16[64,16,128]{2,1,0:T(8,128)(2,1)}), bf16[64,16,128]{2,1,0:T(8,128)(2,1)S(1)}, u32[]{:S(2)}, u32[]{:S(2)}) async-start(bf16[64,16,128]{2,1,0:T(8,128)(2,1)} %bitcast.4), calls=%async_computation | async-start | bytes 524288 | tf_op jit(solution)/shard_map/all_to_all | solution.py:87
  27.8 0.1 copy.36
  27.9 0.1 copy.35
  27.9 0.1 convert_multiply_fusion
  28.0 1.9 %convolution_select_fusion = f32[16,128,128]{2,1,0:T(8,128)S(1)} fusion(pred[128,128]{1,0:T(8,128)(4,1)S(1)} %subtract_compare_fusion, f32[128]{0:T(128)S(1)} %get-tuple-element.29, f32[16,16]{0,1:T(8,128)S(1)} %copy.36, f32[128]{0:T(128)S(1)} %get-tuple-element.28, f32[16,16]{0,1:T(8,128)S(1)} %copy.35), kind=kOutput, calls=%fused_computation.6 | convolution fusion | flops 50692096 | bytes 1068032 | tf_op jit(solution)/shard_map/rcj,rct->cjt/dot_general | solution.py:22
  30.0 9.2 %all-to-all-done = bf16[64,16,128]{2,1,0:T(8,128)(2,1)S(1)} async-done(((bf16[64,16,128]{2,1,0:T(8,128)(2,1)}), bf16[64,16,128]{2,1,0:T(8,128)(2,1)S(1)}, u32[]{:S(2)}, u32[]{:S(2)}) %all-to-all-start) | async-done | bytes 262176 | tf_op jit(solution)/shard_map/all_to_all | solution.py:87
  39.2 0.4 convolution_bitcast_fusion
  39.7 2.6 %fusion.2 = f32[16,16,64]{2,1,0:T(8,128)S(1)} fusion(f32[16,16,64]{2,1,0:T(8,128)S(1)} %copy.37, f32[16,16]{1,0:T(8,128)S(1)} %get-tuple-element.26, f32[64,64]{1,0:T(8,128)S(1)} %convert_multiply_fusion, pred[64,64]{1,0:T(8,128)(4,1)S(1)} %iota_compare_fusion), kind=kLoop, calls=%fused_computation.3 | loop fusion | flops 4177920 | bytes 152576 | tf_op jit(solution)/shard_map/reduce_sum | solution.py:37
  42.3 0.7 fusion.17
  43.1 0.0 copy-start.1
  43.1 0.4 fusion.3
  43.5 0.9 %copy.39 = bf16[16,64,128]{2,0,1:T(8,128)(2,1)} copy(bf16[16,64,128]{2,1,0:T(8,128)(2,1)S(1)} %fusion.3) | data formatting | bytes 524288 | tf_op jit(solution)/shard_map/convert_element_type | solution.py:91
  44.4 5.9 %all-to-all-start.1 = ((bf16[16,64,128]{2,0,1:T(8,128)(2,1)}), bf16[16,64,128]{2,0,1:T(8,128)(2,1)S(1)}, u32[]{:S(2)}, u32[]{:S(2)}) async-start(bf16[16,64,128]{2,0,1:T(8,128)(2,1)} %copy.39), calls=%async_computation.1 | async-start | bytes 524288 | tf_op jit(solution)/shard_map/all_to_all | solution.py:92
  50.3 0.0 copy-done.1
  50.3 2.3 %dynamic_update_slice.6 = f32[1024,128]{1,0:T(8,128)S(1)} dynamic-update-slice(f32[1024,128]{1,0:T(8,128)S(1)} %copy-done.1, f32[1024,2]{1,0:T(8,128)S(1)} %get-tuple-element.10, s32[]{:T(128)} %constant.43.clone.1, s32[]{:T(128)} %constant.43.clone.1) | dynamic-update-slice | bytes 16388 | tf_op jit(solution)/shard_map/dynamic_update_slice | solution.py:84
  52.6 8.5 %all-to-all-done.1 = bf16[16,64,128]{2,0,1:T(8,128)(2,1)S(1)} async-done(((bf16[16,64,128]{2,0,1:T(8,128)(2,1)}), bf16[16,64,128]{2,0,1:T(8,128)(2,1)S(1)}, u32[]{:S(2)}, u32[]{:S(2)}) %all-to-all-start.1) | async-done | bytes 262176 | tf_op jit(solution)/shard_map/all_to_all | solution.py:92
  61.1 0.1 fusion.6
  61.2 4.7 %convolution_convert_fusion = bf16[128,4096]{1,0:T(8,128)(2,1)S(1)} fusion(bf16[1024,128]{1,0:T(8,128)(2,1)S(1)} %fusion.6, bf16[1024,4096]{1,0:T(8,128)(2,1)} %param.9), kind=kOutput, calls=%fused_computation.4 | convolution fusion | flops 1074266112 | bytes 9699328 | tf_op jit(solution)/shard_map/dot_general | solution.py:94
  65.9 0.1 select_bitcast_fusion.3
  66.0 0.1 pad_maximum_fusion
  66.0 3.7 %collective-permute-start.1 = (bf16[2,128,1024]{2,1,0:T(8,128)(2,1)S(1)}, bf16[2,128,1024]{2,1,0:T(8,128)(2,1)S(1)}, u32[]{:S(2)}, u32[]{:S(2)}) collective-permute-start(bf16[2,128,1024]{2,1,0:T(8,128)(2,1)S(1)} %pad_maximum_fusion), channel_id=1, source_target_pairs={{0,1},{1,0},{2,3},{3,2},{4,5},{5,4},{6,7},{7,6},{8,9},{9,8},{10,11... | collective-permute-start | bytes 1572872 | tf_op jit(solution)/shard_map/ppermute | solution.py:51
  69.7 1.5 %collective-permute-done.1 = bf16[2,128,1024]{2,1,0:T(8,128)(2,1)S(1)} collective-permute-done((bf16[2,128,1024]{2,1,0:T(8,128)(2,1)S(1)}, bf16[2,128,1024]{2,1,0:T(8,128)(2,1)S(1)}, u32[]{:S(2)}, u32[]{:S(2)}) %collective-permute-start.1) | collective-permute-done | bytes 524320 | tf_op jit(solution)/shard_map/ppermute | solution.py:51
  71.3 0.2 convert_add_fusion
  71.4 0.1 fusion.8
  71.5 2.7 %collective-permute-start.2 = (bf16[128,1024]{1,0:T(8,128)(2,1)S(1)}, bf16[128,1024]{1,0:T(8,128)(2,1)S(1)}, u32[]{:S(2)}, u32[]{:S(2)}) collective-permute-start(bf16[128,1024]{1,0:T(8,128)(2,1)S(1)} %fusion.8), channel_id=1, source_target_pairs={{0,2},{1,3},{2,0},{3,1},{4,6},{5,7},{6,4},{7,5},{8,10},{9,11},{10,... | collective-permute-start | bytes 786440 | tf_op jit(solution)/shard_map/ppermute | solution.py:56
  74.2 6.4 %collective-permute-done.2 = bf16[128,1024]{1,0:T(8,128)(2,1)S(1)} collective-permute-done((bf16[128,1024]{1,0:T(8,128)(2,1)S(1)}, bf16[128,1024]{1,0:T(8,128)(2,1)S(1)}, u32[]{:S(2)}, u32[]{:S(2)}) %collective-permute-start.2) | collective-permute-done | bytes 262176 | tf_op jit(solution)/shard_map/ppermute | solution.py:56
  80.6 0.1 fusion.9
  80.7 0.8 %copy.40 = bf16[1024,128]{1,0:T(8,128)(2,1)} copy(bf16[1024,128]{0,1:T(8,128)(2,1)S(1)} %fusion.9) | data formatting | bytes 524288 | tf_op jit(solution)/shard_map/transpose | solution.py:57
  (12 shorter events, 0.2 us)
Async XLA Ops:
  0.0 6.4 %copy-start = (bf16[3,1024,128]{2,1,0:T(8,128)(2,1)S(1)}, bf16[3,1024,128]{2,1,0:T(8,128)(2,1)}, u32[]{:S(2)}) copy-start(bf16[3,1024,128]{2,1,0:T(8,128)(2,1)} %param.5) | copy-start | bytes 2359300
  2.1 9.8 %collective-permute-start = (bf16[3,1024,2]{1,2,0:T(2,128)(2,1)S(1)}, bf16[3,1024,2]{1,2,0:T(2,128)(2,1)S(1)}, u32[]{:S(2)}, u32[]{:S(2)}) collective-permute-start(bf16[3,1024,2]{1,2,0:T(2,128)(2,1)S(1)} %copy.44), channel_id=1, source_target_pairs={{0,4},{4,8},{8,12},{12,16},{16,20},{20,24},{24,28},{28,32},{32,36}... | collective-permute-start | bytes 36872 | tf_op jit(solution)/shard_map/ppermute | solution.py:10
  6.6 0.8 copy-start.2
  16.0 23.2 %all-to-all-start = ((bf16[64,16,128]{2,1,0:T(8,128)(2,1)}), bf16[64,16,128]{2,1,0:T(8,128)(2,1)S(1)}, u32[]{:S(2)}, u32[]{:S(2)}) async-start(bf16[64,16,128]{2,1,0:T(8,128)(2,1)} %bitcast.4), calls=%async_computation | async-start | bytes 524288 | tf_op jit(solution)/shard_map/all_to_all | solution.py:87
  43.1 7.3 %copy-start.1 = (f32[1024,128]{1,0:T(8,128)S(1)}, f32[1024,128]{1,0:T(8,128)}, u32[]{:S(2)}) copy-start(f32[1024,128]{1,0:T(8,128)} %get-tuple-element.7) | copy-start | bytes 1572868
  44.4 16.8 %all-to-all-start.1 = ((bf16[16,64,128]{2,0,1:T(8,128)(2,1)}), bf16[16,64,128]{2,0,1:T(8,128)(2,1)S(1)}, u32[]{:S(2)}, u32[]{:S(2)}) async-start(bf16[16,64,128]{2,0,1:T(8,128)(2,1)} %copy.39), calls=%async_computation.1 | async-start | bytes 524288 | tf_op jit(solution)/shard_map/all_to_all | solution.py:92
  66.0 5.3 %collective-permute-start.1 = (bf16[2,128,1024]{2,1,0:T(8,128)(2,1)S(1)}, bf16[2,128,1024]{2,1,0:T(8,128)(2,1)S(1)}, u32[]{:S(2)}, u32[]{:S(2)}) collective-permute-start(bf16[2,128,1024]{2,1,0:T(8,128)(2,1)S(1)} %pad_maximum_fusion), channel_id=1, source_target_pairs={{0,1},{1,0},{2,3},{3,2},{4,5},{5,4},{6,7},{7,6},{8,9},{9,8},{10,11... | collective-permute-start | bytes 1572872 | tf_op jit(solution)/shard_map/ppermute | solution.py:51
  71.5 9.1 %collective-permute-start.2 = (bf16[128,1024]{1,0:T(8,128)(2,1)S(1)}, bf16[128,1024]{1,0:T(8,128)(2,1)S(1)}, u32[]{:S(2)}, u32[]{:S(2)}) collective-permute-start(bf16[128,1024]{1,0:T(8,128)(2,1)S(1)} %fusion.8), channel_id=1, source_target_pairs={{0,2},{1,3},{2,0},{3,1},{4,6},{5,7},{6,4},{7,5},{8,10},{9,11},{10,... | collective-permute-start | bytes 786440 | tf_op jit(solution)/shard_map/ppermute | solution.py:56

commit v16 on v6

--- a/solution.py
+++ b/solution.py
@@ -10,7 +10,7 @@
     return lax.ppermute(x, axis, pairs)
 
 
-def modal_conv(pencils, life_slice, resid_slice, block=128):
+def modal_conv(pencils, life_slice, resid_slice, block=256):
     chan_here, length = pencils.shape
     blocks = length // block
     steps = jnp.arange(block, dtype=jnp.int32).astype(jnp.float32)

time: 78.8 us -> 80.8 us (1.025)
  matrix products: 8.18 us -> 14.1 us
  waiting for transfers between devices: 27.7 us -> 24.5 us
  other arithmetic: 6.96 us -> 5.89 us
    dot_general x1, matrix products: 1.94 us -> 5.3 us  [modal_conv(): jnp.einsum('rcj,rct->cjt', rising, falling, precision=lax.Precision.HIGHEST)]
    all_to_all x1, waiting for transfers between devices: 8.82 us -> 5.61 us  [local(): lax.all_to_all(product, 'seq', split_axis=0, concat_axis=1, tiled=True)]
    dot_general x1, matrix products: 0.42 us -> 3.25 us  [modal_conv(): inside = jnp.einsum('cnj,cjt->cnt', signal, toeplitz, precision=precise)]
    reduce_sum x1, other arithmetic: 2.64 us -> 1.56 us  [modal_conv(): entering = jnp.sum(jnp.exp(exponent) * leaving[:, :, None, :], axis=-1)]
  transfers between devices with their start and end apart: 5 -> 5, of which waited for: 4 -> 4; matrix products, arithmetic and copies ran while one was open for 5% -> 9% of each run, Pallas kernels for 0% -> 0%
where the time goes in v16:
time: 80.8 us; the launch traced here: 80.3 us
  starting transfers between devices  29.4 us (36%)
  waiting for transfers between devices  24.5 us (30%)
  matrix products  14.1 us (17%)
  local copies, waits for them, and re-layouts  6.2 us (8%)
  other arithmetic  5.89 us (7%)
    all_to_all x1, starting transfers between devices, local(): lax.all_to_all(product, 'seq', split_axis=0, concat_axis=1, tiled=True)  12.8 us
    all_to_all x1, waiting for transfers between devices, local(): lax.all_to_all(convolved, 'seq', split_axis=1, concat_axis=0, tiled=True)  11 us
    ppermute x1, waiting for transfers between devices, reduce_scatter_chan(): got2 = lax.ppermute(send2, 'chan', [(j, j ^ 2) for j in range(4)])  6.42 us
    all_to_all x1, waiting for transfers between devices, local(): lax.all_to_all(product, 'seq', split_axis=0, concat_axis=1, tiled=True)  5.61 us
    dot_general x1, matrix products, modal_conv(): jnp.einsum('rcj,rct->cjt', rising, falling, precision=lax.Precision.HIGHEST)  5.3 us
    all_to_all x1, starting transfers between devices, local(): lax.all_to_all(convolved, 'seq', split_axis=1, concat_axis=0, tiled=True)  5.13 us
    dot_general x1, matrix products, local(): lax.dot_general(gated_rows, out_weight, (((0,), (0,)), ((), ())), preferr...  4.67 us
    ppermute x1, starting transfers between devices, reduce_scatter_chan(): got = lax.ppermute(send, 'chan', [(j, j ^ 1) for j in range(4)])  4.42 us
  transfers between devices with their start and end apart: 5, of which 4 were waited for; matrix products, arithmetic and copies ran while one was open for 9% of the time, Pallas kernels for 0%

profile of v16, /device:TPU:1, one launch (start us, length us, event | category | flops | bytes accessed | tf_op | source)
XLA Modules:
  0.0 80.3 jit_solution(15560309006483604833)
XLA Ops:
  0.0 0.0 copy-start
  0.0 1.5 %slice.51 = bf16[3,1024,2]{2,1,0:T(8,128)(2,1)S(1)} slice(bf16[3,1024,128]{2,1,0:T(8,128)(2,1)} %param.5), slice={[0:3], [0:1024], [126:128]} | slice | bytes 24576 | tf_op jit(solution)/shard_map/slice | solution.py:63
  1.5 0.4 copy.36
  1.9 4.4 %collective-permute-start = (bf16[3,1024,2]{1,0,2:T(4,128)(2,1)S(1)}, bf16[3,1024,2]{1,0,2:T(4,128)(2,1)S(1)}, u32[]{:S(2)}, u32[]{:S(2)}) collective-permute-start(bf16[3,1024,2]{1,0,2:T(4,128)(2,1)S(1)} %copy.36), channel_id=1, source_target_pairs={{0,4},{4,8},{8,12},{12,16},{16,20},{20,24},{24,28},{28,32},{32,36}... | collective-permute-start | bytes 36872 | tf_op jit(solution)/shard_map/ppermute | solution.py:10
  6.3 0.9 %fusion.39 = (f32[3,1,1024]{2,1,0:T(1,128)S(1)}, f32[3,1,1024]{2,1,0:T(1,128)S(1)}, f32[3,1,1024]{2,1,0:T(1,128)S(1)}) fusion(f32[3,3,1024]{2,1,0:T(4,128)} %param.6), kind=kLoop, calls=%fused_computation.66 | loop fusion | bytes 73728 | tf_op jit(solution)/shard_map/slice | solution.py:67
  7.3 0.8 constant_dynamic-slice_fusion
  8.1 0.1 copy.28
  8.2 0.1 copy.27
  8.3 0.0 collective-permute-done
  8.3 0.4 copy.25
  8.7 0.0 copy-done
  8.7 0.6 maximum_convert_fusion
  9.3 2.4 %fusion.7 = f32[3,1024,128]{2,1,0:T(8,128)S(1)} fusion(f32[3,1024,130]{2,1,0:T(8,128)S(1)} %maximum_convert_fusion, f32[3,1024]{1,0:T(4,128)S(1)} %get-tuple-element.12, f32[3,1024]{1,0:T(4,128)S(1)} %get-tuple-element.13, f32[3,1024]{1,0:T(4,128)S(1)} %bitcast.44), kind=kLoop, calls=%fused_computation.10 | loop fusion | flops 1966080 | bytes 6328320 | tf_op jit(solution)/shard_map/add | solution.py:67
  11.7 0.8 fusion.15
  12.4 12.8 %all-to-all-start = ((bf16[64,16,128]{2,1,0:T(8,128)(2,1)}), bf16[64,16,128]{2,1,0:T(8,128)(2,1)S(1)}, u32[]{:S(2)}, u32[]{:S(2)}) async-start(bf16[64,16,128]{2,1,0:T(8,128)(2,1)} %bitcast.1), calls=%async_computation | async-start | bytes 524288 | tf_op jit(solution)/shard_map/all_to_all | solution.py:74
  25.2 0.1 convert_multiply_fusion
  25.3 5.3 %fusion.22 = f32[16,256,256]{2,1,0:T(8,128)} fusion(f32[256]{0:T(256)S(1)} %get-tuple-element.17, f32[16,16]{0,1:T(8,128)S(1)} %copy.28, f32[256]{0:T(256)S(1)} %get-tuple-element.16, f32[16,16]{0,1:T(8,128)S(1)} %copy.27), kind=kOutput, calls=%fused_computation.33 | convolution fusion | flops 201523200 | bytes 4198400 | tf_op jit(solution)/shard_map/rcj,rct->cjt/dot_general | solution.py:22
  30.6 5.6 %all-to-all-done = bf16[64,16,128]{2,1,0:T(8,128)(2,1)S(1)} async-done(((bf16[64,16,128]{2,1,0:T(8,128)(2,1)}), bf16[64,16,128]{2,1,0:T(8,128)(2,1)S(1)}, u32[]{:S(2)}, u32[]{:S(2)}) %all-to-all-start) | async-done | bytes 262176 | tf_op jit(solution)/shard_map/all_to_all | solution.py:74
  36.2 0.1 copy.26
  36.3 0.1 reshape.103
  36.4 0.3 convolution_bitcast_fusion
  36.7 1.6 %fusion.2 = f32[16,16,32]{2,1,0:T(8,128)S(1)} fusion(f32[16,16,32]{2,1,0:T(8,128)S(1)} %copy.29, f32[16,16]{1,0:T(8,128)S(1)} %get-tuple-element.14, f32[32,32]{1,0:T(8,128)S(1)} %convert_multiply_fusion, pred[32,32]{1,0:T(8,128)(4,1)S(1)} %iota_compare_fusion), kind=kLoop, calls=%fused_computation.4 | loop fusion | flops 1040384 | bytes 71680 | tf_op jit(solution)/shard_map/reduce_sum | solution.py:37
  38.3 0.5 fusion.20
  38.9 3.2 %fusion.12 = bf16[16,32,256]{2,1,0:T(8,128)(2,1)S(1)} fusion(f32[16,32,256]{2,1,0:T(8,128)S(1)} %fusion.20, bf16[16,32,256]{2,1,0:T(8,128)(2,1)S(1)} %reshape.103, f32[16,256,256]{2,1,0:T(8,128)} %fusion.22, pred[256,256]{1,0:T(8,128)(4,1)S(1)} %subtract_compare_fusion), kind=kOutput, calls=%fused_computation.16 | convolution fusion | flops 202637312 | bytes 5308416 | tf_op jit(solution)/shard_map/cnj,cjt->cnt/dot_general | solution.py:27
  42.1 0.1 convert_element_type.86
  42.2 0.9 %copy.31 = bf16[16,64,128]{2,0,1:T(8,128)(2,1)} copy(bf16[16,64,128]{2,1,0:T(8,128)(2,1)S(1)} %convert_element_type.86) | data formatting | bytes 524288 | tf_op jit(solution)/shard_map/convert_element_type | solution.py:78
  43.1 5.1 %all-to-all-start.1 = ((bf16[16,64,128]{2,0,1:T(8,128)(2,1)}), bf16[16,64,128]{2,0,1:T(8,128)(2,1)S(1)}, u32[]{:S(2)}, u32[]{:S(2)}) async-start(bf16[16,64,128]{2,0,1:T(8,128)(2,1)} %copy.31), calls=%async_computation.1 | async-start | bytes 524288 | tf_op jit(solution)/shard_map/all_to_all | solution.py:79
  48.2 11.0 %all-to-all-done.1 = bf16[16,64,128]{2,0,1:T(8,128)(2,1)S(1)} async-done(((bf16[16,64,128]{2,0,1:T(8,128)(2,1)}), bf16[16,64,128]{2,0,1:T(8,128)(2,1)S(1)}, u32[]{:S(2)}, u32[]{:S(2)}) %all-to-all-start.1) | async-done | bytes 262176 | tf_op jit(solution)/shard_map/all_to_all | solution.py:79
  59.2 0.1 fusion.17
  59.3 4.7 %convolution_convert_fusion = bf16[128,4096]{1,0:T(8,128)(2,1)S(1)} fusion(bf16[1024,128]{1,0:T(8,128)(2,1)S(1)} %fusion.17, bf16[1024,4096]{1,0:T(8,128)(2,1)} %param.9), kind=kOutput, calls=%fused_computation | convolution fusion | flops 1074266112 | bytes 9699328 | tf_op jit(solution)/shard_map/dot_general | solution.py:81
  64.0 0.1 select_bitcast_fusion.3
  64.0 0.1 pad_maximum_fusion
  64.1 4.4 %collective-permute-start.1 = (bf16[2,128,1024]{2,1,0:T(8,128)(2,1)S(1)}, bf16[2,128,1024]{2,1,0:T(8,128)(2,1)S(1)}, u32[]{:S(2)}, u32[]{:S(2)}) collective-permute-start(bf16[2,128,1024]{2,1,0:T(8,128)(2,1)S(1)} %pad_maximum_fusion), channel_id=1, source_target_pairs={{0,1},{1,0},{2,3},{3,2},{4,5},{5,4},{6,7},{7,6},{8,9},{9,8},{10,11... | collective-permute-start | bytes 1572872 | tf_op jit(solution)/shard_map/ppermute | solution.py:51
  68.5 1.5 %collective-permute-done.1 = bf16[2,128,1024]{2,1,0:T(8,128)(2,1)S(1)} collective-permute-done((bf16[2,128,1024]{2,1,0:T(8,128)(2,1)S(1)}, bf16[2,128,1024]{2,1,0:T(8,128)(2,1)S(1)}, u32[]{:S(2)}, u32[]{:S(2)}) %collective-permute-start.1) | collective-permute-done | bytes 524320 | tf_op jit(solution)/shard_map/ppermute | solution.py:51
  70.1 0.2 convert_add_fusion
  70.2 0.1 fusion.25
  70.3 2.7 %collective-permute-start.2 = (bf16[128,1024]{1,0:T(8,128)(2,1)S(1)}, bf16[128,1024]{1,0:T(8,128)(2,1)S(1)}, u32[]{:S(2)}, u32[]{:S(2)}) collective-permute-start(bf16[128,1024]{1,0:T(8,128)(2,1)S(1)} %fusion.25), channel_id=1, source_target_pairs={{0,2},{1,3},{2,0},{3,1},{4,6},{5,7},{6,4},{7,5},{8,10},{9,11},{10,... | collective-permute-start | bytes 786440 | tf_op jit(solution)/shard_map/ppermute | solution.py:56
  73.0 6.4 %collective-permute-done.2 = bf16[128,1024]{1,0:T(8,128)(2,1)S(1)} collective-permute-done((bf16[128,1024]{1,0:T(8,128)(2,1)S(1)}, bf16[128,1024]{1,0:T(8,128)(2,1)S(1)}, u32[]{:S(2)}, u32[]{:S(2)}) %collective-permute-start.2) | collective-permute-done | bytes 262176 | tf_op jit(solution)/shard_map/ppermute | solution.py:56
  79.4 0.1 fusion.26
  79.5 0.8 %copy.32 = bf16[1024,128]{1,0:T(8,128)(2,1)} copy(bf16[1024,128]{0,1:T(8,128)(2,1)S(1)} %fusion.26) | data formatting | bytes 524288 | tf_op jit(solution)/shard_map/transpose | solution.py:57
  (9 shorter events, 0.1 us)
Async XLA Ops:
  0.0 8.7 %copy-start = (bf16[3,1024,128]{2,1,0:T(8,128)(2,1)S(1)}, bf16[3,1024,128]{2,1,0:T(8,128)(2,1)}, u32[]{:S(2)}) copy-start(bf16[3,1024,128]{2,1,0:T(8,128)(2,1)} %param.5) | copy-start | bytes 2359300
  1.9 6.4 %collective-permute-start = (bf16[3,1024,2]{1,0,2:T(4,128)(2,1)S(1)}, bf16[3,1024,2]{1,0,2:T(4,128)(2,1)S(1)}, u32[]{:S(2)}, u32[]{:S(2)}) collective-permute-start(bf16[3,1024,2]{1,0,2:T(4,128)(2,1)S(1)} %copy.36), channel_id=1, source_target_pairs={{0,4},{4,8},{8,12},{12,16},{16,20},{20,24},{24,28},{28,32},{32,36}... | collective-permute-start | bytes 36872 | tf_op jit(solution)/shard_map/ppermute | solution.py:10
  12.4 23.8 %all-to-all-start = ((bf16[64,16,128]{2,1,0:T(8,128)(2,1)}), bf16[64,16,128]{2,1,0:T(8,128)(2,1)S(1)}, u32[]{:S(2)}, u32[]{:S(2)}) async-start(bf16[64,16,128]{2,1,0:T(8,128)(2,1)} %bitcast.1), calls=%async_computation | async-start | bytes 524288 | tf_op jit(solution)/shard_map/all_to_all | solution.py:74
  43.1 16.1 %all-to-all-start.1 = ((bf16[16,64,128]{2,0,1:T(8,128)(2,1)}), bf16[16,64,128]{2,0,1:T(8,128)(2,1)S(1)}, u32[]{:S(2)}, u32[]{:S(2)}) async-start(bf16[16,64,128]{2,0,1:T(8,128)(2,1)} %copy.31), calls=%async_computation.1 | async-start | bytes 524288 | tf_op jit(solution)/shard_map/all_to_all | solution.py:79
  64.1 6.0 %collective-permute-start.1 = (bf16[2,128,1024]{2,1,0:T(8,128)(2,1)S(1)}, bf16[2,128,1024]{2,1,0:T(8,128)(2,1)S(1)}, u32[]{:S(2)}, u32[]{:S(2)}) collective-permute-start(bf16[2,128,1024]{2,1,0:T(8,128)(2,1)S(1)} %pad_maximum_fusion), channel_id=1, source_target_pairs={{0,1},{1,0},{2,3},{3,2},{4,5},{5,4},{6,7},{7,6},{8,9},{9,8},{10,11... | collective-permute-start | bytes 1572872 | tf_op jit(solution)/shard_map/ppermute | solution.py:51
  70.3 9.1 %collective-permute-start.2 = (bf16[128,1024]{1,0:T(8,128)(2,1)S(1)}, bf16[128,1024]{1,0:T(8,128)(2,1)S(1)}, u32[]{:S(2)}, u32[]{:S(2)}) collective-permute-start(bf16[128,1024]{1,0:T(8,128)(2,1)S(1)} %fusion.25), channel_id=1, source_target_pairs={{0,2},{1,3},{2,0},{3,1},{4,6},{5,7},{6,4},{7,5},{8,10},{9,11},{10,... | collective-permute-start | bytes 786440 | tf_op jit(solution)/shard_map/ppermute | solution.py:56

commit v17 on v6

--- a/solution.py
+++ b/solution.py
@@ -34,7 +34,8 @@
         -float(block) * gap[None, None] / life[..., None],
         -jnp.inf,
     )
-    entering = jnp.sum(jnp.exp(exponent) * leaving[:, :, None, :], axis=-1)
+    decays = lax.optimization_barrier(jnp.exp(exponent))
+    entering = jnp.sum(decays * leaving[:, :, None, :], axis=-1)
     from_start = resid * jnp.exp(-(steps + 1.0)[None, None, :] / life)
     carried = jnp.einsum("rcn,rct->cnt", entering, from_start, precision=precise)
     return (inside + carried).reshape(chan_here, length)

time: 78.8 us -> 85 us (1.079)
  other arithmetic: 6.96 us -> 13.9 us
  starting transfers between devices: 29.4 us -> 28.5 us
    exp x0 -> x1, other arithmetic: none -> 3.93 us  [modal_conv(): decays = lax.optimization_barrier(jnp.exp(exponent))]
    reduce_sum x1, other arithmetic: 2.64 us -> 5.66 us  [modal_conv(): entering = jnp.sum(decays * leaving[:, :, None, :], axis=-1)]
    all_to_all x1, starting transfers between devices: 12.9 us -> 11.8 us  [local(): lax.all_to_all(product, 'seq', split_axis=0, concat_axis=1, tiled=True)]
    all_to_all x1, starting transfers between devices: 4.85 us -> 5.94 us  [local(): lax.all_to_all(convolved, 'seq', split_axis=1, concat_axis=0, tiled=True)]
    ppermute x1, starting transfers between devices: 4.63 us -> 3.71 us  [reduce_scatter_chan(): got = lax.ppermute(send, 'chan', [(j, j ^ 1) for j in range(4)])]
  transfers between devices with their start and end apart: 5 -> 5, of which waited for: 4 -> 4; matrix products, arithmetic and copies ran while one was open for 5% -> 9% of each run, Pallas kernels for 0% -> 0%
where the time goes in v17:
time: 85 us; the launch traced here: 84.6 us
  starting transfers between devices  28.5 us (34%)
  waiting for transfers between devices  28 us (33%)
  other arithmetic  13.9 us (16%)
  matrix products  8.17 us (10%)
  local copies, waits for them, and re-layouts  5.81 us (7%)
    all_to_all x1, starting transfers between devices, local(): lax.all_to_all(product, 'seq', split_axis=0, concat_axis=1, tiled=True)  11.8 us
    all_to_all x1, waiting for transfers between devices, local(): lax.all_to_all(convolved, 'seq', split_axis=1, concat_axis=0, tiled=True)  10.8 us
    all_to_all x1, waiting for transfers between devices, local(): lax.all_to_all(product, 'seq', split_axis=0, concat_axis=1, tiled=True)  9.29 us
    ppermute x1, waiting for transfers between devices, reduce_scatter_chan(): got2 = lax.ppermute(send2, 'chan', [(j, j ^ 2) for j in range(4)])  6.38 us
    all_to_all x1, starting transfers between devices, local(): lax.all_to_all(convolved, 'seq', split_axis=1, concat_axis=0, tiled=True)  5.94 us
    reduce_sum x1, other arithmetic, modal_conv(): entering = jnp.sum(decays * leaving[:, :, None, :], axis=-1)  5.66 us
    dot_general x1, matrix products, local(): lax.dot_general(gated_rows, out_weight, (((0,), (0,)), ((), ())), preferr...  4.67 us
    ppermute x1, starting transfers between devices, from_behind(): return lax.ppermute(x, axis, pairs)  4.36 us
  transfers between devices with their start and end apart: 5, of which 4 were waited for; matrix products, arithmetic and copies ran while one was open for 9% of the time, Pallas kernels for 0%

profile of v17, /device:TPU:1, one launch (start us, length us, event | category | flops | bytes accessed | tf_op | source)
XLA Modules:
  0.0 84.6 jit_solution(13043567264813325347)
XLA Ops:
  0.0 1.4 %slice.51 = bf16[3,1024,2]{2,1,0:T(8,128)(2,1)S(1)} slice(bf16[3,1024,128]{2,1,0:T(8,128)(2,1)} %param.5), slice={[0:3], [0:1024], [126:128]} | slice | bytes 24576 | tf_op jit(solution)/shard_map/slice | solution.py:64
  1.4 0.3 copy.34
  1.7 4.4 %collective-permute-start = (bf16[3,1024,2]{1,2,0:T(2,128)(2,1)S(1)}, bf16[3,1024,2]{1,2,0:T(2,128)(2,1)S(1)}, u32[]{:S(2)}, u32[]{:S(2)}) collective-permute-start(bf16[3,1024,2]{1,2,0:T(2,128)(2,1)S(1)} %copy.34), channel_id=1, source_target_pairs={{0,4},{4,8},{8,12},{12,16},{16,20},{20,24},{24,28},{28,32},{32,36}... | collective-permute-start | bytes 36872 | tf_op jit(solution)/shard_map/ppermute | solution.py:10
  6.1 0.9 %fusion.30 = (f32[3,1,1024]{2,1,0:T(1,128)S(1)}, f32[3,1,1024]{2,1,0:T(1,128)S(1)}, f32[3,1,1024]{2,1,0:T(1,128)S(1)}) fusion(f32[3,3,1024]{2,1,0:T(4,128)} %param.6), kind=kLoop, calls=%fused_computation.64 | loop fusion | bytes 73728 | tf_op jit(solution)/shard_map/slice | solution.py:68
  7.1 0.1 convert_multiply_fusion
  7.2 0.8 constant_dynamic-slice_fusion
  8.0 0.0 copy-start
  8.0 3.9 %fusion = f32[16,16,64,64]{3,2,1,0:T(8,128)} fusion(f32[16,16]{1,0:T(8,128)S(1)} %get-tuple-element.14, f32[64,64]{1,0:T(8,128)S(1)} %convert_multiply_fusion, pred[64,64]{1,0:T(8,128)(4,1)S(1)} %iota_compare_fusion), kind=kLoop, calls=%fused_computation.1 | loop fusion | flops 2097152 | bytes 4215808 | tf_op jit(solution)/shard_map/exp | solution.py:37
  11.9 0.0 collective-permute-done
  11.9 0.4 copy.23
  12.3 0.0 copy-done
  12.4 0.6 maximum_convert_fusion
  13.0 2.4 %fusion.1 = f32[3,1024,128]{2,1,0:T(8,128)S(1)} fusion(f32[3,1024,130]{2,1,0:T(8,128)S(1)} %maximum_convert_fusion, f32[3,1024]{1,0:T(4,128)S(1)} %get-tuple-element.12, f32[3,1024]{1,0:T(4,128)S(1)} %get-tuple-element.13, f32[3,1024]{1,0:T(4,128)S(1)} %bitcast.46), kind=kLoop, calls=%fused_computation.5 | loop fusion | flops 1966080 | bytes 6328320 | tf_op jit(solution)/shard_map/add | solution.py:68
  15.3 0.8 fusion.4
  16.1 11.8 %all-to-all-start = ((bf16[64,16,128]{2,1,0:T(8,128)(2,1)}), bf16[64,16,128]{2,1,0:T(8,128)(2,1)S(1)}, u32[]{:S(2)}, u32[]{:S(2)}) async-start(bf16[64,16,128]{2,1,0:T(8,128)(2,1)} %bitcast.1), calls=%async_computation | async-start | bytes 524288 | tf_op jit(solution)/shard_map/all_to_all | solution.py:75
  27.9 0.1 copy.26
  27.9 0.1 copy.25
  28.0 1.9 %convolution_select_fusion = f32[16,128,128]{2,1,0:T(8,128)S(1)} fusion(pred[128,128]{1,0:T(8,128)(4,1)S(1)} %subtract_compare_fusion, f32[128]{0:T(128)S(1)} %get-tuple-element.17, f32[16,16]{0,1:T(8,128)S(1)} %copy.26, f32[128]{0:T(128)S(1)} %get-tuple-element.16, f32[16,16]{0,1:T(8,128)S(1)} %copy.25), kind=kOutput, calls=%fused_computation.10 | convolution fusion | flops 50692096 | bytes 1068032 | tf_op jit(solution)/shard_map/rcj,rct->cjt/dot_general | solution.py:22
  30.0 9.3 %all-to-all-done = bf16[64,16,128]{2,1,0:T(8,128)(2,1)S(1)} async-done(((bf16[64,16,128]{2,1,0:T(8,128)(2,1)}), bf16[64,16,128]{2,1,0:T(8,128)(2,1)S(1)}, u32[]{:S(2)}, u32[]{:S(2)}) %all-to-all-start) | async-done | bytes 262176 | tf_op jit(solution)/shard_map/all_to_all | solution.py:75
  39.3 0.4 convolution_bitcast_fusion
  39.8 5.7 %multiply_reduce_fusion = f32[16,16,64]{2,1,0:T(8,128)S(1)} fusion(f32[16,16,64,64]{3,2,1,0:T(8,128)} %fusion, f32[16,16,64]{2,1,0:T(8,128)S(1)} %copy.27), kind=kLoop, calls=%fused_computation.2 | loop fusion | flops 2080768 | bytes 4325376 | tf_op jit(solution)/shard_map/reduce_sum | solution.py:38
  45.4 0.7 fusion.15
  46.1 0.4 fusion.3
  46.5 0.9 %copy.29 = bf16[16,64,128]{2,0,1:T(8,128)(2,1)} copy(bf16[16,64,128]{2,1,0:T(8,128)(2,1)S(1)} %fusion.3) | data formatting | bytes 524288 | tf_op jit(solution)/shard_map/convert_element_type | solution.py:79
  47.4 5.9 %all-to-all-start.1 = ((bf16[16,64,128]{2,0,1:T(8,128)(2,1)}), bf16[16,64,128]{2,0,1:T(8,128)(2,1)S(1)}, u32[]{:S(2)}, u32[]{:S(2)}) async-start(bf16[16,64,128]{2,0,1:T(8,128)(2,1)} %copy.29), calls=%async_computation.1 | async-start | bytes 524288 | tf_op jit(solution)/shard_map/all_to_all | solution.py:80
  53.4 10.8 %all-to-all-done.1 = bf16[16,64,128]{2,0,1:T(8,128)(2,1)S(1)} async-done(((bf16[16,64,128]{2,0,1:T(8,128)(2,1)}), bf16[16,64,128]{2,0,1:T(8,128)(2,1)S(1)}, u32[]{:S(2)}, u32[]{:S(2)}) %all-to-all-start.1) | async-done | bytes 262176 | tf_op jit(solution)/shard_map/all_to_all | solution.py:80
  64.2 0.1 fusion.6
  64.2 4.7 %convolution_convert_fusion = bf16[128,4096]{1,0:T(8,128)(2,1)S(1)} fusion(bf16[1024,128]{1,0:T(8,128)(2,1)S(1)} %fusion.6, bf16[1024,4096]{1,0:T(8,128)(2,1)} %param.9), kind=kOutput, calls=%fused_computation.3 | convolution fusion | flops 1074266112 | bytes 9699328 | tf_op jit(solution)/shard_map/dot_general | solution.py:82
  68.9 0.1 select_bitcast_fusion.3
  69.0 0.1 pad_maximum_fusion
  69.1 3.7 %collective-permute-start.1 = (bf16[2,128,1024]{2,1,0:T(8,128)(2,1)S(1)}, bf16[2,128,1024]{2,1,0:T(8,128)(2,1)S(1)}, u32[]{:S(2)}, u32[]{:S(2)}) collective-permute-start(bf16[2,128,1024]{2,1,0:T(8,128)(2,1)S(1)} %pad_maximum_fusion), channel_id=1, source_target_pairs={{0,1},{1,0},{2,3},{3,2},{4,5},{5,4},{6,7},{7,6},{8,9},{9,8},{10,11... | collective-permute-start | bytes 1572872 | tf_op jit(solution)/shard_map/ppermute | solution.py:52
  72.8 1.5 %collective-permute-done.1 = bf16[2,128,1024]{2,1,0:T(8,128)(2,1)S(1)} collective-permute-done((bf16[2,128,1024]{2,1,0:T(8,128)(2,1)S(1)}, bf16[2,128,1024]{2,1,0:T(8,128)(2,1)S(1)}, u32[]{:S(2)}, u32[]{:S(2)}) %collective-permute-start.1) | collective-permute-done | bytes 524320 | tf_op jit(solution)/shard_map/ppermute | solution.py:52
  74.3 0.2 convert_add_fusion
  74.5 0.1 fusion.8
  74.5 2.7 %collective-permute-start.2 = (bf16[128,1024]{1,0:T(8,128)(2,1)S(1)}, bf16[128,1024]{1,0:T(8,128)(2,1)S(1)}, u32[]{:S(2)}, u32[]{:S(2)}) collective-permute-start(bf16[128,1024]{1,0:T(8,128)(2,1)S(1)} %fusion.8), channel_id=1, source_target_pairs={{0,2},{1,3},{2,0},{3,1},{4,6},{5,7},{6,4},{7,5},{8,10},{9,11},{10,... | collective-permute-start | bytes 786440 | tf_op jit(solution)/shard_map/ppermute | solution.py:57
  77.3 6.4 %collective-permute-done.2 = bf16[128,1024]{1,0:T(8,128)(2,1)S(1)} collective-permute-done((bf16[128,1024]{1,0:T(8,128)(2,1)S(1)}, bf16[128,1024]{1,0:T(8,128)(2,1)S(1)}, u32[]{:S(2)}, u32[]{:S(2)}) %collective-permute-start.2) | collective-permute-done | bytes 262176 | tf_op jit(solution)/shard_map/ppermute | solution.py:57
  83.6 0.1 fusion.9
  83.7 0.8 copy.30
  (9 shorter events, 0.1 us)
Async XLA Ops:
  1.7 10.2 %collective-permute-start = (bf16[3,1024,2]{1,2,0:T(2,128)(2,1)S(1)}, bf16[3,1024,2]{1,2,0:T(2,128)(2,1)S(1)}, u32[]{:S(2)}, u32[]{:S(2)}) collective-permute-start(bf16[3,1024,2]{1,2,0:T(2,128)(2,1)S(1)} %copy.34), channel_id=1, source_target_pairs={{0,4},{4,8},{8,12},{12,16},{16,20},{20,24},{24,28},{28,32},{32,36}... | collective-permute-start | bytes 36872 | tf_op jit(solution)/shard_map/ppermute | solution.py:10
  8.0 4.4 %copy-start = (bf16[3,1024,128]{2,1,0:T(8,128)(2,1)S(1)}, bf16[3,1024,128]{2,1,0:T(8,128)(2,1)}, u32[]{:S(2)}) copy-start(bf16[3,1024,128]{2,1,0:T(8,128)(2,1)} %param.5) | copy-start | bytes 2359300
  16.1 23.2 %all-to-all-start = ((bf16[64,16,128]{2,1,0:T(8,128)(2,1)}), bf16[64,16,128]{2,1,0:T(8,128)(2,1)S(1)}, u32[]{:S(2)}, u32[]{:S(2)}) async-start(bf16[64,16,128]{2,1,0:T(8,128)(2,1)} %bitcast.1), calls=%async_computation | async-start | bytes 524288 | tf_op jit(solution)/shard_map/all_to_all | solution.py:75
  47.4 16.8 %all-to-all-start.1 = ((bf16[16,64,128]{2,0,1:T(8,128)(2,1)}), bf16[16,64,128]{2,0,1:T(8,128)(2,1)S(1)}, u32[]{:S(2)}, u32[]{:S(2)}) async-start(bf16[16,64,128]{2,0,1:T(8,128)(2,1)} %copy.29), calls=%async_computation.1 | async-start | bytes 524288 | tf_op jit(solution)/shard_map/all_to_all | solution.py:80
  69.1 5.2 %collective-permute-start.1 = (bf16[2,128,1024]{2,1,0:T(8,128)(2,1)S(1)}, bf16[2,128,1024]{2,1,0:T(8,128)(2,1)S(1)}, u32[]{:S(2)}, u32[]{:S(2)}) collective-permute-start(bf16[2,128,1024]{2,1,0:T(8,128)(2,1)S(1)} %pad_maximum_fusion), channel_id=1, source_target_pairs={{0,1},{1,0},{2,3},{3,2},{4,5},{5,4},{6,7},{7,6},{8,9},{9,8},{10,11... | collective-permute-start | bytes 1572872 | tf_op jit(solution)/shard_map/ppermute | solution.py:52
  74.5 9.1 %collective-permute-start.2 = (bf16[128,1024]{1,0:T(8,128)(2,1)S(1)}, bf16[128,1024]{1,0:T(8,128)(2,1)S(1)}, u32[]{:S(2)}, u32[]{:S(2)}) collective-permute-start(bf16[128,1024]{1,0:T(8,128)(2,1)S(1)} %fusion.8), channel_id=1, source_target_pairs={{0,2},{1,3},{2,0},{3,1},{4,6},{5,7},{6,4},{7,5},{8,10},{9,11},{10,... | collective-permute-start | bytes 786440 | tf_op jit(solution)/shard_map/ppermute | solution.py:57

commit v18 on v6

--- a/solution.py
+++ b/solution.py
@@ -61,7 +61,9 @@
     chan_local = qkv.shape[1]
     tok_count = qkv.shape[2]
     edge_block = qkv[:, :, tok_count - 2 :]
-    earlier = from_behind(edge_block, "seq", 1)
+    devices = lax.axis_size("seq")
+    wrapped = lax.ppermute(edge_block, "seq", [(i, (i + 1) % devices) for i in range(devices)])
+    earlier = jnp.where(lax.axis_index("seq") == 0, jnp.zeros_like(wrapped), wrapped)
     extended = jnp.concatenate([earlier, qkv], axis=2).astype(jnp.float32)
     filtered = (
         taps[:, 0, :, None] * extended[:, :, 2:]

time: 78.8 us -> 77 us (0.977)
  starting transfers between devices: 29.4 us -> 21.3 us
  waiting for transfers between devices: 27.7 us -> 34.1 us
    ppermute x1, waiting for transfers between devices: 0.01 us -> 6.39 us  [local(): lax.ppermute(edge_block, 'seq', [(i, (i + 1) % devices) for i in range(de...]
    all_to_all x1, starting transfers between devices: 12.9 us -> 6.56 us  [local(): lax.all_to_all(product, 'seq', split_axis=0, concat_axis=1, tiled=True)]
    ppermute x1, starting transfers between devices: 4.36 us -> 2.51 us  [local(): lax.ppermute(edge_block, 'seq', [(i, (i + 1) % devices) for i in range(de...]
  transfers between devices with their start and end apart: 5 -> 5, of which waited for: 4 -> 5; matrix products, arithmetic and copies ran while one was open for 5% -> 5% of each run, Pallas kernels for 0% -> 0%
where the time goes in v18:
time: 77 us; the launch traced here: 76.6 us
  waiting for transfers between devices  34.1 us (44%)
  starting transfers between devices  21.3 us (28%)
  matrix products  8.18 us (11%)
  other arithmetic  6.97 us (9%)
  local copies, waits for them, and re-layouts  5.87 us (8%)
    all_to_all x1, waiting for transfers between devices, local(): lax.all_to_all(convolved, 'seq', split_axis=1, concat_axis=0, tiled=True)  11 us
    all_to_all x1, waiting for transfers between devices, local(): lax.all_to_all(product, 'seq', split_axis=0, concat_axis=1, tiled=True)  8.82 us
    all_to_all x1, starting transfers between devices, local(): lax.all_to_all(product, 'seq', split_axis=0, concat_axis=1, tiled=True)  6.56 us
    ppermute x1, waiting for transfers between devices, local(): lax.ppermute(edge_block, 'seq', [(i, (i + 1) % devices) for i in range(de...  6.39 us
    ppermute x1, waiting for transfers between devices, reduce_scatter_chan(): got2 = lax.ppermute(send2, 'chan', [(j, j ^ 2) for j in range(4)])  6.37 us
    all_to_all x1, starting transfers between devices, local(): lax.all_to_all(convolved, 'seq', split_axis=1, concat_axis=0, tiled=True)  4.85 us
    dot_general x1, matrix products, local(): lax.dot_general(gated_rows, out_weight, (((0,), (0,)), ((), ())), preferr...  4.68 us
    ppermute x1, starting transfers between devices, reduce_scatter_chan(): got = lax.ppermute(send, 'chan', [(j, j ^ 1) for j in range(4)])  4.62 us
  transfers between devices with their start and end apart: 5, of which 5 were waited for; matrix products, arithmetic and copies ran while one was open for 5% of the time, Pallas kernels for 0%

profile of v18, /device:TPU:1, one launch (start us, length us, event | category | flops | bytes accessed | tf_op | source)
XLA Modules:
  0.0 76.6 jit_solution(18355769512094251003)
XLA Ops:
  0.0 0.0 copy-start
  0.0 1.5 %slice.51 = bf16[3,1024,2]{2,1,0:T(8,128)(2,1)S(1)} slice(bf16[3,1024,128]{2,1,0:T(8,128)(2,1)} %param.5), slice={[0:3], [0:1024], [126:128]} | slice | bytes 24576 | tf_op jit(solution)/shard_map/slice | solution.py:63
  1.5 0.3 copy.49
  1.8 2.5 %collective-permute-start = (bf16[3,1024,2]{1,2,0:T(2,128)(2,1)S(1)}, bf16[3,1024,2]{1,2,0:T(2,128)(2,1)S(1)}, u32[]{:S(2)}, u32[]{:S(2)}) collective-permute-start(bf16[3,1024,2]{1,2,0:T(2,128)(2,1)S(1)} %copy.49), channel_id=1, source_target_pairs={{0,4},{4,8},{8,12},{12,16},{16,20},{20,24},{24,28},{28,32},{32,36}... | collective-permute-start | bytes 36872 | tf_op jit(solution)/shard_map/ppermute | solution.py:65
  4.4 0.9 %fusion.32 = (f32[3,1,1024]{2,1,0:T(1,128)S(1)}, f32[3,1,1024]{2,1,0:T(1,128)S(1)}, f32[3,1,1024]{2,1,0:T(1,128)S(1)}) fusion(f32[3,3,1024]{2,1,0:T(4,128)} %param.6), kind=kLoop, calls=%fused_computation.66 | loop fusion | bytes 73728 | tf_op jit(solution)/shard_map/slice | solution.py:69
  5.3 0.8 %constant_dynamic-slice_fusion = (f32[16,16]{1,0:T(8,128)S(1)}, f32[16,16]{1,0:T(8,128)S(1)}) fusion(f32[16,1024]{1,0:T(8,128)} %param.7, s32[]{:T(128)S(6)} %select_n.73, f32[16,1024]{1,0:T(8,128)} %param.8), kind=kLoop, calls=%fused_computation.63 | loop fusion | bytes 4100 | tf_op jit(solution)/shard_map/dynamic_slice | solution.py:78
  6.1 6.4 %collective-permute-done = bf16[3,1024,2]{1,2,0:T(2,128)(2,1)S(1)} collective-permute-done((bf16[3,1024,2]{1,2,0:T(2,128)(2,1)S(1)}, bf16[3,1024,2]{1,2,0:T(2,128)(2,1)S(1)}, u32[]{:S(2)}, u32[]{:S(2)}) %collective-permute-start) | collective-permute-done | bytes 12320 | tf_op jit(solution)/shard_map/ppermute | solution.py:65
  12.6 0.4 copy.38
  13.0 0.0 copy-done
  13.0 0.6 maximum_convert_fusion
  13.6 2.4 %fusion.3 = f32[3,1024,128]{2,1,0:T(8,128)S(1)} fusion(f32[3,1024,130]{2,1,0:T(8,128)S(1)} %maximum_convert_fusion, f32[3,1024]{1,0:T(4,128)S(1)} %get-tuple-element.12, f32[3,1024]{1,0:T(4,128)S(1)} %get-tuple-element.13, f32[3,1024]{1,0:T(4,128)S(1)} %bitcast.46), kind=kLoop, calls=%fused_computation.6 | loop fusion | flops 1966080 | bytes 6328320 | tf_op jit(solution)/shard_map/add | solution.py:69
  15.9 0.8 fusion.6
  16.7 6.6 %all-to-all-start = ((bf16[64,16,128]{2,1,0:T(8,128)(2,1)}), bf16[64,16,128]{2,1,0:T(8,128)(2,1)S(1)}, u32[]{:S(2)}, u32[]{:S(2)}) async-start(bf16[64,16,128]{2,1,0:T(8,128)(2,1)} %bitcast.1), calls=%async_computation | async-start | bytes 524288 | tf_op jit(solution)/shard_map/all_to_all | solution.py:76
  23.3 0.1 copy.41
  23.3 0.1 copy.40
  23.4 0.1 convert_multiply_fusion
  23.5 1.9 %convolution_select_fusion = f32[16,128,128]{2,1,0:T(8,128)S(1)} fusion(pred[128,128]{1,0:T(8,128)(4,1)S(1)} %subtract_compare_fusion, f32[128]{0:T(128)S(1)} %get-tuple-element.17, f32[16,16]{0,1:T(8,128)S(1)} %copy.41, f32[128]{0:T(128)S(1)} %get-tuple-element.16, f32[16,16]{0,1:T(8,128)S(1)} %copy.40), kind=kOutput, calls=%fused_computation.11 | convolution fusion | flops 50692096 | bytes 1068032 | tf_op jit(solution)/shard_map/rcj,rct->cjt/dot_general | solution.py:22
  25.4 8.8 %all-to-all-done = bf16[64,16,128]{2,1,0:T(8,128)(2,1)S(1)} async-done(((bf16[64,16,128]{2,1,0:T(8,128)(2,1)}), bf16[64,16,128]{2,1,0:T(8,128)(2,1)S(1)}, u32[]{:S(2)}, u32[]{:S(2)}) %all-to-all-start) | async-done | bytes 262176 | tf_op jit(solution)/shard_map/all_to_all | solution.py:76
  34.3 0.4 convolution_bitcast_fusion
  34.8 2.6 %fusion.2 = f32[16,16,64]{2,1,0:T(8,128)S(1)} fusion(f32[16,16,64]{2,1,0:T(8,128)S(1)} %copy.42, f32[16,16]{1,0:T(8,128)S(1)} %get-tuple-element.14, f32[64,64]{1,0:T(8,128)S(1)} %convert_multiply_fusion, pred[64,64]{1,0:T(8,128)(4,1)S(1)} %iota_compare_fusion), kind=kLoop, calls=%fused_computation.3 | loop fusion | flops 4177920 | bytes 152576 | tf_op jit(solution)/shard_map/reduce_sum | solution.py:37
  37.4 0.7 fusion.17
  38.1 0.4 fusion.5
  38.5 0.9 %copy.44 = bf16[16,64,128]{2,0,1:T(8,128)(2,1)} copy(bf16[16,64,128]{2,1,0:T(8,128)(2,1)S(1)} %fusion.5) | data formatting | bytes 524288 | tf_op jit(solution)/shard_map/convert_element_type | solution.py:80
  39.4 4.9 %all-to-all-start.1 = ((bf16[16,64,128]{2,0,1:T(8,128)(2,1)}), bf16[16,64,128]{2,0,1:T(8,128)(2,1)S(1)}, u32[]{:S(2)}, u32[]{:S(2)}) async-start(bf16[16,64,128]{2,0,1:T(8,128)(2,1)} %copy.44), calls=%async_computation.1 | async-start | bytes 524288 | tf_op jit(solution)/shard_map/all_to_all | solution.py:81
  44.3 11.0 %all-to-all-done.1 = bf16[16,64,128]{2,0,1:T(8,128)(2,1)S(1)} async-done(((bf16[16,64,128]{2,0,1:T(8,128)(2,1)}), bf16[16,64,128]{2,0,1:T(8,128)(2,1)S(1)}, u32[]{:S(2)}, u32[]{:S(2)}) %all-to-all-start.1) | async-done | bytes 262176 | tf_op jit(solution)/shard_map/all_to_all | solution.py:81
  55.3 0.1 fusion.8
  55.3 4.7 %convolution_convert_fusion = bf16[128,4096]{1,0:T(8,128)(2,1)S(1)} fusion(bf16[1024,128]{1,0:T(8,128)(2,1)S(1)} %fusion.8, bf16[1024,4096]{1,0:T(8,128)(2,1)} %param.9), kind=kOutput, calls=%fused_computation.4 | convolution fusion | flops 1074266112 | bytes 9699328 | tf_op jit(solution)/shard_map/dot_general | solution.py:83
  60.0 0.1 select_bitcast_fusion.3
  60.1 0.1 pad_maximum_fusion
  60.2 4.6 %collective-permute-start.1 = (bf16[2,128,1024]{2,1,0:T(8,128)(2,1)S(1)}, bf16[2,128,1024]{2,1,0:T(8,128)(2,1)S(1)}, u32[]{:S(2)}, u32[]{:S(2)}) collective-permute-start(bf16[2,128,1024]{2,1,0:T(8,128)(2,1)S(1)} %pad_maximum_fusion), channel_id=1, source_target_pairs={{0,1},{1,0},{2,3},{3,2},{4,5},{5,4},{6,7},{7,6},{8,9},{9,8},{10,11... | collective-permute-start | bytes 1572872 | tf_op jit(solution)/shard_map/ppermute | solution.py:51
  64.8 1.5 %collective-permute-done.1 = bf16[2,128,1024]{2,1,0:T(8,128)(2,1)S(1)} collective-permute-done((bf16[2,128,1024]{2,1,0:T(8,128)(2,1)S(1)}, bf16[2,128,1024]{2,1,0:T(8,128)(2,1)S(1)}, u32[]{:S(2)}, u32[]{:S(2)}) %collective-permute-start.1) | collective-permute-done | bytes 524320 | tf_op jit(solution)/shard_map/ppermute | solution.py:51
  66.3 0.2 convert_add_fusion
  66.5 0.1 fusion.10
  66.6 2.7 %collective-permute-start.2 = (bf16[128,1024]{1,0:T(8,128)(2,1)S(1)}, bf16[128,1024]{1,0:T(8,128)(2,1)S(1)}, u32[]{:S(2)}, u32[]{:S(2)}) collective-permute-start(bf16[128,1024]{1,0:T(8,128)(2,1)S(1)} %fusion.10), channel_id=1, source_target_pairs={{0,2},{1,3},{2,0},{3,1},{4,6},{5,7},{6,4},{7,5},{8,10},{9,11},{10,... | collective-permute-start | bytes 786440 | tf_op jit(solution)/shard_map/ppermute | solution.py:56
  69.3 6.4 %collective-permute-done.2 = bf16[128,1024]{1,0:T(8,128)(2,1)S(1)} collective-permute-done((bf16[128,1024]{1,0:T(8,128)(2,1)S(1)}, bf16[128,1024]{1,0:T(8,128)(2,1)S(1)}, u32[]{:S(2)}, u32[]{:S(2)}) %collective-permute-start.2) | collective-permute-done | bytes 262176 | tf_op jit(solution)/shard_map/ppermute | solution.py:56
  75.6 0.1 fusion.11
  75.7 0.8 %copy.45 = bf16[1024,128]{1,0:T(8,128)(2,1)} copy(bf16[1024,128]{0,1:T(8,128)(2,1)S(1)} %fusion.11) | data formatting | bytes 524288 | tf_op jit(solution)/shard_map/transpose | solution.py:57
  (10 shorter events, 0.1 us)
Async XLA Ops:
  0.0 13.0 %copy-start = (bf16[3,1024,128]{2,1,0:T(8,128)(2,1)S(1)}, bf16[3,1024,128]{2,1,0:T(8,128)(2,1)}, u32[]{:S(2)}) copy-start(bf16[3,1024,128]{2,1,0:T(8,128)(2,1)} %param.5) | copy-start | bytes 2359300
  1.8 10.7 %collective-permute-start = (bf16[3,1024,2]{1,2,0:T(2,128)(2,1)S(1)}, bf16[3,1024,2]{1,2,0:T(2,128)(2,1)S(1)}, u32[]{:S(2)}, u32[]{:S(2)}) collective-permute-start(bf16[3,1024,2]{1,2,0:T(2,128)(2,1)S(1)} %copy.49), channel_id=1, source_target_pairs={{0,4},{4,8},{8,12},{12,16},{16,20},{20,24},{24,28},{28,32},{32,36}... | collective-permute-start | bytes 36872 | tf_op jit(solution)/shard_map/ppermute | solution.py:65
  16.7 17.6 %all-to-all-start = ((bf16[64,16,128]{2,1,0:T(8,128)(2,1)}), bf16[64,16,128]{2,1,0:T(8,128)(2,1)S(1)}, u32[]{:S(2)}, u32[]{:S(2)}) async-start(bf16[64,16,128]{2,1,0:T(8,128)(2,1)} %bitcast.1), calls=%async_computation | async-start | bytes 524288 | tf_op jit(solution)/shard_map/all_to_all | solution.py:76
  39.4 15.9 %all-to-all-start.1 = ((bf16[16,64,128]{2,0,1:T(8,128)(2,1)}), bf16[16,64,128]{2,0,1:T(8,128)(2,1)S(1)}, u32[]{:S(2)}, u32[]{:S(2)}) async-start(bf16[16,64,128]{2,0,1:T(8,128)(2,1)} %copy.44), calls=%async_computation.1 | async-start | bytes 524288 | tf_op jit(solution)/shard_map/all_to_all | solution.py:81
  60.2 6.2 %collective-permute-start.1 = (bf16[2,128,1024]{2,1,0:T(8,128)(2,1)S(1)}, bf16[2,128,1024]{2,1,0:T(8,128)(2,1)S(1)}, u32[]{:S(2)}, u32[]{:S(2)}) collective-permute-start(bf16[2,128,1024]{2,1,0:T(8,128)(2,1)S(1)} %pad_maximum_fusion), channel_id=1, source_target_pairs={{0,1},{1,0},{2,3},{3,2},{4,5},{5,4},{6,7},{7,6},{8,9},{9,8},{10,11... | collective-permute-start | bytes 1572872 | tf_op jit(solution)/shard_map/ppermute | solution.py:51
  66.6 9.1 %collective-permute-start.2 = (bf16[128,1024]{1,0:T(8,128)(2,1)S(1)}, bf16[128,1024]{1,0:T(8,128)(2,1)S(1)}, u32[]{:S(2)}, u32[]{:S(2)}) collective-permute-start(bf16[128,1024]{1,0:T(8,128)(2,1)S(1)} %fusion.10), channel_id=1, source_target_pairs={{0,2},{1,3},{2,0},{3,1},{4,6},{5,7},{6,4},{7,5},{8,10},{9,11},{10,... | collective-permute-start | bytes 786440 | tf_op jit(solution)/shard_map/ppermute | solution.py:56

commit v19 on v18

--- a/solution.py
+++ b/solution.py
@@ -27,14 +27,13 @@
     inside = jnp.einsum("cnj,cjt->cnt", signal, toeplitz, precision=precise)
     to_end = jnp.exp(-(float(block - 1) - steps)[None, None, :] / life)
     leaving = jnp.einsum("cnj,rcj->rcn", signal, to_end, precision=precise)
-    n_idx = jnp.arange(blocks, dtype=jnp.int32)
-    gap = (n_idx[:, None] - 1 - n_idx[None, :]).astype(jnp.float32)
-    exponent = jnp.where(
-        (n_idx[:, None] > n_idx[None, :])[None, None],
-        -float(block) * gap[None, None] / life[..., None],
-        -jnp.inf,
-    )
-    entering = jnp.sum(jnp.exp(exponent) * leaving[:, :, None, :], axis=-1)
+    gaps = jnp.arange(blocks - 1, dtype=jnp.int32).astype(jnp.float32)
+    decay = jnp.exp(-float(block) * gaps[None, None, :] / life)
+    padded = jnp.concatenate([jnp.zeros_like(leaving), leaving], axis=-1)
+    entering = jnp.zeros_like(leaving)
+    for k in range(blocks - 1):
+        start = blocks - 1 - k
+        entering = entering + decay[..., k : k + 1] * padded[..., start : start + blocks]
     from_start = resid * jnp.exp(-(steps + 1.0)[None, None, :] / life)
     carried = jnp.einsum("rcn,rct->cnt", entering, from_start, precision=precise)
     return (inside + carried).reshape(chan_here, length)

time: 77 us -> 82.5 us (1.071)
  matrix products: 8.18 us -> 16.6 us
  other arithmetic: 6.97 us -> 4.4 us
  local copies, waits for them, and re-layouts: 5.87 us -> 4.89 us
    dot_general x1, matrix products: 0.7 us -> 9.11 us  [modal_conv(): jnp.einsum('rcn,rct->cnt', entering, from_start, precision=precise)]
    reduce_sum x1 -> x0, other arithmetic: 2.64 us -> none  [modal_conv(): entering = jnp.sum(jnp.exp(exponent) * leaving[:, :, None, :], axis=-1)]
    slice x1, local copies, waits for them, and re-layouts: 0.95 us -> 0.03 us  [local(): taps[:, 0, :, None] * extended[:, :, 2:]]
  transfers between devices with their start and end apart: 5 -> 5, of which waited for: 5 -> 5; matrix products, arithmetic and copies ran while one was open for 5% -> 4% of each run, Pallas kernels for 0% -> 0%
where the time goes in v19:
time: 82.5 us; the launch traced here: 82.2 us
  waiting for transfers between devices  34.9 us (42%)
  starting transfers between devices  21.3 us (26%)
  matrix products  16.6 us (20%)
  local copies, waits for them, and re-layouts  4.89 us (6%)
  other arithmetic  4.4 us (5%)
    all_to_all x1, waiting for transfers between devices, local(): lax.all_to_all(convolved, 'seq', split_axis=1, concat_axis=0, tiled=True)  11 us
    dot_general x1, matrix products, modal_conv(): jnp.einsum('rcn,rct->cnt', entering, from_start, precision=precise)  9.11 us
    all_to_all x1, waiting for transfers between devices, local(): lax.all_to_all(product, 'seq', split_axis=0, concat_axis=1, tiled=True)  8.95 us
    ppermute x1, waiting for transfers between devices, local(): lax.ppermute(edge_block, 'seq', [(i, (i + 1) % devices) for i in range(de...  7.02 us
    all_to_all x1, starting transfers between devices, local(): lax.all_to_all(product, 'seq', split_axis=0, concat_axis=1, tiled=True)  6.56 us
    ppermute x1, waiting for transfers between devices, reduce_scatter_chan(): got2 = lax.ppermute(send2, 'chan', [(j, j ^ 2) for j in range(4)])  6.37 us
    all_to_all x1, starting transfers between devices, local(): lax.all_to_all(convolved, 'seq', split_axis=1, concat_axis=0, tiled=True)  4.85 us
    dot_general x1, matrix products, local(): lax.dot_general(gated_rows, out_weight, (((0,), (0,)), ((), ())), preferr...  4.67 us
  transfers between devices with their start and end apart: 5, of which 5 were waited for; matrix products, arithmetic and copies ran while one was open for 4% of the time, Pallas kernels for 0%

profile of v19, /device:TPU:1, one launch (start us, length us, event | category | flops | bytes accessed | tf_op | source)
XLA Modules:
  0.0 82.2 jit_solution(14423248430198349198)
XLA Ops:
  0.0 0.0 copy-start.1
  0.0 1.4 %slice.429 = bf16[3,1024,2]{2,1,0:T(8,128)(2,1)S(1)} slice(bf16[3,1024,128]{2,1,0:T(8,128)(2,1)} %param.5), slice={[0:3], [0:1024], [126:128]} | slice | bytes 24576 | tf_op jit(solution)/shard_map/slice | solution.py:62
  1.4 0.0 copy-start
  1.4 0.3 copy.39
  1.7 2.5 %collective-permute-start = (bf16[3,1024,2]{1,2,0:T(2,128)(2,1)S(1)}, bf16[3,1024,2]{1,2,0:T(2,128)(2,1)S(1)}, u32[]{:S(2)}, u32[]{:S(2)}) collective-permute-start(bf16[3,1024,2]{1,2,0:T(2,128)(2,1)S(1)} %copy.39), channel_id=1, source_target_pairs={{0,4},{4,8},{8,12},{12,16},{16,20},{20,24},{24,28},{28,32},{32,36}... | collective-permute-start | bytes 36872 | tf_op jit(solution)/shard_map/ppermute | solution.py:64
  4.3 0.8 constant_dynamic-slice_fusion
  5.0 0.1 copy.32
  5.1 0.1 divide_exponential_fusion
  5.4 0.0 copy-done.1
  5.5 7.0 %collective-permute-done = bf16[3,1024,2]{1,2,0:T(2,128)(2,1)S(1)} collective-permute-done((bf16[3,1024,2]{1,2,0:T(2,128)(2,1)S(1)}, bf16[3,1024,2]{1,2,0:T(2,128)(2,1)S(1)}, u32[]{:S(2)}, u32[]{:S(2)}) %collective-permute-start) | collective-permute-done | bytes 12320 | tf_op jit(solution)/shard_map/ppermute | solution.py:64
  12.5 0.4 copy.29
  12.9 0.0 copy-done
  12.9 0.6 maximum_convert_fusion
  13.5 2.4 %fusion = f32[3,1024,128]{2,1,0:T(8,128)S(1)} fusion(f32[3,1024,130]{2,1,0:T(8,128)S(1)} %maximum_convert_fusion, f32[3,1024]{1,0:T(4,128)S(1)} %get-tuple-element.75, f32[3,1024]{1,0:T(4,128)S(1)} %get-tuple-element.76, f32[3,1024]{1,0:T(4,128)S(1)} %bitcast.172), kind=kLoop, calls=%fused_computation.2 | loop fusion | flops 1966080 | bytes 6328320 | tf_op jit(solution)/shard_map/add | solution.py:68
  15.9 0.8 fusion.3
  16.6 6.6 %all-to-all-start = ((bf16[64,16,128]{2,1,0:T(8,128)(2,1)}), bf16[64,16,128]{2,1,0:T(8,128)(2,1)S(1)}, u32[]{:S(2)}, u32[]{:S(2)}) async-start(bf16[64,16,128]{2,1,0:T(8,128)(2,1)} %bitcast.1), calls=%async_computation | async-start | bytes 524288 | tf_op jit(solution)/shard_map/all_to_all | solution.py:75
  23.2 0.1 copy.31
  23.3 1.9 %convolution_select_fusion = f32[16,128,128]{2,1,0:T(8,128)S(1)} fusion(pred[128,128]{1,0:T(8,128)(4,1)S(1)} %subtract_compare_fusion, f32[128]{0:T(128)S(1)} %get-tuple-element.80, f32[16,16]{0,1:T(8,128)S(1)} %copy.32, f32[128]{0:T(128)S(1)} %get-tuple-element.79, f32[16,16]{0,1:T(8,128)S(1)} %copy.31), kind=kOutput, calls=%fused_computation.7 | convolution fusion | flops 50692096 | bytes 1068032 | tf_op jit(solution)/shard_map/rcj,rct->cjt/dot_general | solution.py:22
  25.2 9.0 %all-to-all-done = bf16[64,16,128]{2,1,0:T(8,128)(2,1)S(1)} async-done(((bf16[64,16,128]{2,1,0:T(8,128)(2,1)}), bf16[64,16,128]{2,1,0:T(8,128)(2,1)S(1)}, u32[]{:S(2)}, u32[]{:S(2)}) %all-to-all-start) | async-done | bytes 262176 | tf_op jit(solution)/shard_map/all_to_all | solution.py:75
  34.2 0.4 convolution_bitcast_fusion
  34.7 9.1 %fusion.14 = f32[16,64,128]{2,1,0:T(8,128)S(1)} fusion(f32[16,16,64]{2,0,1:T(8,128)S(1)} %convolution_bitcast_fusion, f32[128]{0:T(128)S(1)} %add_negate_fusion, f32[16,16]{0,1:T(8,128)S(1)} %get-tuple-element.10, f32[16,16]{0,1:T(8,128)S(1)} %get-tuple-element.11, f32[16,16]{0,1:T(8,128)S(1)} %get-tuple-element.12, f32[16,16]{0,1:T(8,128)S(1)} %get-tuple-element.13, ...), kind=kOutput, calls=%fused_computation.34 | convolution fusion | flops 14696448 | bytes 656896 | tf_op jit(solution)/shard_map/rcn,rct->cnt/dot_general | solution.py:38
  43.8 0.4 fusion.2
  44.2 0.9 %copy.34 = bf16[16,64,128]{2,0,1:T(8,128)(2,1)} copy(bf16[16,64,128]{2,1,0:T(8,128)(2,1)S(1)} %fusion.2) | data formatting | bytes 524288 | tf_op jit(solution)/shard_map/convert_element_type | solution.py:79
  45.1 4.9 %all-to-all-start.1 = ((bf16[16,64,128]{2,0,1:T(8,128)(2,1)}), bf16[16,64,128]{2,0,1:T(8,128)(2,1)S(1)}, u32[]{:S(2)}, u32[]{:S(2)}) async-start(bf16[16,64,128]{2,0,1:T(8,128)(2,1)} %copy.34), calls=%async_computation.1 | async-start | bytes 524288 | tf_op jit(solution)/shard_map/all_to_all | solution.py:80
  49.9 11.0 %all-to-all-done.1 = bf16[16,64,128]{2,0,1:T(8,128)(2,1)S(1)} async-done(((bf16[16,64,128]{2,0,1:T(8,128)(2,1)}), bf16[16,64,128]{2,0,1:T(8,128)(2,1)S(1)}, u32[]{:S(2)}, u32[]{:S(2)}) %all-to-all-start.1) | async-done | bytes 262176 | tf_op jit(solution)/shard_map/all_to_all | solution.py:80
  60.9 0.1 fusion.5
  61.0 4.7 %convolution_convert_fusion = bf16[128,4096]{1,0:T(8,128)(2,1)S(1)} fusion(bf16[1024,128]{1,0:T(8,128)(2,1)S(1)} %fusion.5, bf16[1024,4096]{1,0:T(8,128)(2,1)} %param.9), kind=kOutput, calls=%fused_computation | convolution fusion | flops 1074266112 | bytes 9699328 | tf_op jit(solution)/shard_map/dot_general | solution.py:82
  65.7 0.1 select_bitcast_fusion.3
  65.8 0.1 pad_maximum_fusion
  65.8 4.6 %collective-permute-start.1 = (bf16[2,128,1024]{2,1,0:T(8,128)(2,1)S(1)}, bf16[2,128,1024]{2,1,0:T(8,128)(2,1)S(1)}, u32[]{:S(2)}, u32[]{:S(2)}) collective-permute-start(bf16[2,128,1024]{2,1,0:T(8,128)(2,1)S(1)} %pad_maximum_fusion), channel_id=1, source_target_pairs={{0,1},{1,0},{2,3},{3,2},{4,5},{5,4},{6,7},{7,6},{8,9},{9,8},{10,11... | collective-permute-start | bytes 1572872 | tf_op jit(solution)/shard_map/ppermute | solution.py:50
  70.5 1.5 %collective-permute-done.1 = bf16[2,128,1024]{2,1,0:T(8,128)(2,1)S(1)} collective-permute-done((bf16[2,128,1024]{2,1,0:T(8,128)(2,1)S(1)}, bf16[2,128,1024]{2,1,0:T(8,128)(2,1)S(1)}, u32[]{:S(2)}, u32[]{:S(2)}) %collective-permute-start.1) | collective-permute-done | bytes 524320 | tf_op jit(solution)/shard_map/ppermute | solution.py:50
  72.0 0.2 convert_add_fusion
  72.2 0.1 fusion.7
  72.2 2.7 %collective-permute-start.2 = (bf16[128,1024]{1,0:T(8,128)(2,1)S(1)}, bf16[128,1024]{1,0:T(8,128)(2,1)S(1)}, u32[]{:S(2)}, u32[]{:S(2)}) collective-permute-start(bf16[128,1024]{1,0:T(8,128)(2,1)S(1)} %fusion.7), channel_id=1, source_target_pairs={{0,2},{1,3},{2,0},{3,1},{4,6},{5,7},{6,4},{7,5},{8,10},{9,11},{10,... | collective-permute-start | bytes 786440 | tf_op jit(solution)/shard_map/ppermute | solution.py:55
  74.9 6.4 %collective-permute-done.2 = bf16[128,1024]{1,0:T(8,128)(2,1)S(1)} collective-permute-done((bf16[128,1024]{1,0:T(8,128)(2,1)S(1)}, bf16[128,1024]{1,0:T(8,128)(2,1)S(1)}, u32[]{:S(2)}, u32[]{:S(2)}) %collective-permute-start.2) | collective-permute-done | bytes 262176 | tf_op jit(solution)/shard_map/ppermute | solution.py:55
  81.3 0.1 fusion.8
  81.4 0.8 %copy.35 = bf16[1024,128]{1,0:T(8,128)(2,1)} copy(bf16[1024,128]{0,1:T(8,128)(2,1)S(1)} %fusion.8) | data formatting | bytes 524288 | tf_op jit(solution)/shard_map/transpose | solution.py:56
  (13 shorter events, 0.1 us)
Async XLA Ops:
  0.0 5.4 %copy-start.1 = (f32[3,3,1024]{2,1,0:T(4,128)S(1)}, f32[3,3,1024]{2,1,0:T(4,128)}, u32[]{:S(2)}) copy-start(f32[3,3,1024]{2,1,0:T(4,128)} %param.6) | copy-start | bytes 110596
  1.4 11.5 %copy-start = (bf16[3,1024,128]{2,1,0:T(8,128)(2,1)S(1)}, bf16[3,1024,128]{2,1,0:T(8,128)(2,1)}, u32[]{:S(2)}) copy-start(bf16[3,1024,128]{2,1,0:T(8,128)(2,1)} %param.5) | copy-start | bytes 2359300
  1.7 10.7 %collective-permute-start = (bf16[3,1024,2]{1,2,0:T(2,128)(2,1)S(1)}, bf16[3,1024,2]{1,2,0:T(2,128)(2,1)S(1)}, u32[]{:S(2)}, u32[]{:S(2)}) collective-permute-start(bf16[3,1024,2]{1,2,0:T(2,128)(2,1)S(1)} %copy.39), channel_id=1, source_target_pairs={{0,4},{4,8},{8,12},{12,16},{16,20},{20,24},{24,28},{28,32},{32,36}... | collective-permute-start | bytes 36872 | tf_op jit(solution)/shard_map/ppermute | solution.py:64
  16.6 17.6 %all-to-all-start = ((bf16[64,16,128]{2,1,0:T(8,128)(2,1)}), bf16[64,16,128]{2,1,0:T(8,128)(2,1)S(1)}, u32[]{:S(2)}, u32[]{:S(2)}) async-start(bf16[64,16,128]{2,1,0:T(8,128)(2,1)} %bitcast.1), calls=%async_computation | async-start | bytes 524288 | tf_op jit(solution)/shard_map/all_to_all | solution.py:75
  45.1 15.9 %all-to-all-start.1 = ((bf16[16,64,128]{2,0,1:T(8,128)(2,1)}), bf16[16,64,128]{2,0,1:T(8,128)(2,1)S(1)}, u32[]{:S(2)}, u32[]{:S(2)}) async-start(bf16[16,64,128]{2,0,1:T(8,128)(2,1)} %copy.34), calls=%async_computation.1 | async-start | bytes 524288 | tf_op jit(solution)/shard_map/all_to_all | solution.py:80
  65.8 6.2 %collective-permute-start.1 = (bf16[2,128,1024]{2,1,0:T(8,128)(2,1)S(1)}, bf16[2,128,1024]{2,1,0:T(8,128)(2,1)S(1)}, u32[]{:S(2)}, u32[]{:S(2)}) collective-permute-start(bf16[2,128,1024]{2,1,0:T(8,128)(2,1)S(1)} %pad_maximum_fusion), channel_id=1, source_target_pairs={{0,1},{1,0},{2,3},{3,2},{4,5},{5,4},{6,7},{7,6},{8,9},{9,8},{10,11... | collective-permute-start | bytes 1572872 | tf_op jit(solution)/shard_map/ppermute | solution.py:50
  72.2 9.1 %collective-permute-start.2 = (bf16[128,1024]{1,0:T(8,128)(2,1)S(1)}, bf16[128,1024]{1,0:T(8,128)(2,1)S(1)}, u32[]{:S(2)}, u32[]{:S(2)}) collective-permute-start(bf16[128,1024]{1,0:T(8,128)(2,1)S(1)} %fusion.7), channel_id=1, source_target_pairs={{0,2},{1,3},{2,0},{3,1},{4,6},{5,7},{6,4},{7,5},{8,10},{9,11},{10,... | collective-permute-start | bytes 786440 | tf_op jit(solution)/shard_map/ppermute | solution.py:55

commit v20 on v18

--- a/solution.py
+++ b/solution.py
@@ -34,7 +34,9 @@
         -float(block) * gap[None, None] / life[..., None],
         -jnp.inf,
     )
-    entering = jnp.sum(jnp.exp(exponent) * leaving[:, :, None, :], axis=-1)
+    entering = jnp.einsum(
+        "rcnm,rcm->rcn", jnp.exp(exponent), leaving, precision=lax.Precision.HIGHEST
+    )
     from_start = resid * jnp.exp(-(steps + 1.0)[None, None, :] / life)
     carried = jnp.einsum("rcn,rct->cnt", entering, from_start, precision=precise)
     return (inside + carried).reshape(chan_here, length)

time: 77 us -> 88.4 us (1.15)
  matrix products: 8.18 us -> 22.4 us
  other arithmetic: 6.97 us -> 4.33 us
  local copies, waits for them, and re-layouts: 5.87 us -> 4.92 us
    dot_general x0 -> x1, matrix products: none -> 14.2 us  [modal_conv(): jnp.einsum('rcnm,rcm->rcn', jnp.exp(exponent), leaving, precision=lax.Pre...]
    reduce_sum x1 -> x0, other arithmetic: 2.64 us -> none  [modal_conv(): entering = jnp.sum(jnp.exp(exponent) * leaving[:, :, None, :], axis=-1)]
    slice x1, local copies, waits for them, and re-layouts: 0.95 us -> 0.03 us  [local(): taps[:, 0, :, None] * extended[:, :, 2:]]
    ppermute x1, waiting for transfers between devices: 6.39 us -> 7.3 us  [local(): lax.ppermute(edge_block, 'seq', [(i, (i + 1) % devices) for i in range(de...]
  transfers between devices with their start and end apart: 5 -> 5, of which waited for: 5 -> 5; matrix products, arithmetic and copies ran while one was open for 5% -> 3% of each run, Pallas kernels for 0% -> 0%
where the time goes in v20:
time: 88.4 us; the launch traced here: 88.1 us
  waiting for transfers between devices  34.9 us (39%)
  matrix products  22.4 us (25%)
  starting transfers between devices  21.4 us (24%)
  local copies, waits for them, and re-layouts  4.92 us (6%)
  other arithmetic  4.33 us (5%)
    dot_general x1, matrix products, modal_conv(): jnp.einsum('rcnm,rcm->rcn', jnp.exp(exponent), leaving, precision=lax.Pre...  14.2 us
    all_to_all x1, waiting for transfers between devices, local(): lax.all_to_all(convolved, 'seq', split_axis=1, concat_axis=0, tiled=True)  11 us
    all_to_all x1, waiting for transfers between devices, local(): lax.all_to_all(product, 'seq', split_axis=0, concat_axis=1, tiled=True)  8.64 us
    ppermute x1, waiting for transfers between devices, local(): lax.ppermute(edge_block, 'seq', [(i, (i + 1) % devices) for i in range(de...  7.3 us
    all_to_all x1, starting transfers between devices, local(): lax.all_to_all(product, 'seq', split_axis=0, concat_axis=1, tiled=True)  6.74 us
    ppermute x1, waiting for transfers between devices, reduce_scatter_chan(): got2 = lax.ppermute(send2, 'chan', [(j, j ^ 2) for j in range(4)])  6.37 us
    all_to_all x1, starting transfers between devices, local(): lax.all_to_all(convolved, 'seq', split_axis=1, concat_axis=0, tiled=True)  4.85 us
    dot_general x1, matrix products, local(): lax.dot_general(gated_rows, out_weight, (((0,), (0,)), ((), ())), preferr...  4.67 us
  transfers between devices with their start and end apart: 5, of which 5 were waited for; matrix products, arithmetic and copies ran while one was open for 3% of the time, Pallas kernels for 0%

profile of v20, /device:TPU:1, one launch (start us, length us, event | category | flops | bytes accessed | tf_op | source)
XLA Modules:
  0.0 88.1 jit_solution(4511094436783355295)
XLA Ops:
  0.0 0.0 copy-start
  0.0 0.0 copy-start.1
  0.0 1.5 %slice.51 = bf16[3,1024,2]{2,1,0:T(8,128)(2,1)S(1)} slice(bf16[3,1024,128]{2,1,0:T(8,128)(2,1)} %param.5), slice={[0:3], [0:1024], [126:128]} | slice | bytes 24576 | tf_op jit(solution)/shard_map/slice | solution.py:65
  1.5 0.3 copy.37
  1.8 2.5 %collective-permute-start = (bf16[3,1024,2]{1,2,0:T(2,128)(2,1)S(1)}, bf16[3,1024,2]{1,2,0:T(2,128)(2,1)S(1)}, u32[]{:S(2)}, u32[]{:S(2)}) collective-permute-start(bf16[3,1024,2]{1,2,0:T(2,128)(2,1)S(1)} %copy.37), channel_id=1, source_target_pairs={{0,4},{4,8},{8,12},{12,16},{16,20},{20,24},{24,28},{28,32},{32,36}... | collective-permute-start | bytes 36872 | tf_op jit(solution)/shard_map/ppermute | solution.py:67
  4.4 0.0 copy-done.1
  4.4 0.8 constant_dynamic-slice_fusion
  5.2 7.3 %collective-permute-done = bf16[3,1024,2]{1,2,0:T(2,128)(2,1)S(1)} collective-permute-done((bf16[3,1024,2]{1,2,0:T(2,128)(2,1)S(1)}, bf16[3,1024,2]{1,2,0:T(2,128)(2,1)S(1)}, u32[]{:S(2)}, u32[]{:S(2)}) %collective-permute-start) | collective-permute-done | bytes 12320 | tf_op jit(solution)/shard_map/ppermute | solution.py:67
  12.6 0.4 copy.26
  13.0 0.0 copy-done
  13.0 0.6 maximum_convert_fusion
  13.6 2.4 %fusion.7 = f32[3,1024,128]{2,1,0:T(8,128)S(1)} fusion(f32[3,1024,130]{2,1,0:T(8,128)S(1)} %maximum_convert_fusion, f32[3,1024]{1,0:T(4,128)S(1)} %get-tuple-element.12, f32[3,1024]{1,0:T(4,128)S(1)} %get-tuple-element.13, f32[3,1024]{1,0:T(4,128)S(1)} %bitcast.51), kind=kLoop, calls=%fused_computation.9 | loop fusion | flops 1966080 | bytes 6328320 | tf_op jit(solution)/shard_map/add | solution.py:71
  16.0 0.8 fusion.10
  16.7 6.7 %all-to-all-start = ((bf16[64,16,128]{2,1,0:T(8,128)(2,1)}), bf16[64,16,128]{2,1,0:T(8,128)(2,1)S(1)}, u32[]{:S(2)}, u32[]{:S(2)}) async-start(bf16[64,16,128]{2,1,0:T(8,128)(2,1)} %bitcast.1), calls=%async_computation | async-start | bytes 524288 | tf_op jit(solution)/shard_map/all_to_all | solution.py:78
  23.5 0.1 copy.29
  23.5 0.1 copy.28
  23.6 0.1 convert_multiply_fusion
  23.7 1.9 %convolution_select_fusion = f32[16,128,128]{2,1,0:T(8,128)S(1)} fusion(pred[128,128]{1,0:T(8,128)(4,1)S(1)} %subtract_compare_fusion, f32[128]{0:T(128)S(1)} %get-tuple-element.17, f32[16,16]{0,1:T(8,128)S(1)} %copy.29, f32[128]{0:T(128)S(1)} %get-tuple-element.16, f32[16,16]{0,1:T(8,128)S(1)} %copy.28), kind=kOutput, calls=%fused_computation.14 | convolution fusion | flops 50692096 | bytes 1068032 | tf_op jit(solution)/shard_map/rcj,rct->cjt/dot_general | solution.py:22
  25.6 8.6 %all-to-all-done = bf16[64,16,128]{2,1,0:T(8,128)(2,1)S(1)} async-done(((bf16[64,16,128]{2,1,0:T(8,128)(2,1)}), bf16[64,16,128]{2,1,0:T(8,128)(2,1)S(1)}, u32[]{:S(2)}, u32[]{:S(2)}) %all-to-all-start) | async-done | bytes 262176 | tf_op jit(solution)/shard_map/all_to_all | solution.py:78
  34.3 0.4 convolution_bitcast_fusion
  34.7 14.2 %fusion.1 = f32[16,16,1,64]{3,2,1,0:T(1,128)S(1)} fusion(f32[16,16]{1,0:T(8,128)S(1)} %get-tuple-element.14, f32[64,64]{1,0:T(8,128)S(1)} %convert_multiply_fusion, pred[64,64]{1,0:T(8,128)(4,1)S(1)} %iota_compare_fusion, f32[16,16,64,1]{2,0,1,3:T(8,128)S(1)} %convolution_bitcast_fusion), kind=kOutput, calls=%fused_computation.2 | convolution fusion | flops 14680064 | bytes 152576 | tf_op jit(solution)/shard_map/rcnm,rcm->rcn/dot_general | solution.py:37
  48.9 0.7 fusion.21
  49.6 0.4 fusion.9
  50.1 0.9 copy.30
  50.9 4.9 %all-to-all-start.1 = ((bf16[16,64,128]{2,0,1:T(8,128)(2,1)}), bf16[16,64,128]{2,0,1:T(8,128)(2,1)S(1)}, u32[]{:S(2)}, u32[]{:S(2)}) async-start(bf16[16,64,128]{2,0,1:T(8,128)(2,1)} %copy.30), calls=%async_computation.1 | async-start | bytes 524288 | tf_op jit(solution)/shard_map/all_to_all | solution.py:83
  55.8 11.0 %all-to-all-done.1 = bf16[16,64,128]{2,0,1:T(8,128)(2,1)S(1)} async-done(((bf16[16,64,128]{2,0,1:T(8,128)(2,1)}), bf16[16,64,128]{2,0,1:T(8,128)(2,1)S(1)}, u32[]{:S(2)}, u32[]{:S(2)}) %all-to-all-start.1) | async-done | bytes 262176 | tf_op jit(solution)/shard_map/all_to_all | solution.py:83
  66.8 0.1 fusion.12
  66.9 4.7 %convolution_convert_fusion = bf16[128,4096]{1,0:T(8,128)(2,1)S(1)} fusion(bf16[1024,128]{1,0:T(8,128)(2,1)S(1)} %fusion.12, bf16[1024,4096]{1,0:T(8,128)(2,1)} %param.9), kind=kOutput, calls=%fused_computation.3 | convolution fusion | flops 1074266112 | bytes 9699328 | tf_op jit(solution)/shard_map/dot_general | solution.py:85
  71.5 0.1 select_bitcast_fusion.3
  71.6 0.1 pad_maximum_fusion
  71.7 4.6 %collective-permute-start.1 = (bf16[2,128,1024]{2,1,0:T(8,128)(2,1)S(1)}, bf16[2,128,1024]{2,1,0:T(8,128)(2,1)S(1)}, u32[]{:S(2)}, u32[]{:S(2)}) collective-permute-start(bf16[2,128,1024]{2,1,0:T(8,128)(2,1)S(1)} %pad_maximum_fusion), channel_id=1, source_target_pairs={{0,1},{1,0},{2,3},{3,2},{4,5},{5,4},{6,7},{7,6},{8,9},{9,8},{10,11... | collective-permute-start | bytes 1572872 | tf_op jit(solution)/shard_map/ppermute | solution.py:53
  76.3 1.5 %collective-permute-done.1 = bf16[2,128,1024]{2,1,0:T(8,128)(2,1)S(1)} collective-permute-done((bf16[2,128,1024]{2,1,0:T(8,128)(2,1)S(1)}, bf16[2,128,1024]{2,1,0:T(8,128)(2,1)S(1)}, u32[]{:S(2)}, u32[]{:S(2)}) %collective-permute-start.1) | collective-permute-done | bytes 524320 | tf_op jit(solution)/shard_map/ppermute | solution.py:53
  77.8 0.2 convert_add_fusion
  78.0 0.1 fusion.14
  78.1 2.7 %collective-permute-start.2 = (bf16[128,1024]{1,0:T(8,128)(2,1)S(1)}, bf16[128,1024]{1,0:T(8,128)(2,1)S(1)}, u32[]{:S(2)}, u32[]{:S(2)}) collective-permute-start(bf16[128,1024]{1,0:T(8,128)(2,1)S(1)} %fusion.14), channel_id=1, source_target_pairs={{0,2},{1,3},{2,0},{3,1},{4,6},{5,7},{6,4},{7,5},{8,10},{9,11},{10,... | collective-permute-start | bytes 786440 | tf_op jit(solution)/shard_map/ppermute | solution.py:58
  80.8 6.4 %collective-permute-done.2 = bf16[128,1024]{1,0:T(8,128)(2,1)S(1)} collective-permute-done((bf16[128,1024]{1,0:T(8,128)(2,1)S(1)}, bf16[128,1024]{1,0:T(8,128)(2,1)S(1)}, u32[]{:S(2)}, u32[]{:S(2)}) %collective-permute-start.2) | collective-permute-done | bytes 262176 | tf_op jit(solution)/shard_map/ppermute | solution.py:58
  87.2 0.1 fusion.15
  87.3 0.8 copy.31
  (10 shorter events, 0.1 us)
Async XLA Ops:
  0.0 13.0 %copy-start = (bf16[3,1024,128]{2,1,0:T(8,128)(2,1)S(1)}, bf16[3,1024,128]{2,1,0:T(8,128)(2,1)}, u32[]{:S(2)}) copy-start(bf16[3,1024,128]{2,1,0:T(8,128)(2,1)} %param.5) | copy-start | bytes 2359300
  0.0 4.4 %copy-start.1 = (f32[3,3,1024]{2,1,0:T(4,128)S(1)}, f32[3,3,1024]{2,1,0:T(4,128)}, u32[]{:S(2)}) copy-start(f32[3,3,1024]{2,1,0:T(4,128)} %param.6) | copy-start | bytes 110596
  1.8 10.7 %collective-permute-start = (bf16[3,1024,2]{1,2,0:T(2,128)(2,1)S(1)}, bf16[3,1024,2]{1,2,0:T(2,128)(2,1)S(1)}, u32[]{:S(2)}, u32[]{:S(2)}) collective-permute-start(bf16[3,1024,2]{1,2,0:T(2,128)(2,1)S(1)} %copy.37), channel_id=1, source_target_pairs={{0,4},{4,8},{8,12},{12,16},{16,20},{20,24},{24,28},{28,32},{32,36}... | collective-permute-start | bytes 36872 | tf_op jit(solution)/shard_map/ppermute | solution.py:67
  16.7 17.6 %all-to-all-start = ((bf16[64,16,128]{2,1,0:T(8,128)(2,1)}), bf16[64,16,128]{2,1,0:T(8,128)(2,1)S(1)}, u32[]{:S(2)}, u32[]{:S(2)}) async-start(bf16[64,16,128]{2,1,0:T(8,128)(2,1)} %bitcast.1), calls=%async_computation | async-start | bytes 524288 | tf_op jit(solution)/shard_map/all_to_all | solution.py:78
  50.9 15.9 %all-to-all-start.1 = ((bf16[16,64,128]{2,0,1:T(8,128)(2,1)}), bf16[16,64,128]{2,0,1:T(8,128)(2,1)S(1)}, u32[]{:S(2)}, u32[]{:S(2)}) async-start(bf16[16,64,128]{2,0,1:T(8,128)(2,1)} %copy.30), calls=%async_computation.1 | async-start | bytes 524288 | tf_op jit(solution)/shard_map/all_to_all | solution.py:83
  71.7 6.2 %collective-permute-start.1 = (bf16[2,128,1024]{2,1,0:T(8,128)(2,1)S(1)}, bf16[2,128,1024]{2,1,0:T(8,128)(2,1)S(1)}, u32[]{:S(2)}, u32[]{:S(2)}) collective-permute-start(bf16[2,128,1024]{2,1,0:T(8,128)(2,1)S(1)} %pad_maximum_fusion), channel_id=1, source_target_pairs={{0,1},{1,0},{2,3},{3,2},{4,5},{5,4},{6,7},{7,6},{8,9},{9,8},{10,11... | collective-permute-start | bytes 1572872 | tf_op jit(solution)/shard_map/ppermute | solution.py:53
  78.1 9.1 %collective-permute-start.2 = (bf16[128,1024]{1,0:T(8,128)(2,1)S(1)}, bf16[128,1024]{1,0:T(8,128)(2,1)S(1)}, u32[]{:S(2)}, u32[]{:S(2)}) collective-permute-start(bf16[128,1024]{1,0:T(8,128)(2,1)S(1)} %fusion.14), channel_id=1, source_target_pairs={{0,2},{1,3},{2,0},{3,1},{4,6},{5,7},{6,4},{7,5},{8,10},{9,11},{10,... | collective-permute-start | bytes 786440 | tf_op jit(solution)/shard_map/ppermute | solution.py:58

commit v21 on v18

--- a/solution.py
+++ b/solution.py
@@ -65,12 +65,15 @@
     wrapped = lax.ppermute(edge_block, "seq", [(i, (i + 1) % devices) for i in range(devices)])
     earlier = jnp.where(lax.axis_index("seq") == 0, jnp.zeros_like(wrapped), wrapped)
     extended = jnp.concatenate([earlier, qkv], axis=2).astype(jnp.float32)
-    filtered = (
-        taps[:, 0, :, None] * extended[:, :, 2:]
-        + taps[:, 1, :, None] * extended[:, :, 1:-1]
-        + taps[:, 2, :, None] * extended[:, :, :-2]
-    )
-    product = (filtered[1] * filtered[2]).astype(jnp.bfloat16)
+
+    def filtered(stream):
+        return (
+            taps[stream, 0, :, None] * extended[stream, :, 2:]
+            + taps[stream, 1, :, None] * extended[stream, :, 1:-1]
+            + taps[stream, 2, :, None] * extended[stream, :, :-2]
+        )
+
+    product = (filtered(1) * filtered(2)).astype(jnp.bfloat16)
     groups = lax.axis_size("seq")
     per_group = chan_local // groups
     pencils = lax.all_to_all(product, "seq", split_axis=0, concat_axis=1, tiled=True)
@@ -79,7 +82,7 @@
     resid_slice = lax.dynamic_slice_in_dim(residues, first_chan, per_group, 1)
     convolved = modal_conv(pencils, life_slice, resid_slice).astype(jnp.bfloat16)
     returned = lax.all_to_all(convolved, "seq", split_axis=1, concat_axis=0, tiled=True)
-    gated_rows = (filtered[0] * returned.astype(jnp.float32)).astype(jnp.bfloat16)
+    gated_rows = (filtered(0) * returned.astype(jnp.float32)).astype(jnp.bfloat16)
     partial = lax.dot_general(
         gated_rows, out_weight, (((0,), (0,)), ((), ())), preferred_element_type=jnp.float32
     ).astype(jnp.bfloat16)

time: 77 us -> 80.2 us (1.042)
  matrix products: 8.18 us -> 10.4 us
  local copies, waits for them, and re-layouts: 5.87 us -> 7.63 us
  waiting for transfers between devices: 34.1 us -> 32.5 us
    add x1 -> x0, other arithmetic: 2.35 us -> none  [local(): taps[:, 0, :, None] * extended[:, :, 2:]]
    convert_element_type x2, other arithmetic: 0.81 us -> 2.38 us  [the longest x1 1.63 us: local(): product = (filtered(1) * filtered(2)).astype(jnp.bfloat16)]
    convert_element_type x1, other arithmetic: 0.6 us -> 1.97 us  [local(): extended = jnp.concatenate([earlier, qkv], axis=2).astype(jnp.float32)]
    dot_general x1, matrix products: 0.42 us -> 1.64 us  [modal_conv(): inside = jnp.einsum('cnj,cjt->cnt', signal, toeplitz, precision=precise)]
    dot_general x1, matrix products: 1.94 us -> 2.93 us  [modal_conv(): jnp.einsum('rcj,rct->cjt', rising, falling, precision=lax.Precision.HIGHEST)]
    all_to_all x1, waiting for transfers between devices: 8.82 us -> 7.83 us  [local(): lax.all_to_all(product, 'seq', split_axis=0, concat_axis=1, tiled=True)]
  transfers between devices with their start and end apart: 5 -> 5, of which waited for: 5 -> 5; matrix products, arithmetic and copies ran while one was open for 5% -> 7% of each run, Pallas kernels for 0% -> 0%
where the time goes in v21:
time: 80.2 us; the launch traced here: 79.7 us
  waiting for transfers between devices  32.5 us (41%)
  starting transfers between devices  21.4 us (27%)
  matrix products  10.4 us (13%)
  local copies, waits for them, and re-layouts  7.63 us (10%)
  other arithmetic  7.55 us (9%)
    all_to_all x1, waiting for transfers between devices, local(): lax.all_to_all(convolved, 'seq', split_axis=1, concat_axis=0, tiled=True)  10.8 us
    all_to_all x1, waiting for transfers between devices, local(): lax.all_to_all(product, 'seq', split_axis=0, concat_axis=1, tiled=True)  7.83 us
    all_to_all x1, starting transfers between devices, local(): lax.all_to_all(product, 'seq', split_axis=0, concat_axis=1, tiled=True)  6.56 us
    ppermute x1, waiting for transfers between devices, reduce_scatter_chan(): got2 = lax.ppermute(send2, 'chan', [(j, j ^ 2) for j in range(4)])  6.38 us
    ppermute x1, waiting for transfers between devices, local(): lax.ppermute(edge_block, 'seq', [(i, (i + 1) % devices) for i in range(de...  5.96 us
    all_to_all x1, starting transfers between devices, local(): lax.all_to_all(convolved, 'seq', split_axis=1, concat_axis=0, tiled=True)  5.03 us
    dot_general x1, matrix products, local(): lax.dot_general(gated_rows, out_weight, (((0,), (0,)), ((), ())), preferr...  4.68 us
    ppermute x1, starting transfers between devices, reduce_scatter_chan(): got = lax.ppermute(send, 'chan', [(j, j ^ 1) for j in range(4)])  4.62 us
  transfers between devices with their start and end apart: 5, of which 5 were waited for; matrix products, arithmetic and copies ran while one was open for 7% of the time, Pallas kernels for 0%

profile of v21, /device:TPU:1, one launch (start us, length us, event | category | flops | bytes accessed | tf_op | source)
XLA Modules:
  0.0 79.7 jit_solution(3654740387816205476)
XLA Ops:
  0.0 1.4 %slice.78 = bf16[3,1024,2]{2,1,0:T(8,128)(2,1)S(1)} slice(bf16[3,1024,128]{2,1,0:T(8,128)(2,1)} %param.5), slice={[0:3], [0:1024], [126:128]} | slice | bytes 24576 | tf_op jit(solution)/shard_map/slice | solution.py:63
  1.4 0.3 copy.63
  1.7 2.5 %collective-permute-start = (bf16[3,1024,2]{1,2,0:T(2,128)(2,1)S(1)}, bf16[3,1024,2]{1,2,0:T(2,128)(2,1)S(1)}, u32[]{:S(2)}, u32[]{:S(2)}) collective-permute-start(bf16[3,1024,2]{1,2,0:T(2,128)(2,1)S(1)} %copy.63), channel_id=1, source_target_pairs={{0,4},{4,8},{8,12},{12,16},{16,20},{20,24},{24,28},{28,32},{32,36}... | collective-permute-start | bytes 36872 | tf_op jit(solution)/shard_map/ppermute | solution.py:65
  4.3 1.0 %slice_reduce_fusion.5 = (f32[1024]{0:T(1024)S(1)}, f32[1024]{0:T(1024)S(1)}, f32[1024]{0:T(1024)S(1)}, f32[1024]{0:T(1024)S(1)}, f32[1024]{0:T(1024)S(1)}, /*in...) fusion(f32[3,3,1024]{2,1,0:T(4,128)} %param.6), kind=kLoop, calls=%fused_computation.62 | loop fusion | bytes 73728 | tf_op jit(solution)/shard_map/slice | solution.py:71
  5.3 0.8 constant_dynamic-slice_fusion
  6.0 0.1 mul.148
  6.1 0.1 mul.151
  6.2 0.1 mul.154
  6.3 0.1 mul.157
  6.3 0.1 mul.160
  6.4 0.1 mul.163
  6.5 6.0 %collective-permute-done = bf16[3,1024,2]{1,2,0:T(2,128)(2,1)S(1)} collective-permute-done((bf16[3,1024,2]{1,2,0:T(2,128)(2,1)S(1)}, bf16[3,1024,2]{1,2,0:T(2,128)(2,1)S(1)}, u32[]{:S(2)}, u32[]{:S(2)}) %collective-permute-start) | collective-permute-done | bytes 12320 | tf_op jit(solution)/shard_map/ppermute | solution.py:65
  12.5 1.2 %copy.55 = bf16[3,1024,2]{2,1,0:T(8,128)(2,1)} copy(bf16[3,1024,2]{1,0,2:T(4,128)(2,1)S(1)} %copy_select_fusion) | data formatting | bytes 24576 | tf_op jit(solution)/shard_map/jit(_where)/select_n | solution.py:66
  13.7 2.0 %maximum_convert_fusion = f32[3,1024,130]{2,1,0:T(8,128)S(1)} fusion(bf16[3,1024,128]{2,1,0:T(8,128)(2,1)} %param.5, bf16[3,1024,2]{2,1,0:T(8,128)(2,1)} %copy.55), kind=kLoop, calls=%fused_computation.5 | loop fusion | flops 1597440 | bytes 2396160 | tf_op jit(solution)/shard_map/convert_element_type | solution.py:67
  15.7 0.6 fusion.34
  16.3 1.6 %multiply_convert_fusion = bf16[64,16,128]{2,1,0:T(8,128)(2,1)} fusion(f32[64,16,128]{2,1,0:T(8,128)S(1)} %bitcast.69, f32[64,16,128]{2,1,0:T(8,128)S(1)} %bitcast.70, f32[64,16,128]{2,1,0:T(8,128)S(1)} %bitcast.66, f32[64,16,128]{2,1,0:T(8,128)S(1)} %bitcast.67, f32[64,16,128]{2,1,0:T(8,128)S(1)} %bitcast.68, f32[64,16,128]{2,1,0:T(8,128)S(1)} %bitcast.65, ...), kind=kLoop, calls=%fused_computation.25 | loop fusion | flops 1572864 | bytes 3432448 | tf_op jit(solution)/shard_map/convert_element_type | solution.py:76
  17.9 6.6 %all-to-all-start = ((bf16[64,16,128]{2,1,0:T(8,128)(2,1)}), bf16[64,16,128]{2,1,0:T(8,128)(2,1)S(1)}, u32[]{:S(2)}, u32[]{:S(2)}) async-start(bf16[64,16,128]{2,1,0:T(8,128)(2,1)} %multiply_convert_fusion), calls=%async_computation | async-start | bytes 524288 | tf_op jit(solution)/shard_map/all_to_all | solution.py:79
  24.5 0.1 copy.58
  24.6 0.1 copy.57
  24.6 0.1 convert_multiply_fusion
  24.7 2.9 %convolution_select_fusion = f32[16,128,128]{2,1,0:T(8,128)} fusion(pred[128,128]{1,0:T(8,128)(4,1)S(1)} %subtract_compare_fusion, f32[128]{0:T(128)S(1)} %get-tuple-element.27, f32[16,16]{0,1:T(8,128)S(1)} %copy.58, f32[128]{0:T(128)S(1)} %get-tuple-element.26, f32[16,16]{0,1:T(8,128)S(1)} %copy.57), kind=kOutput, calls=%fused_computation.6 | convolution fusion | flops 50692096 | bytes 1068032 | tf_op jit(solution)/shard_map/rcj,rct->cjt/dot_general | solution.py:22
  27.6 7.8 %all-to-all-done = bf16[64,16,128]{2,1,0:T(8,128)(2,1)S(1)} async-done(((bf16[64,16,128]{2,1,0:T(8,128)(2,1)}), bf16[64,16,128]{2,1,0:T(8,128)(2,1)S(1)}, u32[]{:S(2)}, u32[]{:S(2)}) %all-to-all-start) | async-done | bytes 262176 | tf_op jit(solution)/shard_map/all_to_all | solution.py:79
  35.5 0.4 convolution_bitcast_fusion
  36.0 2.6 %fusion.2 = f32[16,16,64]{2,1,0:T(8,128)S(1)} fusion(f32[16,16,64]{2,1,0:T(8,128)S(1)} %copy.59, f32[16,16]{1,0:T(8,128)S(1)} %get-tuple-element.24, f32[64,64]{1,0:T(8,128)S(1)} %convert_multiply_fusion, pred[64,64]{1,0:T(8,128)(4,1)S(1)} %iota_compare_fusion), kind=kLoop, calls=%fused_computation.3 | loop fusion | flops 4177920 | bytes 152576 | tf_op jit(solution)/shard_map/reduce_sum | solution.py:37
  38.6 0.7 fusion.19
  39.3 1.6 %fusion.3 = bf16[16,64,128]{2,1,0:T(8,128)(2,1)S(1)} fusion(f32[16,64,128]{2,1,0:T(8,128)S(1)} %fusion.19, f32[16,128,128]{2,1,0:T(8,128)} %convolution_select_fusion, bf16[64,16,128]{2,1,0:T(8,128)(2,1)S(1)} %all-to-all-done), kind=kOutput, calls=%fused_computation.8 | convolution fusion | flops 100925440 | bytes 2097152 | tf_op jit(solution)/shard_map/cnj,cjt->cnt/dot_general | solution.py:27
  41.0 0.9 %copy.61 = bf16[16,64,128]{2,0,1:T(8,128)(2,1)} copy(bf16[16,64,128]{2,1,0:T(8,128)(2,1)S(1)} %fusion.3) | data formatting | bytes 524288 | tf_op jit(solution)/shard_map/convert_element_type | solution.py:83
  41.8 5.0 %all-to-all-start.1 = ((bf16[16,64,128]{2,0,1:T(8,128)(2,1)}), bf16[16,64,128]{2,0,1:T(8,128)(2,1)S(1)}, u32[]{:S(2)}, u32[]{:S(2)}) async-start(bf16[16,64,128]{2,0,1:T(8,128)(2,1)} %copy.61), calls=%async_computation.1 | async-start | bytes 524288 | tf_op jit(solution)/shard_map/all_to_all | solution.py:84
  46.9 10.8 %all-to-all-done.1 = bf16[16,64,128]{2,0,1:T(8,128)(2,1)S(1)} async-done(((bf16[16,64,128]{2,0,1:T(8,128)(2,1)}), bf16[16,64,128]{2,0,1:T(8,128)(2,1)S(1)}, u32[]{:S(2)}, u32[]{:S(2)}) %all-to-all-start.1) | async-done | bytes 262176 | tf_op jit(solution)/shard_map/all_to_all | solution.py:84
  57.7 0.7 fusion.7
  58.5 4.7 %convolution_convert_fusion = bf16[128,4096]{1,0:T(8,128)(2,1)S(1)} fusion(bf16[1024,128]{1,0:T(8,128)(2,1)S(1)} %fusion.7, bf16[1024,4096]{1,0:T(8,128)(2,1)} %param.9), kind=kOutput, calls=%fused_computation.4 | convolution fusion | flops 1074266112 | bytes 9699328 | tf_op jit(solution)/shard_map/dot_general | solution.py:86
  63.1 0.1 select_bitcast_fusion.3
  63.2 0.1 pad_maximum_fusion
  63.3 4.6 %collective-permute-start.1 = (bf16[2,128,1024]{2,1,0:T(8,128)(2,1)S(1)}, bf16[2,128,1024]{2,1,0:T(8,128)(2,1)S(1)}, u32[]{:S(2)}, u32[]{:S(2)}) collective-permute-start(bf16[2,128,1024]{2,1,0:T(8,128)(2,1)S(1)} %pad_maximum_fusion), channel_id=1, source_target_pairs={{0,1},{1,0},{2,3},{3,2},{4,5},{5,4},{6,7},{7,6},{8,9},{9,8},{10,11... | collective-permute-start | bytes 1572872 | tf_op jit(solution)/shard_map/ppermute | solution.py:51
  67.9 1.5 %collective-permute-done.1 = bf16[2,128,1024]{2,1,0:T(8,128)(2,1)S(1)} collective-permute-done((bf16[2,128,1024]{2,1,0:T(8,128)(2,1)S(1)}, bf16[2,128,1024]{2,1,0:T(8,128)(2,1)S(1)}, u32[]{:S(2)}, u32[]{:S(2)}) %collective-permute-start.1) | collective-permute-done | bytes 524320 | tf_op jit(solution)/shard_map/ppermute | solution.py:51
  69.5 0.2 convert_add_fusion
  69.6 0.1 fusion.12
  69.7 2.7 %collective-permute-start.2 = (bf16[128,1024]{1,0:T(8,128)(2,1)S(1)}, bf16[128,1024]{1,0:T(8,128)(2,1)S(1)}, u32[]{:S(2)}, u32[]{:S(2)}) collective-permute-start(bf16[128,1024]{1,0:T(8,128)(2,1)S(1)} %fusion.12), channel_id=1, source_target_pairs={{0,2},{1,3},{2,0},{3,1},{4,6},{5,7},{6,4},{7,5},{8,10},{9,11},{10,... | collective-permute-start | bytes 786440 | tf_op jit(solution)/shard_map/ppermute | solution.py:56
  72.4 6.4 %collective-permute-done.2 = bf16[128,1024]{1,0:T(8,128)(2,1)S(1)} collective-permute-done((bf16[128,1024]{1,0:T(8,128)(2,1)S(1)}, bf16[128,1024]{1,0:T(8,128)(2,1)S(1)}, u32[]{:S(2)}, u32[]{:S(2)}) %collective-permute-start.2) | collective-permute-done | bytes 262176 | tf_op jit(solution)/shard_map/ppermute | solution.py:56
  78.8 0.1 fusion.13
  78.9 0.8 %copy.62 = bf16[1024,128]{1,0:T(8,128)(2,1)} copy(bf16[1024,128]{0,1:T(8,128)(2,1)S(1)} %fusion.13) | data formatting | bytes 524288 | tf_op jit(solution)/shard_map/transpose | solution.py:57
  (8 shorter events, 0.1 us)
Async XLA Ops:
  1.7 10.7 %collective-permute-start = (bf16[3,1024,2]{1,2,0:T(2,128)(2,1)S(1)}, bf16[3,1024,2]{1,2,0:T(2,128)(2,1)S(1)}, u32[]{:S(2)}, u32[]{:S(2)}) collective-permute-start(bf16[3,1024,2]{1,2,0:T(2,128)(2,1)S(1)} %copy.63), channel_id=1, source_target_pairs={{0,4},{4,8},{8,12},{12,16},{16,20},{20,24},{24,28},{28,32},{32,36}... | collective-permute-start | bytes 36872 | tf_op jit(solution)/shard_map/ppermute | solution.py:65
  17.9 17.6 %all-to-all-start = ((bf16[64,16,128]{2,1,0:T(8,128)(2,1)}), bf16[64,16,128]{2,1,0:T(8,128)(2,1)S(1)}, u32[]{:S(2)}, u32[]{:S(2)}) async-start(bf16[64,16,128]{2,1,0:T(8,128)(2,1)} %multiply_convert_fusion), calls=%async_computation | async-start | bytes 524288 | tf_op jit(solution)/shard_map/all_to_all | solution.py:79
  41.8 15.9 %all-to-all-start.1 = ((bf16[16,64,128]{2,0,1:T(8,128)(2,1)}), bf16[16,64,128]{2,0,1:T(8,128)(2,1)S(1)}, u32[]{:S(2)}, u32[]{:S(2)}) async-start(bf16[16,64,128]{2,0,1:T(8,128)(2,1)} %copy.61), calls=%async_computation.1 | async-start | bytes 524288 | tf_op jit(solution)/shard_map/all_to_all | solution.py:84
  63.3 6.2 %collective-permute-start.1 = (bf16[2,128,1024]{2,1,0:T(8,128)(2,1)S(1)}, bf16[2,128,1024]{2,1,0:T(8,128)(2,1)S(1)}, u32[]{:S(2)}, u32[]{:S(2)}) collective-permute-start(bf16[2,128,1024]{2,1,0:T(8,128)(2,1)S(1)} %pad_maximum_fusion), channel_id=1, source_target_pairs={{0,1},{1,0},{2,3},{3,2},{4,5},{5,4},{6,7},{7,6},{8,9},{9,8},{10,11... | collective-permute-start | bytes 1572872 | tf_op jit(solution)/shard_map/ppermute | solution.py:51
  69.7 9.1 %collective-permute-start.2 = (bf16[128,1024]{1,0:T(8,128)(2,1)S(1)}, bf16[128,1024]{1,0:T(8,128)(2,1)S(1)}, u32[]{:S(2)}, u32[]{:S(2)}) collective-permute-start(bf16[128,1024]{1,0:T(8,128)(2,1)S(1)} %fusion.12), channel_id=1, source_target_pairs={{0,2},{1,3},{2,0},{3,1},{4,6},{5,7},{6,4},{7,5},{8,10},{9,11},{10,... | collective-permute-start | bytes 786440 | tf_op jit(solution)/shard_map/ppermute | solution.py:56

commit v22 on v21

--- a/solution.py
+++ b/solution.py
@@ -60,20 +60,24 @@
 def local(qkv, taps, lifetimes, residues, out_weight):
     chan_local = qkv.shape[1]
     tok_count = qkv.shape[2]
-    edge_block = qkv[:, :, tok_count - 2 :]
     devices = lax.axis_size("seq")
-    wrapped = lax.ppermute(edge_block, "seq", [(i, (i + 1) % devices) for i in range(devices)])
-    earlier = jnp.where(lax.axis_index("seq") == 0, jnp.zeros_like(wrapped), wrapped)
-    extended = jnp.concatenate([earlier, qkv], axis=2).astype(jnp.float32)
+    first_seq = lax.axis_index("seq") == 0
 
-    def filtered(stream):
+    def halo(block):
+        wrapped = lax.ppermute(block, "seq", [(i, (i + 1) % devices) for i in range(devices)])
+        return jnp.where(first_seq, jnp.zeros_like(wrapped), wrapped)
+
+    def short_filter(stream_x, stream_taps, earlier):
+        extended = jnp.concatenate([earlier, stream_x], axis=-1).astype(jnp.float32)
         return (
-            taps[stream, 0, :, None] * extended[stream, :, 2:]
-            + taps[stream, 1, :, None] * extended[stream, :, 1:-1]
-            + taps[stream, 2, :, None] * extended[stream, :, :-2]
+            stream_taps[..., 0, :, None] * extended[..., 2:]
+            + stream_taps[..., 1, :, None] * extended[..., 1:-1]
+            + stream_taps[..., 2, :, None] * extended[..., :-2]
         )
 
-    product = (filtered(1) * filtered(2)).astype(jnp.bfloat16)
+    kv_filtered = short_filter(qkv[1:], taps[1:], halo(qkv[1:, :, tok_count - 2 :]))
+    product = (kv_filtered[0] * kv_filtered[1]).astype(jnp.bfloat16)
+    q_earlier = halo(qkv[0, :, tok_count - 2 :])
     groups = lax.axis_size("seq")
     per_group = chan_local // groups
     pencils = lax.all_to_all(product, "seq", split_axis=0, concat_axis=1, tiled=True)
@@ -82,7 +86,7 @@
     resid_slice = lax.dynamic_slice_in_dim(residues, first_chan, per_group, 1)
     convolved = modal_conv(pencils, life_slice, resid_slice).astype(jnp.bfloat16)
     returned = lax.all_to_all(convolved, "seq", split_axis=1, concat_axis=0, tiled=True)
-    gated_rows = (filtered(0) * returned.astype(jnp.float32)).astype(jnp.bfloat16)
+    gated_rows = (short_filter(qkv[0], taps[0], q_earlier) * returned.astype(jnp.float32)).astype(jnp.bfloat16)
     partial = lax.dot_general(
         gated_rows, out_weight, (((0,), (0,)), ((), ())), preferred_element_type=jnp.float32
     ).astype(jnp.bfloat16)

time: 80.2 us -> 86.8 us (1.082)
  waiting for transfers between devices: 32.5 us -> 38.5 us
  matrix products: 10.4 us -> 8.18 us
  starting transfers between devices: 21.4 us -> 23.5 us
  local copies, waits for them, and re-layouts: 7.63 us -> 8.83 us
    ppermute x1 -> x2, waiting for transfers between devices: 5.96 us -> 13 us  [halo(): lax.ppermute(block, 'seq', [(i, (i + 1) % devices) for i in range(devices)])]
    convert_element_type x3 -> x4, other arithmetic: 4.34 us -> 2.16 us  [the longest x1 0.76 us: local(): product = (kv_filtered[0] * kv_filtered[1]).astype(jnp.bfloat16)]
    squeeze x0 -> x2, local copies, waits for them, and re-layouts: none -> 2.05 us  [the longest x1 1.08 us: local(): q_earlier = halo(qkv[0, :, tok_count - 2:])]
    ppermute x1 -> x2, starting transfers between devices: 2.51 us -> 4.25 us  [halo(): lax.ppermute(block, 'seq', [(i, (i + 1) % devices) for i in range(devices)])]
    add x0 -> x1, other arithmetic: none -> 1.52 us  [short_filter(): stream_taps[..., 0, :, None] * extended[..., 2:]]
    dot_general x1, matrix products: 1.64 us -> 0.42 us  [modal_conv(): inside = jnp.einsum('cnj,cjt->cnt', signal, toeplitz, precision=precise)]
    select_n x1 -> x0, local copies, waits for them, and re-layouts: 1.22 us -> none  [local(): jnp.where(lax.axis_index('seq') == 0, jnp.zeros_like(wrapped), wrapped)]
    all_to_all x1, waiting for transfers between devices: 10.8 us -> 9.66 us  [local(): lax.all_to_all(convolved, 'seq', split_axis=1, concat_axis=0, tiled=True)]
  transfers between devices with their start and end apart: 5 -> 6, of which waited for: 5 -> 5; matrix products, arithmetic and copies ran while one was open for 7% -> 19% of each run, Pallas kernels for 0% -> 0%
where the time goes in v22:
time: 86.8 us; the launch traced here: 86.2 us
  waiting for transfers between devices  38.5 us (44%)
  starting transfers between devices  23.5 us (27%)
  local copies, waits for them, and re-layouts  8.83 us (10%)
  matrix products  8.18 us (9%)
  other arithmetic  6.95 us (8%)
    ppermute x2, waiting for transfers between devices, halo(): lax.ppermute(block, 'seq', [(i, (i + 1) % devices) for i in range(devices)])  13 us
    all_to_all x1, waiting for transfers between devices, local(): lax.all_to_all(convolved, 'seq', split_axis=1, concat_axis=0, tiled=True)  9.66 us
    all_to_all x1, waiting for transfers between devices, local(): lax.all_to_all(product, 'seq', split_axis=0, concat_axis=1, tiled=True)  7.94 us
    ppermute x1, waiting for transfers between devices, reduce_scatter_chan(): got2 = lax.ppermute(send2, 'chan', [(j, j ^ 2) for j in range(4)])  6.37 us
    all_to_all x1, starting transfers between devices, local(): lax.all_to_all(product, 'seq', split_axis=0, concat_axis=1, tiled=True)  6.28 us
    ppermute x1, starting transfers between devices, reduce_scatter_chan(): got = lax.ppermute(send, 'chan', [(j, j ^ 1) for j in range(4)])  5.46 us
    all_to_all x1, starting transfers between devices, local(): lax.all_to_all(convolved, 'seq', split_axis=1, concat_axis=0, tiled=True)  4.8 us
    dot_general x1, matrix products, local(): lax.dot_general(gated_rows, out_weight, (((0,), (0,)), ((), ())), preferr...  4.68 us
  transfers between devices with their start and end apart: 6, of which 5 were waited for; matrix products, arithmetic and copies ran while one was open for 19% of the time, Pallas kernels for 0%

profile of v22, /device:TPU:1, one launch (start us, length us, event | category | flops | bytes accessed | tf_op | source)
XLA Modules:
  0.0 86.2 jit_solution(11977616787652986016)
XLA Ops:
  0.0 1.2 %slice.94 = bf16[2,1024,2]{2,1,0:T(8,128)(2,1)S(1)} slice(bf16[3,1024,128]{2,1,0:T(8,128)(2,1)} %param.5), slice={[1:3], [0:1024], [126:128]} | slice | bytes 16384 | tf_op jit(solution)/shard_map/slice | solution.py:78
  1.3 2.5 %collective-permute-start.1 = (bf16[2,1024,2]{2,1,0:T(8,128)(2,1)S(1)}, bf16[2,1024,2]{2,1,0:T(8,128)(2,1)S(1)}, u32[]{:S(2)}, u32[]{:S(2)}) collective-permute-start(bf16[2,1024,2]{2,1,0:T(8,128)(2,1)S(1)} %slice.94), channel_id=1, source_target_pairs={{0,4},{4,8},{8,12},{12,16},{16,20},{20,24},{24,28},{28,32},{32,36}... | collective-permute-start | bytes 24584 | tf_op jit(solution)/shard_map/ppermute | solution.py:67
  3.8 1.1 %slice_bitcast_fusion.1 = bf16[1024,2]{1,0:T(8,128)(2,1)S(1)} fusion(bf16[3,1024,128]{2,1,0:T(8,128)(2,1)} %param.5), kind=kLoop, calls=%fused_computation.40 | loop fusion | bytes 8192 | tf_op jit(solution)/shard_map/squeeze | solution.py:80
  4.9 1.7 %collective-permute-start = (bf16[1024,2]{1,0:T(8,128)(2,1)S(1)}, bf16[1024,2]{1,0:T(8,128)(2,1)S(1)}, u32[]{:S(2)}, u32[]{:S(2)}) collective-permute-start(bf16[1024,2]{1,0:T(8,128)(2,1)S(1)} %slice_bitcast_fusion.1), channel_id=1, source_target_pairs={{0,4},{4,8},{8,12},{12,16},{16,20},{20,24},{24,28},{28,32},{32,36}... | collective-permute-start | bytes 12296 | tf_op jit(solution)/shard_map/ppermute | solution.py:67
  6.6 0.9 %fusion.34 = (f32[2,1,1024]{2,1,0:T(1,128)S(1)}, f32[2,1,1024]{2,1,0:T(1,128)S(1)}, f32[2,1,1024]{2,1,0:T(1,128)S(1)}) fusion(f32[3,3,1024]{2,1,0:T(4,128)} %param.6), kind=kLoop, calls=%fused_computation.74 | loop fusion | bytes 49152 | tf_op jit(solution)/shard_map/slice | solution.py:73
  7.5 0.1 convert_multiply_fusion
  7.6 0.8 constant_dynamic-slice_fusion
  8.4 1.1 %slice.95 = bf16[2,1024,128]{2,1,0:T(8,128)(2,1)S(1)} slice(bf16[3,1024,128]{2,1,0:T(8,128)(2,1)} %param.5), slice={[1:3], [0:1024], [0:128]} | slice | bytes 1048576 | tf_op jit(solution)/shard_map/slice | solution.py:78
  9.5 13.0 %collective-permute-done.1 = bf16[2,1024,2]{2,1,0:T(8,128)(2,1)S(1)} collective-permute-done((bf16[2,1024,2]{2,1,0:T(8,128)(2,1)S(1)}, bf16[2,1024,2]{2,1,0:T(8,128)(2,1)S(1)}, u32[]{:S(2)}, u32[]{:S(2)}) %collective-permute-start.1) | collective-permute-done | bytes 8224 | tf_op jit(solution)/shard_map/ppermute | solution.py:67
  22.6 0.4 maximum_convert_fusion
  23.0 1.5 %fusion.4 = f32[2,1024,128]{2,1,0:T(8,128)S(1)} fusion(f32[2,1024,130]{2,1,0:T(8,128)S(1)} %maximum_convert_fusion, f32[2,1024]{1,0:T(2,128)S(1)} %get-tuple-element.15, f32[2,1024]{1,0:T(2,128)S(1)} %get-tuple-element.16, f32[2,1024]{1,0:T(2,128)S(1)} %bitcast.47), kind=kLoop, calls=%fused_computation.10 | loop fusion | flops 1310720 | bytes 4218880 | tf_op jit(solution)/shard_map/add | solution.py:73
  24.6 0.8 fusion.6
  25.3 6.3 %all-to-all-start = ((bf16[64,16,128]{2,1,0:T(8,128)(2,1)}), bf16[64,16,128]{2,1,0:T(8,128)(2,1)S(1)}, u32[]{:S(2)}, u32[]{:S(2)}) async-start(bf16[64,16,128]{2,1,0:T(8,128)(2,1)} %bitcast.5), calls=%async_computation | async-start | bytes 524288 | tf_op jit(solution)/shard_map/all_to_all | solution.py:83
  31.6 0.1 copy.22
  31.7 0.1 copy.21
  31.7 1.0 %slice_bitcast_fusion = bf16[1024,128]{1,0:T(8,128)(2,1)S(1)} fusion(bf16[3,1024,128]{2,1,0:T(8,128)(2,1)} %param.5), kind=kLoop, calls=%fused_computation.39 | loop fusion | bytes 524288 | tf_op jit(solution)/shard_map/squeeze | solution.py:89
  32.7 1.9 %convolution_select_fusion = f32[16,128,128]{2,1,0:T(8,128)S(1)} fusion(pred[128,128]{1,0:T(8,128)(4,1)S(1)} %subtract_compare_fusion, f32[128]{0:T(128)S(1)} %get-tuple-element.20, f32[16,16]{0,1:T(8,128)S(1)} %copy.22, f32[128]{0:T(128)S(1)} %get-tuple-element.19, f32[16,16]{0,1:T(8,128)S(1)} %copy.21), kind=kOutput, calls=%fused_computation.5 | convolution fusion | flops 50692096 | bytes 1068032 | tf_op jit(solution)/shard_map/rcj,rct->cjt/dot_general | solution.py:22
  34.7 7.9 %all-to-all-done = bf16[64,16,128]{2,1,0:T(8,128)(2,1)S(1)} async-done(((bf16[64,16,128]{2,1,0:T(8,128)(2,1)}), bf16[64,16,128]{2,1,0:T(8,128)(2,1)S(1)}, u32[]{:S(2)}, u32[]{:S(2)}) %all-to-all-start) | async-done | bytes 262176 | tf_op jit(solution)/shard_map/all_to_all | solution.py:83
  42.6 0.4 convolution_bitcast_fusion
  43.1 2.6 %fusion.2 = f32[16,16,64]{2,1,0:T(8,128)S(1)} fusion(f32[16,16,64]{2,1,0:T(8,128)S(1)} %copy.23, f32[16,16]{1,0:T(8,128)S(1)} %get-tuple-element.17, f32[64,64]{1,0:T(8,128)S(1)} %convert_multiply_fusion, pred[64,64]{1,0:T(8,128)(4,1)S(1)} %iota_compare_fusion), kind=kLoop, calls=%fused_computation.3 | loop fusion | flops 4177920 | bytes 152576 | tf_op jit(solution)/shard_map/reduce_sum | solution.py:37
  45.8 0.7 fusion.19
  46.5 0.4 fusion.3
  46.9 0.9 %copy.25 = bf16[16,64,128]{2,0,1:T(8,128)(2,1)} copy(bf16[16,64,128]{2,1,0:T(8,128)(2,1)S(1)} %fusion.3) | data formatting | bytes 524288 | tf_op jit(solution)/shard_map/convert_element_type | solution.py:87
  47.8 4.8 %all-to-all-start.1 = ((bf16[16,64,128]{2,0,1:T(8,128)(2,1)}), bf16[16,64,128]{2,0,1:T(8,128)(2,1)S(1)}, u32[]{:S(2)}, u32[]{:S(2)}) async-start(bf16[16,64,128]{2,0,1:T(8,128)(2,1)} %copy.25), calls=%async_computation.1 | async-start | bytes 524288 | tf_op jit(solution)/shard_map/all_to_all | solution.py:88
  52.6 0.8 fusion.35
  53.4 0.0 collective-permute-done
  53.5 0.2 maximum_convert_fusion.1
  53.7 9.7 %all-to-all-done.1 = bf16[16,64,128]{2,0,1:T(8,128)(2,1)S(1)} async-done(((bf16[16,64,128]{2,0,1:T(8,128)(2,1)}), bf16[16,64,128]{2,0,1:T(8,128)(2,1)S(1)}, u32[]{:S(2)}, u32[]{:S(2)}) %all-to-all-start.1) | async-done | bytes 262176 | tf_op jit(solution)/shard_map/all_to_all | solution.py:88
  63.4 0.7 fusion.9
  64.1 4.7 %convolution_convert_fusion = bf16[128,4096]{1,0:T(8,128)(2,1)S(1)} fusion(bf16[1024,128]{1,0:T(8,128)(2,1)S(1)} %fusion.9, bf16[1024,4096]{1,0:T(8,128)(2,1)} %param.9), kind=kOutput, calls=%fused_computation.4 | convolution fusion | flops 1074266112 | bytes 9699328 | tf_op jit(solution)/shard_map/dot_general | solution.py:90
  68.8 0.1 select_bitcast_fusion.3
  68.9 0.1 pad_maximum_fusion
  69.0 5.5 %collective-permute-start.2 = (bf16[2,128,1024]{2,1,0:T(8,128)(2,1)S(1)}, bf16[2,128,1024]{2,1,0:T(8,128)(2,1)S(1)}, u32[]{:S(2)}, u32[]{:S(2)}) collective-permute-start(bf16[2,128,1024]{2,1,0:T(8,128)(2,1)S(1)} %pad_maximum_fusion), channel_id=1, source_target_pairs={{0,1},{1,0},{2,3},{3,2},{4,5},{5,4},{6,7},{7,6},{8,9},{9,8},{10,11... | collective-permute-start | bytes 1572872 | tf_op jit(solution)/shard_map/ppermute | solution.py:51
  74.4 1.5 %collective-permute-done.2 = bf16[2,128,1024]{2,1,0:T(8,128)(2,1)S(1)} collective-permute-done((bf16[2,128,1024]{2,1,0:T(8,128)(2,1)S(1)}, bf16[2,128,1024]{2,1,0:T(8,128)(2,1)S(1)}, u32[]{:S(2)}, u32[]{:S(2)}) %collective-permute-start.2) | collective-permute-done | bytes 524320 | tf_op jit(solution)/shard_map/ppermute | solution.py:51
  76.0 0.2 convert_add_fusion
  76.1 0.1 fusion.12
  76.2 2.7 %collective-permute-start.3 = (bf16[128,1024]{1,0:T(8,128)(2,1)S(1)}, bf16[128,1024]{1,0:T(8,128)(2,1)S(1)}, u32[]{:S(2)}, u32[]{:S(2)}) collective-permute-start(bf16[128,1024]{1,0:T(8,128)(2,1)S(1)} %fusion.12), channel_id=1, source_target_pairs={{0,2},{1,3},{2,0},{3,1},{4,6},{5,7},{6,4},{7,5},{8,10},{9,11},{10,... | collective-permute-start | bytes 786440 | tf_op jit(solution)/shard_map/ppermute | solution.py:56
  78.9 6.4 %collective-permute-done.3 = bf16[128,1024]{1,0:T(8,128)(2,1)S(1)} collective-permute-done((bf16[128,1024]{1,0:T(8,128)(2,1)S(1)}, bf16[128,1024]{1,0:T(8,128)(2,1)S(1)}, u32[]{:S(2)}, u32[]{:S(2)}) %collective-permute-start.3) | collective-permute-done | bytes 262176 | tf_op jit(solution)/shard_map/ppermute | solution.py:56
  85.3 0.1 fusion.13
  85.4 0.8 copy.26
  (11 shorter events, 0.2 us)
Async XLA Ops:
  1.3 21.3 %collective-permute-start.1 = (bf16[2,1024,2]{2,1,0:T(8,128)(2,1)S(1)}, bf16[2,1024,2]{2,1,0:T(8,128)(2,1)S(1)}, u32[]{:S(2)}, u32[]{:S(2)}) collective-permute-start(bf16[2,1024,2]{2,1,0:T(8,128)(2,1)S(1)} %slice.94), channel_id=1, source_target_pairs={{0,4},{4,8},{8,12},{12,16},{16,20},{20,24},{24,28},{28,32},{32,36}... | collective-permute-start | bytes 24584 | tf_op jit(solution)/shard_map/ppermute | solution.py:67
  4.9 48.6 %collective-permute-start = (bf16[1024,2]{1,0:T(8,128)(2,1)S(1)}, bf16[1024,2]{1,0:T(8,128)(2,1)S(1)}, u32[]{:S(2)}, u32[]{:S(2)}) collective-permute-start(bf16[1024,2]{1,0:T(8,128)(2,1)S(1)} %slice_bitcast_fusion.1), channel_id=1, source_target_pairs={{0,4},{4,8},{8,12},{12,16},{16,20},{20,24},{24,28},{28,32},{32,36}... | collective-permute-start | bytes 12296 | tf_op jit(solution)/shard_map/ppermute | solution.py:67
  25.3 17.3 %all-to-all-start = ((bf16[64,16,128]{2,1,0:T(8,128)(2,1)}), bf16[64,16,128]{2,1,0:T(8,128)(2,1)S(1)}, u32[]{:S(2)}, u32[]{:S(2)}) async-start(bf16[64,16,128]{2,1,0:T(8,128)(2,1)} %bitcast.5), calls=%async_computation | async-start | bytes 524288 | tf_op jit(solution)/shard_map/all_to_all | solution.py:83
  47.8 15.6 %all-to-all-start.1 = ((bf16[16,64,128]{2,0,1:T(8,128)(2,1)}), bf16[16,64,128]{2,0,1:T(8,128)(2,1)S(1)}, u32[]{:S(2)}, u32[]{:S(2)}) async-start(bf16[16,64,128]{2,0,1:T(8,128)(2,1)} %copy.25), calls=%async_computation.1 | async-start | bytes 524288 | tf_op jit(solution)/shard_map/all_to_all | solution.py:88
  69.0 7.0 %collective-permute-start.2 = (bf16[2,128,1024]{2,1,0:T(8,128)(2,1)S(1)}, bf16[2,128,1024]{2,1,0:T(8,128)(2,1)S(1)}, u32[]{:S(2)}, u32[]{:S(2)}) collective-permute-start(bf16[2,128,1024]{2,1,0:T(8,128)(2,1)S(1)} %pad_maximum_fusion), channel_id=1, source_target_pairs={{0,1},{1,0},{2,3},{3,2},{4,5},{5,4},{6,7},{7,6},{8,9},{9,8},{10,11... | collective-permute-start | bytes 1572872 | tf_op jit(solution)/shard_map/ppermute | solution.py:51
  76.2 9.1 %collective-permute-start.3 = (bf16[128,1024]{1,0:T(8,128)(2,1)S(1)}, bf16[128,1024]{1,0:T(8,128)(2,1)S(1)}, u32[]{:S(2)}, u32[]{:S(2)}) collective-permute-start(bf16[128,1024]{1,0:T(8,128)(2,1)S(1)} %fusion.12), channel_id=1, source_target_pairs={{0,2},{1,3},{2,0},{3,1},{4,6},{5,7},{6,4},{7,5},{8,10},{9,11},{10,... | collective-permute-start | bytes 786440 | tf_op jit(solution)/shard_map/ppermute | solution.py:56
